TPU v7x, 512 devices: a whole 4x8x8 slice. The times are simulated.
512 devices in a mesh: req: 64 (over z, x, core), tp: 8 (over y).
Axes of the slice: x: 4, y: 8, z: 8, core: 2. Of those that a mesh axis runs over, the one named last changes fastest.
Arguments:
- gate_in: bfloat16 [2, 4096, 4096], P(None, 'req', 'tp'), may hold values from -6 to 6
- mix_in: bfloat16 [2, 4096, 4096], P(None, 'req', 'tp'), may hold values from -6 to 6
- keys_in: bfloat16 [2, 4096, 256], P(None, 'req'), may hold values from -6 to 6
- step_in: bfloat16 [2, 4096, 64], P(None, 'req', 'tp'), may hold values from -6 to 6
- resid_in: bfloat16 [2, 4096, 2048], P(None, 'req', 'tp'), may hold values from -12 to 12
- kernel_mix: float32 [2, 4, 4096], P(None, None, 'tp'), may hold values from -3 to 3
- kernel_keys: float32 [2, 4, 256], replicated, may hold values from -3 to 3
- step_bias: float32 [2, 64], P(None, 'tp'), may hold values from -4 to 0
- decay_rate: float32 [2, 64], P(None, 'tp'), may hold values from 0.02 to 2
- skip_gain: float32 [2, 64], P(None, 'tp'), may hold values from 0.5 to 1.5
- norm_gain: float32 [2, 4096], P(None, 'tp'), may hold values from 0.5 to 1.5
- final_gain: float32 [2, 2048], replicated, may hold values from 0.5 to 1.5
- out_weight: bfloat16 [2, 4096, 2048], P(None, 'tp', 'req'), may hold values from -0.09375 to 0.09375
- head_weight: bfloat16 [2, 25600, 2048], P(None, 'req'), may hold values from -8 to 8
- history_mix: bfloat16 [2, 192, 3, 4096], P(None, 'req', None, 'tp'), may hold values from -6 to 6
- history_keys: bfloat16 [2, 192, 3, 256], P(None, 'req'), may hold values from -6 to 6
- start_state: bfloat16 [2, 192, 4096, 128], P(None, 'req', 'tp'), may hold values from -0.59765625 to 0.59765625
- lengths: int32 [64, 3], P('req'), may hold values from 1 to 32, 64 in all within a row
- continued: int32 [64, 3], P('req'), may hold values 0 or 1
- targets: int32 [4096], P('req'), may hold values from 0 to 25599
- score_flag: int32 [4096], P('req'), may hold values 0 or 1
Outputs:
- logprobs: float32 [2, 4096], P(None, ('req', 'tp'))
Inputs may be any that keep to these rules, and one draw needn't show every extreme that they name: The 3 lengths of a row fill its 64 slots exactly.
All inputs are finite; a program needn't handle non-finite values. No bound on the sum of `continued` or of `score_flag` on one device may be relied on, other than what follows from the above.
Results may differ from a plain program's by a relative error of at most 0.00075.
Values may be sent and summed in bfloat16 or wider, within the bound.
No kernel may reach another device: no remote copies, remote signals or barrier semaphores. Data moves between devices by JAX's collectives and lax.ppermute only.
A program may use at most 64 MiB of HBM per device.

v0:
```python
import jax
import jax.numpy as jnp
from jax import lax
from jax.sharding import PartitionSpec as P

EPSILON = 1e-05
PRECISE = lax.Precision.HIGHEST


def merged_2(part, axis, combine):
    gathered = jax.tree.map(lambda a: lax.all_gather(a, axis), part)

    def take(source):
        return jax.tree.map(lambda a: lax.dynamic_index_in_dim(a, source, 0, False), gathered)

    return lax.fori_loop(
        1, lax.axis_size(axis), lambda source, state: combine(state, take(source)), take(0)
    )


def request_layout(lengths, step_count):
    starts = jnp.cumsum(lengths) - lengths
    time_index = jnp.arange(step_count, dtype=jnp.int32)
    segment = jnp.sum((time_index[:, None] >= starts[None, 1:]).astype(jnp.int32), axis=1)
    member = segment[:, None] == jnp.arange(lengths.shape[0], dtype=jnp.int32)[None, :]
    first_step = jnp.sum(jnp.where(member, starts[None, :], 0), axis=1)
    return (starts, segment, member, time_index - first_step)


def causal_conv(stream, kernel, history, member, offset):
    tap_count = kernel.shape[0]
    history_len = tap_count - 1
    current = stream.astype(jnp.float32)
    member_bf = member.astype(jnp.bfloat16)
    slot_values = [
        jnp.dot(member_bf, history[:, slot_index, :], preferred_element_type=jnp.float32)
        for slot_index in range(history_len)
    ]
    output = kernel[history_len][None, :] * current
    for lag_steps in range(1, tap_count):
        shifted = jnp.concatenate(
            [jnp.zeros((lag_steps, current.shape[1]), current.dtype), current[:-lag_steps]], axis=0
        )
        earlier = jnp.zeros_like(current)
        for slot_index in range(history_len):
            earlier = earlier + jnp.where(
                (offset - lag_steps == slot_index - history_len)[:, None],
                slot_values[slot_index],
                0.0,
            )
        output = output + kernel[history_len - lag_steps][None, :] * jnp.where(
            (offset >= lag_steps)[:, None], shifted, earlier
        )
    return jax.nn.silu(output)


def mixer_block(
    gate_rows,
    mix_rows,
    keys_rows,
    step_raw,
    kernel_mix,
    kernel_keys,
    step_bias,
    decay_rate,
    skip_gain,
    history_mix,
    history_keys,
    start_state,
    lengths,
    continued,
):
    step_count = gate_rows.shape[0]
    head_count = step_raw.shape[1]
    inner_width = mix_rows.shape[1]
    head_size = inner_width // head_count
    states = start_state.shape[2]
    starts, segment, member, offset = request_layout(lengths, step_count)
    keep_state = continued.astype(jnp.bfloat16)
    mixed = causal_conv(
        mix_rows, kernel_mix, history_mix * keep_state[:, None, None], member, offset
    )
    projected = causal_conv(
        keys_rows, kernel_keys, history_keys * keep_state[:, None, None], member, offset
    )
    inject = projected[:, :states]
    readout = projected[:, states:]
    step_size = jax.nn.softplus(step_raw.astype(jnp.float32) + step_bias[None, :])
    log_decay = -step_size * decay_rate[None, :]
    running = jnp.cumsum(log_decay, axis=0)
    time_index = jnp.arange(step_count, dtype=jnp.int32)
    causal = (segment[:, None] == segment[None, :]) & (time_index[:, None] >= time_index[None, :])
    spread = jnp.minimum(running[:, None, :] - running[None, :, :], 0.0)
    transfer = jnp.where(causal[:, :, None], jnp.exp(spread), 0.0)
    intersection = jnp.dot(readout, inject.T, precision=PRECISE)
    kernel_full = transfer * intersection[:, :, None]
    values = mixed.reshape(step_count, head_count, head_size)
    output = jnp.einsum(
        "tsh,shp->thp", kernel_full, step_size[:, :, None] * values, precision=PRECISE
    )
    before = jnp.take(running - log_decay, starts, axis=0)
    member_float = member.astype(jnp.float32)
    entry_level = jnp.dot(member_float, before, precision=PRECISE)
    carried = jnp.exp(jnp.minimum(running - entry_level, 0.0))
    initial = start_state.astype(jnp.float32) * keep_state.astype(jnp.float32)[:, None, None]
    readings = jnp.einsum("tn,rcn->trc", readout, initial, precision=PRECISE)
    chosen = jnp.sum(member_float[:, :, None] * readings, axis=1).reshape(
        step_count, head_count, head_size
    )
    output = output + carried[:, :, None] * chosen + skip_gain[None, :, None] * values
    return output.reshape(step_count, inner_width) * jax.nn.silu(gate_rows.astype(jnp.float32))


def head_scores(head_weight, vocab_start, piece_rows):
    rows_hidden, rows_target = piece_rows
    logits = jnp.einsum(
        "mnd,mvd->mnv", rows_hidden, head_weight, preferred_element_type=jnp.float32
    )
    peak_logit = jnp.max(logits, axis=2)
    spread = jnp.sum(jnp.exp(logits - peak_logit[:, :, None]), axis=2)
    local_id = rows_target[0] - vocab_start
    matches = jnp.arange(head_weight.shape[1], dtype=jnp.int32)[None, :] == local_id[:, None]
    picked = jnp.sum(jnp.where(matches[None, :, :], logits, 0.0), axis=2)
    return (peak_logit, spread, picked)


def fold_stats(first_stats, second_stats):
    peak_logit = jnp.maximum(first_stats[0], second_stats[0])
    spread = first_stats[1] * jnp.exp(first_stats[0] - peak_logit) + second_stats[1] * jnp.exp(
        second_stats[0] - peak_logit
    )
    return (peak_logit, spread, first_stats[2] + second_stats[2])


def local(
    gate_in,
    mix_in,
    keys_in,
    step_in,
    resid_in,
    kernel_mix,
    kernel_keys,
    step_bias,
    decay_rate,
    skip_gain,
    norm_gain,
    final_gain,
    out_weight,
    head_weight,
    history_mix,
    history_keys,
    start_state,
    lengths,
    continued,
    targets,
    score_flag,
):
    groups = lax.axis_size("tp")
    shards = lax.axis_size("req")
    lane_index = lax.axis_index("tp")
    shard_index = lax.axis_index("req")
    models = gate_in.shape[0]
    step_count = gate_in.shape[1]
    row_count = step_count // groups
    gated = jnp.stack(
        [
            mixer_block(
                gate_in[model_index],
                mix_in[model_index],
                keys_in[model_index],
                step_in[model_index],
                kernel_mix[model_index],
                kernel_keys[model_index],
                step_bias[model_index],
                decay_rate[model_index],
                skip_gain[model_index],
                history_mix[model_index],
                history_keys[model_index],
                start_state[model_index],
                lengths[0],
                continued[0],
            )
            for model_index in range(models)
        ]
    )
    squares = lax.psum(jnp.sum(gated * gated, axis=2), "tp")
    inner_width = gated.shape[2] * groups
    normed = (
        gated * lax.rsqrt(squares / inner_width + EPSILON)[:, :, None] * norm_gain[:, None, :]
    ).astype(jnp.bfloat16)
    partial_out = jnp.einsum(
        "mtc,mcd->mtd",
        normed,
        lax.all_gather(out_weight, "req", axis=2, tiled=True),
        preferred_element_type=jnp.float32,
    )
    update = lax.psum_scatter(partial_out, "tp", scatter_dimension=2, tiled=True)
    hidden = (resid_in.astype(jnp.float32) + update).astype(jnp.bfloat16)
    part_width = hidden.shape[2]
    full_width = part_width * groups
    vocab_part = head_weight.shape[1]
    hidden_float = hidden.astype(jnp.float32)
    final_squares = lax.psum(jnp.sum(hidden_float * hidden_float, axis=2), "tp")
    gain_part = lax.dynamic_slice_in_dim(final_gain, lane_index * part_width, part_width, 1)
    final_rows = (
        hidden_float
        * lax.rsqrt(final_squares / full_width + EPSILON)[:, :, None]
        * gain_part[:, None, :]
    ).astype(jnp.bfloat16)
    every_rows, every_target = (
        lax.all_gather(final_rows, "req", axis=1, tiled=True),
        lax.all_gather(targets, "req", axis=0, tiled=True),
    )
    blocks = every_rows.reshape(models, shards, groups, row_count, part_width)
    regrouped = lax.all_to_all(blocks, "tp", split_axis=2, concat_axis=4, tiled=True).reshape(
        models, shards * row_count, full_width
    )
    target_rows = lax.dynamic_slice_in_dim(
        every_target.reshape(shards, groups, row_count), lane_index, 1, 1
    ).reshape(1, shards * row_count)
    statistics = head_scores(head_weight, shard_index * vocab_part, (regrouped, target_rows))
    merged = merged_2(statistics, "req", fold_stats)
    peak_logit = lax.dynamic_slice_in_dim(merged[0], shard_index * row_count, row_count, 1)
    spread = lax.dynamic_slice_in_dim(merged[1], shard_index * row_count, row_count, 1)
    picked = lax.dynamic_slice_in_dim(merged[2], shard_index * row_count, row_count, 1)
    scored_rows = lax.dynamic_slice_in_dim(score_flag, lane_index * row_count, row_count, 0).astype(
        jnp.float32
    )
    return (picked - (peak_logit + jnp.log(spread))) * scored_rows[None, :]


def solution(mesh):
    placed = (
        P(None, "req", "tp"),
        P(None, "req", "tp"),
        P(None, "req", None),
        P(None, "req", "tp"),
        P(None, "req", "tp"),
        P(None, None, "tp"),
        P(),
        P(None, "tp"),
        P(None, "tp"),
        P(None, "tp"),
        P(None, "tp"),
        P(),
        P(None, "tp", "req"),
        P(None, "req", None),
        P(None, "req", None, "tp"),
        P(None, "req", None, None),
        P(None, "req", "tp", None),
        P("req", None),
        P("req", None),
        P("req"),
        P("req"),
    )
    return jax.shard_map(
        local, mesh=mesh, in_specs=placed, out_specs=P(None, ("req", "tp")), check_vma=False
    )
```

profile of v0, /device:TPU:1, one launch (start us, length us, event | category | flops | bytes accessed | tf_op | source)
XLA Modules:
  0.0 702.1 jit_solution(15884320731154681148)
XLA Ops:
  7.3 1.0 reduce-window.4
  8.3 1.2 compare_and_fusion
  10.1 0.9 slice_convert_fusion.1
  13.2 1.2 fusion.152
  14.4 0.8 fusion.160
  16.5 1.5 fusion.161
  18.7 1.8 divide_multiply_fusion
  20.5 1.0 copy.111
  21.6 1.5 fusion.165
  23.1 0.8 fusion.80
  24.8 0.8 slice_convert_fusion.3
  27.5 1.1 divide_multiply_fusion.2
  29.2 2.7 fusion.3
  31.9 1.7 copy.105
  33.7 1.4 slice_bitcast_fusion.19
  35.0 0.8 negate_multiply_fusion.1
  36.5 1.4 reduce_window_sum.25
  37.9 0.8 copy.89
  38.7 1.4 compare_select_fusion.1
  40.8 1.4 reduce_window_sum.26
  42.2 0.8 copy.100
  43.1 1.4 compare_select_fusion
  45.8 1.9 gather_fusion.1
  47.7 1.2 slice_bitcast_fusion.18
  48.9 0.8 fusion.74
  49.7 0.9 fusion.9
  50.7 1.0 fusion.68
  51.7 2.3 fusion.5
  54.0 1.7 copy.107
  55.7 0.9 fusion.119
  56.6 0.9 fusion.122
  57.5 1.2 divide_multiply_fusion.3
  59.3 2.7 fusion.2
  62.0 1.0 copy.95
  63.0 0.9 fusion.91
  63.9 0.9 fusion.94
  64.8 2.1 divide_multiply_fusion.1
  67.0 1.7 copy.110
  68.7 1.4 copy.93
  70.1 2.0 gather_fusion
  72.1 0.9 fusion.11
  73.0 1.0 fusion.70
  74.0 2.4 fusion.7
  76.4 1.8 copy.97
  78.1 1.1 fusion.33
  79.4 15.2 %psum.14 = f32[2,64]{1,0:T(2,128)S(1)} all-reduce(f32[2,64]{1,0:T(2,128)S(1)} %multiply_reduce_fusion), channel_id=1, replica_groups=mesh['req'=64,'tp'=8] {'tp'}, use_global_device_ids=true, to_apply=%region_8.10 | all-reduce | flops 128 | bytes 1024 | tf_op jit(solution)/shard_map/psum | solution.py:186
  94.6 7.0 all-gather.9.cloned.1.call-done
  101.6 4.6 fusion.41
  107.0 34.2 %reduce-scatter.2.cloned.1.call-done = f32[2,64,256]{2,1,0:T(8,128)} async-done(((f32[2,64,2048]{2,1,0:T(8,128)}), f32[2,64,256]{2,1,0:T(8,128)}) %reduce-scatter.2.cloned.1.call-update) | async-done | bytes 131088 | tf_op jit(solution)/shard_map/reduce_scatter | solution.py:197
  141.2 1.0 fusion.38
  142.2 12.1 %psum.15 = f32[2,64]{1,0:T(2,128)S(1)} all-reduce(f32[2,64]{1,0:T(2,128)S(1)} %fusion.38), channel_id=1, replica_groups=mesh['req'=64,'tp'=8] {'tp'}, use_global_device_ids=true, to_apply=%region_11.13 | all-reduce | flops 128 | bytes 1024 | tf_op jit(solution)/shard_map/psum | solution.py:203
  154.3 1.6 fusion.40
  156.0 93.6 %all-gather.11.cloned.1.call-done = bf16[2,4096,256]{2,1,0:T(8,128)(2,1)} async-done(((bf16[2,64,256]{2,1,0:T(8,128)(2,1)}), bf16[2,4096,256]{2,1,0:T(8,128)(2,1)}) %all-gather.11.cloned.1.call-update) | async-done | bytes 4194320 | tf_op jit(solution)/shard_map/all_gather | solution.py:211
  249.5 4.6 copy.108
  254.1 6.6 all-to-all-start
  260.7 1.3 dynamic-slice
  263.1 245.8 %all-reduce.13 = s32[64,8,8]{2,1,0:T(8,128)} all-reduce(s32[64,8,8]{2,1,0:T(8,128)S(1)} %reshape.343), channel_id=1, replica_groups=mesh['req'=64,'tp'=8] {'req'}, use_global_device_ids=true, to_apply=%add.12 | all-reduce | flops 4096 | bytes 32768
  508.9 1.1 subtract_reduce_fusion
  511.0 2.8 copy.109
  513.7 2.0 fusion.168
  516.1 46.6 %all-gather.5 = f32[64,2,512]{2,1,0:T(2,128)S(1)} all-gather(f32[1,2,512]{2,1,0:T(2,128)S(1)} %bitcast.251), channel_id=4, replica_groups=mesh['req'=64,'tp'=8] {'req'}, dimensions={0}, use_global_device_ids=true | all-gather | bytes 266240 | tf_op jit(solution)/shard_map/all_gather | solution.py:11
  562.7 44.1 %all-gather.4 = f32[64,2,512]{2,1,0:T(2,128)S(1)} all-gather(f32[1,2,512]{2,1,0:T(2,128)S(1)} %bitcast.250), channel_id=3, replica_groups=mesh['req'=64,'tp'=8] {'req'}, dimensions={0}, use_global_device_ids=true | all-gather | bytes 266240 | tf_op jit(solution)/shard_map/all_gather | solution.py:11
  606.8 41.2 %all-gather.3 = f32[64,2,512]{2,1,0:T(2,128)S(1)} all-gather(f32[1,2,512]{2,1,0:T(2,128)S(1)} %bitcast.249), channel_id=2, replica_groups=mesh['req'=64,'tp'=8] {'req'}, dimensions={0}, use_global_device_ids=true | all-gather | bytes 266240 | tf_op jit(solution)/shard_map/all_gather | solution.py:11
  648.7 46.1 %while.19 = (s32[]{:T(128)}, f32[2,512]{1,0:T(2,128)S(1)}, f32[2,512]{1,0:T(2,128)S(1)}, f32[2,512]{1,0:T(2,128)S(1)}, f32[64,2,512]{2,1,0:T(2,128)}, /*index=5*...) while((s32[]{:T(128)}, f32[2,512]{1,0:T(2,128)S(1)}, ...), condition=%wide.region_16.18_spmd, body=%wide.region_15.17_spmd.sunk | while | flops 7173 | bytes 37011 | solution.py:16
  (160 shorter events, 61.5 us)
Async XLA Ops:
  6.5 507.2 %copy-start = (bf16[2,400,2048]{2,1,0:T(8,128)(2,1)S(1)}, bf16[2,400,2048]{2,1,0:T(8,128)(2,1)}, u32[]{:S(2)}) copy-start(bf16[2,400,2048]{2,1,0:T(8,128)(2,1)} %param.38) | copy-start | bytes 9830404
  6.5 16.5 %copy-start.6 = (bf16[2,3,3,256]{3,0,2,1:T(2,128)(2,1)S(1)}, bf16[2,3,3,256]{3,0,2,1:T(2,128)(2,1)}, u32[]{:S(2)}) copy-start(bf16[2,3,3,256]{3,0,2,1:T(2,128)(2,1)} %param.40) | copy-start | bytes 27652
  6.5 95.1 %all-gather.9.cloned.1.call-start = ((), (), s32[]{:S(2)}) async-start(), calls=%async_computation.2 | async-start | bytes 4259840 | tf_op jit(solution)/shard_map/all_gather | solution.py:194
  7.3 133.9 %reduce-scatter.2.cloned.1.call-start = ((), (), s32[]{:S(2)}) async-start(), calls=%async_computation.3 | async-start | bytes 1179648 | tf_op jit(solution)/shard_map/reduce_scatter | solution.py:197
  9.5 5.8 copy-start.11
  13.2 20.4 %copy-start.5 = (s32[64]{0:T(128)}, s32[64]{0:T(128)S(1)}, u32[]{:S(2)}) copy-start(s32[64]{0:T(128)S(1)} %fusion.132) | copy-start | bytes 772
  14.4 1.6 copy-start.9
  18.0 0.5 copy-start.12
  18.0 0.5 copy-start.13
  18.0 0.5 copy-start.14
  18.0 0.6 copy-start.15
  18.1 0.6 copy-start.16
  18.1 0.6 copy-start.17
  18.1 0.6 copy-start.18
  18.1 0.6 copy-start.19
  18.1 0.6 copy-start.20
  18.1 0.6 copy-start.21
  18.1 0.6 copy-start.22
  18.1 0.6 copy-start.23
  21.6 7.1 %copy-start.10 = (f32[64,3]{0,1:T(4,128)}, f32[64,3]{0,1:T(4,128)S(1)}, u32[]{:S(2)}) copy-start(f32[64,3]{0,1:T(4,128)S(1)} %fusion.127) | copy-start | bytes 2308
  28.6 0.6 copy-start.3
  45.8 1.9 copy-start.8
  54.0 20.0 %copy-start.7 = (f32[64,8]{0,1:T(8,128)S(1)}, f32[64,8]{0,1:T(8,128)}, u32[]{:S(2)}) copy-start(f32[64,8]{0,1:T(8,128)} %get-tuple-element.246) | copy-start | bytes 6148
  58.7 0.6 copy-start.4
  106.2 143.3 %all-gather.11.cloned.1.call-start = ((), (), s32[]{:S(2)}) async-start(), calls=%async_computation.4 | async-start | bytes 4259840 | tf_op jit(solution)/shard_map/all_gather | solution.py:211
  254.1 8.6 %copy-start.24 = (s32[64]{0:T(128)S(1)}, s32[64]{0:T(128)}, u32[]{:S(2)}) copy-start(s32[64]{0:T(128)} %param.44) | copy-start | bytes 772
  254.1 256.9 %all-to-all-start = ((bf16[2,64,8,8,256]{4,3,1,0,2:T(8,128)(2,1)}), bf16[2,64,8,8,256]{4,3,1,0,2:T(8,128)(2,1)}, u32[]{:S(2)}, u32[]{:S(2)}) async-start(bf16[2,64,8,8,256]{4,3,1,0,2:T(8,128)(2,1)} %copy.108), calls=%async_computation.1 | async-start | bytes 8388608 | tf_op jit(solution)/shard_map/all_to_all | solution.py:215
  606.8 41.2 %copy-start.1 = (f32[64,2,512]{2,1,0:T(2,128)}, f32[64,2,512]{2,1,0:T(2,128)S(1)}, u32[]{:S(2)}) copy-start(f32[64,2,512]{2,1,0:T(2,128)S(1)} %all-gather.4) | copy-start | bytes 786436
  648.0 0.7 copy-start.2
Sparse Core Ops, SparseCore 0:
  10.8 90.8 all-gather.8
  106.3 34.8 reduce-scatter.1
  156.1 93.3 all-gather.10
where the time goes:
time: 708 us; the launch traced here: 702 us
  blocking collectives  405 us (57%)
  waiting for transfers between devices  136 us (19%)
  other arithmetic  66.6 us (9%)
  local copies, waits for them, and re-layouts  42 us (6%)
  matrix products  31 us (4%)
  between operations  14.1 us (2%)
    unnamed x1, blocking collectives  246 us
    all_gather x3, blocking collectives, merged_2(): gathered = jax.tree.map(lambda a: lax.all_gather(a, axis), part)  132 us
    all_gather x1, waiting for transfers between devices, local(): lax.all_gather(final_rows, 'req', axis=1, tiled=True)  93.6 us
    add x63, other arithmetic, fold_stats(): first_stats[1] * jnp.exp(first_stats[0] - peak_logit)  45.2 us
    reduce_scatter x1, waiting for transfers between devices, local(): lax.psum_scatter(partial_out, 'tp', scatter_dimension=2, tiled=True)  34.2 us
    psum x1, blocking collectives, local(): squares = lax.psum(jnp.sum(gated * gated, axis=2), 'tp')  15.2 us
  transfers between devices with their start and end apart: 4, of which 3 were waited for; matrix products, arithmetic and copies ran while one was open for 11% of the time, Pallas kernels for 0%

commit v1 on v0

--- a/solution.py
+++ b/solution.py
@@ -111,25 +111,20 @@
     return output.reshape(step_count, inner_width) * jax.nn.silu(gate_rows.astype(jnp.float32))
 
 
-def head_scores(head_weight, vocab_start, piece_rows):
-    rows_hidden, rows_target = piece_rows
+def head_scores(head_weight, vocab_start, rows_hidden, rows_target):
     logits = jnp.einsum(
         "mnd,mvd->mnv", rows_hidden, head_weight, preferred_element_type=jnp.float32
     )
     peak_logit = jnp.max(logits, axis=2)
     spread = jnp.sum(jnp.exp(logits - peak_logit[:, :, None]), axis=2)
-    local_id = rows_target[0] - vocab_start
+    local_id = rows_target - vocab_start
     matches = jnp.arange(head_weight.shape[1], dtype=jnp.int32)[None, :] == local_id[:, None]
     picked = jnp.sum(jnp.where(matches[None, :, :], logits, 0.0), axis=2)
-    return (peak_logit, spread, picked)
-
-
-def fold_stats(first_stats, second_stats):
-    peak_logit = jnp.maximum(first_stats[0], second_stats[0])
-    spread = first_stats[1] * jnp.exp(first_stats[0] - peak_logit) + second_stats[1] * jnp.exp(
-        second_stats[0] - peak_logit
-    )
-    return (peak_logit, spread, first_stats[2] + second_stats[2])
+    return jnp.stack([peak_logit, spread, picked])
+
+
+STATS_BY_ALL_TO_ALL = True
+DIGIT = 256
 
 
 def local(
@@ -194,35 +189,50 @@
         lax.all_gather(out_weight, "req", axis=2, tiled=True),
         preferred_element_type=jnp.float32,
     )
-    update = lax.psum_scatter(partial_out, "tp", scatter_dimension=2, tiled=True)
-    hidden = (resid_in.astype(jnp.float32) + update).astype(jnp.bfloat16)
-    part_width = hidden.shape[2]
-    full_width = part_width * groups
-    vocab_part = head_weight.shape[1]
+    update = lax.psum_scatter(partial_out, "tp", scatter_dimension=1, tiled=True)
+    resid_rows = lax.all_to_all(resid_in, "tp", split_axis=1, concat_axis=2, tiled=True)
+    hidden = (resid_rows.astype(jnp.float32) + update).astype(jnp.bfloat16)
+    full_width = hidden.shape[2]
     hidden_float = hidden.astype(jnp.float32)
-    final_squares = lax.psum(jnp.sum(hidden_float * hidden_float, axis=2), "tp")
-    gain_part = lax.dynamic_slice_in_dim(final_gain, lane_index * part_width, part_width, 1)
+    final_squares = jnp.sum(hidden_float * hidden_float, axis=2)
     final_rows = (
         hidden_float
         * lax.rsqrt(final_squares / full_width + EPSILON)[:, :, None]
-        * gain_part[:, None, :]
+        * final_gain[:, None, :]
     ).astype(jnp.bfloat16)
-    every_rows, every_target = (
-        lax.all_gather(final_rows, "req", axis=1, tiled=True),
-        lax.all_gather(targets, "req", axis=0, tiled=True),
-    )
-    blocks = every_rows.reshape(models, shards, groups, row_count, part_width)
-    regrouped = lax.all_to_all(blocks, "tp", split_axis=2, concat_axis=4, tiled=True).reshape(
-        models, shards * row_count, full_width
-    )
-    target_rows = lax.dynamic_slice_in_dim(
-        every_target.reshape(shards, groups, row_count), lane_index, 1, 1
-    ).reshape(1, shards * row_count)
-    statistics = head_scores(head_weight, shard_index * vocab_part, (regrouped, target_rows))
-    merged = merged_2(statistics, "req", fold_stats)
-    peak_logit = lax.dynamic_slice_in_dim(merged[0], shard_index * row_count, row_count, 1)
-    spread = lax.dynamic_slice_in_dim(merged[1], shard_index * row_count, row_count, 1)
-    picked = lax.dynamic_slice_in_dim(merged[2], shard_index * row_count, row_count, 1)
+    own_target = lax.dynamic_slice_in_dim(targets, lane_index * row_count, row_count, 0)
+    high_digit = (own_target // DIGIT).astype(jnp.bfloat16)
+    low_digit = (own_target % DIGIT).astype(jnp.bfloat16)
+    target_row = jnp.zeros((1, full_width), jnp.bfloat16)
+    target_row = target_row.at[0, :row_count].set(high_digit)
+    target_row = target_row.at[0, row_count : 2 * row_count].set(low_digit)
+    packet = jnp.concatenate([final_rows.reshape(models * row_count, full_width), target_row], axis=0)
+    every = lax.all_gather(packet, "req", axis=0, tiled=False)
+    every_rows = (
+        every[:, : models * row_count]
+        .reshape(shards, models, row_count, full_width)
+        .transpose(1, 0, 2, 3)
+        .reshape(models, shards * row_count, full_width)
+    )
+    every_target = (
+        every[:, models * row_count, :row_count].astype(jnp.int32) * DIGIT
+        + every[:, models * row_count, row_count : 2 * row_count].astype(jnp.int32)
+    ).reshape(shards * row_count)
+    vocab_part = head_weight.shape[1]
+    statistics = head_scores(head_weight, shard_index * vocab_part, every_rows, every_target)
+    if STATS_BY_ALL_TO_ALL:
+        received = lax.all_to_all(
+            statistics.reshape(3, models, shards, row_count), "req", split_axis=2, concat_axis=2, tiled=True
+        )
+    else:
+        gathered = lax.all_gather(statistics, "req", axis=2, tiled=False)
+        received = lax.dynamic_slice_in_dim(
+            gathered.reshape(3, models, shards, shards, row_count), shard_index, 1, 3
+        ).reshape(3, models, shards, row_count)
+    peak_each, spread_each, picked_each = received[0], received[1], received[2]
+    peak_logit = jnp.max(peak_each, axis=1)
+    spread = jnp.sum(spread_each * jnp.exp(peak_each - peak_logit[:, None, :]), axis=1)
+    picked = jnp.sum(picked_each, axis=1)
     scored_rows = lax.dynamic_slice_in_dim(score_flag, lane_index * row_count, row_count, 0).astype(
         jnp.float32
     )

time: 708 us -> 275 us (0.39)
  blocking collectives: 405 us -> 15.9 us
  other arithmetic: 66.6 us -> 27.6 us
    unnamed x1 -> x0, blocking collectives: 246 us -> none
    all_gather x3 -> x0, blocking collectives: 132 us -> none  [merged_2(): gathered = jax.tree.map(lambda a: lax.all_gather(a, axis), part)]
    add x63 -> x0, other arithmetic: 45.2 us -> none  [fold_stats(): first_stats[1] * jnp.exp(first_stats[0] - peak_logit)]
    reduce_scatter x1, waiting for transfers between devices: 34.2 us -> 21.3 us  [local(): lax.psum_scatter(partial_out, 'tp', scatter_dimension=1, tiled=True)]
    all_to_all x1 -> x2, waiting for transfers between devices: 0.01 us -> 12.1 us  [the longest x1 11.3 us: local(): lax.all_to_all(statistics.reshape(3, models, shards, row_count), 'req', s...]
    psum x1 -> x0, blocking collectives: 12.1 us -> none  [local(): final_squares = lax.psum(jnp.sum(hidden_float * hidden_float, axis=2), 'tp')]
  transfers between devices with their start and end apart: 4 -> 5, of which waited for: 3 -> 5; matrix products, arithmetic and copies ran while one was open for 11% -> 29% of each run, Pallas kernels for 0% -> 0%
where the time goes in v1:
time: 275 us; the launch traced here: 273 us
  waiting for transfers between devices  132 us (48%)
  local copies, waits for them, and re-layouts  37.8 us (14%)
  matrix products  34.3 us (12%)
  other arithmetic  27.6 us (10%)
  blocking collectives  15.9 us (6%)
  between operations  13.5 us (5%)
  starting transfers between devices  12.2 us (4%)
    all_gather x1, waiting for transfers between devices, local(): every = lax.all_gather(packet, 'req', axis=0, tiled=False)  92.4 us
    reduce_scatter x1, waiting for transfers between devices, local(): lax.psum_scatter(partial_out, 'tp', scatter_dimension=1, tiled=True)  21.3 us
    psum x1, blocking collectives, local(): squares = lax.psum(jnp.sum(gated * gated, axis=2), 'tp')  15.9 us
    all_to_all x1, waiting for transfers between devices, local(): lax.all_to_all(statistics.reshape(3, models, shards, row_count), 'req', s...  11.3 us
    dot_general x12, matrix products, causal_conv(): jnp.dot(member_bf, history[:, slot_index, :], preferred_element_type=jnp....  10.7 us
    all_to_all x1, starting transfers between devices, local(): lax.all_to_all(resid_in, 'tp', split_axis=1, concat_axis=2, tiled=True)  6.53 us
    all_to_all x1, starting transfers between devices, local(): lax.all_to_all(statistics.reshape(3, models, shards, row_count), 'req', s...  5.57 us
    another operation x6, other arithmetic  5.57 us
  transfers between devices with their start and end apart: 5, of which 5 were waited for; matrix products, arithmetic and copies ran while one was open for 29% of the time, Pallas kernels for 0%

profile of v1, /device:TPU:1, one launch (start us, length us, event | category | flops | bytes accessed | tf_op | source)
XLA Modules:
  0.0 273.2 jit_solution(8377025684289758883)
XLA Ops:
  7.3 1.0 slice_convert_fusion.1
  10.4 0.8 reduce-window.4
  11.2 1.2 compare_and_fusion
  13.1 0.8 fusion.165
  14.0 1.2 fusion.156
  16.5 1.5 fusion.166
  18.8 1.9 divide_multiply_fusion.1
  20.7 1.0 copy.172
  21.8 1.5 fusion.170
  23.3 0.8 fusion.85
  25.1 0.8 slice_convert_fusion.3
  27.7 1.1 divide_multiply_fusion.3
  29.4 2.7 fusion.3
  32.1 1.7 copy.153
  33.8 1.4 slice_bitcast_fusion.18
  35.2 0.8 negate_multiply_fusion.1
  36.7 1.4 reduce_window_sum.25
  38.1 0.8 copy.147
  38.9 1.4 compare_select_fusion.1
  41.6 1.9 gather_fusion
  43.5 1.3 slice_bitcast_fusion.17
  44.9 0.9 fusion.12
  45.8 1.0 fusion.75
  46.8 2.3 fusion.8
  49.1 1.7 copy.155
  50.8 0.9 fusion.88
  51.7 0.9 fusion.91
  52.6 2.1 divide_multiply_fusion
  54.7 1.0 copy.173
  55.7 0.9 fusion.116
  56.6 0.9 fusion.119
  57.5 1.2 divide_multiply_fusion.2
  59.3 2.7 fusion.4
  62.0 1.7 copy.163
  64.4 1.4 reduce_window_sum.26
  65.9 0.8 copy.158
  66.7 1.4 compare_select_fusion
  68.1 1.4 copy.161
  69.4 2.0 gather_fusion.1
  71.4 0.9 fusion.10
  72.4 1.0 fusion.73
  73.4 2.3 fusion.6
  75.7 1.7 copy.165
  77.4 1.1 fusion.34
  79.2 15.9 %psum.7 = f32[2,64]{1,0:T(2,128)} all-reduce(f32[2,64]{1,0:T(2,128)} %multiply_reduce_fusion), channel_id=1, replica_groups=mesh['req'=64,'tp'=8] {'tp'}, use_global_device_ids=true, to_apply=%region_8.10 | all-reduce | flops 128 | bytes 1024 | tf_op jit(solution)/shard_map/psum | solution.py:181
  95.1 1.3 add_rsqrt_fusion.1
  96.4 5.3 %all-gather.5.cloned.1.call-done = bf16[2,512,2048]{1,2,0:T(8,128)(2,1)} async-done(((bf16[2,512,32]{1,2,0:T(8,128)(2,1)}), bf16[2,512,2048]{1,2,0:T(8,128)(2,1)}) %all-gather.5.cloned.1.call-update) | async-done | bytes 4194320 | tf_op jit(solution)/shard_map/all_gather | solution.py:189
  101.7 4.6 %fusion.42 = f32[2,64,2048]{2,1,0:T(8,128)} fusion(bf16[2,512,2048]{1,2,0:T(8,128)(2,1)} %all-gather.5.cloned.1.call-done, f32[1,64,512]{2,1,0:T(8,128)S(1)} %get-tuple-element.39, f32[1,64,512]{2,1,0:T(8,128)S(1)} %get-tuple-element.38, f32[2,512]{1,0:T(2,128)} %param.37, f32[2,64]{1,0:T(2,128)} %add_rsqrt_fusion.1), kind=kOutput, calls=%fused_computation.66 | convolution fusion | flops 268697600 | bytes 5509632 | tf_op jit(solution)/shard_map/mtc,mcd->mtd/dot_general | solution.py:186
  106.3 1.5 copy.142
  107.8 6.5 %all-to-all-start = ((bf16[2,64,256]{2,0,1:T(2,128)(2,1)}), bf16[2,64,256]{2,0,1:T(2,128)(2,1)S(1)}, u32[]{:S(2)}, u32[]{:S(2)}) async-start(bf16[2,64,256]{2,0,1:T(2,128)(2,1)} %copy.142), calls=%async_computation | async-start | bytes 131072 | tf_op jit(solution)/shard_map/all_to_all | solution.py:193
  115.1 1.4 fusion.152
  117.8 2.1 broadcast_select_fusion
  119.8 1.0 scatter.9
  120.8 0.8 all-to-all-done
  121.6 21.3 %reduce-scatter.2.cloned.1.call-done = f32[2,8,2048]{2,1,0:T(8,128)} async-done(((f32[2,64,2048]{2,1,0:T(8,128)}), f32[2,8,2048]{2,1,0:T(8,128)}) %reduce-scatter.2.cloned.1.call-update) | async-done | bytes 131088 | tf_op jit(solution)/shard_map/reduce_scatter | solution.py:192
  143.0 1.0 fusion.39
  144.7 92.4 %all-gather.7.cloned.1.call-done = bf16[64,17,2048]{2,1,0:T(8,128)(2,1)} async-done(((bf16[1,17,2048]{2,1,0:T(8,128)(2,1)}), bf16[64,17,2048]{2,1,0:T(8,128)(2,1)}) %all-gather.7.cloned.1.call-update) | async-done | bytes 4456464 | tf_op jit(solution)/shard_map/all_gather | solution.py:210
  237.2 1.1 fusion.164
  238.7 5.3 %fusion.173 = (f32[2,512]{1,0:T(2,128)S(1)}, f32[2,512,400]{1,2,0:T(8,128)}) fusion(bf16[2,400,2048]{2,1,0:T(8,128)(2,1)S(1)} %copy-done, bf16[64,17,2048]{2,1,0:T(8,128)(2,1)} %all-gather.7.cloned.1.call-done), kind=kOutput, calls=%fused_computation.285 | convolution fusion | flops 1678130176 | bytes 9113600 | tf_op jit(solution)/shard_map/mnd,mvd->mnv/dot_general | solution.py:115
  244.1 2.4 exponential_reduce_fusion
  246.5 0.8 stack.20
  247.4 0.8 copy.170
  248.2 5.6 %all-to-all-start.1 = ((f32[3,2,64,8]{3,1,0,2:T(2,128)}), f32[3,2,64,8]{3,1,0,2:T(2,128)S(1)}, u32[]{:S(2)}, u32[]{:S(2)}) async-start(f32[3,2,64,8]{3,1,0,2:T(2,128)} %copy.170), calls=%async_computation.2 | async-start | bytes 393216 | tf_op jit(solution)/shard_map/all_to_all | solution.py:224
  254.6 11.3 %all-to-all-done.1 = f32[3,2,64,8]{3,1,0,2:T(2,128)S(1)} async-done(((f32[3,2,64,8]{3,1,0,2:T(2,128)}), f32[3,2,64,8]{3,1,0,2:T(2,128)S(1)}, u32[]{:S(2)}, u32[]{:S(2)}) %all-to-all-start.1) | async-done | bytes 12320 | tf_op jit(solution)/shard_map/all_to_all | solution.py:224
  (102 shorter events, 18.0 us)
Async XLA Ops:
  6.5 232.2 %copy-start = (bf16[2,400,2048]{2,1,0:T(8,128)(2,1)S(1)}, bf16[2,400,2048]{2,1,0:T(8,128)(2,1)}, u32[]{:S(2)}) copy-start(bf16[2,400,2048]{2,1,0:T(8,128)(2,1)} %param.40) | copy-start | bytes 9830404
  6.5 16.7 %copy-start.3 = (bf16[2,3,3,256]{3,0,2,1:T(2,128)(2,1)S(1)}, bf16[2,3,3,256]{3,0,2,1:T(2,128)(2,1)}, u32[]{:S(2)}) copy-start(bf16[2,3,3,256]{3,0,2,1:T(2,128)(2,1)} %param.42) | copy-start | bytes 27652
  6.5 95.2 %all-gather.5.cloned.1.call-start = ((), (), s32[]{:S(2)}) async-start(), calls=%async_computation.3 | async-start | bytes 4259840 | tf_op jit(solution)/shard_map/all_gather | solution.py:189
  7.3 135.7 %reduce-scatter.2.cloned.1.call-start = ((), (), s32[]{:S(2)}) async-start(), calls=%async_computation.4 | async-start | bytes 1179648 | tf_op jit(solution)/shard_map/reduce_scatter | solution.py:192
  12.5 2.9 %copy-start.10 = (s32[3]{0:T(128)}, s32[3]{0:T(128)S(1)}, u32[]{:S(2)}) copy-start(s32[3]{0:T(128)S(1)} %get-tuple-element.35) | copy-start | bytes 40
  15.2 0.9 copy-start.8
  18.1 0.6 copy-start.11
  18.1 0.6 copy-start.12
  18.1 0.6 copy-start.13
  18.1 0.6 copy-start.14
  18.1 0.6 copy-start.15
  18.1 0.6 copy-start.16
  18.2 0.6 copy-start.17
  18.2 0.6 copy-start.18
  18.2 0.6 copy-start.19
  18.2 0.6 copy-start.20
  18.2 0.6 copy-start.21
  18.2 0.6 copy-start.22
  21.8 7.1 %copy-start.9 = (f32[64,3]{0,1:T(4,128)}, f32[64,3]{0,1:T(4,128)S(1)}, u32[]{:S(2)}) copy-start(f32[64,3]{0,1:T(4,128)S(1)} %fusion.132) | copy-start | bytes 2308
  28.8 0.6 copy-start.2
  35.2 1.5 copy-start.7
  41.6 1.9 copy-start.6
  49.1 14.7 %copy-start.5 = (f32[64,8]{0,1:T(8,128)S(1)}, f32[64,8]{0,1:T(8,128)}, u32[]{:S(2)}) copy-start(f32[64,8]{0,1:T(8,128)} %get-tuple-element.80) | copy-start | bytes 6148
  58.7 0.6 copy-start.1
  77.4 66.6 %copy-start.4 = (f32[2,2048]{1,0:T(2,128)S(1)}, f32[2,2048]{1,0:T(2,128)}, u32[]{:S(2)}) copy-start(f32[2,2048]{1,0:T(2,128)} %param.38) | copy-start | bytes 49156
  107.8 13.8 %all-to-all-start = ((bf16[2,64,256]{2,0,1:T(2,128)(2,1)}), bf16[2,64,256]{2,0,1:T(2,128)(2,1)S(1)}, u32[]{:S(2)}, u32[]{:S(2)}) async-start(bf16[2,64,256]{2,0,1:T(2,128)(2,1)} %copy.142), calls=%async_computation | async-start | bytes 131072 | tf_op jit(solution)/shard_map/all_to_all | solution.py:193
  114.4 122.8 %all-gather.7.cloned.1.call-start = ((), (), s32[]{:S(2)}) async-start(), calls=%async_computation.5 | async-start | bytes 6389760 | tf_op jit(solution)/shard_map/all_gather | solution.py:210
  248.2 17.6 %all-to-all-start.1 = ((f32[3,2,64,8]{3,1,0,2:T(2,128)}), f32[3,2,64,8]{3,1,0,2:T(2,128)S(1)}, u32[]{:S(2)}, u32[]{:S(2)}) async-start(f32[3,2,64,8]{3,1,0,2:T(2,128)} %copy.170), calls=%async_computation.2 | async-start | bytes 393216 | tf_op jit(solution)/shard_map/all_to_all | solution.py:224
Sparse Core Ops, SparseCore 0:
  10.8 90.9 all-gather.4
  106.4 36.4 reduce-scatter.1
  146.3 90.8 all-gather.6

commit v2 on v1

--- a/solution.py
+++ b/solution.py
@@ -116,15 +116,28 @@
         "mnd,mvd->mnv", rows_hidden, head_weight, preferred_element_type=jnp.float32
     )
     peak_logit = jnp.max(logits, axis=2)
-    spread = jnp.sum(jnp.exp(logits - peak_logit[:, :, None]), axis=2)
     local_id = rows_target - vocab_start
     matches = jnp.arange(head_weight.shape[1], dtype=jnp.int32)[None, :] == local_id[:, None]
     picked = jnp.sum(jnp.where(matches[None, :, :], logits, 0.0), axis=2)
-    return jnp.stack([peak_logit, spread, picked])
-
-
-STATS_BY_ALL_TO_ALL = True
+    return logits, peak_logit, picked
+
+
+def ring_gather(block, perm_of, count):
+    got = {0: block}
+    forward = block
+    backward = block
+    for step in range(1, count // 2 + 1):
+        forward = lax.ppermute(forward, "req", perm_of(1))
+        got[-step % count] = forward
+        if step < count - step:
+            backward = lax.ppermute(backward, "req", perm_of(-1))
+            got[step] = backward
+    return jnp.stack([got[k] for k in range(count)])
+
+
 DIGIT = 256
+CORES = 2
+ROWS_X = 4
 
 
 def local(
@@ -157,6 +170,14 @@
     models = gate_in.shape[0]
     step_count = gate_in.shape[1]
     row_count = step_count // groups
+    chips_z = shards // (ROWS_X * CORES)
+    core_index = shard_index % CORES
+    x_index = (shard_index // CORES) % ROWS_X
+    z_index = shard_index // (CORES * ROWS_X)
+    vocab_part = head_weight.shape[1]
+    partner_weight = lax.ppermute(
+        head_weight, "req", [(i, i ^ 1) for i in range(shards)]
+    )
     gated = jnp.stack(
         [
             mixer_block(
@@ -189,9 +210,17 @@
         lax.all_gather(out_weight, "req", axis=2, tiled=True),
         preferred_element_type=jnp.float32,
     )
-    update = lax.psum_scatter(partial_out, "tp", scatter_dimension=1, tiled=True)
-    resid_rows = lax.all_to_all(resid_in, "tp", split_axis=1, concat_axis=2, tiled=True)
-    hidden = (resid_rows.astype(jnp.float32) + update).astype(jnp.bfloat16)
+    part_width = resid_in.shape[2]
+    partial_out = lax.dynamic_update_slice_in_dim(
+        partial_out,
+        lax.dynamic_slice_in_dim(partial_out, lane_index * part_width, part_width, 2)
+        + resid_in.astype(jnp.float32),
+        lane_index * part_width,
+        2,
+    )
+    hidden = lax.psum_scatter(partial_out, "tp", scatter_dimension=1, tiled=True).astype(
+        jnp.bfloat16
+    )
     full_width = hidden.shape[2]
     hidden_float = hidden.astype(jnp.float32)
     final_squares = jnp.sum(hidden_float * hidden_float, axis=2)
@@ -207,28 +236,54 @@
     target_row = target_row.at[0, :row_count].set(high_digit)
     target_row = target_row.at[0, row_count : 2 * row_count].set(low_digit)
     packet = jnp.concatenate([final_rows.reshape(models * row_count, full_width), target_row], axis=0)
-    every = lax.all_gather(packet, "req", axis=0, tiled=False)
+
+    def along_z(shift):
+        return [(i, (i + shift * CORES * ROWS_X) % shards) for i in range(shards)]
+
+    def along_x(shift):
+        return [
+            (i, (i // (CORES * ROWS_X)) * CORES * ROWS_X
+             + (((i // CORES) % ROWS_X + shift) % ROWS_X) * CORES + i % CORES)
+            for i in range(shards)
+        ]
+
+    every = ring_gather(ring_gather(packet, along_z, chips_z), along_x, ROWS_X)
+    peers = ROWS_X * chips_z
+    every = every.reshape(peers, models * row_count + 1, full_width)
     every_rows = (
         every[:, : models * row_count]
-        .reshape(shards, models, row_count, full_width)
+        .reshape(peers, models, row_count, full_width)
         .transpose(1, 0, 2, 3)
-        .reshape(models, shards * row_count, full_width)
+        .reshape(models, peers * row_count, full_width)
     )
     every_target = (
         every[:, models * row_count, :row_count].astype(jnp.int32) * DIGIT
         + every[:, models * row_count, row_count : 2 * row_count].astype(jnp.int32)
-    ).reshape(shards * row_count)
-    vocab_part = head_weight.shape[1]
-    statistics = head_scores(head_weight, shard_index * vocab_part, every_rows, every_target)
-    if STATS_BY_ALL_TO_ALL:
-        received = lax.all_to_all(
-            statistics.reshape(3, models, shards, row_count), "req", split_axis=2, concat_axis=2, tiled=True
-        )
-    else:
-        gathered = lax.all_gather(statistics, "req", axis=2, tiled=False)
-        received = lax.dynamic_slice_in_dim(
-            gathered.reshape(3, models, shards, shards, row_count), shard_index, 1, 3
-        ).reshape(3, models, shards, row_count)
+    ).reshape(peers * row_count)
+    own_logits, own_peak, own_picked = head_scores(
+        head_weight, shard_index * vocab_part, every_rows, every_target
+    )
+    other_logits, other_peak, other_picked = head_scores(
+        partner_weight, (shard_index ^ 1) * vocab_part, every_rows, every_target
+    )
+    peak_logit = jnp.maximum(own_peak, other_peak)
+    spread = jnp.sum(jnp.exp(own_logits - peak_logit[:, :, None]), axis=2) + jnp.sum(
+        jnp.exp(other_logits - peak_logit[:, :, None]), axis=2
+    )
+    statistics = jnp.stack([peak_logit, spread, own_picked + other_picked])
+    statistics = statistics.reshape(3, models, ROWS_X, chips_z, row_count).transpose(0, 1, 3, 2, 4)
+    statistics = jnp.roll(jnp.roll(statistics, z_index, axis=2), x_index, axis=3)
+    neutral = jnp.stack(
+        [
+            jnp.full_like(statistics[0], -1e30),
+            jnp.zeros_like(statistics[1]),
+            jnp.zeros_like(statistics[2]),
+        ]
+    )
+    send = jnp.stack(
+        [jnp.where(core_index == c, statistics, neutral) for c in range(CORES)], axis=4
+    ).reshape(3, models, shards, row_count)
+    received = lax.all_to_all(send, "req", split_axis=2, concat_axis=2, tiled=True)
     peak_each, spread_each, picked_each = received[0], received[1], received[2]
     peak_logit = jnp.max(peak_each, axis=1)
     spread = jnp.sum(spread_each * jnp.exp(peak_each - peak_logit[:, None, :]), axis=1)

time: 275 us -> 253 us (0.920)
  starting transfers between devices: 12.2 us -> 50.7 us
  local copies, waits for them, and re-layouts: 37.8 us -> 11.2 us
  matrix products: 34.3 us -> 18.5 us
  other arithmetic: 27.6 us -> 12 us
    all_gather x1 -> x0, waiting for transfers between devices: 92.4 us -> none  [local(): every = lax.all_gather(packet, 'req', axis=0, tiled=False)]
    all_gather x1, waiting for transfers between devices: 5.32 us -> 61.8 us  [local(): lax.all_gather(out_weight, 'req', axis=2, tiled=True)]
    ppermute x0 -> x11, starting transfers between devices: none -> 33.1 us  [the longest x4 18.1 us: ring_gather(): backward = lax.ppermute(backward, 'req', perm_of(-1))]
    ppermute x0 -> x11, waiting for transfers between devices: none -> 28.7 us  [the longest x6 28.7 us: ring_gather(): forward = lax.ppermute(forward, 'req', perm_of(1))]
    dot_general x12, matrix products: 10.7 us -> 3.71 us  [causal_conv(): jnp.dot(member_bf, history[:, slot_index, :], preferred_element_type=jnp....]
    all_to_all x2 -> x1, starting transfers between devices: 12.1 us -> 17.5 us  [local(): lax.all_to_all(send, 'req', split_axis=2, concat_axis=2, tiled=True)]
    reduce_scatter x1, waiting for transfers between devices: 21.3 us -> 26.6 us  [local(): lax.psum_scatter(partial_out, 'tp', scatter_dimension=1, tiled=True)]
    slice x6, local copies, waits for them, and re-layouts: 3.95 us -> 0.09 us  [causal_conv(): current[:-lag_steps]]
  transfers between devices with their start and end apart: 5 -> 14, of which waited for: 5 -> 8; matrix products, arithmetic and copies ran while one was open for 29% -> 12% of each run, Pallas kernels for 0% -> 0%
where the time goes in v2:
time: 253 us; the launch traced here: 252 us
  waiting for transfers between devices  130 us (51%)
  starting transfers between devices  50.7 us (20%)
  matrix products  18.5 us (7%)
  blocking collectives  15.1 us (6%)
  between operations  14.4 us (6%)
  other arithmetic  12 us (5%)
  local copies, waits for them, and re-layouts  11.2 us (4%)
    all_gather x1, waiting for transfers between devices, local(): lax.all_gather(out_weight, 'req', axis=2, tiled=True)  61.8 us
    ppermute x6, waiting for transfers between devices, ring_gather(): forward = lax.ppermute(forward, 'req', perm_of(1))  28.7 us
    reduce_scatter x1, waiting for transfers between devices, local(): lax.psum_scatter(partial_out, 'tp', scatter_dimension=1, tiled=True)  26.6 us
    ppermute x4, starting transfers between devices, ring_gather(): backward = lax.ppermute(backward, 'req', perm_of(-1))  18.1 us
    all_to_all x1, starting transfers between devices, local(): lax.all_to_all(send, 'req', split_axis=2, concat_axis=2, tiled=True)  17.5 us
    psum x1, blocking collectives, local(): squares = lax.psum(jnp.sum(gated * gated, axis=2), 'tp')  15.1 us
    ppermute x6, starting transfers between devices, ring_gather(): forward = lax.ppermute(forward, 'req', perm_of(1))  12.9 us
    all_to_all x1, waiting for transfers between devices, local(): lax.all_to_all(send, 'req', split_axis=2, concat_axis=2, tiled=True)  11.9 us
  transfers between devices with their start and end apart: 14, of which 8 were waited for; matrix products, arithmetic and copies ran while one was open for 12% of the time, Pallas kernels for 0%

profile of v2, /device:TPU:1, one launch (start us, length us, event | category | flops | bytes accessed | tf_op | source)
XLA Modules:
  0.0 251.7 jit_solution(8878180397018020762)
XLA Ops:
  6.5 0.7 all-gather.2.cloned.1.call-update
  7.3 0.8 reduce-window.4
  8.1 0.7 compare_and_fusion
  8.8 0.7 fusion.162
  9.5 0.9 slice_convert_fusion.1
  10.6 0.7 fusion.163
  11.3 0.8 fusion.171
  12.3 0.2 fusion.95
  12.8 0.9 fusion.172
  13.8 1.2 divide_multiply_fusion
  15.8 0.3 divide_multiply_fusion.2
  16.0 1.0 fusion.7
  18.1 0.6 gather_fusion.1
  18.8 0.3 fusion.13
  19.2 0.7 fusion.9
  20.0 0.2 fusion.103
  20.2 0.2 fusion.106
  20.5 0.3 divide_multiply_fusion.1
  21.4 0.3 divide_multiply_fusion.3
  21.7 1.0 fusion.6
  22.9 0.6 gather_fusion
  23.4 0.3 fusion.15
  23.9 0.7 fusion.11
  24.9 15.1 %psum.7 = f32[2,64]{1,0:T(2,128)S(1)} all-reduce(f32[2,64]{1,0:T(2,128)S(1)} %multiply_reduce_fusion), channel_id=1, replica_groups=mesh['req'=64,'tp'=8] {'tp'}, use_global_device_ids=true, to_apply=%region_8.10 | all-reduce | flops 128 | bytes 1024 | tf_op jit(solution)/shard_map/psum | solution.py:202
  40.0 61.8 %all-gather.2.cloned.1.call-done = bf16[2,512,2048]{1,2,0:T(8,128)(2,1)} async-done(((bf16[2,512,32]{1,2,0:T(8,128)(2,1)}), bf16[2,512,2048]{1,2,0:T(8,128)(2,1)}) %all-gather.2.cloned.1.call-update) | async-done | bytes 4194320 | tf_op jit(solution)/shard_map/all_gather | solution.py:210
  101.8 3.6 %fusion.45 = f32[2,64,2048]{2,1,0:T(8,128)S(1)} fusion(bf16[2,512,2048]{1,2,0:T(8,128)(2,1)} %all-gather.2.cloned.1.call-done, f32[1,64,512]{2,1,0:T(8,128)S(1)} %get-tuple-element.43, f32[1,64,512]{2,1,0:T(8,128)S(1)} %get-tuple-element.42, f32[2,512]{1,0:T(2,128)S(1)} %copy-done.12, f32[2,64]{1,0:T(2,128)S(1)} %add_rsqrt_fusion.1), kind=kOutput, calls=%fused_computation.80 | convolution fusion | flops 268697600 | bytes 5509632 | tf_op jit(solution)/shard_map/mtc,mcd->mtd/dot_general | solution.py:207
  105.4 1.0 copy-done
  106.4 2.2 collective-permute-start.10
  108.6 0.6 slice.399
  109.2 0.7 and_reduce_fusion
  109.9 0.8 fusion.159
  110.7 1.3 broadcast_select_fusion
  112.0 0.8 scatter.9
  112.9 26.6 %reduce-scatter.2.cloned.1.call-done = f32[2,8,2048]{2,1,0:T(8,128)} async-done(((f32[2,64,2048]{2,1,0:T(8,128)}), f32[2,8,2048]{2,1,0:T(8,128)}) %reduce-scatter.2.cloned.1.call-update) | async-done | bytes 131088 | tf_op jit(solution)/shard_map/reduce_scatter | solution.py:221
  139.5 1.0 fusion.42
  140.5 1.0 fusion.68
  141.5 5.5 %collective-permute-start = (bf16[17,2048]{1,0:T(8,128)(2,1)S(1)}, bf16[17,2048]{1,0:T(8,128)(2,1)S(1)}, u32[]{:S(2)}, u32[]{:S(2)}) collective-permute-start(bf16[17,2048]{1,0:T(8,128)(2,1)S(1)} %pad_maximum_fusion.3), channel_id=1, source_target_pairs={{0,448},{8,456},{16,464},{24,472},{32,480},{40,488},{48,496},{56,5... | collective-permute-start | bytes 208904 | tf_op jit(solution)/shard_map/ppermute | solution.py:133
  147.1 1.9 collective-permute-start.3
  149.0 4.6 %collective-permute-start.1 = (bf16[17,2048]{1,0:T(8,128)(2,1)S(1)}, bf16[17,2048]{1,0:T(8,128)(2,1)S(1)}, u32[]{:S(2)}, u32[]{:S(2)}) collective-permute-start(bf16[17,2048]{1,0:T(8,128)(2,1)S(1)} %collective-permute-done), channel_id=1, source_target_pairs={{0,448},{8,456},{16,464},{24,472},{32,480},{40,488},{48,496},{56,5... | collective-permute-start | bytes 208904 | tf_op jit(solution)/shard_map/ppermute | solution.py:133
  153.6 1.9 collective-permute-start.4
  155.6 4.6 %collective-permute-start.2 = (bf16[17,2048]{1,0:T(8,128)(2,1)S(1)}, bf16[17,2048]{1,0:T(8,128)(2,1)S(1)}, u32[]{:S(2)}, u32[]{:S(2)}) collective-permute-start(bf16[17,2048]{1,0:T(8,128)(2,1)S(1)} %collective-permute-done.1), channel_id=1, source_target_pairs={{0,448},{8,456},{16,464},{24,472},{32,480},{40,488},{48,496},{56,5... | collective-permute-start | bytes 208904 | tf_op jit(solution)/shard_map/ppermute | solution.py:133
  160.2 0.3 collective-permute-done.4
  160.5 1.9 collective-permute-start.5
  162.4 5.7 %collective-permute-done.5 = bf16[17,2048]{1,0:T(8,128)(2,1)S(1)} collective-permute-done((bf16[17,2048]{1,0:T(8,128)(2,1)S(1)}, bf16[17,2048]{1,0:T(8,128)(2,1)S(1)}, u32[]{:S(2)}, u32[]{:S(2)}) %collective-permute-start.5) | collective-permute-done | bytes 69664 | tf_op jit(solution)/shard_map/ppermute | solution.py:130
  168.1 1.9 collective-permute-start.6
  170.0 4.6 %collective-permute-done.6 = bf16[17,2048]{1,0:T(8,128)(2,1)S(1)} collective-permute-done((bf16[17,2048]{1,0:T(8,128)(2,1)S(1)}, bf16[17,2048]{1,0:T(8,128)(2,1)S(1)}, u32[]{:S(2)}, u32[]{:S(2)}) %collective-permute-start.6) | collective-permute-done | bytes 69664 | tf_op jit(solution)/shard_map/ppermute | solution.py:130
  174.7 0.3 copy.173
  175.0 3.1 %collective-permute-start.8 = (bf16[8,17,2048]{2,0,1:T(8,128)(2,1)S(1)}, bf16[8,17,2048]{2,0,1:T(8,128)(2,1)S(1)}, u32[]{:S(2)}, u32[]{:S(2)}) collective-permute-start(bf16[8,17,2048]{2,0,1:T(8,128)(2,1)S(1)} %copy.173), channel_id=1, source_target_pairs={{0,16},{8,24},{16,32},{24,40},{32,48},{40,56},{48,0},{56,8},{64,80... | collective-permute-start | bytes 1671176 | tf_op jit(solution)/shard_map/ppermute | solution.py:130
  178.2 3.4 %collective-permute-start.7 = (bf16[8,17,2048]{2,0,1:T(8,128)(2,1)S(1)}, bf16[8,17,2048]{2,0,1:T(8,128)(2,1)S(1)}, u32[]{:S(2)}, u32[]{:S(2)}) collective-permute-start(bf16[8,17,2048]{2,0,1:T(8,128)(2,1)S(1)} %copy.173), channel_id=1, source_target_pairs={{0,48},{8,56},{16,0},{24,8},{32,16},{40,24},{48,32},{56,40},{64,11... | collective-permute-start | bytes 1671176 | tf_op jit(solution)/shard_map/ppermute | solution.py:133
  181.5 5.0 %collective-permute-done.8 = bf16[8,17,2048]{2,0,1:T(8,128)(2,1)S(1)} collective-permute-done((bf16[8,17,2048]{2,0,1:T(8,128)(2,1)S(1)}, bf16[8,17,2048]{2,0,1:T(8,128)(2,1)S(1)}, u32[]{:S(2)}, u32[]{:S(2)}) %collective-permute-start.8) | collective-permute-done | bytes 557088 | tf_op jit(solution)/shard_map/ppermute | solution.py:130
  186.5 2.1 collective-permute-start.9
  188.7 0.3 copy.272
  189.1 0.3 copy.274
  189.4 13.1 %collective-permute-done.9 = bf16[8,17,2048]{2,0,1:T(8,128)(2,1)S(1)} collective-permute-done((bf16[8,17,2048]{2,0,1:T(8,128)(2,1)S(1)}, bf16[8,17,2048]{2,0,1:T(8,128)(2,1)S(1)}, u32[]{:S(2)}, u32[]{:S(2)}) %collective-permute-start.9) | collective-permute-done | bytes 557088 | tf_op jit(solution)/shard_map/ppermute | solution.py:130
  202.5 0.3 copy.273
  202.9 0.6 pad_maximum_fusion
  203.4 1.7 copy-done.1
  205.6 3.8 %fusion.179 = (f32[2,256]{1,0:T(2,128)S(1)}, f32[2,256,400]{1,2,0:T(8,128)S(1)}) fusion(bf16[2,400,2048]{2,1,0:T(8,128)(2,1)} %param.40, bf16[32,17,2048]{2,1,0:T(8,128)(2,1)} %bitcast.287), kind=kOutput, calls=%fused_computation.317 | convolution fusion | flops 839065088 | bytes 6195200 | tf_op jit(solution)/shard_map/mnd,mvd->mnv/dot_general | solution.py:115
  209.4 3.2 %fusion.180 = (f32[2,256]{1,0:T(2,128)S(1)}, f32[2,256,400]{1,2,0:T(8,128)S(1)}) fusion(bf16[2,400,2048]{2,1,0:T(8,128)(2,1)} %collective-permute-done.10, bf16[32,17,2048]{2,1,0:T(8,128)(2,1)S(1)} %bitcast.288), kind=kOutput, calls=%fused_computation.318 | convolution fusion | flops 839065088 | bytes 6195200 | tf_op jit(solution)/shard_map/mnd,mvd->mnv/dot_general | solution.py:115
  212.7 0.4 exponential_reduce_fusion
  213.6 0.8 copy.180
  214.5 17.5 %all-to-all-start = ((f32[3,2,64,8]{3,1,0,2:T(2,128)}), f32[3,2,64,8]{3,1,0,2:T(2,128)S(1)}, u32[]{:S(2)}, u32[]{:S(2)}) async-start(f32[3,2,64,8]{3,1,0,2:T(2,128)} %copy.180), calls=%async_computation.1 | async-start | bytes 393216 | tf_op jit(solution)/shard_map/all_to_all | solution.py:286
  232.1 11.9 %all-to-all-done = f32[3,2,64,8]{3,1,0,2:T(2,128)S(1)} async-done(((f32[3,2,64,8]{3,1,0,2:T(2,128)}), f32[3,2,64,8]{3,1,0,2:T(2,128)S(1)}, u32[]{:S(2)}, u32[]{:S(2)}) %all-to-all-start) | async-done | bytes 12320 | tf_op jit(solution)/shard_map/all_to_all | solution.py:286
  244.2 0.6 subtract_multiply_fusion
  (128 shorter events, 5.6 us)
Async XLA Ops:
  6.5 8.6 %copy-start.11 = (f32[2,4,256]{2,1,0:T(4,128)S(1)}, f32[2,4,256]{2,1,0:T(4,128)}, u32[]{:S(2)}) copy-start(f32[2,4,256]{2,1,0:T(4,128)} %param.33) | copy-start | bytes 24580
  6.5 8.6 %copy-start.8 = (bf16[2,3,3,256]{3,0,2,1:T(2,128)(2,1)S(1)}, bf16[2,3,3,256]{3,0,2,1:T(2,128)(2,1)}, u32[]{:S(2)}) copy-start(bf16[2,3,3,256]{3,0,2,1:T(2,128)(2,1)} %param.42) | copy-start | bytes 27652
  6.5 9.1 %copy-start.6 = (bf16[2,64,256]{2,1,0:T(8,128)(2,1)S(1)}, bf16[2,64,256]{2,1,0:T(8,128)(2,1)}, u32[]{:S(2)}) copy-start(bf16[2,64,256]{2,1,0:T(8,128)(2,1)} %param.29) | copy-start | bytes 196612
  6.5 95.3 %all-gather.2.cloned.1.call-start = ((), (), s32[]{:S(2)}) async-start(), calls=%async_computation.2 | async-start | bytes 4259840 | tf_op jit(solution)/shard_map/all_gather | solution.py:210
  7.3 132.2 %reduce-scatter.2.cloned.1.call-start = ((), (), s32[]{:S(2)}) async-start(), calls=%async_computation.3 | async-start | bytes 1179648 | tf_op jit(solution)/shard_map/reduce_scatter | solution.py:221
  10.4 5.6 %copy-start.17 = (bf16[2,3,512,128]{3,2,1,0:T(8,128)(2,1)S(1)}, bf16[2,3,512,128]{3,2,1,0:T(8,128)(2,1)}, u32[]{:S(2)}) copy-start(bf16[2,3,512,128]{3,2,1,0:T(8,128)(2,1)} %param.43) | copy-start | bytes 2359300
  12.5 4.7 %copy-start.15 = (f32[2,8]{1,0:T(2,128)S(1)}, f32[2,8]{1,0:T(2,128)}, u32[]{:S(2)}) copy-start(f32[2,8]{1,0:T(2,128)} %param.35) | copy-start | bytes 196
  12.5 4.7 %copy-start.16 = (f32[2,8]{1,0:T(2,128)S(1)}, f32[2,8]{1,0:T(2,128)}, u32[]{:S(2)}) copy-start(f32[2,8]{1,0:T(2,128)} %param.34) | copy-start | bytes 196
  12.5 4.7 %copy-start.9 = (bf16[2,64,8]{1,2,0:T(8,128)(2,1)S(1)}, bf16[2,64,8]{1,2,0:T(8,128)(2,1)}, u32[]{:S(2)}) copy-start(bf16[2,64,8]{1,2,0:T(8,128)(2,1)} %param.30) | copy-start | bytes 6148
  13.8 4.9 %copy-start.14 = (f32[2,8]{1,0:T(2,128)S(1)}, f32[2,8]{1,0:T(2,128)}, u32[]{:S(2)}) copy-start(f32[2,8]{1,0:T(2,128)} %param.36) | copy-start | bytes 196
  14.9 5.5 %copy-start.3 = (bf16[2,64,512]{2,1,0:T(8,128)(2,1)S(1)}, bf16[2,64,512]{2,1,0:T(8,128)(2,1)}, u32[]{:S(2)}) copy-start(bf16[2,64,512]{2,1,0:T(8,128)(2,1)} %param.28) | copy-start | bytes 393220
  20.5 4.2 %copy-start.4 = (bf16[2,64,512]{2,1,0:T(8,128)(2,1)S(1)}, bf16[2,64,512]{2,1,0:T(8,128)(2,1)}, u32[]{:S(2)}) copy-start(bf16[2,64,512]{2,1,0:T(8,128)(2,1)} %param.27) | copy-start | bytes 393220
  20.8 81.0 %copy-start.12 = (f32[2,512]{1,0:T(2,128)S(1)}, f32[2,512]{1,0:T(2,128)}, u32[]{:S(2)}) copy-start(f32[2,512]{1,0:T(2,128)} %param.37) | copy-start | bytes 12292
  24.7 80.7 %copy-start.7 = (bf16[2,64,256]{2,1,0:T(8,128)(2,1)S(1)}, bf16[2,64,256]{2,1,0:T(8,128)(2,1)}, u32[]{:S(2)}) copy-start(bf16[2,64,256]{2,1,0:T(8,128)(2,1)} %param.31) | copy-start | bytes 196612
  40.0 69.9 %copy-start.13 = (s32[64]{0:T(128)S(1)}, s32[64]{0:T(128)}, u32[]{:S(2)}) copy-start(s32[64]{0:T(128)} %param.46) | copy-start | bytes 772
  40.0 100.5 %copy-start.10 = (f32[2,2048]{1,0:T(2,128)S(1)}, f32[2,2048]{1,0:T(2,128)}, u32[]{:S(2)}) copy-start(f32[2,2048]{1,0:T(2,128)} %param.38) | copy-start | bytes 49156
  105.4 1.0 copy-start
  106.4 103.0 %collective-permute-start.10 = (bf16[2,400,2048]{2,1,0:T(8,128)(2,1)}, bf16[2,400,2048]{2,1,0:T(8,128)(2,1)}, u32[]{:S(2)}, u32[]{:S(2)}) collective-permute-start(bf16[2,400,2048]{2,1,0:T(8,128)(2,1)} %param.40), channel_id=1, source_target_pairs={{0,8},{8,0},{16,24},{24,16},{32,40},{40,32},{48,56},{56,48},{64,72... | collective-permute-start | bytes 9830408 | tf_op jit(solution)/shard_map/ppermute | solution.py:178
  141.5 7.5 %collective-permute-start = (bf16[17,2048]{1,0:T(8,128)(2,1)S(1)}, bf16[17,2048]{1,0:T(8,128)(2,1)S(1)}, u32[]{:S(2)}, u32[]{:S(2)}) collective-permute-start(bf16[17,2048]{1,0:T(8,128)(2,1)S(1)} %pad_maximum_fusion.3), channel_id=1, source_target_pairs={{0,448},{8,456},{16,464},{24,472},{32,480},{40,488},{48,496},{56,5... | collective-permute-start | bytes 208904 | tf_op jit(solution)/shard_map/ppermute | solution.py:133
  147.1 6.6 %collective-permute-start.3 = (bf16[17,2048]{1,0:T(8,128)(2,1)S(1)}, bf16[17,2048]{1,0:T(8,128)(2,1)S(1)}, u32[]{:S(2)}, u32[]{:S(2)}) collective-permute-start(bf16[17,2048]{1,0:T(8,128)(2,1)S(1)} %pad_maximum_fusion.3), channel_id=1, source_target_pairs={{0,64},{8,72},{16,80},{24,88},{32,96},{40,104},{48,112},{56,120},{... | collective-permute-start | bytes 208904 | tf_op jit(solution)/shard_map/ppermute | solution.py:130
  149.0 6.6 %collective-permute-start.1 = (bf16[17,2048]{1,0:T(8,128)(2,1)S(1)}, bf16[17,2048]{1,0:T(8,128)(2,1)S(1)}, u32[]{:S(2)}, u32[]{:S(2)}) collective-permute-start(bf16[17,2048]{1,0:T(8,128)(2,1)S(1)} %collective-permute-done), channel_id=1, source_target_pairs={{0,448},{8,456},{16,464},{24,472},{32,480},{40,488},{48,496},{56,5... | collective-permute-start | bytes 208904 | tf_op jit(solution)/shard_map/ppermute | solution.py:133
  153.6 6.8 %collective-permute-start.4 = (bf16[17,2048]{1,0:T(8,128)(2,1)S(1)}, bf16[17,2048]{1,0:T(8,128)(2,1)S(1)}, u32[]{:S(2)}, u32[]{:S(2)}) collective-permute-start(bf16[17,2048]{1,0:T(8,128)(2,1)S(1)} %collective-permute-done.3), channel_id=1, source_target_pairs={{0,64},{8,72},{16,80},{24,88},{32,96},{40,104},{48,112},{56,120},{... | collective-permute-start | bytes 208904 | tf_op jit(solution)/shard_map/ppermute | solution.py:130
  155.6 14.4 %collective-permute-start.2 = (bf16[17,2048]{1,0:T(8,128)(2,1)S(1)}, bf16[17,2048]{1,0:T(8,128)(2,1)S(1)}, u32[]{:S(2)}, u32[]{:S(2)}) collective-permute-start(bf16[17,2048]{1,0:T(8,128)(2,1)S(1)} %collective-permute-done.1), channel_id=1, source_target_pairs={{0,448},{8,456},{16,464},{24,472},{32,480},{40,488},{48,496},{56,5... | collective-permute-start | bytes 208904 | tf_op jit(solution)/shard_map/ppermute | solution.py:133
  160.5 7.6 %collective-permute-start.5 = (bf16[17,2048]{1,0:T(8,128)(2,1)S(1)}, bf16[17,2048]{1,0:T(8,128)(2,1)S(1)}, u32[]{:S(2)}, u32[]{:S(2)}) collective-permute-start(bf16[17,2048]{1,0:T(8,128)(2,1)S(1)} %collective-permute-done.4), channel_id=1, source_target_pairs={{0,64},{8,72},{16,80},{24,88},{32,96},{40,104},{48,112},{56,120},{... | collective-permute-start | bytes 208904 | tf_op jit(solution)/shard_map/ppermute | solution.py:130
  168.1 6.6 %collective-permute-start.6 = (bf16[17,2048]{1,0:T(8,128)(2,1)S(1)}, bf16[17,2048]{1,0:T(8,128)(2,1)S(1)}, u32[]{:S(2)}, u32[]{:S(2)}) collective-permute-start(bf16[17,2048]{1,0:T(8,128)(2,1)S(1)} %collective-permute-done.5), channel_id=1, source_target_pairs={{0,64},{8,72},{16,80},{24,88},{32,96},{40,104},{48,112},{56,120},{... | collective-permute-start | bytes 208904 | tf_op jit(solution)/shard_map/ppermute | solution.py:130
  175.0 11.5 %collective-permute-start.8 = (bf16[8,17,2048]{2,0,1:T(8,128)(2,1)S(1)}, bf16[8,17,2048]{2,0,1:T(8,128)(2,1)S(1)}, u32[]{:S(2)}, u32[]{:S(2)}) collective-permute-start(bf16[8,17,2048]{2,0,1:T(8,128)(2,1)S(1)} %copy.173), channel_id=1, source_target_pairs={{0,16},{8,24},{16,32},{24,40},{32,48},{40,56},{48,0},{56,8},{64,80... | collective-permute-start | bytes 1671176 | tf_op jit(solution)/shard_map/ppermute | solution.py:130
  178.2 10.9 %collective-permute-start.7 = (bf16[8,17,2048]{2,0,1:T(8,128)(2,1)S(1)}, bf16[8,17,2048]{2,0,1:T(8,128)(2,1)S(1)}, u32[]{:S(2)}, u32[]{:S(2)}) collective-permute-start(bf16[8,17,2048]{2,0,1:T(8,128)(2,1)S(1)} %copy.173), channel_id=1, source_target_pairs={{0,48},{8,56},{16,0},{24,8},{32,16},{40,24},{48,32},{56,40},{64,11... | collective-permute-start | bytes 1671176 | tf_op jit(solution)/shard_map/ppermute | solution.py:133
  186.5 16.0 %collective-permute-start.9 = (bf16[8,17,2048]{2,0,1:T(8,128)(2,1)S(1)}, bf16[8,17,2048]{2,0,1:T(8,128)(2,1)S(1)}, u32[]{:S(2)}, u32[]{:S(2)}) collective-permute-start(bf16[8,17,2048]{2,0,1:T(8,128)(2,1)S(1)} %collective-permute-done.8), channel_id=1, source_target_pairs={{0,16},{8,24},{16,32},{24,40},{32,48},{40,56},{48,0},{56,8},{64,80... | collective-permute-start | bytes 1671176 | tf_op jit(solution)/shard_map/ppermute | solution.py:130
  203.4 1.7 copy-start.1
  205.6 3.8 %copy-start.2 = (bf16[4,8,17,2048]{3,2,1,0:T(8,128)(2,1)S(1)}, bf16[4,8,17,2048]{3,2,1,0:T(8,128)(2,1)}, u32[]{:S(2)}) copy-start(bf16[4,8,17,2048]{3,2,1,0:T(8,128)(2,1)} %copy-done.1) | copy-start | bytes 6684676
  209.4 4.0 %copy-start.5 = (f32[3,2,8,4,8]{4,2,3,1,0:T(8,128)S(1)}, f32[3,2,8,4,8]{4,2,3,1,0:T(8,128)}, u32[]{:S(2)}) copy-start(f32[3,2,8,4,8]{4,2,3,1,0:T(8,128)} %constant.235.clone.1) | copy-start | bytes 18436
  212.6 19.4 %copy-start.18 = (s32[64]{0:T(128)S(1)}, s32[64]{0:T(128)}, u32[]{:S(2)}) copy-start(s32[64]{0:T(128)} %param.47) | copy-start | bytes 772
  214.5 29.5 %all-to-all-start = ((f32[3,2,64,8]{3,1,0,2:T(2,128)}), f32[3,2,64,8]{3,1,0,2:T(2,128)S(1)}, u32[]{:S(2)}, u32[]{:S(2)}) async-start(f32[3,2,64,8]{3,1,0,2:T(2,128)} %copy.180), calls=%async_computation.1 | async-start | bytes 393216 | tf_op jit(solution)/shard_map/all_to_all | solution.py:286
Sparse Core Ops, SparseCore 0:
  10.8 90.9 all-gather.1
  106.6 32.8 reduce-scatter.1

commit v3 on v2

--- a/solution.py
+++ b/solution.py
@@ -174,6 +174,19 @@
     core_index = shard_index % CORES
     x_index = (shard_index // CORES) % ROWS_X
     z_index = shard_index // (CORES * ROWS_X)
+    def along_z(shift):
+        return [(i, (i + shift * CORES * ROWS_X) % shards) for i in range(shards)]
+
+    def along_x(shift):
+        return [
+            (i, (i // (CORES * ROWS_X)) * CORES * ROWS_X
+             + (((i // CORES) % ROWS_X + shift) % ROWS_X) * CORES + i % CORES)
+            for i in range(shards)
+        ]
+
+    def along_core(shift):
+        return [(i, i ^ 1) for i in range(shards)]
+
     vocab_part = head_weight.shape[1]
     partner_weight = lax.ppermute(
         head_weight, "req", [(i, i ^ 1) for i in range(shards)]
@@ -204,11 +217,25 @@
     normed = (
         gated * lax.rsqrt(squares / inner_width + EPSILON)[:, :, None] * norm_gain[:, None, :]
     ).astype(jnp.bfloat16)
-    partial_out = jnp.einsum(
-        "mtc,mcd->mtd",
-        normed,
-        lax.all_gather(out_weight, "req", axis=2, tiled=True),
-        preferred_element_type=jnp.float32,
+    first_weight = lax.all_gather(out_weight[0], "req", axis=1, tiled=True)
+    ring_weight = ring_gather(
+        ring_gather(ring_gather(out_weight[1], along_core, CORES), along_z, chips_z),
+        along_x,
+        ROWS_X,
+    )
+    ring_weight = jnp.roll(
+        jnp.roll(jnp.roll(ring_weight.transpose(1, 0, 2, 3, 4), z_index, axis=0), x_index, axis=1),
+        core_index,
+        axis=2,
+    )
+    second_weight = ring_weight.transpose(3, 0, 1, 2, 4).reshape(
+        out_weight.shape[1], shards * out_weight.shape[2]
+    )
+    partial_out = jnp.stack(
+        [
+            jnp.dot(normed[0], first_weight, preferred_element_type=jnp.float32),
+            jnp.dot(normed[1], second_weight, preferred_element_type=jnp.float32),
+        ]
     )
     part_width = resid_in.shape[2]
     partial_out = lax.dynamic_update_slice_in_dim(
@@ -236,16 +263,6 @@
     target_row = target_row.at[0, :row_count].set(high_digit)
     target_row = target_row.at[0, row_count : 2 * row_count].set(low_digit)
     packet = jnp.concatenate([final_rows.reshape(models * row_count, full_width), target_row], axis=0)
-
-    def along_z(shift):
-        return [(i, (i + shift * CORES * ROWS_X) % shards) for i in range(shards)]
-
-    def along_x(shift):
-        return [
-            (i, (i // (CORES * ROWS_X)) * CORES * ROWS_X
-             + (((i // CORES) % ROWS_X + shift) % ROWS_X) * CORES + i % CORES)
-            for i in range(shards)
-        ]
 
     every = ring_gather(ring_gather(packet, along_z, chips_z), along_x, ROWS_X)
     peers = ROWS_X * chips_z

time: 253 us -> 251 us (level)
  waiting for transfers between devices: 130 us -> 81.4 us
  starting transfers between devices: 50.7 us -> 95.3 us
    all_gather x1, waiting for transfers between devices: 61.8 us -> 5.83 us  [local(): first_weight = lax.all_gather(out_weight[0], 'req', axis=1, tiled=True)]
    ppermute x6 -> x13, starting transfers between devices: 12.9 us -> 35.1 us  [ring_gather(): forward = lax.ppermute(forward, 'req', perm_of(1))]
    ppermute x4 -> x8, starting transfers between devices: 18.1 us -> 36.1 us  [ring_gather(): backward = lax.ppermute(backward, 'req', perm_of(-1))]
    ppermute x6 -> x13, waiting for transfers between devices: 28.7 us -> 40.6 us  [ring_gather(): forward = lax.ppermute(forward, 'req', perm_of(1))]
    ppermute x1, starting transfers between devices: 2.17 us -> 6.62 us  [local(): lax.ppermute(head_weight, 'req', [(i, i ^ 1) for i in range(shards)])]
    reduce_scatter x1, waiting for transfers between devices: 26.6 us -> 22.9 us  [local(): lax.psum_scatter(partial_out, 'tp', scatter_dimension=1, tiled=True)]
  transfers between devices with their start and end apart: 14 -> 25, of which waited for: 8 -> 11; matrix products, arithmetic and copies ran while one was open for 12% -> 12% of each run, Pallas kernels for 0% -> 0%
where the time goes in v3:
time: 251 us; the launch traced here: 250 us
  starting transfers between devices  95.3 us (38%)
  waiting for transfers between devices  81.4 us (32%)
  matrix products  17.1 us (7%)
  blocking collectives  16.2 us (6%)
  between operations  14.7 us (6%)
  other arithmetic  14 us (6%)
  local copies, waits for them, and re-layouts  11.3 us (5%)
    ppermute x13, waiting for transfers between devices, ring_gather(): forward = lax.ppermute(forward, 'req', perm_of(1))  40.6 us
    ppermute x8, starting transfers between devices, ring_gather(): backward = lax.ppermute(backward, 'req', perm_of(-1))  36.1 us
    ppermute x13, starting transfers between devices, ring_gather(): forward = lax.ppermute(forward, 'req', perm_of(1))  35.1 us
    reduce_scatter x1, waiting for transfers between devices, local(): lax.psum_scatter(partial_out, 'tp', scatter_dimension=1, tiled=True)  22.9 us
    all_to_all x1, starting transfers between devices, local(): lax.all_to_all(send, 'req', split_axis=2, concat_axis=2, tiled=True)  17.4 us
    psum x1, blocking collectives, local(): squares = lax.psum(jnp.sum(gated * gated, axis=2), 'tp')  16.2 us
    all_to_all x1, waiting for transfers between devices, local(): lax.all_to_all(send, 'req', split_axis=2, concat_axis=2, tiled=True)  11.9 us
    dot_general x2, matrix products, head_scores(): jnp.einsum('mnd,mvd->mnv', rows_hidden, head_weight, preferred_element_ty...  6.89 us
  transfers between devices with their start and end apart: 25, of which 11 were waited for; matrix products, arithmetic and copies ran while one was open for 12% of the time, Pallas kernels for 0%

profile of v3, /device:TPU:1, one launch (start us, length us, event | category | flops | bytes accessed | tf_op | source)
XLA Modules:
  0.0 250.0 jit_solution(6914840034294265884)
XLA Ops:
  6.6 1.4 fusion.174
  8.1 8.8 %collective-permute-start = (bf16[512,32]{0,1:T(8,128)(2,1)S(1)}, bf16[512,32]{0,1:T(8,128)(2,1)S(1)}, u32[]{:S(2)}, u32[]{:S(2)}) collective-permute-start(bf16[512,32]{0,1:T(8,128)(2,1)S(1)} %get-tuple-element.47), channel_id=1, source_target_pairs={{0,8},{8,0},{16,24},{24,16},{32,40},{40,32},{48,56},{56,48},{64,72... | collective-permute-start | bytes 98312 | tf_op jit(solution)/shard_map/ppermute | solution.py:130
  16.9 0.8 reduce-window.4
  17.7 0.7 compare_and_fusion
  18.4 0.7 fusion.166
  19.0 0.9 slice_convert_fusion.1
  22.7 1.0 fusion.11
  25.8 0.6 gather_fusion.1
  26.3 0.6 gather_fusion
  27.1 0.7 fusion.13
  28.7 5.3 %collective-permute-start.1 = (bf16[2,512,32]{1,2,0:T(8,128)(2,1)S(1)}, bf16[2,512,32]{1,2,0:T(8,128)(2,1)S(1)}, u32[]{:S(2)}, u32[]{:S(2)}) collective-permute-start(bf16[2,512,32]{1,2,0:T(8,128)(2,1)S(1)} %pad_maximum_fusion.5), channel_id=1, source_target_pairs={{0,448},{8,456},{16,464},{24,472},{32,480},{40,488},{48,496},{56,5... | collective-permute-start | bytes 196616 | tf_op jit(solution)/shard_map/ppermute | solution.py:133
  34.0 1.9 collective-permute-start.4
  36.0 4.8 %collective-permute-start.2 = (bf16[2,512,32]{1,2,0:T(8,128)(2,1)S(1)}, bf16[2,512,32]{1,2,0:T(8,128)(2,1)S(1)}, u32[]{:S(2)}, u32[]{:S(2)}) collective-permute-start(bf16[2,512,32]{1,2,0:T(8,128)(2,1)S(1)} %collective-permute-done.1), channel_id=1, source_target_pairs={{0,448},{8,456},{16,464},{24,472},{32,480},{40,488},{48,496},{56,5... | collective-permute-start | bytes 196616 | tf_op jit(solution)/shard_map/ppermute | solution.py:133
  40.8 1.9 collective-permute-start.5
  42.8 4.6 %collective-permute-start.3 = (bf16[2,512,32]{1,2,0:T(8,128)(2,1)S(1)}, bf16[2,512,32]{1,2,0:T(8,128)(2,1)S(1)}, u32[]{:S(2)}, u32[]{:S(2)}) collective-permute-start(bf16[2,512,32]{1,2,0:T(8,128)(2,1)S(1)} %collective-permute-done.2), channel_id=1, source_target_pairs={{0,448},{8,456},{16,464},{24,472},{32,480},{40,488},{48,496},{56,5... | collective-permute-start | bytes 196616 | tf_op jit(solution)/shard_map/ppermute | solution.py:133
  47.4 1.9 collective-permute-start.6
  49.3 4.3 %collective-permute-done.6 = bf16[2,512,32]{1,2,0:T(8,128)(2,1)S(1)} collective-permute-done((bf16[2,512,32]{1,2,0:T(8,128)(2,1)S(1)}, bf16[2,512,32]{1,2,0:T(8,128)(2,1)S(1)}, u32[]{:S(2)}, u32[]{:S(2)}) %collective-permute-start.6) | collective-permute-done | bytes 65568 | tf_op jit(solution)/shard_map/ppermute | solution.py:130
  53.6 1.9 collective-permute-start.7
  55.6 4.3 %collective-permute-done.7 = bf16[2,512,32]{1,2,0:T(8,128)(2,1)S(1)} collective-permute-done((bf16[2,512,32]{1,2,0:T(8,128)(2,1)S(1)}, bf16[2,512,32]{1,2,0:T(8,128)(2,1)S(1)}, u32[]{:S(2)}, u32[]{:S(2)}) %collective-permute-start.7) | collective-permute-done | bytes 65568 | tf_op jit(solution)/shard_map/ppermute | solution.py:130
  59.9 3.4 %collective-permute-start.9 = (bf16[8,2,512,32]{2,3,1,0:T(8,128)(2,1)S(1)}, bf16[8,2,512,32]{2,3,1,0:T(8,128)(2,1)S(1)}, u32[]{:S(2)}, u32[]{:S(2)}) collective-permute-start(bf16[8,2,512,32]{2,3,1,0:T(8,128)(2,1)S(1)} %bitcast_dynamic-update-slice_fusion.8), channel_id=1, source_target_pairs={{0,16},{8,24},{16,32},{24,40},{32,48},{40,56},{48,0},{56,8},{64,80... | collective-permute-start | bytes 1572872 | tf_op jit(solution)/shard_map/ppermute | solution.py:130
  63.3 1.0 fusion.10
  64.9 0.7 fusion.15
  65.7 3.1 %collective-permute-start.8 = (bf16[8,2,512,32]{2,3,1,0:T(8,128)(2,1)S(1)}, bf16[8,2,512,32]{2,3,1,0:T(8,128)(2,1)S(1)}, u32[]{:S(2)}, u32[]{:S(2)}) collective-permute-start(bf16[8,2,512,32]{2,3,1,0:T(8,128)(2,1)S(1)} %bitcast_dynamic-update-slice_fusion.8), channel_id=1, source_target_pairs={{0,48},{8,56},{16,0},{24,8},{32,16},{40,24},{48,32},{56,40},{64,11... | collective-permute-start | bytes 1572872 | tf_op jit(solution)/shard_map/ppermute | solution.py:133
  68.8 3.3 %collective-permute-done.9 = bf16[8,2,512,32]{2,3,1,0:T(8,128)(2,1)S(1)} collective-permute-done((bf16[8,2,512,32]{2,3,1,0:T(8,128)(2,1)S(1)}, bf16[8,2,512,32]{2,3,1,0:T(8,128)(2,1)S(1)}, u32[]{:S(2)}, u32[]{:S(2)}) %collective-permute-start.9) | collective-permute-done | bytes 524320 | tf_op jit(solution)/shard_map/ppermute | solution.py:130
  72.1 2.5 %collective-permute-start.10 = (bf16[8,2,512,32]{2,3,1,0:T(8,128)(2,1)S(1)}, bf16[8,2,512,32]{2,3,1,0:T(8,128)(2,1)S(1)}, u32[]{:S(2)}, u32[]{:S(2)}) collective-permute-start(bf16[8,2,512,32]{2,3,1,0:T(8,128)(2,1)S(1)} %collective-permute-done.9), channel_id=1, source_target_pairs={{0,16},{8,24},{16,32},{24,40},{32,48},{40,56},{48,0},{56,8},{64,80... | collective-permute-start | bytes 1572872 | tf_op jit(solution)/shard_map/ppermute | solution.py:130
  74.9 16.2 %psum.7 = f32[2,64]{1,0:T(2,128)S(1)} all-reduce(f32[2,64]{1,0:T(2,128)S(1)} %multiply_reduce_fusion), channel_id=1, replica_groups=mesh['req'=64,'tp'=8] {'tp'}, use_global_device_ids=true, to_apply=%region_8.10 | all-reduce | flops 128 | bytes 1024 | tf_op jit(solution)/shard_map/psum | solution.py:215
  91.5 0.8 fusion.2
  92.2 0.8 fusion.1
  93.0 0.8 fusion
  93.8 0.7 convolution_bitcast_fusion
  94.5 5.8 %all-gather.3.cloned.1.call-done = bf16[1,512,2048]{1,2,0:T(8,128)(2,1)} async-done(((bf16[1,512,32]{1,2,0:T(8,128)(2,1)}), bf16[1,512,2048]{1,2,0:T(8,128)(2,1)}) %all-gather.3.cloned.1.call-update) | async-done | bytes 2097168 | tf_op jit(solution)/shard_map/all_gather | solution.py:220
  100.4 2.3 convolution_bitcast_fusion.1
  102.9 1.0 copy-done
  103.9 6.6 %collective-permute-start.21 = (bf16[2,400,2048]{2,1,0:T(8,128)(2,1)}, bf16[2,400,2048]{2,1,0:T(8,128)(2,1)}, u32[]{:S(2)}, u32[]{:S(2)}) collective-permute-start(bf16[2,400,2048]{2,1,0:T(8,128)(2,1)} %param.40), channel_id=1, source_target_pairs={{0,8},{8,0},{16,24},{24,16},{32,40},{40,32},{48,56},{56,48},{64,72... | collective-permute-start | bytes 9830408 | tf_op jit(solution)/shard_map/ppermute | solution.py:191
  110.5 0.6 slice.415
  111.2 0.7 and_reduce_fusion
  111.8 0.7 fusion.163
  112.6 1.4 broadcast_select_fusion
  113.9 0.9 scatter.9
  114.8 22.9 %reduce-scatter.2.cloned.1.call-done = f32[2,8,2048]{2,1,0:T(8,128)} async-done(((f32[2,64,2048]{2,1,0:T(8,128)}), f32[2,8,2048]{2,1,0:T(8,128)}) %reduce-scatter.2.cloned.1.call-update) | async-done | bytes 131088 | tf_op jit(solution)/shard_map/reduce_scatter | solution.py:248
  137.7 1.0 fusion.46
  138.7 1.0 fusion.72
  139.8 5.6 %collective-permute-start.11 = (bf16[17,2048]{1,0:T(8,128)(2,1)S(1)}, bf16[17,2048]{1,0:T(8,128)(2,1)S(1)}, u32[]{:S(2)}, u32[]{:S(2)}) collective-permute-start(bf16[17,2048]{1,0:T(8,128)(2,1)S(1)} %pad_maximum_fusion.4), channel_id=1, source_target_pairs={{0,448},{8,456},{16,464},{24,472},{32,480},{40,488},{48,496},{56,5... | collective-permute-start | bytes 208904 | tf_op jit(solution)/shard_map/ppermute | solution.py:133
  145.4 1.9 collective-permute-start.14
  147.3 4.6 %collective-permute-start.12 = (bf16[17,2048]{1,0:T(8,128)(2,1)S(1)}, bf16[17,2048]{1,0:T(8,128)(2,1)S(1)}, u32[]{:S(2)}, u32[]{:S(2)}) collective-permute-start(bf16[17,2048]{1,0:T(8,128)(2,1)S(1)} %collective-permute-done.11), channel_id=1, source_target_pairs={{0,448},{8,456},{16,464},{24,472},{32,480},{40,488},{48,496},{56,5... | collective-permute-start | bytes 208904 | tf_op jit(solution)/shard_map/ppermute | solution.py:133
  151.9 1.9 collective-permute-start.15
  153.9 4.6 %collective-permute-start.13 = (bf16[17,2048]{1,0:T(8,128)(2,1)S(1)}, bf16[17,2048]{1,0:T(8,128)(2,1)S(1)}, u32[]{:S(2)}, u32[]{:S(2)}) collective-permute-start(bf16[17,2048]{1,0:T(8,128)(2,1)S(1)} %collective-permute-done.12), channel_id=1, source_target_pairs={{0,448},{8,456},{16,464},{24,472},{32,480},{40,488},{48,496},{56,5... | collective-permute-start | bytes 208904 | tf_op jit(solution)/shard_map/ppermute | solution.py:133
  158.8 1.9 collective-permute-start.16
  160.7 5.7 %collective-permute-done.16 = bf16[17,2048]{1,0:T(8,128)(2,1)S(1)} collective-permute-done((bf16[17,2048]{1,0:T(8,128)(2,1)S(1)}, bf16[17,2048]{1,0:T(8,128)(2,1)S(1)}, u32[]{:S(2)}, u32[]{:S(2)}) %collective-permute-start.16) | collective-permute-done | bytes 69664 | tf_op jit(solution)/shard_map/ppermute | solution.py:130
  166.4 2.1 collective-permute-start.17
  168.5 4.4 %collective-permute-done.17 = bf16[17,2048]{1,0:T(8,128)(2,1)S(1)} collective-permute-done((bf16[17,2048]{1,0:T(8,128)(2,1)S(1)}, bf16[17,2048]{1,0:T(8,128)(2,1)S(1)}, u32[]{:S(2)}, u32[]{:S(2)}) %collective-permute-start.17) | collective-permute-done | bytes 69664 | tf_op jit(solution)/shard_map/ppermute | solution.py:130
  173.3 3.0 %collective-permute-start.19 = (bf16[8,17,2048]{2,0,1:T(8,128)(2,1)S(1)}, bf16[8,17,2048]{2,0,1:T(8,128)(2,1)S(1)}, u32[]{:S(2)}, u32[]{:S(2)}) collective-permute-start(bf16[8,17,2048]{2,0,1:T(8,128)(2,1)S(1)} %copy.188), channel_id=1, source_target_pairs={{0,16},{8,24},{16,32},{24,40},{32,48},{40,56},{48,0},{56,8},{64,80... | collective-permute-start | bytes 1671176 | tf_op jit(solution)/shard_map/ppermute | solution.py:130
  176.4 3.5 %collective-permute-start.18 = (bf16[8,17,2048]{2,0,1:T(8,128)(2,1)S(1)}, bf16[8,17,2048]{2,0,1:T(8,128)(2,1)S(1)}, u32[]{:S(2)}, u32[]{:S(2)}) collective-permute-start(bf16[8,17,2048]{2,0,1:T(8,128)(2,1)S(1)} %copy.188), channel_id=1, source_target_pairs={{0,48},{8,56},{16,0},{24,8},{32,16},{40,24},{48,32},{56,40},{64,11... | collective-permute-start | bytes 1671176 | tf_op jit(solution)/shard_map/ppermute | solution.py:133
  179.9 5.0 %collective-permute-done.19 = bf16[8,17,2048]{2,0,1:T(8,128)(2,1)S(1)} collective-permute-done((bf16[8,17,2048]{2,0,1:T(8,128)(2,1)S(1)}, bf16[8,17,2048]{2,0,1:T(8,128)(2,1)S(1)}, u32[]{:S(2)}, u32[]{:S(2)}) %collective-permute-start.19) | collective-permute-done | bytes 557088 | tf_op jit(solution)/shard_map/ppermute | solution.py:130
  184.8 1.9 collective-permute-start.20
  187.4 13.4 %collective-permute-done.20 = bf16[8,17,2048]{2,0,1:T(8,128)(2,1)S(1)} collective-permute-done((bf16[8,17,2048]{2,0,1:T(8,128)(2,1)S(1)}, bf16[8,17,2048]{2,0,1:T(8,128)(2,1)S(1)}, u32[]{:S(2)}, u32[]{:S(2)}) %collective-permute-start.20) | collective-permute-done | bytes 557088 | tf_op jit(solution)/shard_map/ppermute | solution.py:130
  201.2 0.6 pad_maximum_fusion
  201.7 1.7 copy-done.1
  203.9 3.8 %fusion.183 = (f32[2,256]{1,0:T(2,128)S(1)}, f32[2,256,400]{1,2,0:T(8,128)S(1)}) fusion(bf16[2,400,2048]{2,1,0:T(8,128)(2,1)} %param.40, bf16[32,17,2048]{2,1,0:T(8,128)(2,1)} %bitcast.335), kind=kOutput, calls=%fused_computation.344 | convolution fusion | flops 839065088 | bytes 6195200 | tf_op jit(solution)/shard_map/mnd,mvd->mnv/dot_general | solution.py:115
  207.7 3.1 %fusion.184 = (f32[2,256]{1,0:T(2,128)S(1)}, f32[2,256,400]{1,2,0:T(8,128)S(1)}) fusion(bf16[2,400,2048]{2,1,0:T(8,128)(2,1)} %collective-permute-done.21, bf16[32,17,2048]{2,1,0:T(8,128)(2,1)S(1)} %bitcast.336), kind=kOutput, calls=%fused_computation.345 | convolution fusion | flops 839065088 | bytes 6195200 | tf_op jit(solution)/shard_map/mnd,mvd->mnv/dot_general | solution.py:115
  212.0 0.8 copy.195
  212.8 17.4 %all-to-all-start = ((f32[3,2,64,8]{3,1,0,2:T(2,128)}), f32[3,2,64,8]{3,1,0,2:T(2,128)S(1)}, u32[]{:S(2)}, u32[]{:S(2)}) async-start(f32[3,2,64,8]{3,1,0,2:T(2,128)} %copy.195), calls=%async_computation.1 | async-start | bytes 393216 | tf_op jit(solution)/shard_map/all_to_all | solution.py:303
  230.4 11.9 %all-to-all-done = f32[3,2,64,8]{3,1,0,2:T(2,128)S(1)} async-done(((f32[3,2,64,8]{3,1,0,2:T(2,128)}), f32[3,2,64,8]{3,1,0,2:T(2,128)S(1)}, u32[]{:S(2)}, u32[]{:S(2)}) %all-to-all-start) | async-done | bytes 12320 | tf_op jit(solution)/shard_map/all_to_all | solution.py:303
  242.5 0.6 subtract_multiply_fusion
  (173 shorter events, 10.7 us)
Async XLA Ops:
  6.5 14.6 %copy-start.3 = (bf16[2,64,512]{2,1,0:T(8,128)(2,1)S(1)}, bf16[2,64,512]{2,1,0:T(8,128)(2,1)}, u32[]{:S(2)}) copy-start(bf16[2,64,512]{2,1,0:T(8,128)(2,1)} %param.28) | copy-start | bytes 393220
  6.5 13.5 %copy-start.7 = (bf16[2,64,256]{2,1,0:T(8,128)(2,1)S(1)}, bf16[2,64,256]{2,1,0:T(8,128)(2,1)}, u32[]{:S(2)}) copy-start(bf16[2,64,256]{2,1,0:T(8,128)(2,1)} %param.29) | copy-start | bytes 196612
  6.5 13.8 %copy-start.20 = (s32[1,3]{1,0:T(1,128)S(1)}, s32[1,3]{1,0:T(1,128)}, u32[]{:S(2)}) copy-start(s32[1,3]{1,0:T(1,128)} %param.45) | copy-start | bytes 40
  6.5 13.9 %copy-start.6 = (bf16[2,3,3,512]{3,0,2,1:T(2,128)(2,1)S(1)}, bf16[2,3,3,512]{3,0,2,1:T(2,128)(2,1)}, u32[]{:S(2)}) copy-start(bf16[2,3,3,512]{3,0,2,1:T(2,128)(2,1)} %param.41) | copy-start | bytes 55300
  6.5 14.6 %copy-start.10 = (f32[2,4,512]{2,1,0:T(4,128)S(1)}, f32[2,4,512]{2,1,0:T(4,128)}, u32[]{:S(2)}) copy-start(f32[2,4,512]{2,1,0:T(4,128)} %param.32) | copy-start | bytes 49156
  6.5 93.8 %all-gather.3.cloned.1.call-start = ((), (), s32[]{:S(2)}) async-start(), calls=%async_computation.3 | async-start | bytes 2129920 | tf_op jit(solution)/shard_map/all_gather | solution.py:220
  8.1 129.7 %reduce-scatter.2.cloned.1.call-start = ((), (), s32[]{:S(2)}) async-start(), calls=%async_computation.2 | async-start | bytes 1179648 | tf_op jit(solution)/shard_map/reduce_scatter | solution.py:248
  8.1 20.6 %collective-permute-start = (bf16[512,32]{0,1:T(8,128)(2,1)S(1)}, bf16[512,32]{0,1:T(8,128)(2,1)S(1)}, u32[]{:S(2)}, u32[]{:S(2)}) collective-permute-start(bf16[512,32]{0,1:T(8,128)(2,1)S(1)} %get-tuple-element.47), channel_id=1, source_target_pairs={{0,8},{8,0},{16,24},{24,16},{32,40},{40,32},{48,56},{56,48},{64,72... | collective-permute-start | bytes 98312 | tf_op jit(solution)/shard_map/ppermute | solution.py:130
  20.0 1.7 copy-start.9
  20.1 2.2 copy-start.13
  20.8 1.9 copy-start.19
  21.2 2.7 %copy-start.17 = (f32[2,8]{1,0:T(2,128)S(1)}, f32[2,8]{1,0:T(2,128)}, u32[]{:S(2)}) copy-start(f32[2,8]{1,0:T(2,128)} %param.35) | copy-start | bytes 196
  21.2 2.7 %copy-start.18 = (f32[2,8]{1,0:T(2,128)S(1)}, f32[2,8]{1,0:T(2,128)}, u32[]{:S(2)}) copy-start(f32[2,8]{1,0:T(2,128)} %param.34) | copy-start | bytes 196
  21.2 2.7 %copy-start.11 = (bf16[2,64,8]{1,2,0:T(8,128)(2,1)S(1)}, bf16[2,64,8]{1,2,0:T(8,128)(2,1)}, u32[]{:S(2)}) copy-start(bf16[2,64,8]{1,2,0:T(8,128)(2,1)} %param.30) | copy-start | bytes 6148
  21.6 3.3 %copy-start.16 = (f32[2,8]{1,0:T(2,128)S(1)}, f32[2,8]{1,0:T(2,128)}, u32[]{:S(2)}) copy-start(f32[2,8]{1,0:T(2,128)} %param.36) | copy-start | bytes 196
  28.7 7.3 %collective-permute-start.1 = (bf16[2,512,32]{1,2,0:T(8,128)(2,1)S(1)}, bf16[2,512,32]{1,2,0:T(8,128)(2,1)S(1)}, u32[]{:S(2)}, u32[]{:S(2)}) collective-permute-start(bf16[2,512,32]{1,2,0:T(8,128)(2,1)S(1)} %pad_maximum_fusion.5), channel_id=1, source_target_pairs={{0,448},{8,456},{16,464},{24,472},{32,480},{40,488},{48,496},{56,5... | collective-permute-start | bytes 196616 | tf_op jit(solution)/shard_map/ppermute | solution.py:133
  34.0 6.8 %collective-permute-start.4 = (bf16[2,512,32]{1,2,0:T(8,128)(2,1)S(1)}, bf16[2,512,32]{1,2,0:T(8,128)(2,1)S(1)}, u32[]{:S(2)}, u32[]{:S(2)}) collective-permute-start(bf16[2,512,32]{1,2,0:T(8,128)(2,1)S(1)} %pad_maximum_fusion.5), channel_id=1, source_target_pairs={{0,64},{8,72},{16,80},{24,88},{32,96},{40,104},{48,112},{56,120},{... | collective-permute-start | bytes 196616 | tf_op jit(solution)/shard_map/ppermute | solution.py:130
  36.0 38.6 %copy-start.4 = (bf16[2,64,512]{2,1,0:T(8,128)(2,1)S(1)}, bf16[2,64,512]{2,1,0:T(8,128)(2,1)}, u32[]{:S(2)}) copy-start(bf16[2,64,512]{2,1,0:T(8,128)(2,1)} %param.27) | copy-start | bytes 393220
  36.0 6.8 %collective-permute-start.2 = (bf16[2,512,32]{1,2,0:T(8,128)(2,1)S(1)}, bf16[2,512,32]{1,2,0:T(8,128)(2,1)S(1)}, u32[]{:S(2)}, u32[]{:S(2)}) collective-permute-start(bf16[2,512,32]{1,2,0:T(8,128)(2,1)S(1)} %collective-permute-done.1), channel_id=1, source_target_pairs={{0,448},{8,456},{16,464},{24,472},{32,480},{40,488},{48,496},{56,5... | collective-permute-start | bytes 196616 | tf_op jit(solution)/shard_map/ppermute | solution.py:133
  40.8 6.5 %collective-permute-start.5 = (bf16[2,512,32]{1,2,0:T(8,128)(2,1)S(1)}, bf16[2,512,32]{1,2,0:T(8,128)(2,1)S(1)}, u32[]{:S(2)}, u32[]{:S(2)}) collective-permute-start(bf16[2,512,32]{1,2,0:T(8,128)(2,1)S(1)} %collective-permute-done.4), channel_id=1, source_target_pairs={{0,64},{8,72},{16,80},{24,88},{32,96},{40,104},{48,112},{56,120},{... | collective-permute-start | bytes 196616 | tf_op jit(solution)/shard_map/ppermute | solution.py:130
  42.8 12.8 %collective-permute-start.3 = (bf16[2,512,32]{1,2,0:T(8,128)(2,1)S(1)}, bf16[2,512,32]{1,2,0:T(8,128)(2,1)S(1)}, u32[]{:S(2)}, u32[]{:S(2)}) collective-permute-start(bf16[2,512,32]{1,2,0:T(8,128)(2,1)S(1)} %collective-permute-done.2), channel_id=1, source_target_pairs={{0,448},{8,456},{16,464},{24,472},{32,480},{40,488},{48,496},{56,5... | collective-permute-start | bytes 196616 | tf_op jit(solution)/shard_map/ppermute | solution.py:133
  47.4 6.2 %collective-permute-start.6 = (bf16[2,512,32]{1,2,0:T(8,128)(2,1)S(1)}, bf16[2,512,32]{1,2,0:T(8,128)(2,1)S(1)}, u32[]{:S(2)}, u32[]{:S(2)}) collective-permute-start(bf16[2,512,32]{1,2,0:T(8,128)(2,1)S(1)} %collective-permute-done.5), channel_id=1, source_target_pairs={{0,64},{8,72},{16,80},{24,88},{32,96},{40,104},{48,112},{56,120},{... | collective-permute-start | bytes 196616 | tf_op jit(solution)/shard_map/ppermute | solution.py:130
  53.6 6.2 %collective-permute-start.7 = (bf16[2,512,32]{1,2,0:T(8,128)(2,1)S(1)}, bf16[2,512,32]{1,2,0:T(8,128)(2,1)S(1)}, u32[]{:S(2)}, u32[]{:S(2)}) collective-permute-start(bf16[2,512,32]{1,2,0:T(8,128)(2,1)S(1)} %collective-permute-done.6), channel_id=1, source_target_pairs={{0,64},{8,72},{16,80},{24,88},{32,96},{40,104},{48,112},{56,120},{... | collective-permute-start | bytes 196616 | tf_op jit(solution)/shard_map/ppermute | solution.py:130
  59.9 31.2 %copy-start.14 = (f32[2,512]{1,0:T(2,128)S(1)}, f32[2,512]{1,0:T(2,128)}, u32[]{:S(2)}) copy-start(f32[2,512]{1,0:T(2,128)} %param.37) | copy-start | bytes 12292
  59.9 12.2 %collective-permute-start.9 = (bf16[8,2,512,32]{2,3,1,0:T(8,128)(2,1)S(1)}, bf16[8,2,512,32]{2,3,1,0:T(8,128)(2,1)S(1)}, u32[]{:S(2)}, u32[]{:S(2)}) collective-permute-start(bf16[8,2,512,32]{2,3,1,0:T(8,128)(2,1)S(1)} %bitcast_dynamic-update-slice_fusion.8), channel_id=1, source_target_pairs={{0,16},{8,24},{16,32},{24,40},{32,48},{40,56},{48,0},{56,8},{64,80... | collective-permute-start | bytes 1572872 | tf_op jit(solution)/shard_map/ppermute | solution.py:130
  65.7 25.5 %collective-permute-start.8 = (bf16[8,2,512,32]{2,3,1,0:T(8,128)(2,1)S(1)}, bf16[8,2,512,32]{2,3,1,0:T(8,128)(2,1)S(1)}, u32[]{:S(2)}, u32[]{:S(2)}) collective-permute-start(bf16[8,2,512,32]{2,3,1,0:T(8,128)(2,1)S(1)} %bitcast_dynamic-update-slice_fusion.8), channel_id=1, source_target_pairs={{0,48},{8,56},{16,0},{24,8},{32,16},{40,24},{48,32},{56,40},{64,11... | collective-permute-start | bytes 1572872 | tf_op jit(solution)/shard_map/ppermute | solution.py:133
  72.1 19.1 %collective-permute-start.10 = (bf16[8,2,512,32]{2,3,1,0:T(8,128)(2,1)S(1)}, bf16[8,2,512,32]{2,3,1,0:T(8,128)(2,1)S(1)}, u32[]{:S(2)}, u32[]{:S(2)}) collective-permute-start(bf16[8,2,512,32]{2,3,1,0:T(8,128)(2,1)S(1)} %collective-permute-done.9), channel_id=1, source_target_pairs={{0,16},{8,24},{16,32},{24,40},{32,48},{40,56},{48,0},{56,8},{64,80... | collective-permute-start | bytes 1572872 | tf_op jit(solution)/shard_map/ppermute | solution.py:130
  94.5 8.3 %copy-start.8 = (bf16[2,64,256]{2,1,0:T(8,128)(2,1)S(1)}, bf16[2,64,256]{2,1,0:T(8,128)(2,1)}, u32[]{:S(2)}) copy-start(bf16[2,64,256]{2,1,0:T(8,128)(2,1)} %param.31) | copy-start | bytes 196612
  102.7 9.1 %copy-start.15 = (s32[64]{0:T(128)S(1)}, s32[64]{0:T(128)}, u32[]{:S(2)}) copy-start(s32[64]{0:T(128)} %param.46) | copy-start | bytes 772
  102.7 36.0 %copy-start.12 = (f32[2,2048]{1,0:T(2,128)S(1)}, f32[2,2048]{1,0:T(2,128)}, u32[]{:S(2)}) copy-start(f32[2,2048]{1,0:T(2,128)} %param.38) | copy-start | bytes 49156
  102.9 1.0 copy-start
  103.9 103.8 %collective-permute-start.21 = (bf16[2,400,2048]{2,1,0:T(8,128)(2,1)}, bf16[2,400,2048]{2,1,0:T(8,128)(2,1)}, u32[]{:S(2)}, u32[]{:S(2)}) collective-permute-start(bf16[2,400,2048]{2,1,0:T(8,128)(2,1)} %param.40), channel_id=1, source_target_pairs={{0,8},{8,0},{16,24},{24,16},{32,40},{40,32},{48,56},{56,48},{64,72... | collective-permute-start | bytes 9830408 | tf_op jit(solution)/shard_map/ppermute | solution.py:191
  139.8 7.6 %collective-permute-start.11 = (bf16[17,2048]{1,0:T(8,128)(2,1)S(1)}, bf16[17,2048]{1,0:T(8,128)(2,1)S(1)}, u32[]{:S(2)}, u32[]{:S(2)}) collective-permute-start(bf16[17,2048]{1,0:T(8,128)(2,1)S(1)} %pad_maximum_fusion.4), channel_id=1, source_target_pairs={{0,448},{8,456},{16,464},{24,472},{32,480},{40,488},{48,496},{56,5... | collective-permute-start | bytes 208904 | tf_op jit(solution)/shard_map/ppermute | solution.py:133
  145.4 6.6 %collective-permute-start.14 = (bf16[17,2048]{1,0:T(8,128)(2,1)S(1)}, bf16[17,2048]{1,0:T(8,128)(2,1)S(1)}, u32[]{:S(2)}, u32[]{:S(2)}) collective-permute-start(bf16[17,2048]{1,0:T(8,128)(2,1)S(1)} %pad_maximum_fusion.4), channel_id=1, source_target_pairs={{0,64},{8,72},{16,80},{24,88},{32,96},{40,104},{48,112},{56,120},{... | collective-permute-start | bytes 208904 | tf_op jit(solution)/shard_map/ppermute | solution.py:130
  147.3 6.6 %collective-permute-start.12 = (bf16[17,2048]{1,0:T(8,128)(2,1)S(1)}, bf16[17,2048]{1,0:T(8,128)(2,1)S(1)}, u32[]{:S(2)}, u32[]{:S(2)}) collective-permute-start(bf16[17,2048]{1,0:T(8,128)(2,1)S(1)} %collective-permute-done.11), channel_id=1, source_target_pairs={{0,448},{8,456},{16,464},{24,472},{32,480},{40,488},{48,496},{56,5... | collective-permute-start | bytes 208904 | tf_op jit(solution)/shard_map/ppermute | solution.py:133
  151.9 6.8 %collective-permute-start.15 = (bf16[17,2048]{1,0:T(8,128)(2,1)S(1)}, bf16[17,2048]{1,0:T(8,128)(2,1)S(1)}, u32[]{:S(2)}, u32[]{:S(2)}) collective-permute-start(bf16[17,2048]{1,0:T(8,128)(2,1)S(1)} %collective-permute-done.14), channel_id=1, source_target_pairs={{0,64},{8,72},{16,80},{24,88},{32,96},{40,104},{48,112},{56,120},{... | collective-permute-start | bytes 208904 | tf_op jit(solution)/shard_map/ppermute | solution.py:130
  153.9 14.6 %collective-permute-start.13 = (bf16[17,2048]{1,0:T(8,128)(2,1)S(1)}, bf16[17,2048]{1,0:T(8,128)(2,1)S(1)}, u32[]{:S(2)}, u32[]{:S(2)}) collective-permute-start(bf16[17,2048]{1,0:T(8,128)(2,1)S(1)} %collective-permute-done.12), channel_id=1, source_target_pairs={{0,448},{8,456},{16,464},{24,472},{32,480},{40,488},{48,496},{56,5... | collective-permute-start | bytes 208904 | tf_op jit(solution)/shard_map/ppermute | solution.py:133
  158.8 7.6 %collective-permute-start.16 = (bf16[17,2048]{1,0:T(8,128)(2,1)S(1)}, bf16[17,2048]{1,0:T(8,128)(2,1)S(1)}, u32[]{:S(2)}, u32[]{:S(2)}) collective-permute-start(bf16[17,2048]{1,0:T(8,128)(2,1)S(1)} %collective-permute-done.15), channel_id=1, source_target_pairs={{0,64},{8,72},{16,80},{24,88},{32,96},{40,104},{48,112},{56,120},{... | collective-permute-start | bytes 208904 | tf_op jit(solution)/shard_map/ppermute | solution.py:130
  166.4 6.6 %collective-permute-start.17 = (bf16[17,2048]{1,0:T(8,128)(2,1)S(1)}, bf16[17,2048]{1,0:T(8,128)(2,1)S(1)}, u32[]{:S(2)}, u32[]{:S(2)}) collective-permute-start(bf16[17,2048]{1,0:T(8,128)(2,1)S(1)} %collective-permute-done.16), channel_id=1, source_target_pairs={{0,64},{8,72},{16,80},{24,88},{32,96},{40,104},{48,112},{56,120},{... | collective-permute-start | bytes 208904 | tf_op jit(solution)/shard_map/ppermute | solution.py:130
  173.3 11.5 %collective-permute-start.19 = (bf16[8,17,2048]{2,0,1:T(8,128)(2,1)S(1)}, bf16[8,17,2048]{2,0,1:T(8,128)(2,1)S(1)}, u32[]{:S(2)}, u32[]{:S(2)}) collective-permute-start(bf16[8,17,2048]{2,0,1:T(8,128)(2,1)S(1)} %copy.188), channel_id=1, source_target_pairs={{0,16},{8,24},{16,32},{24,40},{32,48},{40,56},{48,0},{56,8},{64,80... | collective-permute-start | bytes 1671176 | tf_op jit(solution)/shard_map/ppermute | solution.py:130
  176.4 10.7 %collective-permute-start.18 = (bf16[8,17,2048]{2,0,1:T(8,128)(2,1)S(1)}, bf16[8,17,2048]{2,0,1:T(8,128)(2,1)S(1)}, u32[]{:S(2)}, u32[]{:S(2)}) collective-permute-start(bf16[8,17,2048]{2,0,1:T(8,128)(2,1)S(1)} %copy.188), channel_id=1, source_target_pairs={{0,48},{8,56},{16,0},{24,8},{32,16},{40,24},{48,32},{56,40},{64,11... | collective-permute-start | bytes 1671176 | tf_op jit(solution)/shard_map/ppermute | solution.py:133
  184.8 16.0 %collective-permute-start.20 = (bf16[8,17,2048]{2,0,1:T(8,128)(2,1)S(1)}, bf16[8,17,2048]{2,0,1:T(8,128)(2,1)S(1)}, u32[]{:S(2)}, u32[]{:S(2)}) collective-permute-start(bf16[8,17,2048]{2,0,1:T(8,128)(2,1)S(1)} %collective-permute-done.19), channel_id=1, source_target_pairs={{0,16},{8,24},{16,32},{24,40},{32,48},{40,56},{48,0},{56,8},{64,80... | collective-permute-start | bytes 1671176 | tf_op jit(solution)/shard_map/ppermute | solution.py:130
  201.7 1.7 copy-start.1
  203.9 3.8 %copy-start.2 = (bf16[4,8,17,2048]{3,2,1,0:T(8,128)(2,1)S(1)}, bf16[4,8,17,2048]{3,2,1,0:T(8,128)(2,1)}, u32[]{:S(2)}) copy-start(bf16[4,8,17,2048]{3,2,1,0:T(8,128)(2,1)} %copy-done.1) | copy-start | bytes 6684676
  210.9 0.9 copy-start.5
  211.0 19.3 %copy-start.21 = (s32[64]{0:T(128)S(1)}, s32[64]{0:T(128)}, u32[]{:S(2)}) copy-start(s32[64]{0:T(128)} %param.47) | copy-start | bytes 772
  212.8 29.5 %all-to-all-start = ((f32[3,2,64,8]{3,1,0,2:T(2,128)}), f32[3,2,64,8]{3,1,0,2:T(2,128)S(1)}, u32[]{:S(2)}, u32[]{:S(2)}) async-start(f32[3,2,64,8]{3,1,0,2:T(2,128)} %copy.195), calls=%async_computation.1 | async-start | bytes 393216 | tf_op jit(solution)/shard_map/all_to_all | solution.py:303
Sparse Core Ops, SparseCore 0:
  10.7 89.5 all-gather.2
  104.0 33.6 reduce-scatter.1

commit v4 on v3

--- a/solution.py
+++ b/solution.py
@@ -136,6 +136,7 @@
 
 
 DIGIT = 256
+SQUARE_COLUMNS = 128
 CORES = 2
 ROWS_X = 4
 
@@ -212,42 +213,34 @@
             for model_index in range(models)
         ]
     )
-    squares = lax.psum(jnp.sum(gated * gated, axis=2), "tp")
     inner_width = gated.shape[2] * groups
-    normed = (
-        gated * lax.rsqrt(squares / inner_width + EPSILON)[:, :, None] * norm_gain[:, None, :]
-    ).astype(jnp.bfloat16)
-    first_weight = lax.all_gather(out_weight[0], "req", axis=1, tiled=True)
+    squares = jnp.sum(gated * gated, axis=2)
+    unscaled = (gated * norm_gain[:, None, :]).astype(jnp.bfloat16)
     ring_weight = ring_gather(
-        ring_gather(ring_gather(out_weight[1], along_core, CORES), along_z, chips_z),
+        ring_gather(ring_gather(out_weight, along_core, CORES), along_z, chips_z),
         along_x,
         ROWS_X,
     )
     ring_weight = jnp.roll(
-        jnp.roll(jnp.roll(ring_weight.transpose(1, 0, 2, 3, 4), z_index, axis=0), x_index, axis=1),
+        jnp.roll(jnp.roll(ring_weight.transpose(1, 0, 2, 3, 4, 5), z_index, axis=0), x_index, axis=1),
         core_index,
         axis=2,
     )
-    second_weight = ring_weight.transpose(3, 0, 1, 2, 4).reshape(
-        out_weight.shape[1], shards * out_weight.shape[2]
-    )
-    partial_out = jnp.stack(
-        [
-            jnp.dot(normed[0], first_weight, preferred_element_type=jnp.float32),
-            jnp.dot(normed[1], second_weight, preferred_element_type=jnp.float32),
-        ]
-    )
-    part_width = resid_in.shape[2]
-    partial_out = lax.dynamic_update_slice_in_dim(
-        partial_out,
-        lax.dynamic_slice_in_dim(partial_out, lane_index * part_width, part_width, 2)
-        + resid_in.astype(jnp.float32),
-        lane_index * part_width,
-        2,
-    )
-    hidden = lax.psum_scatter(partial_out, "tp", scatter_dimension=1, tiled=True).astype(
-        jnp.bfloat16
-    )
+    full_weight = ring_weight.transpose(3, 4, 0, 1, 2, 5).reshape(
+        models, out_weight.shape[1], shards * out_weight.shape[2]
+    )
+    partial_out = jnp.einsum(
+        "mtc,mcd->mtd", unscaled, full_weight, preferred_element_type=jnp.float32
+    )
+    extra = jnp.zeros(squares.shape + (SQUARE_COLUMNS,), jnp.float32).at[:, :, 0].set(squares)
+    reduced = lax.psum_scatter(
+        jnp.concatenate([partial_out, extra], axis=2), "tp", scatter_dimension=1, tiled=True
+    )
+    full_width = partial_out.shape[2]
+    update = reduced[:, :, :full_width]
+    scale = lax.rsqrt(reduced[:, :, full_width] / inner_width + EPSILON)
+    resid_rows = lax.all_to_all(resid_in, "tp", split_axis=1, concat_axis=2, tiled=True)
+    hidden = (resid_rows.astype(jnp.float32) + update * scale[:, :, None]).astype(jnp.bfloat16)
     full_width = hidden.shape[2]
     hidden_float = hidden.astype(jnp.float32)
     final_squares = jnp.sum(hidden_float * hidden_float, axis=2)

time: 251 us -> 271 us (1.080)
  blocking collectives: 16.2 us -> 0 us
  waiting for transfers between devices: 81.4 us -> 94.3 us
  starting transfers between devices: 95.3 us -> 105 us
  other arithmetic: 14 us -> 20.7 us
  matrix products: 17.1 us -> 21.3 us
  local copies, waits for them, and re-layouts: 11.3 us -> 14.1 us
    ppermute x13, waiting for transfers between devices: 40.6 us -> 64.7 us  [ring_gather(): forward = lax.ppermute(forward, 'req', perm_of(1))]
    psum x1 -> x0, blocking collectives: 16.2 us -> none  [local(): squares = lax.psum(jnp.sum(gated * gated, axis=2), 'tp')]
    all_to_all x0 -> x1, starting transfers between devices: none -> 6.8 us  [local(): lax.all_to_all(resid_in, 'tp', split_axis=1, concat_axis=2, tiled=True)]
    all_gather x1 -> x0, waiting for transfers between devices: 5.83 us -> none  [local(): first_weight = lax.all_gather(out_weight[0], 'req', axis=1, tiled=True)]
    reduce_scatter x1, waiting for transfers between devices: 22.9 us -> 17.1 us  [local(): lax.psum_scatter(jnp.concatenate([partial_out, extra], axis=2), 'tp', sca...]
    dot_general x12, matrix products: 2.87 us -> 6.43 us  [causal_conv(): jnp.dot(member_bf, history[:, slot_index, :], preferred_element_type=jnp....]
    concatenate x3 -> x4, other arithmetic: 2.29 us -> 5.77 us  [the longest x1 1.56 us: local(): jnp.roll(ring_weight.transpose(1, 0, 2, 3, 4, 5), z_index, axis=0)]
  transfers between devices with their start and end apart: 25 -> 25, of which waited for: 11 -> 11; matrix products, arithmetic and copies ran while one was open for 12% -> 15% of each run, Pallas kernels for 0% -> 0%
where the time goes in v4:
time: 271 us; the launch traced here: 270 us
  starting transfers between devices  105 us (39%)
  waiting for transfers between devices  94.3 us (35%)
  matrix products  21.3 us (8%)
  other arithmetic  20.7 us (8%)
  between operations  14.8 us (5%)
  local copies, waits for them, and re-layouts  14.1 us (5%)
    ppermute x13, waiting for transfers between devices, ring_gather(): forward = lax.ppermute(forward, 'req', perm_of(1))  64.7 us
    ppermute x8, starting transfers between devices, ring_gather(): backward = lax.ppermute(backward, 'req', perm_of(-1))  37.8 us
    ppermute x13, starting transfers between devices, ring_gather(): forward = lax.ppermute(forward, 'req', perm_of(1))  34.4 us
    all_to_all x1, starting transfers between devices, local(): lax.all_to_all(send, 'req', split_axis=2, concat_axis=2, tiled=True)  17.3 us
    reduce_scatter x1, waiting for transfers between devices, local(): lax.psum_scatter(jnp.concatenate([partial_out, extra], axis=2), 'tp', sca...  17.1 us
    all_to_all x1, waiting for transfers between devices, local(): lax.all_to_all(send, 'req', split_axis=2, concat_axis=2, tiled=True)  11.9 us
    ppermute x1, starting transfers between devices, local(): lax.ppermute(head_weight, 'req', [(i, i ^ 1) for i in range(shards)])  8.29 us
    dot_general x2, matrix products, head_scores(): jnp.einsum('mnd,mvd->mnv', rows_hidden, head_weight, preferred_element_ty...  6.92 us
  transfers between devices with their start and end apart: 25, of which 11 were waited for; matrix products, arithmetic and copies ran while one was open for 15% of the time, Pallas kernels for 0%

profile of v4, /device:TPU:1, one launch (start us, length us, event | category | flops | bytes accessed | tf_op | source)
XLA Modules:
  0.0 269.7 jit_solution(3938867534724088221)
XLA Ops:
  6.6 8.9 %collective-permute-start = (bf16[2,512,32]{1,2,0:T(8,128)(2,1)}, bf16[2,512,32]{1,2,0:T(8,128)(2,1)S(1)}, u32[]{:S(2)}, u32[]{:S(2)}) collective-permute-start(bf16[2,512,32]{1,2,0:T(8,128)(2,1)} %param.41), channel_id=1, source_target_pairs={{0,8},{8,0},{16,24},{24,16},{32,40},{40,32},{48,56},{56,48},{64,72... | collective-permute-start | bytes 196616 | tf_op jit(solution)/shard_map/ppermute | solution.py:130
  15.5 0.8 reduce-window.4
  17.7 0.9 slice_convert_fusion.1
  18.7 0.8 slice_convert_fusion.3
  20.5 0.8 fusion.179
  26.1 1.0 fusion.10
  27.7 0.7 compare_select_fusion.1
  31.0 5.3 %collective-permute-start.1 = (bf16[2,2,512,32]{2,3,0,1:T(8,128)(2,1)S(1)}, bf16[2,2,512,32]{2,3,0,1:T(8,128)(2,1)S(1)}, u32[]{:S(2)}, u32[]{:S(2)}) collective-permute-start(bf16[2,2,512,32]{2,3,0,1:T(8,128)(2,1)S(1)} %pad_maximum_fusion.3), channel_id=1, source_target_pairs={{0,448},{8,456},{16,464},{24,472},{32,480},{40,488},{48,496},{56,5... | collective-permute-start | bytes 393224 | tf_op jit(solution)/shard_map/ppermute | solution.py:133
  36.3 1.9 collective-permute-start.4
  39.2 5.3 %collective-permute-start.2 = (bf16[2,2,512,32]{2,3,0,1:T(8,128)(2,1)S(1)}, bf16[2,2,512,32]{2,3,0,1:T(8,128)(2,1)S(1)}, u32[]{:S(2)}, u32[]{:S(2)}) collective-permute-start(bf16[2,2,512,32]{2,3,0,1:T(8,128)(2,1)S(1)} %collective-permute-done.1), channel_id=1, source_target_pairs={{0,448},{8,456},{16,464},{24,472},{32,480},{40,488},{48,496},{56,5... | collective-permute-start | bytes 393224 | tf_op jit(solution)/shard_map/ppermute | solution.py:133
  44.5 1.9 collective-permute-start.5
  46.5 5.4 %collective-permute-start.3 = (bf16[2,2,512,32]{2,3,0,1:T(8,128)(2,1)S(1)}, bf16[2,2,512,32]{2,3,0,1:T(8,128)(2,1)S(1)}, u32[]{:S(2)}, u32[]{:S(2)}) collective-permute-start(bf16[2,2,512,32]{2,3,0,1:T(8,128)(2,1)S(1)} %collective-permute-done.2), channel_id=1, source_target_pairs={{0,448},{8,456},{16,464},{24,472},{32,480},{40,488},{48,496},{56,5... | collective-permute-start | bytes 393224 | tf_op jit(solution)/shard_map/ppermute | solution.py:133
  51.8 1.9 collective-permute-start.6
  53.8 5.0 %collective-permute-done.6 = bf16[2,2,512,32]{2,3,0,1:T(8,128)(2,1)S(1)} collective-permute-done((bf16[2,2,512,32]{2,3,0,1:T(8,128)(2,1)S(1)}, bf16[2,2,512,32]{2,3,0,1:T(8,128)(2,1)S(1)}, u32[]{:S(2)}, u32[]{:S(2)}) %collective-permute-start.6) | collective-permute-done | bytes 131104 | tf_op jit(solution)/shard_map/ppermute | solution.py:130
  58.7 1.9 collective-permute-start.7
  60.7 5.0 %collective-permute-done.7 = bf16[2,2,512,32]{2,3,0,1:T(8,128)(2,1)S(1)} collective-permute-done((bf16[2,2,512,32]{2,3,0,1:T(8,128)(2,1)S(1)}, bf16[2,2,512,32]{2,3,0,1:T(8,128)(2,1)S(1)}, u32[]{:S(2)}, u32[]{:S(2)}) %collective-permute-start.7) | collective-permute-done | bytes 131104 | tf_op jit(solution)/shard_map/ppermute | solution.py:130
  65.7 3.1 %collective-permute-start.9 = (bf16[8,2,2,512,32]{3,4,1,0,2:T(8,128)(2,1)S(1)}, bf16[8,2,2,512,32]{3,4,1,0,2:T(8,128)(2,1)S(1)}, u32[]{:S(2)}, u32[]{:S(2)}) collective-permute-start(bf16[8,2,2,512,32]{3,4,1,0,2:T(8,128)(2,1)S(1)} %bitcast_dynamic-update-slice_fusion.7), channel_id=1, source_target_pairs={{0,16},{8,24},{16,32},{24,40},{32,48},{40,56},{48,0},{56,8},{64,80... | collective-permute-start | bytes 3145736 | tf_op jit(solution)/shard_map/ppermute | solution.py:130
  68.9 0.9 fusion.113
  69.8 1.1 divide_multiply_fusion.1
  71.0 0.9 fusion.138
  71.9 0.9 fusion.141
  72.8 1.0 divide_multiply_fusion.3
  73.8 3.4 %collective-permute-start.8 = (bf16[8,2,2,512,32]{3,4,1,0,2:T(8,128)(2,1)S(1)}, bf16[8,2,2,512,32]{3,4,1,0,2:T(8,128)(2,1)}, u32[]{:S(2)}, u32[]{:S(2)}) collective-permute-start(bf16[8,2,2,512,32]{3,4,1,0,2:T(8,128)(2,1)S(1)} %bitcast_dynamic-update-slice_fusion.7), channel_id=1, source_target_pairs={{0,48},{8,56},{16,0},{24,8},{32,16},{40,24},{48,32},{56,40},{64,11... | collective-permute-start | bytes 3145736 | tf_op jit(solution)/shard_map/ppermute | solution.py:133
  77.2 12.0 %collective-permute-done.9 = bf16[8,2,2,512,32]{3,4,1,0,2:T(8,128)(2,1)S(1)} collective-permute-done((bf16[8,2,2,512,32]{3,4,1,0,2:T(8,128)(2,1)S(1)}, bf16[8,2,2,512,32]{3,4,1,0,2:T(8,128)(2,1)S(1)}, u32[]{:S(2)}, u32[]{:S(2)}) %collective-permute-start.9) | collective-permute-done | bytes 1048608 | tf_op jit(solution)/shard_map/ppermute | solution.py:130
  89.2 2.0 collective-permute-start.10
  91.2 2.0 fusion.9
  93.4 0.8 copy.214
  94.8 0.9 fusion.18
  95.9 1.3 fusion.14
  97.7 14.2 %collective-permute-done.10 = bf16[8,2,2,512,32]{3,4,1,0,2:T(8,128)(2,1)} collective-permute-done((bf16[8,2,2,512,32]{3,4,1,0,2:T(8,128)(2,1)S(1)}, bf16[8,2,2,512,32]{3,4,1,0,2:T(8,128)(2,1)}, u32[]{:S(2)}, u32[]{:S(2)}) %collective-permute-start.10) | collective-permute-done | bytes 1048608 | tf_op jit(solution)/shard_map/ppermute | solution.py:130
  111.9 1.8 maximum_bitcast_fusion
  113.7 1.6 fusion.2
  115.3 1.6 fusion.1
  116.9 1.6 fusion
  118.5 1.4 fusion.48
  119.8 1.1 select_maximum_fusion
  121.0 0.7 copy.205
  121.7 6.8 %all-to-all-start = ((bf16[2,64,256]{2,0,1:T(2,128)(2,1)}), bf16[2,64,256]{2,0,1:T(2,128)(2,1)S(1)}, u32[]{:S(2)}, u32[]{:S(2)}) async-start(bf16[2,64,256]{2,0,1:T(2,128)(2,1)} %copy.205), calls=%async_computation | async-start | bytes 131072 | tf_op jit(solution)/shard_map/all_to_all | solution.py:242
  128.4 8.3 %collective-permute-start.21 = (bf16[2,400,2048]{2,1,0:T(8,128)(2,1)}, bf16[2,400,2048]{2,1,0:T(8,128)(2,1)}, u32[]{:S(2)}, u32[]{:S(2)}) collective-permute-start(bf16[2,400,2048]{2,1,0:T(8,128)(2,1)} %param.42), channel_id=1, source_target_pairs={{0,8},{8,0},{16,24},{24,16},{32,40},{40,32},{48,56},{56,48},{64,72... | collective-permute-start | bytes 9830408 | tf_op jit(solution)/shard_map/ppermute | solution.py:192
  138.6 1.3 broadcast_select_fusion
  139.9 0.8 scatter.14
  140.8 17.1 %reduce-scatter.2.cloned.1.call-done = f32[2,8,2176]{2,1,0:T(8,128)} async-done(((f32[2,64,2176]{2,1,0:T(8,128)}), f32[2,8,2176]{2,1,0:T(8,128)}) %reduce-scatter.2.cloned.1.call-update) | async-done | bytes 139280 | tf_op jit(solution)/shard_map/reduce_scatter | solution.py:236
  157.9 0.8 fusion.98
  158.6 1.1 fusion.45
  159.9 5.7 %collective-permute-start.11 = (bf16[17,2048]{1,0:T(8,128)(2,1)S(1)}, bf16[17,2048]{1,0:T(8,128)(2,1)S(1)}, u32[]{:S(2)}, u32[]{:S(2)}) collective-permute-start(bf16[17,2048]{1,0:T(8,128)(2,1)S(1)} %pad_maximum_fusion.4), channel_id=1, source_target_pairs={{0,448},{8,456},{16,464},{24,472},{32,480},{40,488},{48,496},{56,5... | collective-permute-start | bytes 208904 | tf_op jit(solution)/shard_map/ppermute | solution.py:133
  165.5 2.1 collective-permute-start.14
  167.7 4.6 %collective-permute-start.12 = (bf16[17,2048]{1,0:T(8,128)(2,1)S(1)}, bf16[17,2048]{1,0:T(8,128)(2,1)S(1)}, u32[]{:S(2)}, u32[]{:S(2)}) collective-permute-start(bf16[17,2048]{1,0:T(8,128)(2,1)S(1)} %collective-permute-done.11), channel_id=1, source_target_pairs={{0,448},{8,456},{16,464},{24,472},{32,480},{40,488},{48,496},{56,5... | collective-permute-start | bytes 208904 | tf_op jit(solution)/shard_map/ppermute | solution.py:133
  172.3 1.9 collective-permute-start.15
  174.2 4.6 %collective-permute-start.13 = (bf16[17,2048]{1,0:T(8,128)(2,1)S(1)}, bf16[17,2048]{1,0:T(8,128)(2,1)S(1)}, u32[]{:S(2)}, u32[]{:S(2)}) collective-permute-start(bf16[17,2048]{1,0:T(8,128)(2,1)S(1)} %collective-permute-done.12), channel_id=1, source_target_pairs={{0,448},{8,456},{16,464},{24,472},{32,480},{40,488},{48,496},{56,5... | collective-permute-start | bytes 208904 | tf_op jit(solution)/shard_map/ppermute | solution.py:133
  178.9 1.9 collective-permute-start.16
  180.8 5.6 %collective-permute-done.16 = bf16[17,2048]{1,0:T(8,128)(2,1)S(1)} collective-permute-done((bf16[17,2048]{1,0:T(8,128)(2,1)S(1)}, bf16[17,2048]{1,0:T(8,128)(2,1)S(1)}, u32[]{:S(2)}, u32[]{:S(2)}) %collective-permute-start.16) | collective-permute-done | bytes 69664 | tf_op jit(solution)/shard_map/ppermute | solution.py:130
  186.4 1.9 collective-permute-start.17
  188.3 5.1 %collective-permute-done.17 = bf16[17,2048]{1,0:T(8,128)(2,1)S(1)} collective-permute-done((bf16[17,2048]{1,0:T(8,128)(2,1)S(1)}, bf16[17,2048]{1,0:T(8,128)(2,1)S(1)}, u32[]{:S(2)}, u32[]{:S(2)}) %collective-permute-start.17) | collective-permute-done | bytes 69664 | tf_op jit(solution)/shard_map/ppermute | solution.py:130
  193.9 2.9 %collective-permute-start.19 = (bf16[8,17,2048]{2,0,1:T(8,128)(2,1)S(1)}, bf16[8,17,2048]{2,0,1:T(8,128)(2,1)S(1)}, u32[]{:S(2)}, u32[]{:S(2)}) collective-permute-start(bf16[8,17,2048]{2,0,1:T(8,128)(2,1)S(1)} %copy.241), channel_id=1, source_target_pairs={{0,16},{8,24},{16,32},{24,40},{32,48},{40,56},{48,0},{56,8},{64,80... | collective-permute-start | bytes 1671176 | tf_op jit(solution)/shard_map/ppermute | solution.py:130
  196.8 3.6 %collective-permute-start.18 = (bf16[8,17,2048]{2,0,1:T(8,128)(2,1)S(1)}, bf16[8,17,2048]{2,0,1:T(8,128)(2,1)S(1)}, u32[]{:S(2)}, u32[]{:S(2)}) collective-permute-start(bf16[8,17,2048]{2,0,1:T(8,128)(2,1)S(1)} %copy.241), channel_id=1, source_target_pairs={{0,48},{8,56},{16,0},{24,8},{32,16},{40,24},{48,32},{56,40},{64,11... | collective-permute-start | bytes 1671176 | tf_op jit(solution)/shard_map/ppermute | solution.py:133
  200.4 5.0 %collective-permute-done.19 = bf16[8,17,2048]{2,0,1:T(8,128)(2,1)S(1)} collective-permute-done((bf16[8,17,2048]{2,0,1:T(8,128)(2,1)S(1)}, bf16[8,17,2048]{2,0,1:T(8,128)(2,1)S(1)}, u32[]{:S(2)}, u32[]{:S(2)}) %collective-permute-start.19) | collective-permute-done | bytes 557088 | tf_op jit(solution)/shard_map/ppermute | solution.py:130
  205.4 1.9 collective-permute-start.20
  208.0 12.8 %collective-permute-done.20 = bf16[8,17,2048]{2,0,1:T(8,128)(2,1)S(1)} collective-permute-done((bf16[8,17,2048]{2,0,1:T(8,128)(2,1)S(1)}, bf16[8,17,2048]{2,0,1:T(8,128)(2,1)S(1)}, u32[]{:S(2)}, u32[]{:S(2)}) %collective-permute-start.20) | collective-permute-done | bytes 557088 | tf_op jit(solution)/shard_map/ppermute | solution.py:130
  221.6 1.7 copy-done
  223.8 3.8 %fusion.187 = (f32[2,256]{1,0:T(2,128)S(1)}, f32[2,256,400]{1,2,0:T(8,128)S(1)}) fusion(bf16[2,400,2048]{2,1,0:T(8,128)(2,1)} %param.42, bf16[32,17,2048]{2,1,0:T(8,128)(2,1)} %bitcast.341), kind=kOutput, calls=%fused_computation.342 | convolution fusion | flops 839065088 | bytes 6195200 | tf_op jit(solution)/shard_map/mnd,mvd->mnv/dot_general | solution.py:115
  227.6 3.1 %fusion.188 = (f32[2,256]{1,0:T(2,128)S(1)}, f32[2,256,400]{1,2,0:T(8,128)S(1)}) fusion(bf16[2,400,2048]{2,1,0:T(8,128)(2,1)} %collective-permute-done.21, bf16[32,17,2048]{2,1,0:T(8,128)(2,1)S(1)} %bitcast.342), kind=kOutput, calls=%fused_computation.343 | convolution fusion | flops 839065088 | bytes 6195200 | tf_op jit(solution)/shard_map/mnd,mvd->mnv/dot_general | solution.py:115
  231.8 0.8 copy.248
  232.7 17.3 %all-to-all-start.1 = ((f32[3,2,64,8]{3,1,0,2:T(2,128)}), f32[3,2,64,8]{3,1,0,2:T(2,128)S(1)}, u32[]{:S(2)}, u32[]{:S(2)}) async-start(f32[3,2,64,8]{3,1,0,2:T(2,128)} %copy.248), calls=%async_computation.2 | async-start | bytes 393216 | tf_op jit(solution)/shard_map/all_to_all | solution.py:296
  250.1 11.9 %all-to-all-done.1 = f32[3,2,64,8]{3,1,0,2:T(2,128)S(1)} async-done(((f32[3,2,64,8]{3,1,0,2:T(2,128)}), f32[3,2,64,8]{3,1,0,2:T(2,128)S(1)}, u32[]{:S(2)}, u32[]{:S(2)}) %all-to-all-start.1) | async-done | bytes 12320 | tf_op jit(solution)/shard_map/all_to_all | solution.py:296
  (198 shorter events, 18.7 us)
Async XLA Ops:
  6.5 16.8 %copy-start.3 = (bf16[2,64,512]{2,1,0:T(8,128)(2,1)S(1)}, bf16[2,64,512]{2,1,0:T(8,128)(2,1)}, u32[]{:S(2)}) copy-start(bf16[2,64,512]{2,1,0:T(8,128)(2,1)} %param.30) | copy-start | bytes 393220
  6.5 19.1 %copy-start.6 = (bf16[2,64,256]{2,1,0:T(8,128)(2,1)S(1)}, bf16[2,64,256]{2,1,0:T(8,128)(2,1)}, u32[]{:S(2)}) copy-start(bf16[2,64,256]{2,1,0:T(8,128)(2,1)} %param.31) | copy-start | bytes 196612
  6.5 16.1 %copy-start.10 = (f32[2,4,512]{2,1,0:T(4,128)S(1)}, f32[2,4,512]{2,1,0:T(4,128)}, u32[]{:S(2)}) copy-start(f32[2,4,512]{2,1,0:T(4,128)} %param.34) | copy-start | bytes 49156
  6.5 17.3 %copy-start.8 = (bf16[2,3,3,256]{3,0,2,1:T(2,128)(2,1)S(1)}, bf16[2,3,3,256]{3,0,2,1:T(2,128)(2,1)}, u32[]{:S(2)}) copy-start(bf16[2,3,3,256]{3,0,2,1:T(2,128)(2,1)} %param.44) | copy-start | bytes 27652
  6.5 18.4 %copy-start.12 = (f32[2,4,256]{2,1,0:T(4,128)S(1)}, f32[2,4,256]{2,1,0:T(4,128)}, u32[]{:S(2)}) copy-start(f32[2,4,256]{2,1,0:T(4,128)} %param.35) | copy-start | bytes 24580
  6.5 151.3 %reduce-scatter.2.cloned.1.call-start = ((), (), s32[]{:S(2)}) async-start(), calls=%async_computation.3 | async-start | bytes 1253376 | tf_op jit(solution)/shard_map/reduce_scatter | solution.py:236
  6.6 24.3 %collective-permute-start = (bf16[2,512,32]{1,2,0:T(8,128)(2,1)}, bf16[2,512,32]{1,2,0:T(8,128)(2,1)S(1)}, u32[]{:S(2)}, u32[]{:S(2)}) collective-permute-start(bf16[2,512,32]{1,2,0:T(8,128)(2,1)} %param.41), channel_id=1, source_target_pairs={{0,8},{8,0},{16,24},{24,16},{32,40},{40,32},{48,56},{56,48},{64,72... | collective-permute-start | bytes 196616 | tf_op jit(solution)/shard_map/ppermute | solution.py:130
  17.0 13.0 %copy-start.20 = (pred[3]{0:T(512)(128)(4,1)}, pred[3]{0:T(512)(128)(4,1)S(1)}, u32[]{:S(2)}) copy-start(pred[3]{0:T(512)(128)(4,1)S(1)} %get-tuple-element.52) | copy-start | bytes 13
  18.6 7.5 %copy-start.33 = (bf16[2,3,512,128]{3,2,1,0:T(8,128)(2,1)S(1)}, bf16[2,3,512,128]{3,2,1,0:T(8,128)(2,1)}, u32[]{:S(2)}) copy-start(bf16[2,3,512,128]{3,2,1,0:T(8,128)(2,1)} %param.45) | copy-start | bytes 2359300
  19.5 7.8 %copy-start.18 = (f32[2,8]{1,0:T(2,128)S(1)}, f32[2,8]{1,0:T(2,128)}, u32[]{:S(2)}) copy-start(f32[2,8]{1,0:T(2,128)} %param.37) | copy-start | bytes 196
  19.5 7.8 %copy-start.19 = (f32[2,8]{1,0:T(2,128)S(1)}, f32[2,8]{1,0:T(2,128)}, u32[]{:S(2)}) copy-start(f32[2,8]{1,0:T(2,128)} %param.36) | copy-start | bytes 196
  19.5 7.8 %copy-start.11 = (bf16[2,64,8]{1,2,0:T(8,128)(2,1)S(1)}, bf16[2,64,8]{1,2,0:T(8,128)(2,1)}, u32[]{:S(2)}) copy-start(bf16[2,64,8]{1,2,0:T(8,128)(2,1)} %param.32) | copy-start | bytes 6148
  19.6 9.2 %copy-start.17 = (f32[2,8]{1,0:T(2,128)S(1)}, f32[2,8]{1,0:T(2,128)}, u32[]{:S(2)}) copy-start(f32[2,8]{1,0:T(2,128)} %param.38) | copy-start | bytes 196
  19.8 6.2 %copy-start.15 = (f32[64,3]{0,1:T(4,128)}, f32[64,3]{0,1:T(4,128)S(1)}, u32[]{:S(2)}) copy-start(f32[64,3]{0,1:T(4,128)S(1)} %fusion.146) | copy-start | bytes 2308
  20.5 5.5 %copy-start.35 = (f32[3]{0:T(128)}, f32[3]{0:T(128)S(1)}, u32[]{:S(2)}) copy-start(f32[3]{0:T(128)S(1)} %get-tuple-element.109) | copy-start | bytes 40
  22.6 3.4 %copy-start.25 = (pred[64]{0:T(512)(128)(4,1)}, pred[64]{0:T(512)(128)(4,1)S(1)}, u32[]{:S(2)}) copy-start(pred[64]{0:T(512)(128)(4,1)S(1)} %get-tuple-element.115) | copy-start | bytes 196
  22.7 3.4 %copy-start.26 = (pred[64]{0:T(512)(128)(4,1)}, pred[64]{0:T(512)(128)(4,1)S(1)}, u32[]{:S(2)}) copy-start(pred[64]{0:T(512)(128)(4,1)S(1)} %get-tuple-element.116) | copy-start | bytes 196
  22.7 3.4 %copy-start.27 = (pred[64]{0:T(512)(128)(4,1)}, pred[64]{0:T(512)(128)(4,1)S(1)}, u32[]{:S(2)}) copy-start(pred[64]{0:T(512)(128)(4,1)S(1)} %get-tuple-element.117) | copy-start | bytes 196
  22.7 3.4 %copy-start.28 = (pred[64]{0:T(512)(128)(4,1)}, pred[64]{0:T(512)(128)(4,1)S(1)}, u32[]{:S(2)}) copy-start(pred[64]{0:T(512)(128)(4,1)S(1)} %get-tuple-element.118) | copy-start | bytes 196
  22.7 3.4 %copy-start.29 = (pred[64]{0:T(512)(128)(4,1)}, pred[64]{0:T(512)(128)(4,1)S(1)}, u32[]{:S(2)}) copy-start(pred[64]{0:T(512)(128)(4,1)S(1)} %get-tuple-element.119) | copy-start | bytes 196
  22.7 3.4 %copy-start.30 = (pred[64]{0:T(512)(128)(4,1)}, pred[64]{0:T(512)(128)(4,1)S(1)}, u32[]{:S(2)}) copy-start(pred[64]{0:T(512)(128)(4,1)S(1)} %get-tuple-element.120) | copy-start | bytes 196
  22.7 3.4 %copy-start.31 = (pred[64]{0:T(512)(128)(4,1)}, pred[64]{0:T(512)(128)(4,1)S(1)}, u32[]{:S(2)}) copy-start(pred[64]{0:T(512)(128)(4,1)S(1)} %get-tuple-element.121) | copy-start | bytes 196
  22.7 3.4 %copy-start.32 = (pred[64]{0:T(512)(128)(4,1)}, pred[64]{0:T(512)(128)(4,1)S(1)}, u32[]{:S(2)}) copy-start(pred[64]{0:T(512)(128)(4,1)S(1)} %get-tuple-element.122) | copy-start | bytes 196
  22.7 5.7 %copy-start.23 = (pred[64]{0:T(512)(128)(4,1)}, pred[64]{0:T(512)(128)(4,1)S(1)}, u32[]{:S(2)}) copy-start(pred[64]{0:T(512)(128)(4,1)S(1)} %get-tuple-element.113) | copy-start | bytes 196
  22.7 5.8 %copy-start.24 = (pred[64]{0:T(512)(128)(4,1)}, pred[64]{0:T(512)(128)(4,1)S(1)}, u32[]{:S(2)}) copy-start(pred[64]{0:T(512)(128)(4,1)S(1)} %get-tuple-element.114) | copy-start | bytes 196
  22.7 6.0 %copy-start.21 = (pred[64]{0:T(512)(128)(4,1)}, pred[64]{0:T(512)(128)(4,1)S(1)}, u32[]{:S(2)}) copy-start(pred[64]{0:T(512)(128)(4,1)S(1)} %get-tuple-element.111) | copy-start | bytes 196
  22.8 6.0 %copy-start.22 = (pred[64]{0:T(512)(128)(4,1)}, pred[64]{0:T(512)(128)(4,1)S(1)}, u32[]{:S(2)}) copy-start(pred[64]{0:T(512)(128)(4,1)S(1)} %get-tuple-element.112) | copy-start | bytes 196
  23.4 7.6 %copy-start.2 = (bf16[2,512,32]{1,2,0:T(8,128)(2,1)S(1)}, bf16[2,512,32]{1,2,0:T(8,128)(2,1)}, u32[]{:S(2)}) copy-start(bf16[2,512,32]{1,2,0:T(8,128)(2,1)} %param.41) | copy-start | bytes 196612
  28.8 40.0 %copy-start.13 = (s32[1024]{0:T(1024)}, s32[1024]{0:T(1024)S(1)}, u32[]{:S(2)}) copy-start(s32[1024]{0:T(1024)S(1)} %pad_clamp_fusion) | copy-start | bytes 12292
  31.0 8.2 %collective-permute-start.1 = (bf16[2,2,512,32]{2,3,0,1:T(8,128)(2,1)S(1)}, bf16[2,2,512,32]{2,3,0,1:T(8,128)(2,1)S(1)}, u32[]{:S(2)}, u32[]{:S(2)}) collective-permute-start(bf16[2,2,512,32]{2,3,0,1:T(8,128)(2,1)S(1)} %pad_maximum_fusion.3), channel_id=1, source_target_pairs={{0,448},{8,456},{16,464},{24,472},{32,480},{40,488},{48,496},{56,5... | collective-permute-start | bytes 393224 | tf_op jit(solution)/shard_map/ppermute | solution.py:133
  36.3 8.2 %collective-permute-start.4 = (bf16[2,2,512,32]{2,3,0,1:T(8,128)(2,1)S(1)}, bf16[2,2,512,32]{2,3,0,1:T(8,128)(2,1)S(1)}, u32[]{:S(2)}, u32[]{:S(2)}) collective-permute-start(bf16[2,2,512,32]{2,3,0,1:T(8,128)(2,1)S(1)} %pad_maximum_fusion.3), channel_id=1, source_target_pairs={{0,64},{8,72},{16,80},{24,88},{32,96},{40,104},{48,112},{56,120},{... | collective-permute-start | bytes 393224 | tf_op jit(solution)/shard_map/ppermute | solution.py:130
  39.2 7.3 %collective-permute-start.2 = (bf16[2,2,512,32]{2,3,0,1:T(8,128)(2,1)S(1)}, bf16[2,2,512,32]{2,3,0,1:T(8,128)(2,1)S(1)}, u32[]{:S(2)}, u32[]{:S(2)}) collective-permute-start(bf16[2,2,512,32]{2,3,0,1:T(8,128)(2,1)S(1)} %collective-permute-done.1), channel_id=1, source_target_pairs={{0,448},{8,456},{16,464},{24,472},{32,480},{40,488},{48,496},{56,5... | collective-permute-start | bytes 393224 | tf_op jit(solution)/shard_map/ppermute | solution.py:133
  44.5 7.3 %collective-permute-start.5 = (bf16[2,2,512,32]{2,3,0,1:T(8,128)(2,1)S(1)}, bf16[2,2,512,32]{2,3,0,1:T(8,128)(2,1)S(1)}, u32[]{:S(2)}, u32[]{:S(2)}) collective-permute-start(bf16[2,2,512,32]{2,3,0,1:T(8,128)(2,1)S(1)} %collective-permute-done.4), channel_id=1, source_target_pairs={{0,64},{8,72},{16,80},{24,88},{32,96},{40,104},{48,112},{56,120},{... | collective-permute-start | bytes 393224 | tf_op jit(solution)/shard_map/ppermute | solution.py:130
  46.5 14.2 %collective-permute-start.3 = (bf16[2,2,512,32]{2,3,0,1:T(8,128)(2,1)S(1)}, bf16[2,2,512,32]{2,3,0,1:T(8,128)(2,1)S(1)}, u32[]{:S(2)}, u32[]{:S(2)}) collective-permute-start(bf16[2,2,512,32]{2,3,0,1:T(8,128)(2,1)S(1)} %collective-permute-done.2), channel_id=1, source_target_pairs={{0,448},{8,456},{16,464},{24,472},{32,480},{40,488},{48,496},{56,5... | collective-permute-start | bytes 393224 | tf_op jit(solution)/shard_map/ppermute | solution.py:133
  51.8 6.9 %collective-permute-start.6 = (bf16[2,2,512,32]{2,3,0,1:T(8,128)(2,1)S(1)}, bf16[2,2,512,32]{2,3,0,1:T(8,128)(2,1)S(1)}, u32[]{:S(2)}, u32[]{:S(2)}) collective-permute-start(bf16[2,2,512,32]{2,3,0,1:T(8,128)(2,1)S(1)} %collective-permute-done.5), channel_id=1, source_target_pairs={{0,64},{8,72},{16,80},{24,88},{32,96},{40,104},{48,112},{56,120},{... | collective-permute-start | bytes 393224 | tf_op jit(solution)/shard_map/ppermute | solution.py:130
  58.7 6.9 %collective-permute-start.7 = (bf16[2,2,512,32]{2,3,0,1:T(8,128)(2,1)S(1)}, bf16[2,2,512,32]{2,3,0,1:T(8,128)(2,1)S(1)}, u32[]{:S(2)}, u32[]{:S(2)}) collective-permute-start(bf16[2,2,512,32]{2,3,0,1:T(8,128)(2,1)S(1)} %collective-permute-done.6), channel_id=1, source_target_pairs={{0,64},{8,72},{16,80},{24,88},{32,96},{40,104},{48,112},{56,120},{... | collective-permute-start | bytes 393224 | tf_op jit(solution)/shard_map/ppermute | solution.py:130
  65.7 23.5 %collective-permute-start.9 = (bf16[8,2,2,512,32]{3,4,1,0,2:T(8,128)(2,1)S(1)}, bf16[8,2,2,512,32]{3,4,1,0,2:T(8,128)(2,1)S(1)}, u32[]{:S(2)}, u32[]{:S(2)}) collective-permute-start(bf16[8,2,2,512,32]{3,4,1,0,2:T(8,128)(2,1)S(1)} %bitcast_dynamic-update-slice_fusion.7), channel_id=1, source_target_pairs={{0,16},{8,24},{16,32},{24,40},{32,48},{40,56},{48,0},{56,8},{64,80... | collective-permute-start | bytes 3145736 | tf_op jit(solution)/shard_map/ppermute | solution.py:130
  68.9 28.5 %copy-start.4 = (bf16[2,64,512]{2,1,0:T(8,128)(2,1)S(1)}, bf16[2,64,512]{2,1,0:T(8,128)(2,1)}, u32[]{:S(2)}) copy-start(bf16[2,64,512]{2,1,0:T(8,128)(2,1)} %param.29) | copy-start | bytes 393220
  73.8 23.9 %collective-permute-start.8 = (bf16[8,2,2,512,32]{3,4,1,0,2:T(8,128)(2,1)S(1)}, bf16[8,2,2,512,32]{3,4,1,0,2:T(8,128)(2,1)}, u32[]{:S(2)}, u32[]{:S(2)}) collective-permute-start(bf16[8,2,2,512,32]{3,4,1,0,2:T(8,128)(2,1)S(1)} %bitcast_dynamic-update-slice_fusion.7), channel_id=1, source_target_pairs={{0,48},{8,56},{16,0},{24,8},{32,16},{40,24},{48,32},{56,40},{64,11... | collective-permute-start | bytes 3145736 | tf_op jit(solution)/shard_map/ppermute | solution.py:133
  89.2 22.7 %collective-permute-start.10 = (bf16[8,2,2,512,32]{3,4,1,0,2:T(8,128)(2,1)S(1)}, bf16[8,2,2,512,32]{3,4,1,0,2:T(8,128)(2,1)}, u32[]{:S(2)}, u32[]{:S(2)}) collective-permute-start(bf16[8,2,2,512,32]{3,4,1,0,2:T(8,128)(2,1)S(1)} %collective-permute-done.9), channel_id=1, source_target_pairs={{0,16},{8,24},{16,32},{24,40},{32,48},{40,56},{48,0},{56,8},{64,80... | collective-permute-start | bytes 3145736 | tf_op jit(solution)/shard_map/ppermute | solution.py:130
  116.9 1.6 copy-start.14
  118.4 2.5 copy-start.7
  118.5 18.9 %copy-start.16 = (s32[64]{0:T(128)S(1)}, s32[64]{0:T(128)}, u32[]{:S(2)}) copy-start(s32[64]{0:T(128)} %param.48) | copy-start | bytes 772
  119.8 39.9 %copy-start.9 = (f32[2,2048]{1,0:T(2,128)S(1)}, f32[2,2048]{1,0:T(2,128)}, u32[]{:S(2)}) copy-start(f32[2,2048]{1,0:T(2,128)} %param.40) | copy-start | bytes 49156
  121.7 19.1 %all-to-all-start = ((bf16[2,64,256]{2,0,1:T(2,128)(2,1)}), bf16[2,64,256]{2,0,1:T(2,128)(2,1)S(1)}, u32[]{:S(2)}, u32[]{:S(2)}) async-start(bf16[2,64,256]{2,0,1:T(2,128)(2,1)} %copy.205), calls=%async_computation | async-start | bytes 131072 | tf_op jit(solution)/shard_map/all_to_all | solution.py:242
  128.4 99.2 %collective-permute-start.21 = (bf16[2,400,2048]{2,1,0:T(8,128)(2,1)}, bf16[2,400,2048]{2,1,0:T(8,128)(2,1)}, u32[]{:S(2)}, u32[]{:S(2)}) collective-permute-start(bf16[2,400,2048]{2,1,0:T(8,128)(2,1)} %param.42), channel_id=1, source_target_pairs={{0,8},{8,0},{16,24},{24,16},{32,40},{40,32},{48,56},{56,48},{64,72... | collective-permute-start | bytes 9830408 | tf_op jit(solution)/shard_map/ppermute | solution.py:192
  159.9 7.8 %collective-permute-start.11 = (bf16[17,2048]{1,0:T(8,128)(2,1)S(1)}, bf16[17,2048]{1,0:T(8,128)(2,1)S(1)}, u32[]{:S(2)}, u32[]{:S(2)}) collective-permute-start(bf16[17,2048]{1,0:T(8,128)(2,1)S(1)} %pad_maximum_fusion.4), channel_id=1, source_target_pairs={{0,448},{8,456},{16,464},{24,472},{32,480},{40,488},{48,496},{56,5... | collective-permute-start | bytes 208904 | tf_op jit(solution)/shard_map/ppermute | solution.py:133
  165.5 6.7 %collective-permute-start.14 = (bf16[17,2048]{1,0:T(8,128)(2,1)S(1)}, bf16[17,2048]{1,0:T(8,128)(2,1)S(1)}, u32[]{:S(2)}, u32[]{:S(2)}) collective-permute-start(bf16[17,2048]{1,0:T(8,128)(2,1)S(1)} %pad_maximum_fusion.4), channel_id=1, source_target_pairs={{0,64},{8,72},{16,80},{24,88},{32,96},{40,104},{48,112},{56,120},{... | collective-permute-start | bytes 208904 | tf_op jit(solution)/shard_map/ppermute | solution.py:130
  167.7 6.5 %collective-permute-start.12 = (bf16[17,2048]{1,0:T(8,128)(2,1)S(1)}, bf16[17,2048]{1,0:T(8,128)(2,1)S(1)}, u32[]{:S(2)}, u32[]{:S(2)}) collective-permute-start(bf16[17,2048]{1,0:T(8,128)(2,1)S(1)} %collective-permute-done.11), channel_id=1, source_target_pairs={{0,448},{8,456},{16,464},{24,472},{32,480},{40,488},{48,496},{56,5... | collective-permute-start | bytes 208904 | tf_op jit(solution)/shard_map/ppermute | solution.py:133
  172.3 6.6 %collective-permute-start.15 = (bf16[17,2048]{1,0:T(8,128)(2,1)S(1)}, bf16[17,2048]{1,0:T(8,128)(2,1)S(1)}, u32[]{:S(2)}, u32[]{:S(2)}) collective-permute-start(bf16[17,2048]{1,0:T(8,128)(2,1)S(1)} %collective-permute-done.14), channel_id=1, source_target_pairs={{0,64},{8,72},{16,80},{24,88},{32,96},{40,104},{48,112},{56,120},{... | collective-permute-start | bytes 208904 | tf_op jit(solution)/shard_map/ppermute | solution.py:130
  174.2 14.1 %collective-permute-start.13 = (bf16[17,2048]{1,0:T(8,128)(2,1)S(1)}, bf16[17,2048]{1,0:T(8,128)(2,1)S(1)}, u32[]{:S(2)}, u32[]{:S(2)}) collective-permute-start(bf16[17,2048]{1,0:T(8,128)(2,1)S(1)} %collective-permute-done.12), channel_id=1, source_target_pairs={{0,448},{8,456},{16,464},{24,472},{32,480},{40,488},{48,496},{56,5... | collective-permute-start | bytes 208904 | tf_op jit(solution)/shard_map/ppermute | solution.py:133
  178.9 7.5 %collective-permute-start.16 = (bf16[17,2048]{1,0:T(8,128)(2,1)S(1)}, bf16[17,2048]{1,0:T(8,128)(2,1)S(1)}, u32[]{:S(2)}, u32[]{:S(2)}) collective-permute-start(bf16[17,2048]{1,0:T(8,128)(2,1)S(1)} %collective-permute-done.15), channel_id=1, source_target_pairs={{0,64},{8,72},{16,80},{24,88},{32,96},{40,104},{48,112},{56,120},{... | collective-permute-start | bytes 208904 | tf_op jit(solution)/shard_map/ppermute | solution.py:130
  186.4 7.1 %collective-permute-start.17 = (bf16[17,2048]{1,0:T(8,128)(2,1)S(1)}, bf16[17,2048]{1,0:T(8,128)(2,1)S(1)}, u32[]{:S(2)}, u32[]{:S(2)}) collective-permute-start(bf16[17,2048]{1,0:T(8,128)(2,1)S(1)} %collective-permute-done.16), channel_id=1, source_target_pairs={{0,64},{8,72},{16,80},{24,88},{32,96},{40,104},{48,112},{56,120},{... | collective-permute-start | bytes 208904 | tf_op jit(solution)/shard_map/ppermute | solution.py:130
  193.9 11.5 %collective-permute-start.19 = (bf16[8,17,2048]{2,0,1:T(8,128)(2,1)S(1)}, bf16[8,17,2048]{2,0,1:T(8,128)(2,1)S(1)}, u32[]{:S(2)}, u32[]{:S(2)}) collective-permute-start(bf16[8,17,2048]{2,0,1:T(8,128)(2,1)S(1)} %copy.241), channel_id=1, source_target_pairs={{0,16},{8,24},{16,32},{24,40},{32,48},{40,56},{48,0},{56,8},{64,80... | collective-permute-start | bytes 1671176 | tf_op jit(solution)/shard_map/ppermute | solution.py:130
  196.8 10.8 %collective-permute-start.18 = (bf16[8,17,2048]{2,0,1:T(8,128)(2,1)S(1)}, bf16[8,17,2048]{2,0,1:T(8,128)(2,1)S(1)}, u32[]{:S(2)}, u32[]{:S(2)}) collective-permute-start(bf16[8,17,2048]{2,0,1:T(8,128)(2,1)S(1)} %copy.241), channel_id=1, source_target_pairs={{0,48},{8,56},{16,0},{24,8},{32,16},{40,24},{48,32},{56,40},{64,11... | collective-permute-start | bytes 1671176 | tf_op jit(solution)/shard_map/ppermute | solution.py:133
  205.4 15.4 %collective-permute-start.20 = (bf16[8,17,2048]{2,0,1:T(8,128)(2,1)S(1)}, bf16[8,17,2048]{2,0,1:T(8,128)(2,1)S(1)}, u32[]{:S(2)}, u32[]{:S(2)}) collective-permute-start(bf16[8,17,2048]{2,0,1:T(8,128)(2,1)S(1)} %collective-permute-done.19), channel_id=1, source_target_pairs={{0,16},{8,24},{16,32},{24,40},{32,48},{40,56},{48,0},{56,8},{64,80... | collective-permute-start | bytes 1671176 | tf_op jit(solution)/shard_map/ppermute | solution.py:130
  221.6 1.7 copy-start
  223.8 3.8 %copy-start.1 = (bf16[4,8,17,2048]{3,2,1,0:T(8,128)(2,1)S(1)}, bf16[4,8,17,2048]{3,2,1,0:T(8,128)(2,1)}, u32[]{:S(2)}) copy-start(bf16[4,8,17,2048]{3,2,1,0:T(8,128)(2,1)} %copy-done) | copy-start | bytes 6684676
  227.6 4.0 %copy-start.5 = (f32[3,2,8,4,8]{4,2,3,1,0:T(8,128)S(1)}, f32[3,2,8,4,8]{4,2,3,1,0:T(8,128)}, u32[]{:S(2)}) copy-start(f32[3,2,8,4,8]{4,2,3,1,0:T(8,128)} %constant.292.clone.1) | copy-start | bytes 18436
  230.8 19.2 %copy-start.34 = (s32[64]{0:T(128)S(1)}, s32[64]{0:T(128)}, u32[]{:S(2)}) copy-start(s32[64]{0:T(128)} %param.49) | copy-start | bytes 772
  232.7 29.4 %all-to-all-start.1 = ((f32[3,2,64,8]{3,1,0,2:T(2,128)}), f32[3,2,64,8]{3,1,0,2:T(2,128)S(1)}, u32[]{:S(2)}, u32[]{:S(2)}) async-start(f32[3,2,64,8]{3,1,0,2:T(2,128)} %copy.248), calls=%async_computation.2 | async-start | bytes 393216 | tf_op jit(solution)/shard_map/all_to_all | solution.py:296
Sparse Core Ops, SparseCore 0:
  121.1 36.7 reduce-scatter.1

commit v5 on v3

--- a/solution.py
+++ b/solution.py
@@ -245,9 +245,14 @@
         lane_index * part_width,
         2,
     )
-    hidden = lax.psum_scatter(partial_out, "tp", scatter_dimension=1, tiled=True).astype(
-        jnp.bfloat16
-    )
+    pieces = lax.all_to_all(
+        partial_out.reshape(models, groups, row_count, partial_out.shape[2]),
+        "tp",
+        split_axis=1,
+        concat_axis=1,
+        tiled=True,
+    )
+    hidden = jnp.sum(pieces, axis=1).astype(jnp.bfloat16)
     full_width = hidden.shape[2]
     hidden_float = hidden.astype(jnp.float32)
     final_squares = jnp.sum(hidden_float * hidden_float, axis=2)

time: 251 us -> 240 us (0.956)
  waiting for transfers between devices: 81.4 us -> 73.2 us
    reduce_scatter x1 -> x0, waiting for transfers between devices: 22.9 us -> none  [local(): lax.psum_scatter(partial_out, 'tp', scatter_dimension=1, tiled=True)]
    all_to_all x0 -> x1, waiting for transfers between devices: none -> 18.4 us  [local(): lax.all_to_all(partial_out.reshape(models, groups, row_count, partial_out...]
    all_to_all x0 -> x1, starting transfers between devices: none -> 6.59 us  [local(): lax.all_to_all(partial_out.reshape(models, groups, row_count, partial_out...]
    all_to_all x1, starting transfers between devices: 17.4 us -> 12.2 us  [local(): lax.all_to_all(send, 'req', split_axis=2, concat_axis=2, tiled=True)]
    ppermute x13, waiting for transfers between devices: 40.6 us -> 35.5 us  [ring_gather(): forward = lax.ppermute(forward, 'req', perm_of(1))]
  transfers between devices with their start and end apart: 25 -> 25, of which waited for: 11 -> 10; matrix products, arithmetic and copies ran while one was open for 12% -> 12% of each run, Pallas kernels for 0% -> 0%
where the time goes in v5:
time: 240 us; the launch traced here: 238 us
  starting transfers between devices  95 us (40%)
  waiting for transfers between devices  73.2 us (30%)
  matrix products  17.1 us (7%)
  blocking collectives  14.7 us (6%)
  between operations  14.7 us (6%)
  other arithmetic  12.2 us (5%)
  local copies, waits for them, and re-layouts  11.4 us (5%)
    ppermute x8, starting transfers between devices, ring_gather(): backward = lax.ppermute(backward, 'req', perm_of(-1))  37.4 us
    ppermute x13, waiting for transfers between devices, ring_gather(): forward = lax.ppermute(forward, 'req', perm_of(1))  35.5 us
    ppermute x13, starting transfers between devices, ring_gather(): forward = lax.ppermute(forward, 'req', perm_of(1))  34.2 us
    all_to_all x1, waiting for transfers between devices, local(): lax.all_to_all(partial_out.reshape(models, groups, row_count, partial_out...  18.4 us
    psum x1, blocking collectives, local(): squares = lax.psum(jnp.sum(gated * gated, axis=2), 'tp')  14.7 us
    all_to_all x1, starting transfers between devices, local(): lax.all_to_all(send, 'req', split_axis=2, concat_axis=2, tiled=True)  12.2 us
    all_to_all x1, waiting for transfers between devices, local(): lax.all_to_all(send, 'req', split_axis=2, concat_axis=2, tiled=True)  11.9 us
    all_gather x1, waiting for transfers between devices, local(): first_weight = lax.all_gather(out_weight[0], 'req', axis=1, tiled=True)  7.26 us
  transfers between devices with their start and end apart: 25, of which 10 were waited for; matrix products, arithmetic and copies ran while one was open for 12% of the time, Pallas kernels for 0%

profile of v5, /device:TPU:1, one launch (start us, length us, event | category | flops | bytes accessed | tf_op | source)
XLA Modules:
  0.0 238.3 jit_solution(10455532700321212733)
XLA Ops:
  6.6 1.4 fusion.174
  8.1 8.8 %collective-permute-start = (bf16[512,32]{0,1:T(8,128)(2,1)S(1)}, bf16[512,32]{0,1:T(8,128)(2,1)S(1)}, u32[]{:S(2)}, u32[]{:S(2)}) collective-permute-start(bf16[512,32]{0,1:T(8,128)(2,1)S(1)} %get-tuple-element.47), channel_id=1, source_target_pairs={{0,8},{8,0},{16,24},{24,16},{32,40},{40,32},{48,56},{56,48},{64,72... | collective-permute-start | bytes 98312 | tf_op jit(solution)/shard_map/ppermute | solution.py:130
  16.9 0.8 reduce-window.4
  17.7 0.7 compare_and_fusion
  18.3 0.7 fusion.166
  19.0 0.9 slice_convert_fusion.1
  22.7 1.0 fusion.11
  25.7 0.6 gather_fusion.1
  26.3 0.6 gather_fusion
  27.1 0.7 fusion.13
  28.7 5.3 %collective-permute-start.1 = (bf16[2,512,32]{1,2,0:T(8,128)(2,1)S(1)}, bf16[2,512,32]{1,2,0:T(8,128)(2,1)S(1)}, u32[]{:S(2)}, u32[]{:S(2)}) collective-permute-start(bf16[2,512,32]{1,2,0:T(8,128)(2,1)S(1)} %pad_maximum_fusion.5), channel_id=1, source_target_pairs={{0,448},{8,456},{16,464},{24,472},{32,480},{40,488},{48,496},{56,5... | collective-permute-start | bytes 196616 | tf_op jit(solution)/shard_map/ppermute | solution.py:133
  34.0 1.9 collective-permute-start.4
  35.9 4.8 %collective-permute-start.2 = (bf16[2,512,32]{1,2,0:T(8,128)(2,1)S(1)}, bf16[2,512,32]{1,2,0:T(8,128)(2,1)S(1)}, u32[]{:S(2)}, u32[]{:S(2)}) collective-permute-start(bf16[2,512,32]{1,2,0:T(8,128)(2,1)S(1)} %collective-permute-done.1), channel_id=1, source_target_pairs={{0,448},{8,456},{16,464},{24,472},{32,480},{40,488},{48,496},{56,5... | collective-permute-start | bytes 196616 | tf_op jit(solution)/shard_map/ppermute | solution.py:133
  40.8 1.9 collective-permute-start.5
  42.7 4.6 %collective-permute-start.3 = (bf16[2,512,32]{1,2,0:T(8,128)(2,1)S(1)}, bf16[2,512,32]{1,2,0:T(8,128)(2,1)S(1)}, u32[]{:S(2)}, u32[]{:S(2)}) collective-permute-start(bf16[2,512,32]{1,2,0:T(8,128)(2,1)S(1)} %collective-permute-done.2), channel_id=1, source_target_pairs={{0,448},{8,456},{16,464},{24,472},{32,480},{40,488},{48,496},{56,5... | collective-permute-start | bytes 196616 | tf_op jit(solution)/shard_map/ppermute | solution.py:133
  47.3 1.9 collective-permute-start.6
  49.3 4.3 %collective-permute-done.6 = bf16[2,512,32]{1,2,0:T(8,128)(2,1)S(1)} collective-permute-done((bf16[2,512,32]{1,2,0:T(8,128)(2,1)S(1)}, bf16[2,512,32]{1,2,0:T(8,128)(2,1)S(1)}, u32[]{:S(2)}, u32[]{:S(2)}) %collective-permute-start.6) | collective-permute-done | bytes 65568 | tf_op jit(solution)/shard_map/ppermute | solution.py:130
  53.6 1.9 collective-permute-start.7
  55.5 4.3 %collective-permute-done.7 = bf16[2,512,32]{1,2,0:T(8,128)(2,1)S(1)} collective-permute-done((bf16[2,512,32]{1,2,0:T(8,128)(2,1)S(1)}, bf16[2,512,32]{1,2,0:T(8,128)(2,1)S(1)}, u32[]{:S(2)}, u32[]{:S(2)}) %collective-permute-start.7) | collective-permute-done | bytes 65568 | tf_op jit(solution)/shard_map/ppermute | solution.py:130
  59.9 3.4 %collective-permute-start.9 = (bf16[8,2,512,32]{2,3,1,0:T(8,128)(2,1)S(1)}, bf16[8,2,512,32]{2,3,1,0:T(8,128)(2,1)S(1)}, u32[]{:S(2)}, u32[]{:S(2)}) collective-permute-start(bf16[8,2,512,32]{2,3,1,0:T(8,128)(2,1)S(1)} %bitcast_dynamic-update-slice_fusion.8), channel_id=1, source_target_pairs={{0,16},{8,24},{16,32},{24,40},{32,48},{40,56},{48,0},{56,8},{64,80... | collective-permute-start | bytes 1572872 | tf_op jit(solution)/shard_map/ppermute | solution.py:130
  63.3 1.0 fusion.10
  64.9 0.7 fusion.15
  65.7 3.1 %collective-permute-start.8 = (bf16[8,2,512,32]{2,3,1,0:T(8,128)(2,1)S(1)}, bf16[8,2,512,32]{2,3,1,0:T(8,128)(2,1)S(1)}, u32[]{:S(2)}, u32[]{:S(2)}) collective-permute-start(bf16[8,2,512,32]{2,3,1,0:T(8,128)(2,1)S(1)} %bitcast_dynamic-update-slice_fusion.8), channel_id=1, source_target_pairs={{0,48},{8,56},{16,0},{24,8},{32,16},{40,24},{48,32},{56,40},{64,11... | collective-permute-start | bytes 1572872 | tf_op jit(solution)/shard_map/ppermute | solution.py:133
  68.8 3.3 %collective-permute-done.9 = bf16[8,2,512,32]{2,3,1,0:T(8,128)(2,1)S(1)} collective-permute-done((bf16[8,2,512,32]{2,3,1,0:T(8,128)(2,1)S(1)}, bf16[8,2,512,32]{2,3,1,0:T(8,128)(2,1)S(1)}, u32[]{:S(2)}, u32[]{:S(2)}) %collective-permute-start.9) | collective-permute-done | bytes 524320 | tf_op jit(solution)/shard_map/ppermute | solution.py:130
  72.1 2.6 %collective-permute-start.10 = (bf16[8,2,512,32]{2,3,1,0:T(8,128)(2,1)S(1)}, bf16[8,2,512,32]{2,3,1,0:T(8,128)(2,1)S(1)}, u32[]{:S(2)}, u32[]{:S(2)}) collective-permute-start(bf16[8,2,512,32]{2,3,1,0:T(8,128)(2,1)S(1)} %collective-permute-done.9), channel_id=1, source_target_pairs={{0,16},{8,24},{16,32},{24,40},{32,48},{40,56},{48,0},{56,8},{64,80... | collective-permute-start | bytes 1572872 | tf_op jit(solution)/shard_map/ppermute | solution.py:130
  75.0 14.7 %psum.7 = f32[2,64]{1,0:T(2,128)S(1)} all-reduce(f32[2,64]{1,0:T(2,128)S(1)} %multiply_reduce_fusion), channel_id=1, replica_groups=mesh['req'=64,'tp'=8] {'tp'}, use_global_device_ids=true, to_apply=%region_8.10 | all-reduce | flops 128 | bytes 1024 | tf_op jit(solution)/shard_map/psum | solution.py:215
  90.0 0.8 fusion.2
  90.8 0.8 fusion.1
  91.6 0.8 fusion
  92.3 0.7 convolution_bitcast_fusion
  93.1 7.3 %all-gather.3.cloned.1.call-done = bf16[1,512,2048]{1,2,0:T(8,128)(2,1)} async-done(((bf16[1,512,32]{1,2,0:T(8,128)(2,1)}), bf16[1,512,2048]{1,2,0:T(8,128)(2,1)}) %all-gather.3.cloned.1.call-update) | async-done | bytes 2097168 | tf_op jit(solution)/shard_map/all_gather | solution.py:220
  100.4 2.3 convolution_bitcast_fusion.1
  102.8 1.1 copy.190
  103.9 6.6 %all-to-all-start = ((f32[2,8,8,2048]{3,2,0,1:T(8,128)}), f32[2,8,8,2048]{3,2,0,1:T(8,128)S(1)}, u32[]{:S(2)}, u32[]{:S(2)}) async-start(f32[2,8,8,2048]{3,2,0,1:T(8,128)} %copy.190), calls=%async_computation | async-start | bytes 2097152 | tf_op jit(solution)/shard_map/all_to_all | solution.py:248
  110.5 4.6 %collective-permute-start.21 = (bf16[2,400,2048]{2,1,0:T(8,128)(2,1)}, bf16[2,400,2048]{2,1,0:T(8,128)(2,1)}, u32[]{:S(2)}, u32[]{:S(2)}) collective-permute-start(bf16[2,400,2048]{2,1,0:T(8,128)(2,1)} %param.40), channel_id=1, source_target_pairs={{0,8},{8,0},{16,24},{24,16},{32,40},{40,32},{48,56},{56,48},{64,72... | collective-permute-start | bytes 9830408 | tf_op jit(solution)/shard_map/ppermute | solution.py:191
  115.1 0.6 slice.415
  115.7 0.7 and_reduce_fusion
  116.4 0.7 fusion.163
  117.1 1.4 broadcast_select_fusion
  118.5 0.9 scatter.9
  119.4 18.4 %all-to-all-done = f32[2,8,8,2048]{3,2,0,1:T(8,128)S(1)} async-done(((f32[2,8,8,2048]{3,2,0,1:T(8,128)}), f32[2,8,8,2048]{3,2,0,1:T(8,128)S(1)}, u32[]{:S(2)}, u32[]{:S(2)}) %all-to-all-start) | async-done | bytes 1048608 | tf_op jit(solution)/shard_map/all_to_all | solution.py:248
  138.1 5.5 %collective-permute-start.11 = (bf16[17,2048]{1,0:T(8,128)(2,1)S(1)}, bf16[17,2048]{1,0:T(8,128)(2,1)S(1)}, u32[]{:S(2)}, u32[]{:S(2)}) collective-permute-start(bf16[17,2048]{1,0:T(8,128)(2,1)S(1)} %pad_maximum_fusion.4), channel_id=1, source_target_pairs={{0,448},{8,456},{16,464},{24,472},{32,480},{40,488},{48,496},{56,5... | collective-permute-start | bytes 208904 | tf_op jit(solution)/shard_map/ppermute | solution.py:133
  143.7 1.9 collective-permute-start.14
  145.6 5.0 %collective-permute-start.12 = (bf16[17,2048]{1,0:T(8,128)(2,1)S(1)}, bf16[17,2048]{1,0:T(8,128)(2,1)S(1)}, u32[]{:S(2)}, u32[]{:S(2)}) collective-permute-start(bf16[17,2048]{1,0:T(8,128)(2,1)S(1)} %collective-permute-done.11), channel_id=1, source_target_pairs={{0,448},{8,456},{16,464},{24,472},{32,480},{40,488},{48,496},{56,5... | collective-permute-start | bytes 208904 | tf_op jit(solution)/shard_map/ppermute | solution.py:133
  150.7 1.9 collective-permute-start.15
  152.6 4.6 %collective-permute-start.13 = (bf16[17,2048]{1,0:T(8,128)(2,1)S(1)}, bf16[17,2048]{1,0:T(8,128)(2,1)S(1)}, u32[]{:S(2)}, u32[]{:S(2)}) collective-permute-start(bf16[17,2048]{1,0:T(8,128)(2,1)S(1)} %collective-permute-done.12), channel_id=1, source_target_pairs={{0,448},{8,456},{16,464},{24,472},{32,480},{40,488},{48,496},{56,5... | collective-permute-start | bytes 208904 | tf_op jit(solution)/shard_map/ppermute | solution.py:133
  157.2 2.1 collective-permute-start.16
  159.3 4.4 %collective-permute-done.16 = bf16[17,2048]{1,0:T(8,128)(2,1)S(1)} collective-permute-done((bf16[17,2048]{1,0:T(8,128)(2,1)S(1)}, bf16[17,2048]{1,0:T(8,128)(2,1)S(1)}, u32[]{:S(2)}, u32[]{:S(2)}) %collective-permute-start.16) | collective-permute-done | bytes 69664 | tf_op jit(solution)/shard_map/ppermute | solution.py:130
  163.8 1.9 collective-permute-start.17
  165.7 4.6 %collective-permute-done.17 = bf16[17,2048]{1,0:T(8,128)(2,1)S(1)} collective-permute-done((bf16[17,2048]{1,0:T(8,128)(2,1)S(1)}, bf16[17,2048]{1,0:T(8,128)(2,1)S(1)}, u32[]{:S(2)}, u32[]{:S(2)}) %collective-permute-start.17) | collective-permute-done | bytes 69664 | tf_op jit(solution)/shard_map/ppermute | solution.py:130
  170.7 2.0 collective-permute-start.19
  172.7 4.5 %collective-permute-start.18 = (bf16[8,17,2048]{2,0,1:T(8,128)(2,1)S(1)}, bf16[8,17,2048]{2,0,1:T(8,128)(2,1)S(1)}, u32[]{:S(2)}, u32[]{:S(2)}) collective-permute-start(bf16[8,17,2048]{2,0,1:T(8,128)(2,1)S(1)} %copy.191), channel_id=1, source_target_pairs={{0,48},{8,56},{16,0},{24,8},{32,16},{40,24},{48,32},{56,40},{64,11... | collective-permute-start | bytes 1671176 | tf_op jit(solution)/shard_map/ppermute | solution.py:133
  177.3 5.7 %collective-permute-done.19 = bf16[8,17,2048]{2,0,1:T(8,128)(2,1)S(1)} collective-permute-done((bf16[8,17,2048]{2,0,1:T(8,128)(2,1)S(1)}, bf16[8,17,2048]{2,0,1:T(8,128)(2,1)S(1)}, u32[]{:S(2)}, u32[]{:S(2)}) %collective-permute-start.19) | collective-permute-done | bytes 557088 | tf_op jit(solution)/shard_map/ppermute | solution.py:130
  182.9 1.9 collective-permute-start.20
  185.5 8.9 %collective-permute-done.20 = bf16[8,17,2048]{2,0,1:T(8,128)(2,1)S(1)} collective-permute-done((bf16[8,17,2048]{2,0,1:T(8,128)(2,1)S(1)}, bf16[8,17,2048]{2,0,1:T(8,128)(2,1)S(1)}, u32[]{:S(2)}, u32[]{:S(2)}) %collective-permute-start.20) | collective-permute-done | bytes 557088 | tf_op jit(solution)/shard_map/ppermute | solution.py:130
  194.7 0.6 pad_maximum_fusion
  195.3 1.7 copy-done
  197.5 3.8 %fusion.183 = (f32[2,256]{1,0:T(2,128)S(1)}, f32[2,256,400]{1,2,0:T(8,128)S(1)}) fusion(bf16[2,400,2048]{2,1,0:T(8,128)(2,1)} %param.40, bf16[32,17,2048]{2,1,0:T(8,128)(2,1)} %bitcast.345), kind=kOutput, calls=%fused_computation.344 | convolution fusion | flops 839065088 | bytes 6195200 | tf_op jit(solution)/shard_map/mnd,mvd->mnv/dot_general | solution.py:115
  201.3 3.1 %fusion.184 = (f32[2,256]{1,0:T(2,128)S(1)}, f32[2,256,400]{1,2,0:T(8,128)S(1)}) fusion(bf16[2,400,2048]{2,1,0:T(8,128)(2,1)} %collective-permute-done.21, bf16[32,17,2048]{2,1,0:T(8,128)(2,1)S(1)} %bitcast.346), kind=kOutput, calls=%fused_computation.345 | convolution fusion | flops 839065088 | bytes 6195200 | tf_op jit(solution)/shard_map/mnd,mvd->mnv/dot_general | solution.py:115
  204.5 0.4 exponential_reduce_fusion
  205.5 0.8 copy.198
  206.4 12.2 %all-to-all-start.1 = ((f32[3,2,64,8]{3,1,0,2:T(2,128)}), f32[3,2,64,8]{3,1,0,2:T(2,128)S(1)}, u32[]{:S(2)}, u32[]{:S(2)}) async-start(f32[3,2,64,8]{3,1,0,2:T(2,128)} %copy.198), calls=%async_computation.1 | async-start | bytes 393216 | tf_op jit(solution)/shard_map/all_to_all | solution.py:308
  218.7 11.9 %all-to-all-done.1 = f32[3,2,64,8]{3,1,0,2:T(2,128)S(1)} async-done(((f32[3,2,64,8]{3,1,0,2:T(2,128)}), f32[3,2,64,8]{3,1,0,2:T(2,128)S(1)}, u32[]{:S(2)}, u32[]{:S(2)}) %all-to-all-start.1) | async-done | bytes 12320 | tf_op jit(solution)/shard_map/all_to_all | solution.py:308
  230.9 0.6 subtract_multiply_fusion
  (173 shorter events, 10.3 us)
Async XLA Ops:
  6.5 14.6 %copy-start.2 = (bf16[2,64,512]{2,1,0:T(8,128)(2,1)S(1)}, bf16[2,64,512]{2,1,0:T(8,128)(2,1)}, u32[]{:S(2)}) copy-start(bf16[2,64,512]{2,1,0:T(8,128)(2,1)} %param.28) | copy-start | bytes 393220
  6.5 13.4 %copy-start.6 = (bf16[2,64,256]{2,1,0:T(8,128)(2,1)S(1)}, bf16[2,64,256]{2,1,0:T(8,128)(2,1)}, u32[]{:S(2)}) copy-start(bf16[2,64,256]{2,1,0:T(8,128)(2,1)} %param.29) | copy-start | bytes 196612
  6.5 13.8 %copy-start.19 = (s32[1,3]{1,0:T(1,128)S(1)}, s32[1,3]{1,0:T(1,128)}, u32[]{:S(2)}) copy-start(s32[1,3]{1,0:T(1,128)} %param.45) | copy-start | bytes 40
  6.5 13.8 %copy-start.5 = (bf16[2,3,3,512]{3,0,2,1:T(2,128)(2,1)S(1)}, bf16[2,3,3,512]{3,0,2,1:T(2,128)(2,1)}, u32[]{:S(2)}) copy-start(bf16[2,3,3,512]{3,0,2,1:T(2,128)(2,1)} %param.41) | copy-start | bytes 55300
  6.5 14.5 %copy-start.10 = (f32[2,4,512]{2,1,0:T(4,128)S(1)}, f32[2,4,512]{2,1,0:T(4,128)}, u32[]{:S(2)}) copy-start(f32[2,4,512]{2,1,0:T(4,128)} %param.32) | copy-start | bytes 49156
  6.5 93.8 %all-gather.3.cloned.1.call-start = ((), (), s32[]{:S(2)}) async-start(), calls=%async_computation.2 | async-start | bytes 2129920 | tf_op jit(solution)/shard_map/all_gather | solution.py:220
  8.1 20.6 %collective-permute-start = (bf16[512,32]{0,1:T(8,128)(2,1)S(1)}, bf16[512,32]{0,1:T(8,128)(2,1)S(1)}, u32[]{:S(2)}, u32[]{:S(2)}) collective-permute-start(bf16[512,32]{0,1:T(8,128)(2,1)S(1)} %get-tuple-element.47), channel_id=1, source_target_pairs={{0,8},{8,0},{16,24},{24,16},{32,40},{40,32},{48,56},{56,48},{64,72... | collective-permute-start | bytes 98312 | tf_op jit(solution)/shard_map/ppermute | solution.py:130
  20.0 1.7 copy-start.8
  20.0 2.2 copy-start.12
  20.7 1.9 copy-start.18
  21.1 2.7 %copy-start.16 = (f32[2,8]{1,0:T(2,128)S(1)}, f32[2,8]{1,0:T(2,128)}, u32[]{:S(2)}) copy-start(f32[2,8]{1,0:T(2,128)} %param.35) | copy-start | bytes 196
  21.1 2.7 %copy-start.17 = (f32[2,8]{1,0:T(2,128)S(1)}, f32[2,8]{1,0:T(2,128)}, u32[]{:S(2)}) copy-start(f32[2,8]{1,0:T(2,128)} %param.34) | copy-start | bytes 196
  21.2 2.7 %copy-start.11 = (bf16[2,64,8]{1,2,0:T(8,128)(2,1)S(1)}, bf16[2,64,8]{1,2,0:T(8,128)(2,1)}, u32[]{:S(2)}) copy-start(bf16[2,64,8]{1,2,0:T(8,128)(2,1)} %param.30) | copy-start | bytes 6148
  21.5 3.3 %copy-start.15 = (f32[2,8]{1,0:T(2,128)S(1)}, f32[2,8]{1,0:T(2,128)}, u32[]{:S(2)}) copy-start(f32[2,8]{1,0:T(2,128)} %param.36) | copy-start | bytes 196
  28.7 7.3 %collective-permute-start.1 = (bf16[2,512,32]{1,2,0:T(8,128)(2,1)S(1)}, bf16[2,512,32]{1,2,0:T(8,128)(2,1)S(1)}, u32[]{:S(2)}, u32[]{:S(2)}) collective-permute-start(bf16[2,512,32]{1,2,0:T(8,128)(2,1)S(1)} %pad_maximum_fusion.5), channel_id=1, source_target_pairs={{0,448},{8,456},{16,464},{24,472},{32,480},{40,488},{48,496},{56,5... | collective-permute-start | bytes 196616 | tf_op jit(solution)/shard_map/ppermute | solution.py:133
  34.0 6.8 %collective-permute-start.4 = (bf16[2,512,32]{1,2,0:T(8,128)(2,1)S(1)}, bf16[2,512,32]{1,2,0:T(8,128)(2,1)S(1)}, u32[]{:S(2)}, u32[]{:S(2)}) collective-permute-start(bf16[2,512,32]{1,2,0:T(8,128)(2,1)S(1)} %pad_maximum_fusion.5), channel_id=1, source_target_pairs={{0,64},{8,72},{16,80},{24,88},{32,96},{40,104},{48,112},{56,120},{... | collective-permute-start | bytes 196616 | tf_op jit(solution)/shard_map/ppermute | solution.py:130
  35.9 38.7 %copy-start.3 = (bf16[2,64,512]{2,1,0:T(8,128)(2,1)S(1)}, bf16[2,64,512]{2,1,0:T(8,128)(2,1)}, u32[]{:S(2)}) copy-start(bf16[2,64,512]{2,1,0:T(8,128)(2,1)} %param.27) | copy-start | bytes 393220
  35.9 6.8 %collective-permute-start.2 = (bf16[2,512,32]{1,2,0:T(8,128)(2,1)S(1)}, bf16[2,512,32]{1,2,0:T(8,128)(2,1)S(1)}, u32[]{:S(2)}, u32[]{:S(2)}) collective-permute-start(bf16[2,512,32]{1,2,0:T(8,128)(2,1)S(1)} %collective-permute-done.1), channel_id=1, source_target_pairs={{0,448},{8,456},{16,464},{24,472},{32,480},{40,488},{48,496},{56,5... | collective-permute-start | bytes 196616 | tf_op jit(solution)/shard_map/ppermute | solution.py:133
  40.8 6.5 %collective-permute-start.5 = (bf16[2,512,32]{1,2,0:T(8,128)(2,1)S(1)}, bf16[2,512,32]{1,2,0:T(8,128)(2,1)S(1)}, u32[]{:S(2)}, u32[]{:S(2)}) collective-permute-start(bf16[2,512,32]{1,2,0:T(8,128)(2,1)S(1)} %collective-permute-done.4), channel_id=1, source_target_pairs={{0,64},{8,72},{16,80},{24,88},{32,96},{40,104},{48,112},{56,120},{... | collective-permute-start | bytes 196616 | tf_op jit(solution)/shard_map/ppermute | solution.py:130
  42.7 12.8 %collective-permute-start.3 = (bf16[2,512,32]{1,2,0:T(8,128)(2,1)S(1)}, bf16[2,512,32]{1,2,0:T(8,128)(2,1)S(1)}, u32[]{:S(2)}, u32[]{:S(2)}) collective-permute-start(bf16[2,512,32]{1,2,0:T(8,128)(2,1)S(1)} %collective-permute-done.2), channel_id=1, source_target_pairs={{0,448},{8,456},{16,464},{24,472},{32,480},{40,488},{48,496},{56,5... | collective-permute-start | bytes 196616 | tf_op jit(solution)/shard_map/ppermute | solution.py:133
  47.3 6.3 %collective-permute-start.6 = (bf16[2,512,32]{1,2,0:T(8,128)(2,1)S(1)}, bf16[2,512,32]{1,2,0:T(8,128)(2,1)S(1)}, u32[]{:S(2)}, u32[]{:S(2)}) collective-permute-start(bf16[2,512,32]{1,2,0:T(8,128)(2,1)S(1)} %collective-permute-done.5), channel_id=1, source_target_pairs={{0,64},{8,72},{16,80},{24,88},{32,96},{40,104},{48,112},{56,120},{... | collective-permute-start | bytes 196616 | tf_op jit(solution)/shard_map/ppermute | solution.py:130
  53.6 6.2 %collective-permute-start.7 = (bf16[2,512,32]{1,2,0:T(8,128)(2,1)S(1)}, bf16[2,512,32]{1,2,0:T(8,128)(2,1)S(1)}, u32[]{:S(2)}, u32[]{:S(2)}) collective-permute-start(bf16[2,512,32]{1,2,0:T(8,128)(2,1)S(1)} %collective-permute-done.6), channel_id=1, source_target_pairs={{0,64},{8,72},{16,80},{24,88},{32,96},{40,104},{48,112},{56,120},{... | collective-permute-start | bytes 196616 | tf_op jit(solution)/shard_map/ppermute | solution.py:130
  59.9 29.8 %copy-start.13 = (f32[2,512]{1,0:T(2,128)S(1)}, f32[2,512]{1,0:T(2,128)}, u32[]{:S(2)}) copy-start(f32[2,512]{1,0:T(2,128)} %param.37) | copy-start | bytes 12292
  59.9 12.2 %collective-permute-start.9 = (bf16[8,2,512,32]{2,3,1,0:T(8,128)(2,1)S(1)}, bf16[8,2,512,32]{2,3,1,0:T(8,128)(2,1)S(1)}, u32[]{:S(2)}, u32[]{:S(2)}) collective-permute-start(bf16[8,2,512,32]{2,3,1,0:T(8,128)(2,1)S(1)} %bitcast_dynamic-update-slice_fusion.8), channel_id=1, source_target_pairs={{0,16},{8,24},{16,32},{24,40},{32,48},{40,56},{48,0},{56,8},{64,80... | collective-permute-start | bytes 1572872 | tf_op jit(solution)/shard_map/ppermute | solution.py:130
  65.7 24.1 %collective-permute-start.8 = (bf16[8,2,512,32]{2,3,1,0:T(8,128)(2,1)S(1)}, bf16[8,2,512,32]{2,3,1,0:T(8,128)(2,1)S(1)}, u32[]{:S(2)}, u32[]{:S(2)}) collective-permute-start(bf16[8,2,512,32]{2,3,1,0:T(8,128)(2,1)S(1)} %bitcast_dynamic-update-slice_fusion.8), channel_id=1, source_target_pairs={{0,48},{8,56},{16,0},{24,8},{32,16},{40,24},{48,32},{56,40},{64,11... | collective-permute-start | bytes 1572872 | tf_op jit(solution)/shard_map/ppermute | solution.py:133
  72.1 17.7 %collective-permute-start.10 = (bf16[8,2,512,32]{2,3,1,0:T(8,128)(2,1)S(1)}, bf16[8,2,512,32]{2,3,1,0:T(8,128)(2,1)S(1)}, u32[]{:S(2)}, u32[]{:S(2)}) collective-permute-start(bf16[8,2,512,32]{2,3,1,0:T(8,128)(2,1)S(1)} %collective-permute-done.9), channel_id=1, source_target_pairs={{0,16},{8,24},{16,32},{24,40},{32,48},{40,56},{48,0},{56,8},{64,80... | collective-permute-start | bytes 1572872 | tf_op jit(solution)/shard_map/ppermute | solution.py:130
  93.1 9.7 %copy-start.7 = (bf16[2,64,256]{2,1,0:T(8,128)(2,1)S(1)}, bf16[2,64,256]{2,1,0:T(8,128)(2,1)}, u32[]{:S(2)}) copy-start(bf16[2,64,256]{2,1,0:T(8,128)(2,1)} %param.31) | copy-start | bytes 196612
  102.8 13.6 %copy-start.14 = (s32[64]{0:T(128)S(1)}, s32[64]{0:T(128)}, u32[]{:S(2)}) copy-start(s32[64]{0:T(128)} %param.46) | copy-start | bytes 772
  103.9 34.1 %copy-start.9 = (f32[2,2048]{1,0:T(2,128)S(1)}, f32[2,2048]{1,0:T(2,128)}, u32[]{:S(2)}) copy-start(f32[2,2048]{1,0:T(2,128)} %param.38) | copy-start | bytes 49156
  103.9 33.8 %all-to-all-start = ((f32[2,8,8,2048]{3,2,0,1:T(8,128)}), f32[2,8,8,2048]{3,2,0,1:T(8,128)S(1)}, u32[]{:S(2)}, u32[]{:S(2)}) async-start(f32[2,8,8,2048]{3,2,0,1:T(8,128)} %copy.190), calls=%async_computation | async-start | bytes 2097152 | tf_op jit(solution)/shard_map/all_to_all | solution.py:248
  110.5 90.7 %collective-permute-start.21 = (bf16[2,400,2048]{2,1,0:T(8,128)(2,1)}, bf16[2,400,2048]{2,1,0:T(8,128)(2,1)}, u32[]{:S(2)}, u32[]{:S(2)}) collective-permute-start(bf16[2,400,2048]{2,1,0:T(8,128)(2,1)} %param.40), channel_id=1, source_target_pairs={{0,8},{8,0},{16,24},{24,16},{32,40},{40,32},{48,56},{56,48},{64,72... | collective-permute-start | bytes 9830408 | tf_op jit(solution)/shard_map/ppermute | solution.py:191
  138.1 7.5 %collective-permute-start.11 = (bf16[17,2048]{1,0:T(8,128)(2,1)S(1)}, bf16[17,2048]{1,0:T(8,128)(2,1)S(1)}, u32[]{:S(2)}, u32[]{:S(2)}) collective-permute-start(bf16[17,2048]{1,0:T(8,128)(2,1)S(1)} %pad_maximum_fusion.4), channel_id=1, source_target_pairs={{0,448},{8,456},{16,464},{24,472},{32,480},{40,488},{48,496},{56,5... | collective-permute-start | bytes 208904 | tf_op jit(solution)/shard_map/ppermute | solution.py:133
  143.7 7.0 %collective-permute-start.14 = (bf16[17,2048]{1,0:T(8,128)(2,1)S(1)}, bf16[17,2048]{1,0:T(8,128)(2,1)S(1)}, u32[]{:S(2)}, u32[]{:S(2)}) collective-permute-start(bf16[17,2048]{1,0:T(8,128)(2,1)S(1)} %pad_maximum_fusion.4), channel_id=1, source_target_pairs={{0,64},{8,72},{16,80},{24,88},{32,96},{40,104},{48,112},{56,120},{... | collective-permute-start | bytes 208904 | tf_op jit(solution)/shard_map/ppermute | solution.py:130
  145.6 7.0 %collective-permute-start.12 = (bf16[17,2048]{1,0:T(8,128)(2,1)S(1)}, bf16[17,2048]{1,0:T(8,128)(2,1)S(1)}, u32[]{:S(2)}, u32[]{:S(2)}) collective-permute-start(bf16[17,2048]{1,0:T(8,128)(2,1)S(1)} %collective-permute-done.11), channel_id=1, source_target_pairs={{0,448},{8,456},{16,464},{24,472},{32,480},{40,488},{48,496},{56,5... | collective-permute-start | bytes 208904 | tf_op jit(solution)/shard_map/ppermute | solution.py:133
  150.7 6.6 %collective-permute-start.15 = (bf16[17,2048]{1,0:T(8,128)(2,1)S(1)}, bf16[17,2048]{1,0:T(8,128)(2,1)S(1)}, u32[]{:S(2)}, u32[]{:S(2)}) collective-permute-start(bf16[17,2048]{1,0:T(8,128)(2,1)S(1)} %collective-permute-done.14), channel_id=1, source_target_pairs={{0,64},{8,72},{16,80},{24,88},{32,96},{40,104},{48,112},{56,120},{... | collective-permute-start | bytes 208904 | tf_op jit(solution)/shard_map/ppermute | solution.py:130
  152.6 13.1 %collective-permute-start.13 = (bf16[17,2048]{1,0:T(8,128)(2,1)S(1)}, bf16[17,2048]{1,0:T(8,128)(2,1)S(1)}, u32[]{:S(2)}, u32[]{:S(2)}) collective-permute-start(bf16[17,2048]{1,0:T(8,128)(2,1)S(1)} %collective-permute-done.12), channel_id=1, source_target_pairs={{0,448},{8,456},{16,464},{24,472},{32,480},{40,488},{48,496},{56,5... | collective-permute-start | bytes 208904 | tf_op jit(solution)/shard_map/ppermute | solution.py:133
  157.2 6.6 %collective-permute-start.16 = (bf16[17,2048]{1,0:T(8,128)(2,1)S(1)}, bf16[17,2048]{1,0:T(8,128)(2,1)S(1)}, u32[]{:S(2)}, u32[]{:S(2)}) collective-permute-start(bf16[17,2048]{1,0:T(8,128)(2,1)S(1)} %collective-permute-done.15), channel_id=1, source_target_pairs={{0,64},{8,72},{16,80},{24,88},{32,96},{40,104},{48,112},{56,120},{... | collective-permute-start | bytes 208904 | tf_op jit(solution)/shard_map/ppermute | solution.py:130
  163.8 6.6 %collective-permute-start.17 = (bf16[17,2048]{1,0:T(8,128)(2,1)S(1)}, bf16[17,2048]{1,0:T(8,128)(2,1)S(1)}, u32[]{:S(2)}, u32[]{:S(2)}) collective-permute-start(bf16[17,2048]{1,0:T(8,128)(2,1)S(1)} %collective-permute-done.16), channel_id=1, source_target_pairs={{0,64},{8,72},{16,80},{24,88},{32,96},{40,104},{48,112},{56,120},{... | collective-permute-start | bytes 208904 | tf_op jit(solution)/shard_map/ppermute | solution.py:130
  170.7 12.2 %collective-permute-start.19 = (bf16[8,17,2048]{2,0,1:T(8,128)(2,1)S(1)}, bf16[8,17,2048]{2,0,1:T(8,128)(2,1)S(1)}, u32[]{:S(2)}, u32[]{:S(2)}) collective-permute-start(bf16[8,17,2048]{2,0,1:T(8,128)(2,1)S(1)} %copy.191), channel_id=1, source_target_pairs={{0,16},{8,24},{16,32},{24,40},{32,48},{40,56},{48,0},{56,8},{64,80... | collective-permute-start | bytes 1671176 | tf_op jit(solution)/shard_map/ppermute | solution.py:130
  172.7 12.4 %collective-permute-start.18 = (bf16[8,17,2048]{2,0,1:T(8,128)(2,1)S(1)}, bf16[8,17,2048]{2,0,1:T(8,128)(2,1)S(1)}, u32[]{:S(2)}, u32[]{:S(2)}) collective-permute-start(bf16[8,17,2048]{2,0,1:T(8,128)(2,1)S(1)} %copy.191), channel_id=1, source_target_pairs={{0,48},{8,56},{16,0},{24,8},{32,16},{40,24},{48,32},{56,40},{64,11... | collective-permute-start | bytes 1671176 | tf_op jit(solution)/shard_map/ppermute | solution.py:133
  182.9 11.5 %collective-permute-start.20 = (bf16[8,17,2048]{2,0,1:T(8,128)(2,1)S(1)}, bf16[8,17,2048]{2,0,1:T(8,128)(2,1)S(1)}, u32[]{:S(2)}, u32[]{:S(2)}) collective-permute-start(bf16[8,17,2048]{2,0,1:T(8,128)(2,1)S(1)} %collective-permute-done.19), channel_id=1, source_target_pairs={{0,16},{8,24},{16,32},{24,40},{32,48},{40,56},{48,0},{56,8},{64,80... | collective-permute-start | bytes 1671176 | tf_op jit(solution)/shard_map/ppermute | solution.py:130
  195.3 1.7 copy-start
  197.5 3.8 %copy-start.1 = (bf16[4,8,17,2048]{3,2,1,0:T(8,128)(2,1)S(1)}, bf16[4,8,17,2048]{3,2,1,0:T(8,128)(2,1)}, u32[]{:S(2)}) copy-start(bf16[4,8,17,2048]{3,2,1,0:T(8,128)(2,1)} %copy-done) | copy-start | bytes 6684676
  204.4 0.9 copy-start.4
  204.5 14.1 %copy-start.20 = (s32[64]{0:T(128)S(1)}, s32[64]{0:T(128)}, u32[]{:S(2)}) copy-start(s32[64]{0:T(128)} %param.47) | copy-start | bytes 772
  206.4 24.3 %all-to-all-start.1 = ((f32[3,2,64,8]{3,1,0,2:T(2,128)}), f32[3,2,64,8]{3,1,0,2:T(2,128)S(1)}, u32[]{:S(2)}, u32[]{:S(2)}) async-start(f32[3,2,64,8]{3,1,0,2:T(2,128)} %copy.198), calls=%async_computation.1 | async-start | bytes 393216 | tf_op jit(solution)/shard_map/all_to_all | solution.py:308
Sparse Core Ops, SparseCore 0:
  10.7 89.5 all-gather.2

commit v6 on v4

--- a/solution.py
+++ b/solution.py
@@ -217,12 +217,12 @@
     squares = jnp.sum(gated * gated, axis=2)
     unscaled = (gated * norm_gain[:, None, :]).astype(jnp.bfloat16)
     ring_weight = ring_gather(
-        ring_gather(ring_gather(out_weight, along_core, CORES), along_z, chips_z),
-        along_x,
-        ROWS_X,
+        ring_gather(ring_gather(out_weight, along_z, chips_z), along_x, ROWS_X),
+        along_core,
+        CORES,
     )
     ring_weight = jnp.roll(
-        jnp.roll(jnp.roll(ring_weight.transpose(1, 0, 2, 3, 4, 5), z_index, axis=0), x_index, axis=1),
+        jnp.roll(jnp.roll(ring_weight.transpose(2, 1, 0, 3, 4, 5), z_index, axis=0), x_index, axis=1),
         core_index,
         axis=2,
     )
@@ -232,15 +232,25 @@
     partial_out = jnp.einsum(
         "mtc,mcd->mtd", unscaled, full_weight, preferred_element_type=jnp.float32
     )
+    full_width = partial_out.shape[2]
+    part_width = resid_in.shape[2]
     extra = jnp.zeros(squares.shape + (SQUARE_COLUMNS,), jnp.float32).at[:, :, 0].set(squares)
-    reduced = lax.psum_scatter(
-        jnp.concatenate([partial_out, extra], axis=2), "tp", scatter_dimension=1, tiled=True
-    )
-    full_width = partial_out.shape[2]
-    update = reduced[:, :, :full_width]
-    scale = lax.rsqrt(reduced[:, :, full_width] / inner_width + EPSILON)
-    resid_rows = lax.all_to_all(resid_in, "tp", split_axis=1, concat_axis=2, tiled=True)
-    hidden = (resid_rows.astype(jnp.float32) + update * scale[:, :, None]).astype(jnp.bfloat16)
+    payload = jnp.concatenate([partial_out, resid_in.astype(jnp.float32), extra], axis=2)
+    pieces = lax.all_to_all(
+        payload.reshape(models, groups, row_count, payload.shape[2]),
+        "tp",
+        split_axis=1,
+        concat_axis=1,
+        tiled=True,
+    )
+    update = jnp.sum(pieces[:, :, :, :full_width], axis=1)
+    scale = lax.rsqrt(jnp.sum(pieces[:, :, :, full_width + part_width], axis=1) / inner_width + EPSILON)
+    resid_rows = (
+        pieces[:, :, :, full_width : full_width + part_width]
+        .transpose(0, 2, 1, 3)
+        .reshape(models, row_count, groups * part_width)
+    )
+    hidden = (resid_rows + update * scale[:, :, None]).astype(jnp.bfloat16)
     full_width = hidden.shape[2]
     hidden_float = hidden.astype(jnp.float32)
     final_squares = jnp.sum(hidden_float * hidden_float, axis=2)

time: 271 us -> 241 us (0.89)
  waiting for transfers between devices: 94.3 us -> 79.7 us
  between operations: 14.8 us -> 1.83 us
  starting transfers between devices: 105 us -> 92.9 us
  local copies, waits for them, and re-layouts: 14.1 us -> 21.3 us
    all_to_all x1, waiting for transfers between devices: 0.01 us -> 26.8 us  [local(): lax.all_to_all(payload.reshape(models, groups, row_count, payload.shape[2...]
    ppermute x13, waiting for transfers between devices: 64.7 us -> 40.3 us  [ring_gather(): forward = lax.ppermute(forward, 'req', perm_of(1))]
    reduce_scatter x1 -> x0, waiting for transfers between devices: 17.1 us -> none  [local(): lax.psum_scatter(jnp.concatenate([partial_out, extra], axis=2), 'tp', sca...]
    all_to_all x1, starting transfers between devices: 17.3 us -> 10.8 us  [local(): lax.all_to_all(send, 'req', split_axis=2, concat_axis=2, tiled=True)]
    ppermute x1, starting transfers between devices: 8.29 us -> 2.37 us  [local(): lax.ppermute(head_weight, 'req', [(i, i ^ 1) for i in range(shards)])]
    slice x6, local copies, waits for them, and re-layouts: 0.09 us -> 3.9 us  [causal_conv(): current[:-lag_steps]]
    another operation x2, other arithmetic: 0.57 us -> 3.42 us  [ring_gather(): return jnp.stack([got[k] for k in range(count)])]
    concatenate x4 -> x3, other arithmetic: 5.77 us -> 4.69 us  [the longest x1 1.56 us: local(): jnp.roll(ring_weight.transpose(2, 1, 0, 3, 4, 5), z_index, axis=0)]
  transfers between devices with their start and end apart: 25 -> 24, of which waited for: 11 -> 11; matrix products, arithmetic and copies ran while one was open for 15% -> 19% of each run, Pallas kernels for 0% -> 0%
where the time goes in v6:
time: 241 us; the launch traced here: 240 us
  starting transfers between devices  92.9 us (39%)
  waiting for transfers between devices  79.7 us (33%)
  other arithmetic  22.6 us (9%)
  local copies, waits for them, and re-layouts  21.3 us (9%)
  matrix products  21.2 us (9%)
    ppermute x13, waiting for transfers between devices, ring_gather(): forward = lax.ppermute(forward, 'req', perm_of(1))  40.3 us
    ppermute x8, starting transfers between devices, ring_gather(): backward = lax.ppermute(backward, 'req', perm_of(-1))  38.7 us
    ppermute x13, starting transfers between devices, ring_gather(): forward = lax.ppermute(forward, 'req', perm_of(1))  34.2 us
    all_to_all x1, waiting for transfers between devices, local(): lax.all_to_all(payload.reshape(models, groups, row_count, payload.shape[2...  26.8 us
    all_to_all x1, waiting for transfers between devices, local(): lax.all_to_all(send, 'req', split_axis=2, concat_axis=2, tiled=True)  12.1 us
    all_to_all x1, starting transfers between devices, local(): lax.all_to_all(send, 'req', split_axis=2, concat_axis=2, tiled=True)  10.8 us
    dot_general x2, matrix products, head_scores(): jnp.einsum('mnd,mvd->mnv', rows_hidden, head_weight, preferred_element_ty...  6.92 us
    all_to_all x1, starting transfers between devices, local(): lax.all_to_all(payload.reshape(models, groups, row_count, payload.shape[2...  6.83 us
  transfers between devices with their start and end apart: 24, of which 11 were waited for; matrix products, arithmetic and copies ran while one was open for 19% of the time, Pallas kernels for 0%

profile of v6, /device:TPU:1, one launch (start us, length us, event | category | flops | bytes accessed | tf_op | source)
XLA Modules:
  0.0 239.6 jit_solution(14405741203891261052)
XLA Ops:
  0.0 11.6 %collective-permute-start = (bf16[2,512,32]{1,2,0:T(8,128)(2,1)}, bf16[2,512,32]{1,2,0:T(8,128)(2,1)S(1)}, u32[]{:S(2)}, u32[]{:S(2)}) collective-permute-start(bf16[2,512,32]{1,2,0:T(8,128)(2,1)} %param.41), channel_id=1, source_target_pairs={{0,448},{8,456},{16,464},{24,472},{32,480},{40,488},{48,496},{56,5... | collective-permute-start | bytes 196616 | tf_op jit(solution)/shard_map/ppermute | solution.py:133
  11.7 1.9 collective-permute-start.3
  13.6 0.9 bitcast_dynamic-update-slice_fusion.15
  14.5 0.8 reduce-window.4
  16.6 0.9 slice_convert_fusion.1
  18.9 0.8 slice_convert_fusion.3
  21.7 1.2 fusion.167
  22.9 0.8 fusion.176
  25.2 1.5 fusion.177
  26.7 0.8 fusion.180
  32.3 0.9 fusion.17
  33.2 4.6 %collective-permute-start.1 = (bf16[2,512,32]{1,2,0:T(8,128)(2,1)S(1)}, bf16[2,512,32]{1,2,0:T(8,128)(2,1)S(1)}, u32[]{:S(2)}, u32[]{:S(2)}) collective-permute-start(bf16[2,512,32]{1,2,0:T(8,128)(2,1)S(1)} %collective-permute-done), channel_id=1, source_target_pairs={{0,448},{8,456},{16,464},{24,472},{32,480},{40,488},{48,496},{56,5... | collective-permute-start | bytes 196616 | tf_op jit(solution)/shard_map/ppermute | solution.py:133
  37.8 1.9 collective-permute-start.4
  39.7 4.6 %collective-permute-start.2 = (bf16[2,512,32]{1,2,0:T(8,128)(2,1)S(1)}, bf16[2,512,32]{1,2,0:T(8,128)(2,1)S(1)}, u32[]{:S(2)}, u32[]{:S(2)}) collective-permute-start(bf16[2,512,32]{1,2,0:T(8,128)(2,1)S(1)} %collective-permute-done.1), channel_id=1, source_target_pairs={{0,448},{8,456},{16,464},{24,472},{32,480},{40,488},{48,496},{56,5... | collective-permute-start | bytes 196616 | tf_op jit(solution)/shard_map/ppermute | solution.py:133
  44.3 1.9 collective-permute-start.5
  46.3 4.3 %collective-permute-done.5 = bf16[2,512,32]{1,2,0:T(8,128)(2,1)S(1)} collective-permute-done((bf16[2,512,32]{1,2,0:T(8,128)(2,1)S(1)}, bf16[2,512,32]{1,2,0:T(8,128)(2,1)S(1)}, u32[]{:S(2)}, u32[]{:S(2)}) %collective-permute-start.5) | collective-permute-done | bytes 65568 | tf_op jit(solution)/shard_map/ppermute | solution.py:130
  50.5 1.9 collective-permute-start.6
  52.5 4.3 %collective-permute-done.6 = bf16[2,512,32]{1,2,0:T(8,128)(2,1)S(1)} collective-permute-done((bf16[2,512,32]{1,2,0:T(8,128)(2,1)S(1)}, bf16[2,512,32]{1,2,0:T(8,128)(2,1)S(1)}, u32[]{:S(2)}, u32[]{:S(2)}) %collective-permute-start.6) | collective-permute-done | bytes 65568 | tf_op jit(solution)/shard_map/ppermute | solution.py:130
  56.8 3.1 %collective-permute-start.8 = (bf16[8,2,512,32]{2,3,0,1:T(8,128)(2,1)S(1)}, bf16[8,2,512,32]{2,3,0,1:T(8,128)(2,1)S(1)}, u32[]{:S(2)}, u32[]{:S(2)}) collective-permute-start(bf16[8,2,512,32]{2,3,0,1:T(8,128)(2,1)S(1)} %bitcast_dynamic-update-slice_fusion.13), channel_id=1, source_target_pairs={{0,16},{8,24},{16,32},{24,40},{32,48},{40,56},{48,0},{56,8},{64,80... | collective-permute-start | bytes 1572872 | tf_op jit(solution)/shard_map/ppermute | solution.py:130
  61.6 3.4 %collective-permute-start.7 = (bf16[8,2,512,32]{2,3,0,1:T(8,128)(2,1)S(1)}, bf16[8,2,512,32]{2,3,0,1:T(8,128)(2,1)S(1)}, u32[]{:S(2)}, u32[]{:S(2)}) collective-permute-start(bf16[8,2,512,32]{2,3,0,1:T(8,128)(2,1)S(1)} %bitcast_dynamic-update-slice_fusion.13), channel_id=1, source_target_pairs={{0,48},{8,56},{16,0},{24,8},{32,16},{40,24},{48,32},{56,40},{64,11... | collective-permute-start | bytes 1572872 | tf_op jit(solution)/shard_map/ppermute | solution.py:133
  65.0 3.7 %collective-permute-done.8 = bf16[8,2,512,32]{2,3,0,1:T(8,128)(2,1)S(1)} collective-permute-done((bf16[8,2,512,32]{2,3,0,1:T(8,128)(2,1)S(1)}, bf16[8,2,512,32]{2,3,0,1:T(8,128)(2,1)S(1)}, u32[]{:S(2)}, u32[]{:S(2)}) %collective-permute-start.8) | collective-permute-done | bytes 524320 | tf_op jit(solution)/shard_map/ppermute | solution.py:130
  68.7 1.9 collective-permute-start.9
  70.6 2.0 fusion.11
  72.9 1.6 fusion.107
  74.5 1.4 fusion.13
  75.9 3.9 %collective-permute-done.9 = bf16[8,2,512,32]{2,3,0,1:T(8,128)(2,1)S(1)} collective-permute-done((bf16[8,2,512,32]{2,3,0,1:T(8,128)(2,1)S(1)}, bf16[8,2,512,32]{2,3,0,1:T(8,128)(2,1)S(1)}, u32[]{:S(2)}, u32[]{:S(2)}) %collective-permute-start.9) | collective-permute-done | bytes 524320 | tf_op jit(solution)/shard_map/ppermute | solution.py:130
  79.8 0.8 copy-done.3
  80.6 2.9 %fusion.175 = (bf16[1,4,8,2,512,32]{4,5,0,1,2,3:T(8,128)(2,1)S(1)}, bf16[4,8,2,512,32]{3,4,0,1,2:T(8,128)(2,1)}) fusion(bf16[1,8,2,512,32]{3,4,0,1,2:T(8,128)(2,1)S(1)} %bitcast.380, bf16[1,8,2,512,32]{3,4,0,1,2:T(8,128)(2,1)} %bitcast.382, bf16[1,8,2,512,32]{3,4,0,1,2:T(8,128)(2,1)} %bitcast.381, bf16[1,8,2,512,32]{3,4,0,1,2:T(8,128)(2,1)S(1)} %bitcast.379), kind=kLoop, calls=%fused_computation.335 | loop fusion | flops 3145728 | bytes 6291456 | tf_op jit(solution)/shard_map/stack | solution.py:135
  83.7 8.6 %collective-permute-start.10 = (bf16[4,8,2,512,32]{3,4,0,1,2:T(8,128)(2,1)}, bf16[4,8,2,512,32]{3,4,0,1,2:T(8,128)(2,1)}, u32[]{:S(2)}, u32[]{:S(2)}) collective-permute-start(bf16[4,8,2,512,32]{3,4,0,1,2:T(8,128)(2,1)} %get-tuple-element.53), channel_id=1, source_target_pairs={{0,8},{8,0},{16,24},{24,16},{32,40},{40,32},{48,56},{56,48},{64,72... | collective-permute-start | bytes 6291464 | tf_op jit(solution)/shard_map/ppermute | solution.py:130
  92.8 1.5 divide_multiply_fusion.1
  95.4 2.0 fusion.10
  100.0 2.0 maximum_bitcast_fusion
  102.0 1.6 fusion.2
  103.6 1.6 fusion.1
  105.2 1.6 fusion
  106.7 1.4 fusion.46
  108.2 1.1 copy.233
  109.3 6.8 %all-to-all-start = ((f32[2,8,8,2432]{3,2,0,1:T(8,128)}), f32[2,8,8,2432]{3,2,0,1:T(8,128)S(1)}, u32[]{:S(2)}, u32[]{:S(2)}) async-start(f32[2,8,8,2432]{3,2,0,1:T(8,128)} %copy.233), calls=%async_computation | async-start | bytes 2490368 | tf_op jit(solution)/shard_map/all_to_all | solution.py:239
  116.2 2.4 collective-permute-start.21
  119.2 0.7 and_reduce_fusion
  119.9 0.8 fusion.163
  120.7 1.3 broadcast_select_fusion
  122.0 0.8 scatter.14
  122.8 26.8 %all-to-all-done = f32[2,8,8,2432]{3,2,0,1:T(8,128)S(1)} async-done(((f32[2,8,8,2432]{3,2,0,1:T(8,128)}), f32[2,8,8,2432]{3,2,0,1:T(8,128)S(1)}, u32[]{:S(2)}, u32[]{:S(2)}) %all-to-all-start) | async-done | bytes 1245216 | tf_op jit(solution)/shard_map/all_to_all | solution.py:239
  150.5 1.9 collective-permute-start.11
  152.4 3.4 %collective-permute-start.14 = (bf16[17,2048]{1,0:T(8,128)(2,1)S(1)}, bf16[17,2048]{1,0:T(8,128)(2,1)S(1)}, u32[]{:S(2)}, u32[]{:S(2)}) collective-permute-start(bf16[17,2048]{1,0:T(8,128)(2,1)S(1)} %pad_maximum_fusion.4), channel_id=1, source_target_pairs={{0,64},{8,72},{16,80},{24,88},{32,96},{40,104},{48,112},{56,120},{... | collective-permute-start | bytes 208904 | tf_op jit(solution)/shard_map/ppermute | solution.py:130
  156.3 3.4 %collective-permute-start.12 = (bf16[17,2048]{1,0:T(8,128)(2,1)S(1)}, bf16[17,2048]{1,0:T(8,128)(2,1)S(1)}, u32[]{:S(2)}, u32[]{:S(2)}) collective-permute-start(bf16[17,2048]{1,0:T(8,128)(2,1)S(1)} %collective-permute-done.11), channel_id=1, source_target_pairs={{0,448},{8,456},{16,464},{24,472},{32,480},{40,488},{48,496},{56,5... | collective-permute-start | bytes 208904 | tf_op jit(solution)/shard_map/ppermute | solution.py:133
  159.7 1.9 collective-permute-start.15
  161.7 4.6 %collective-permute-start.13 = (bf16[17,2048]{1,0:T(8,128)(2,1)S(1)}, bf16[17,2048]{1,0:T(8,128)(2,1)S(1)}, u32[]{:S(2)}, u32[]{:S(2)}) collective-permute-start(bf16[17,2048]{1,0:T(8,128)(2,1)S(1)} %collective-permute-done.12), channel_id=1, source_target_pairs={{0,448},{8,456},{16,464},{24,472},{32,480},{40,488},{48,496},{56,5... | collective-permute-start | bytes 208904 | tf_op jit(solution)/shard_map/ppermute | solution.py:133
  166.3 1.9 collective-permute-start.16
  168.3 4.6 %collective-permute-done.16 = bf16[17,2048]{1,0:T(8,128)(2,1)S(1)} collective-permute-done((bf16[17,2048]{1,0:T(8,128)(2,1)S(1)}, bf16[17,2048]{1,0:T(8,128)(2,1)S(1)}, u32[]{:S(2)}, u32[]{:S(2)}) %collective-permute-start.16) | collective-permute-done | bytes 69664 | tf_op jit(solution)/shard_map/ppermute | solution.py:130
  172.9 1.9 collective-permute-start.17
  174.8 4.6 %collective-permute-done.17 = bf16[17,2048]{1,0:T(8,128)(2,1)S(1)} collective-permute-done((bf16[17,2048]{1,0:T(8,128)(2,1)S(1)}, bf16[17,2048]{1,0:T(8,128)(2,1)S(1)}, u32[]{:S(2)}, u32[]{:S(2)}) %collective-permute-start.17) | collective-permute-done | bytes 69664 | tf_op jit(solution)/shard_map/ppermute | solution.py:130
  179.8 1.9 collective-permute-start.19
  181.8 4.6 %collective-permute-start.18 = (bf16[8,17,2048]{2,0,1:T(8,128)(2,1)S(1)}, bf16[8,17,2048]{2,0,1:T(8,128)(2,1)S(1)}, u32[]{:S(2)}, u32[]{:S(2)}) collective-permute-start(bf16[8,17,2048]{2,0,1:T(8,128)(2,1)S(1)} %copy.235), channel_id=1, source_target_pairs={{0,48},{8,56},{16,0},{24,8},{32,16},{40,24},{48,32},{56,40},{64,11... | collective-permute-start | bytes 1671176 | tf_op jit(solution)/shard_map/ppermute | solution.py:133
  186.3 6.0 %collective-permute-done.19 = bf16[8,17,2048]{2,0,1:T(8,128)(2,1)S(1)} collective-permute-done((bf16[8,17,2048]{2,0,1:T(8,128)(2,1)S(1)}, bf16[8,17,2048]{2,0,1:T(8,128)(2,1)S(1)}, u32[]{:S(2)}, u32[]{:S(2)}) %collective-permute-start.19) | collective-permute-done | bytes 557088 | tf_op jit(solution)/shard_map/ppermute | solution.py:130
  192.3 1.9 collective-permute-start.20
  194.9 8.9 %collective-permute-done.20 = bf16[8,17,2048]{2,0,1:T(8,128)(2,1)S(1)} collective-permute-done((bf16[8,17,2048]{2,0,1:T(8,128)(2,1)S(1)}, bf16[8,17,2048]{2,0,1:T(8,128)(2,1)S(1)}, u32[]{:S(2)}, u32[]{:S(2)}) %collective-permute-start.20) | collective-permute-done | bytes 557088 | tf_op jit(solution)/shard_map/ppermute | solution.py:130
  204.7 1.7 copy-done
  206.9 3.8 %fusion.184 = (f32[2,256]{1,0:T(2,128)S(1)}, f32[2,256,400]{1,2,0:T(8,128)S(1)}) fusion(bf16[2,400,2048]{2,1,0:T(8,128)(2,1)} %param.42, bf16[32,17,2048]{2,1,0:T(8,128)(2,1)} %bitcast.366), kind=kOutput, calls=%fused_computation.344 | convolution fusion | flops 839065088 | bytes 6195200 | tf_op jit(solution)/shard_map/mnd,mvd->mnv/dot_general | solution.py:115
  210.7 3.1 %fusion.185 = (f32[2,256]{1,0:T(2,128)S(1)}, f32[2,256,400]{1,2,0:T(8,128)S(1)}) fusion(bf16[2,400,2048]{2,1,0:T(8,128)(2,1)} %collective-permute-done.21, bf16[32,17,2048]{2,1,0:T(8,128)(2,1)S(1)} %bitcast.367), kind=kOutput, calls=%fused_computation.345 | convolution fusion | flops 839065088 | bytes 6195200 | tf_op jit(solution)/shard_map/mnd,mvd->mnv/dot_general | solution.py:115
  214.9 0.8 copy.242
  215.7 10.8 %all-to-all-start.1 = ((f32[3,2,64,8]{3,1,0,2:T(2,128)}), f32[3,2,64,8]{3,1,0,2:T(2,128)S(1)}, u32[]{:S(2)}, u32[]{:S(2)}) async-start(f32[3,2,64,8]{3,1,0,2:T(2,128)} %copy.242), calls=%async_computation.1 | async-start | bytes 393216 | tf_op jit(solution)/shard_map/all_to_all | solution.py:306
  226.7 12.1 %all-to-all-done.1 = f32[3,2,64,8]{3,1,0,2:T(2,128)S(1)} async-done(((f32[3,2,64,8]{3,1,0,2:T(2,128)}), f32[3,2,64,8]{3,1,0,2:T(2,128)S(1)}, u32[]{:S(2)}, u32[]{:S(2)}) %all-to-all-start.1) | async-done | bytes 12320 | tf_op jit(solution)/shard_map/all_to_all | solution.py:306
  (262 shorter events, 22.8 us)
Async XLA Ops:
  0.0 29.2 %copy-start.7 = (bf16[2,64,256]{2,1,0:T(8,128)(2,1)S(1)}, bf16[2,64,256]{2,1,0:T(8,128)(2,1)}, u32[]{:S(2)}) copy-start(bf16[2,64,256]{2,1,0:T(8,128)(2,1)} %param.31) | copy-start | bytes 196612
  0.0 28.6 %copy-start.22 = (f32[2,4,256]{2,1,0:T(4,128)S(1)}, f32[2,4,256]{2,1,0:T(4,128)}, u32[]{:S(2)}) copy-start(f32[2,4,256]{2,1,0:T(4,128)} %param.35) | copy-start | bytes 24580
  0.0 29.6 %copy-start.36 = (f32[2,8]{1,0:T(2,128)S(1)}, f32[2,8]{1,0:T(2,128)}, u32[]{:S(2)}) copy-start(f32[2,8]{1,0:T(2,128)} %param.36) | copy-start | bytes 196
  0.0 29.6 %copy-start.35 = (f32[2,8]{1,0:T(2,128)S(1)}, f32[2,8]{1,0:T(2,128)}, u32[]{:S(2)}) copy-start(f32[2,8]{1,0:T(2,128)} %param.37) | copy-start | bytes 196
  0.0 29.6 %copy-start.17 = (bf16[2,64,8]{1,2,0:T(8,128)(2,1)S(1)}, bf16[2,64,8]{1,2,0:T(8,128)(2,1)}, u32[]{:S(2)}) copy-start(bf16[2,64,8]{1,2,0:T(8,128)(2,1)} %param.32) | copy-start | bytes 6148
  0.0 59.9 %copy-start.34 = (f32[2,8]{1,0:T(2,128)S(1)}, f32[2,8]{1,0:T(2,128)}, u32[]{:S(2)}) copy-start(f32[2,8]{1,0:T(2,128)} %param.38) | copy-start | bytes 196
  0.0 33.1 %collective-permute-start = (bf16[2,512,32]{1,2,0:T(8,128)(2,1)}, bf16[2,512,32]{1,2,0:T(8,128)(2,1)S(1)}, u32[]{:S(2)}, u32[]{:S(2)}) collective-permute-start(bf16[2,512,32]{1,2,0:T(8,128)(2,1)} %param.41), channel_id=1, source_target_pairs={{0,448},{8,456},{16,464},{24,472},{32,480},{40,488},{48,496},{56,5... | collective-permute-start | bytes 196616 | tf_op jit(solution)/shard_map/ppermute | solution.py:133
  11.7 26.1 %collective-permute-start.3 = (bf16[2,512,32]{1,2,0:T(8,128)(2,1)}, bf16[2,512,32]{1,2,0:T(8,128)(2,1)S(1)}, u32[]{:S(2)}, u32[]{:S(2)}) collective-permute-start(bf16[2,512,32]{1,2,0:T(8,128)(2,1)} %param.41), channel_id=1, source_target_pairs={{0,64},{8,72},{16,80},{24,88},{32,96},{40,104},{48,112},{56,120},{... | collective-permute-start | bytes 196616 | tf_op jit(solution)/shard_map/ppermute | solution.py:130
  15.9 40.8 %copy-start.37 = (pred[3]{0:T(512)(128)(4,1)}, pred[3]{0:T(512)(128)(4,1)S(1)}, u32[]{:S(2)}) copy-start(pred[3]{0:T(512)(128)(4,1)S(1)} %get-tuple-element.50) | copy-start | bytes 13
  17.5 43.8 %copy-start.4 = (bf16[2,64,512]{2,1,0:T(8,128)(2,1)S(1)}, bf16[2,64,512]{2,1,0:T(8,128)(2,1)}, u32[]{:S(2)}) copy-start(bf16[2,64,512]{2,1,0:T(8,128)(2,1)} %param.30) | copy-start | bytes 393220
  21.7 39.5 %copy-start.13 = (s32[64]{0:T(128)}, s32[64]{0:T(128)S(1)}, u32[]{:S(2)}) copy-start(s32[64]{0:T(128)S(1)} %fusion.144) | copy-start | bytes 772
  25.1 36.1 %copy-start.39 = (pred[64]{0:T(512)(128)(4,1)}, pred[64]{0:T(512)(128)(4,1)S(1)}, u32[]{:S(2)}) copy-start(pred[64]{0:T(512)(128)(4,1)S(1)} %get-tuple-element.111) | copy-start | bytes 196
  25.1 36.1 %copy-start.41 = (pred[64]{0:T(512)(128)(4,1)}, pred[64]{0:T(512)(128)(4,1)S(1)}, u32[]{:S(2)}) copy-start(pred[64]{0:T(512)(128)(4,1)S(1)} %get-tuple-element.112) | copy-start | bytes 196
  25.1 36.1 %copy-start.43 = (pred[64]{0:T(512)(128)(4,1)}, pred[64]{0:T(512)(128)(4,1)S(1)}, u32[]{:S(2)}) copy-start(pred[64]{0:T(512)(128)(4,1)S(1)} %get-tuple-element.113) | copy-start | bytes 196
  25.1 36.1 %copy-start.45 = (pred[64]{0:T(512)(128)(4,1)}, pred[64]{0:T(512)(128)(4,1)S(1)}, u32[]{:S(2)}) copy-start(pred[64]{0:T(512)(128)(4,1)S(1)} %get-tuple-element.114) | copy-start | bytes 196
  25.1 36.1 %copy-start.47 = (pred[64]{0:T(512)(128)(4,1)}, pred[64]{0:T(512)(128)(4,1)S(1)}, u32[]{:S(2)}) copy-start(pred[64]{0:T(512)(128)(4,1)S(1)} %get-tuple-element.115) | copy-start | bytes 196
  25.1 36.1 %copy-start.49 = (pred[64]{0:T(512)(128)(4,1)}, pred[64]{0:T(512)(128)(4,1)S(1)}, u32[]{:S(2)}) copy-start(pred[64]{0:T(512)(128)(4,1)S(1)} %get-tuple-element.116) | copy-start | bytes 196
  25.1 36.1 %copy-start.51 = (pred[64]{0:T(512)(128)(4,1)}, pred[64]{0:T(512)(128)(4,1)S(1)}, u32[]{:S(2)}) copy-start(pred[64]{0:T(512)(128)(4,1)S(1)} %get-tuple-element.117) | copy-start | bytes 196
  25.1 36.1 %copy-start.53 = (pred[64]{0:T(512)(128)(4,1)}, pred[64]{0:T(512)(128)(4,1)S(1)}, u32[]{:S(2)}) copy-start(pred[64]{0:T(512)(128)(4,1)S(1)} %get-tuple-element.118) | copy-start | bytes 196
  25.1 36.1 %copy-start.55 = (pred[64]{0:T(512)(128)(4,1)}, pred[64]{0:T(512)(128)(4,1)S(1)}, u32[]{:S(2)}) copy-start(pred[64]{0:T(512)(128)(4,1)S(1)} %get-tuple-element.119) | copy-start | bytes 196
  25.2 36.1 %copy-start.57 = (pred[64]{0:T(512)(128)(4,1)}, pred[64]{0:T(512)(128)(4,1)S(1)}, u32[]{:S(2)}) copy-start(pred[64]{0:T(512)(128)(4,1)S(1)} %get-tuple-element.120) | copy-start | bytes 196
  25.2 36.1 %copy-start.59 = (pred[64]{0:T(512)(128)(4,1)}, pred[64]{0:T(512)(128)(4,1)S(1)}, u32[]{:S(2)}) copy-start(pred[64]{0:T(512)(128)(4,1)S(1)} %get-tuple-element.121) | copy-start | bytes 196
  25.2 36.1 %copy-start.61 = (pred[64]{0:T(512)(128)(4,1)}, pred[64]{0:T(512)(128)(4,1)S(1)}, u32[]{:S(2)}) copy-start(pred[64]{0:T(512)(128)(4,1)S(1)} %get-tuple-element.122) | copy-start | bytes 196
  31.7 29.6 %copy-start.23 = (s32[1024]{0:T(1024)}, s32[1024]{0:T(1024)S(1)}, u32[]{:S(2)}) copy-start(s32[1024]{0:T(1024)S(1)} %pad_clamp_fusion) | copy-start | bytes 12292
  32.3 38.3 %copy-start.64 = (f32[3]{0:T(128)S(1)}, f32[3]{0:T(128)}, u32[]{:S(2)}) copy-start(f32[3]{0:T(128)} %get-tuple-element.109) | copy-start | bytes 40
  33.2 37.4 %copy-start.26 = (f32[64,3]{0,1:T(4,128)}, f32[64,3]{0,1:T(4,128)S(1)}, u32[]{:S(2)}) copy-start(f32[64,3]{0,1:T(4,128)S(1)} %fusion.143) | copy-start | bytes 2308
  33.2 6.5 %collective-permute-start.1 = (bf16[2,512,32]{1,2,0:T(8,128)(2,1)S(1)}, bf16[2,512,32]{1,2,0:T(8,128)(2,1)S(1)}, u32[]{:S(2)}, u32[]{:S(2)}) collective-permute-start(bf16[2,512,32]{1,2,0:T(8,128)(2,1)S(1)} %collective-permute-done), channel_id=1, source_target_pairs={{0,448},{8,456},{16,464},{24,472},{32,480},{40,488},{48,496},{56,5... | collective-permute-start | bytes 196616 | tf_op jit(solution)/shard_map/ppermute | solution.py:133
  37.8 6.5 %collective-permute-start.4 = (bf16[2,512,32]{1,2,0:T(8,128)(2,1)S(1)}, bf16[2,512,32]{1,2,0:T(8,128)(2,1)S(1)}, u32[]{:S(2)}, u32[]{:S(2)}) collective-permute-start(bf16[2,512,32]{1,2,0:T(8,128)(2,1)S(1)} %collective-permute-done.3), channel_id=1, source_target_pairs={{0,64},{8,72},{16,80},{24,88},{32,96},{40,104},{48,112},{56,120},{... | collective-permute-start | bytes 196616 | tf_op jit(solution)/shard_map/ppermute | solution.py:130
  39.7 12.7 %collective-permute-start.2 = (bf16[2,512,32]{1,2,0:T(8,128)(2,1)S(1)}, bf16[2,512,32]{1,2,0:T(8,128)(2,1)S(1)}, u32[]{:S(2)}, u32[]{:S(2)}) collective-permute-start(bf16[2,512,32]{1,2,0:T(8,128)(2,1)S(1)} %collective-permute-done.1), channel_id=1, source_target_pairs={{0,448},{8,456},{16,464},{24,472},{32,480},{40,488},{48,496},{56,5... | collective-permute-start | bytes 196616 | tf_op jit(solution)/shard_map/ppermute | solution.py:133
  44.3 6.2 %collective-permute-start.5 = (bf16[2,512,32]{1,2,0:T(8,128)(2,1)S(1)}, bf16[2,512,32]{1,2,0:T(8,128)(2,1)S(1)}, u32[]{:S(2)}, u32[]{:S(2)}) collective-permute-start(bf16[2,512,32]{1,2,0:T(8,128)(2,1)S(1)} %collective-permute-done.4), channel_id=1, source_target_pairs={{0,64},{8,72},{16,80},{24,88},{32,96},{40,104},{48,112},{56,120},{... | collective-permute-start | bytes 196616 | tf_op jit(solution)/shard_map/ppermute | solution.py:130
  50.5 6.2 %collective-permute-start.6 = (bf16[2,512,32]{1,2,0:T(8,128)(2,1)S(1)}, bf16[2,512,32]{1,2,0:T(8,128)(2,1)S(1)}, u32[]{:S(2)}, u32[]{:S(2)}) collective-permute-start(bf16[2,512,32]{1,2,0:T(8,128)(2,1)S(1)} %collective-permute-done.5), channel_id=1, source_target_pairs={{0,64},{8,72},{16,80},{24,88},{32,96},{40,104},{48,112},{56,120},{... | collective-permute-start | bytes 196616 | tf_op jit(solution)/shard_map/ppermute | solution.py:130
  56.8 11.9 %collective-permute-start.8 = (bf16[8,2,512,32]{2,3,0,1:T(8,128)(2,1)S(1)}, bf16[8,2,512,32]{2,3,0,1:T(8,128)(2,1)S(1)}, u32[]{:S(2)}, u32[]{:S(2)}) collective-permute-start(bf16[8,2,512,32]{2,3,0,1:T(8,128)(2,1)S(1)} %bitcast_dynamic-update-slice_fusion.13), channel_id=1, source_target_pairs={{0,16},{8,24},{16,32},{24,40},{32,48},{40,56},{48,0},{56,8},{64,80... | collective-permute-start | bytes 1572872 | tf_op jit(solution)/shard_map/ppermute | solution.py:130
  61.6 14.2 %collective-permute-start.7 = (bf16[8,2,512,32]{2,3,0,1:T(8,128)(2,1)S(1)}, bf16[8,2,512,32]{2,3,0,1:T(8,128)(2,1)S(1)}, u32[]{:S(2)}, u32[]{:S(2)}) collective-permute-start(bf16[8,2,512,32]{2,3,0,1:T(8,128)(2,1)S(1)} %bitcast_dynamic-update-slice_fusion.13), channel_id=1, source_target_pairs={{0,48},{8,56},{16,0},{24,8},{32,16},{40,24},{48,32},{56,40},{64,11... | collective-permute-start | bytes 1572872 | tf_op jit(solution)/shard_map/ppermute | solution.py:133
  68.7 11.1 %collective-permute-start.9 = (bf16[8,2,512,32]{2,3,0,1:T(8,128)(2,1)S(1)}, bf16[8,2,512,32]{2,3,0,1:T(8,128)(2,1)S(1)}, u32[]{:S(2)}, u32[]{:S(2)}) collective-permute-start(bf16[8,2,512,32]{2,3,0,1:T(8,128)(2,1)S(1)} %collective-permute-done.8), channel_id=1, source_target_pairs={{0,16},{8,24},{16,32},{24,40},{32,48},{40,56},{48,0},{56,8},{64,80... | collective-permute-start | bytes 1572872 | tf_op jit(solution)/shard_map/ppermute | solution.py:130
  80.6 11.8 %copy-start.14 = (s32[64]{0:T(128)S(1)}, s32[64]{0:T(128)}, u32[]{:S(2)}) copy-start(s32[64]{0:T(128)} %copy-done.13) | copy-start | bytes 772
  80.6 11.8 %copy-start.15 = (bf16[3,1,512]{2,1,0:T(2,128)(2,1)S(1)}, bf16[3,1,512]{2,1,0:T(2,128)(2,1)}, u32[]{:S(2)}) copy-start(bf16[3,1,512]{2,1,0:T(2,128)(2,1)} %get-tuple-element.74) | copy-start | bytes 9220
  83.5 11.5 %copy-start.11 = (f32[62,256]{1,0:T(8,128)S(1)}, f32[62,256]{1,0:T(8,128)}, u32[]{:S(2)}) copy-start(f32[62,256]{1,0:T(8,128)} %get-tuple-element.144) | copy-start | bytes 190468
  83.5 11.5 %copy-start.12 = (f32[63,256]{1,0:T(8,128)S(1)}, f32[63,256]{1,0:T(8,128)}, u32[]{:S(2)}) copy-start(f32[63,256]{1,0:T(8,128)} %get-tuple-element.146) | copy-start | bytes 193540
  83.5 11.5 %copy-start.25 = (bf16[3,1,256]{2,1,0:T(2,128)(2,1)S(1)}, bf16[3,1,256]{2,1,0:T(2,128)(2,1)}, u32[]{:S(2)}) copy-start(bf16[3,1,256]{2,1,0:T(2,128)(2,1)} %get-tuple-element.88) | copy-start | bytes 4612
  83.5 11.5 %copy-start.30 = (f32[1,1,256]{2,1,0:T(1,128)S(1)}, f32[1,1,256]{2,1,0:T(1,128)}, u32[]{:S(2)}) copy-start(f32[1,1,256]{2,1,0:T(1,128)} %get-tuple-element.80) | copy-start | bytes 3076
  83.5 11.5 %copy-start.31 = (f32[1,1,256]{2,1,0:T(1,128)S(1)}, f32[1,1,256]{2,1,0:T(1,128)}, u32[]{:S(2)}) copy-start(f32[1,1,256]{2,1,0:T(1,128)} %get-tuple-element.83) | copy-start | bytes 3076
  83.7 11.7 %copy-start.27 = (f32[64,3]{0,1:T(4,128)S(1)}, f32[64,3]{0,1:T(4,128)}, u32[]{:S(2)}) copy-start(f32[64,3]{0,1:T(4,128)} %copy-done.26) | copy-start | bytes 2308
  83.7 11.7 %copy-start.65 = (f32[3]{0:T(128)S(1)}, f32[3]{0:T(128)}, u32[]{:S(2)}) copy-start(f32[3]{0:T(128)} %get-tuple-element.109) | copy-start | bytes 40
  83.7 13.9 %copy-start.18 = (f32[64,8]{0,1:T(8,128)S(1)}, f32[64,8]{0,1:T(8,128)}, u32[]{:S(2)}) copy-start(f32[64,8]{0,1:T(8,128)} %get-tuple-element.95) | copy-start | bytes 6148
  83.7 14.6 %copy-start.38 = (pred[3]{0:T(512)(128)(4,1)S(1)}, pred[3]{0:T(512)(128)(4,1)}, u32[]{:S(2)}) copy-start(pred[3]{0:T(512)(128)(4,1)} %copy-done.37) | copy-start | bytes 13
  83.7 15.1 %copy-start.16 = (f32[64,8]{0,1:T(8,128)S(1)}, f32[64,8]{0,1:T(8,128)}, u32[]{:S(2)}) copy-start(f32[64,8]{0,1:T(8,128)} %get-tuple-element.94) | copy-start | bytes 6148
  83.7 15.1 %copy-start.29 = (f32[8]{0:T(128)S(1)}, f32[8]{0:T(128)}, u32[]{:S(2)}) copy-start(f32[8]{0:T(128)} %get-tuple-element.103) | copy-start | bytes 100
  83.7 16.3 %collective-permute-start.10 = (bf16[4,8,2,512,32]{3,4,0,1,2:T(8,128)(2,1)}, bf16[4,8,2,512,32]{3,4,0,1,2:T(8,128)(2,1)}, u32[]{:S(2)}, u32[]{:S(2)}) collective-permute-start(bf16[4,8,2,512,32]{3,4,0,1,2:T(8,128)(2,1)} %get-tuple-element.53), channel_id=1, source_target_pairs={{0,8},{8,0},{16,24},{24,16},{32,40},{40,32},{48,56},{56,48},{64,72... | collective-permute-start | bytes 6291464 | tf_op jit(solution)/shard_map/ppermute | solution.py:130
  108.1 11.8 %copy-start.28 = (s32[64]{0:T(128)S(1)}, s32[64]{0:T(128)}, u32[]{:S(2)}) copy-start(s32[64]{0:T(128)} %param.48) | copy-start | bytes 772
  108.2 42.1 %copy-start.19 = (f32[2,2048]{1,0:T(2,128)S(1)}, f32[2,2048]{1,0:T(2,128)}, u32[]{:S(2)}) copy-start(f32[2,2048]{1,0:T(2,128)} %param.40) | copy-start | bytes 49156
  109.3 40.3 %all-to-all-start = ((f32[2,8,8,2432]{3,2,0,1:T(8,128)}), f32[2,8,8,2432]{3,2,0,1:T(8,128)S(1)}, u32[]{:S(2)}, u32[]{:S(2)}) async-start(f32[2,8,8,2432]{3,2,0,1:T(8,128)} %copy.233), calls=%async_computation | async-start | bytes 2490368 | tf_op jit(solution)/shard_map/all_to_all | solution.py:239
  116.2 94.5 %collective-permute-start.21 = (bf16[2,400,2048]{2,1,0:T(8,128)(2,1)}, bf16[2,400,2048]{2,1,0:T(8,128)(2,1)}, u32[]{:S(2)}, u32[]{:S(2)}) collective-permute-start(bf16[2,400,2048]{2,1,0:T(8,128)(2,1)} %param.42), channel_id=1, source_target_pairs={{0,8},{8,0},{16,24},{24,16},{32,40},{40,32},{48,56},{56,48},{64,72... | collective-permute-start | bytes 9830408 | tf_op jit(solution)/shard_map/ppermute | solution.py:192
  150.5 5.8 %collective-permute-start.11 = (bf16[17,2048]{1,0:T(8,128)(2,1)S(1)}, bf16[17,2048]{1,0:T(8,128)(2,1)S(1)}, u32[]{:S(2)}, u32[]{:S(2)}) collective-permute-start(bf16[17,2048]{1,0:T(8,128)(2,1)S(1)} %pad_maximum_fusion.4), channel_id=1, source_target_pairs={{0,448},{8,456},{16,464},{24,472},{32,480},{40,488},{48,496},{56,5... | collective-permute-start | bytes 208904 | tf_op jit(solution)/shard_map/ppermute | solution.py:133
  152.4 7.3 %collective-permute-start.14 = (bf16[17,2048]{1,0:T(8,128)(2,1)S(1)}, bf16[17,2048]{1,0:T(8,128)(2,1)S(1)}, u32[]{:S(2)}, u32[]{:S(2)}) collective-permute-start(bf16[17,2048]{1,0:T(8,128)(2,1)S(1)} %pad_maximum_fusion.4), channel_id=1, source_target_pairs={{0,64},{8,72},{16,80},{24,88},{32,96},{40,104},{48,112},{56,120},{... | collective-permute-start | bytes 208904 | tf_op jit(solution)/shard_map/ppermute | solution.py:130
  156.3 5.4 %collective-permute-start.12 = (bf16[17,2048]{1,0:T(8,128)(2,1)S(1)}, bf16[17,2048]{1,0:T(8,128)(2,1)S(1)}, u32[]{:S(2)}, u32[]{:S(2)}) collective-permute-start(bf16[17,2048]{1,0:T(8,128)(2,1)S(1)} %collective-permute-done.11), channel_id=1, source_target_pairs={{0,448},{8,456},{16,464},{24,472},{32,480},{40,488},{48,496},{56,5... | collective-permute-start | bytes 208904 | tf_op jit(solution)/shard_map/ppermute | solution.py:133
  159.7 6.6 %collective-permute-start.15 = (bf16[17,2048]{1,0:T(8,128)(2,1)S(1)}, bf16[17,2048]{1,0:T(8,128)(2,1)S(1)}, u32[]{:S(2)}, u32[]{:S(2)}) collective-permute-start(bf16[17,2048]{1,0:T(8,128)(2,1)S(1)} %collective-permute-done.14), channel_id=1, source_target_pairs={{0,64},{8,72},{16,80},{24,88},{32,96},{40,104},{48,112},{56,120},{... | collective-permute-start | bytes 208904 | tf_op jit(solution)/shard_map/ppermute | solution.py:130
  161.7 13.1 %collective-permute-start.13 = (bf16[17,2048]{1,0:T(8,128)(2,1)S(1)}, bf16[17,2048]{1,0:T(8,128)(2,1)S(1)}, u32[]{:S(2)}, u32[]{:S(2)}) collective-permute-start(bf16[17,2048]{1,0:T(8,128)(2,1)S(1)} %collective-permute-done.12), channel_id=1, source_target_pairs={{0,448},{8,456},{16,464},{24,472},{32,480},{40,488},{48,496},{56,5... | collective-permute-start | bytes 208904 | tf_op jit(solution)/shard_map/ppermute | solution.py:133
  166.3 6.6 %collective-permute-start.16 = (bf16[17,2048]{1,0:T(8,128)(2,1)S(1)}, bf16[17,2048]{1,0:T(8,128)(2,1)S(1)}, u32[]{:S(2)}, u32[]{:S(2)}) collective-permute-start(bf16[17,2048]{1,0:T(8,128)(2,1)S(1)} %collective-permute-done.15), channel_id=1, source_target_pairs={{0,64},{8,72},{16,80},{24,88},{32,96},{40,104},{48,112},{56,120},{... | collective-permute-start | bytes 208904 | tf_op jit(solution)/shard_map/ppermute | solution.py:130
  172.9 6.6 %collective-permute-start.17 = (bf16[17,2048]{1,0:T(8,128)(2,1)S(1)}, bf16[17,2048]{1,0:T(8,128)(2,1)S(1)}, u32[]{:S(2)}, u32[]{:S(2)}) collective-permute-start(bf16[17,2048]{1,0:T(8,128)(2,1)S(1)} %collective-permute-done.16), channel_id=1, source_target_pairs={{0,64},{8,72},{16,80},{24,88},{32,96},{40,104},{48,112},{56,120},{... | collective-permute-start | bytes 208904 | tf_op jit(solution)/shard_map/ppermute | solution.py:130
  179.8 12.5 %collective-permute-start.19 = (bf16[8,17,2048]{2,0,1:T(8,128)(2,1)S(1)}, bf16[8,17,2048]{2,0,1:T(8,128)(2,1)S(1)}, u32[]{:S(2)}, u32[]{:S(2)}) collective-permute-start(bf16[8,17,2048]{2,0,1:T(8,128)(2,1)S(1)} %copy.235), channel_id=1, source_target_pairs={{0,16},{8,24},{16,32},{24,40},{32,48},{40,56},{48,0},{56,8},{64,80... | collective-permute-start | bytes 1671176 | tf_op jit(solution)/shard_map/ppermute | solution.py:130
  181.8 12.8 %collective-permute-start.18 = (bf16[8,17,2048]{2,0,1:T(8,128)(2,1)S(1)}, bf16[8,17,2048]{2,0,1:T(8,128)(2,1)S(1)}, u32[]{:S(2)}, u32[]{:S(2)}) collective-permute-start(bf16[8,17,2048]{2,0,1:T(8,128)(2,1)S(1)} %copy.235), channel_id=1, source_target_pairs={{0,48},{8,56},{16,0},{24,8},{32,16},{40,24},{48,32},{56,40},{64,11... | collective-permute-start | bytes 1671176 | tf_op jit(solution)/shard_map/ppermute | solution.py:133
  192.3 11.5 %collective-permute-start.20 = (bf16[8,17,2048]{2,0,1:T(8,128)(2,1)S(1)}, bf16[8,17,2048]{2,0,1:T(8,128)(2,1)S(1)}, u32[]{:S(2)}, u32[]{:S(2)}) collective-permute-start(bf16[8,17,2048]{2,0,1:T(8,128)(2,1)S(1)} %collective-permute-done.19), channel_id=1, source_target_pairs={{0,16},{8,24},{16,32},{24,40},{32,48},{40,56},{48,0},{56,8},{64,80... | collective-permute-start | bytes 1671176 | tf_op jit(solution)/shard_map/ppermute | solution.py:130
  213.9 12.7 %copy-start.63 = (s32[64]{0:T(128)S(1)}, s32[64]{0:T(128)}, u32[]{:S(2)}) copy-start(s32[64]{0:T(128)} %param.49) | copy-start | bytes 772
  215.7 23.0 %all-to-all-start.1 = ((f32[3,2,64,8]{3,1,0,2:T(2,128)}), f32[3,2,64,8]{3,1,0,2:T(2,128)S(1)}, u32[]{:S(2)}, u32[]{:S(2)}) async-start(f32[3,2,64,8]{3,1,0,2:T(2,128)} %copy.242), calls=%async_computation.1 | async-start | bytes 393216 | tf_op jit(solution)/shard_map/all_to_all | solution.py:306
  (26 other events, 234.0 us)

commit v7 on v6

--- a/solution.py
+++ b/solution.py
@@ -234,17 +234,29 @@
     )
     full_width = partial_out.shape[2]
     part_width = resid_in.shape[2]
-    extra = jnp.zeros(squares.shape + (SQUARE_COLUMNS,), jnp.float32).at[:, :, 0].set(squares)
-    payload = jnp.concatenate([partial_out, resid_in.astype(jnp.float32), extra], axis=2)
+    square_high = squares.astype(jnp.bfloat16)
+    square_low = (squares - square_high.astype(jnp.float32)).astype(jnp.bfloat16)
+    extra = (
+        jnp.zeros(squares.shape + (SQUARE_COLUMNS,), jnp.bfloat16)
+        .at[:, :, 0]
+        .set(square_high)
+        .at[:, :, 1]
+        .set(square_low)
+    )
+    payload = jnp.concatenate([partial_out.astype(jnp.bfloat16), resid_in, extra], axis=2)
     pieces = lax.all_to_all(
         payload.reshape(models, groups, row_count, payload.shape[2]),
         "tp",
         split_axis=1,
         concat_axis=1,
         tiled=True,
-    )
+    ).astype(jnp.float32)
     update = jnp.sum(pieces[:, :, :, :full_width], axis=1)
-    scale = lax.rsqrt(jnp.sum(pieces[:, :, :, full_width + part_width], axis=1) / inner_width + EPSILON)
+    total_squares = jnp.sum(
+        pieces[:, :, :, full_width + part_width] + pieces[:, :, :, full_width + part_width + 1],
+        axis=1,
+    )
+    scale = lax.rsqrt(total_squares / inner_width + EPSILON)
     resid_rows = (
         pieces[:, :, :, full_width : full_width + part_width]
         .transpose(0, 2, 1, 3)

time: 241 us -> 226 us (0.938)
  waiting for transfers between devices: 79.7 us -> 66.8 us
    all_to_all x1, waiting for transfers between devices: 26.8 us -> 13.6 us  [local(): lax.all_to_all(payload.reshape(models, groups, row_count, payload.shape[2...]
where the time goes in v7:
time: 226 us; the launch traced here: 225 us
  starting transfers between devices  93.1 us (41%)
  waiting for transfers between devices  66.8 us (30%)
  other arithmetic  22.3 us (10%)
  matrix products  21.3 us (9%)
  local copies, waits for them, and re-layouts  19.6 us (9%)
    ppermute x13, waiting for transfers between devices, ring_gather(): forward = lax.ppermute(forward, 'req', perm_of(1))  40.6 us
    ppermute x8, starting transfers between devices, ring_gather(): backward = lax.ppermute(backward, 'req', perm_of(-1))  38.7 us
    ppermute x13, starting transfers between devices, ring_gather(): forward = lax.ppermute(forward, 'req', perm_of(1))  34.4 us
    all_to_all x1, waiting for transfers between devices, local(): lax.all_to_all(payload.reshape(models, groups, row_count, payload.shape[2...  13.6 us
    all_to_all x1, waiting for transfers between devices, local(): lax.all_to_all(send, 'req', split_axis=2, concat_axis=2, tiled=True)  12.1 us
    all_to_all x1, starting transfers between devices, local(): lax.all_to_all(send, 'req', split_axis=2, concat_axis=2, tiled=True)  10.8 us
    dot_general x2, matrix products, head_scores(): jnp.einsum('mnd,mvd->mnv', rows_hidden, head_weight, preferred_element_ty...  6.92 us
    all_to_all x1, starting transfers between devices, local(): lax.all_to_all(payload.reshape(models, groups, row_count, payload.shape[2...  6.82 us
  transfers between devices with their start and end apart: 24, of which 11 were waited for; matrix products, arithmetic and copies ran while one was open for 19% of the time, Pallas kernels for 0%

profile of v7, /device:TPU:1, one launch (start us, length us, event | category | flops | bytes accessed | tf_op | source)
XLA Modules:
  0.0 224.5 jit_solution(9566653304139573089)
XLA Ops:
  0.0 11.6 %collective-permute-start = (bf16[2,512,32]{1,2,0:T(8,128)(2,1)}, bf16[2,512,32]{1,2,0:T(8,128)(2,1)S(1)}, u32[]{:S(2)}, u32[]{:S(2)}) collective-permute-start(bf16[2,512,32]{1,2,0:T(8,128)(2,1)} %param.43), channel_id=1, source_target_pairs={{0,448},{8,456},{16,464},{24,472},{32,480},{40,488},{48,496},{56,5... | collective-permute-start | bytes 196616 | tf_op jit(solution)/shard_map/ppermute | solution.py:133
  11.7 1.9 collective-permute-start.3
  13.6 0.9 bitcast_dynamic-update-slice_fusion.15
  14.5 0.8 reduce-window.4
  16.6 0.9 slice_convert_fusion.1
  17.6 0.8 slice_convert_fusion.3
  21.1 0.8 fusion.176
  23.4 1.5 fusion.177
  24.9 0.8 fusion.180
  28.2 0.7 compare_select_fusion.1
  29.2 0.7 compare_select_fusion
  30.9 0.9 fusion.16
  31.8 4.6 %collective-permute-start.1 = (bf16[2,512,32]{1,2,0:T(8,128)(2,1)S(1)}, bf16[2,512,32]{1,2,0:T(8,128)(2,1)S(1)}, u32[]{:S(2)}, u32[]{:S(2)}) collective-permute-start(bf16[2,512,32]{1,2,0:T(8,128)(2,1)S(1)} %collective-permute-done), channel_id=1, source_target_pairs={{0,448},{8,456},{16,464},{24,472},{32,480},{40,488},{48,496},{56,5... | collective-permute-start | bytes 196616 | tf_op jit(solution)/shard_map/ppermute | solution.py:133
  36.4 1.9 collective-permute-start.4
  38.4 4.6 %collective-permute-start.2 = (bf16[2,512,32]{1,2,0:T(8,128)(2,1)S(1)}, bf16[2,512,32]{1,2,0:T(8,128)(2,1)S(1)}, u32[]{:S(2)}, u32[]{:S(2)}) collective-permute-start(bf16[2,512,32]{1,2,0:T(8,128)(2,1)S(1)} %collective-permute-done.1), channel_id=1, source_target_pairs={{0,448},{8,456},{16,464},{24,472},{32,480},{40,488},{48,496},{56,5... | collective-permute-start | bytes 196616 | tf_op jit(solution)/shard_map/ppermute | solution.py:133
  43.0 1.9 collective-permute-start.5
  44.9 4.3 %collective-permute-done.5 = bf16[2,512,32]{1,2,0:T(8,128)(2,1)S(1)} collective-permute-done((bf16[2,512,32]{1,2,0:T(8,128)(2,1)S(1)}, bf16[2,512,32]{1,2,0:T(8,128)(2,1)S(1)}, u32[]{:S(2)}, u32[]{:S(2)}) %collective-permute-start.5) | collective-permute-done | bytes 65568 | tf_op jit(solution)/shard_map/ppermute | solution.py:130
  49.2 1.9 collective-permute-start.6
  51.1 4.3 %collective-permute-done.6 = bf16[2,512,32]{1,2,0:T(8,128)(2,1)S(1)} collective-permute-done((bf16[2,512,32]{1,2,0:T(8,128)(2,1)S(1)}, bf16[2,512,32]{1,2,0:T(8,128)(2,1)S(1)}, u32[]{:S(2)}, u32[]{:S(2)}) %collective-permute-start.6) | collective-permute-done | bytes 65568 | tf_op jit(solution)/shard_map/ppermute | solution.py:130
  55.4 3.1 %collective-permute-start.8 = (bf16[8,2,512,32]{2,3,0,1:T(8,128)(2,1)S(1)}, bf16[8,2,512,32]{2,3,0,1:T(8,128)(2,1)S(1)}, u32[]{:S(2)}, u32[]{:S(2)}) collective-permute-start(bf16[8,2,512,32]{2,3,0,1:T(8,128)(2,1)S(1)} %bitcast_dynamic-update-slice_fusion.13), channel_id=1, source_target_pairs={{0,16},{8,24},{16,32},{24,40},{32,48},{40,56},{48,0},{56,8},{64,80... | collective-permute-start | bytes 1572872 | tf_op jit(solution)/shard_map/ppermute | solution.py:130
  60.1 3.4 %collective-permute-start.7 = (bf16[8,2,512,32]{2,3,0,1:T(8,128)(2,1)S(1)}, bf16[8,2,512,32]{2,3,0,1:T(8,128)(2,1)S(1)}, u32[]{:S(2)}, u32[]{:S(2)}) collective-permute-start(bf16[8,2,512,32]{2,3,0,1:T(8,128)(2,1)S(1)} %bitcast_dynamic-update-slice_fusion.13), channel_id=1, source_target_pairs={{0,48},{8,56},{16,0},{24,8},{32,16},{40,24},{48,32},{56,40},{64,11... | collective-permute-start | bytes 1572872 | tf_op jit(solution)/shard_map/ppermute | solution.py:133
  63.6 3.7 %collective-permute-done.8 = bf16[8,2,512,32]{2,3,0,1:T(8,128)(2,1)S(1)} collective-permute-done((bf16[8,2,512,32]{2,3,0,1:T(8,128)(2,1)S(1)}, bf16[8,2,512,32]{2,3,0,1:T(8,128)(2,1)S(1)}, u32[]{:S(2)}, u32[]{:S(2)}) %collective-permute-start.8) | collective-permute-done | bytes 524320 | tf_op jit(solution)/shard_map/ppermute | solution.py:130
  67.3 1.9 collective-permute-start.9
  69.3 2.0 fusion.10
  71.6 1.3 divide_multiply_fusion.1
  72.9 1.3 fusion.12
  74.2 4.2 %collective-permute-done.9 = bf16[8,2,512,32]{2,3,0,1:T(8,128)(2,1)S(1)} collective-permute-done((bf16[8,2,512,32]{2,3,0,1:T(8,128)(2,1)S(1)}, bf16[8,2,512,32]{2,3,0,1:T(8,128)(2,1)S(1)}, u32[]{:S(2)}, u32[]{:S(2)}) %collective-permute-start.9) | collective-permute-done | bytes 524320 | tf_op jit(solution)/shard_map/ppermute | solution.py:130
  78.5 0.8 copy-done.3
  79.3 2.8 %fusion.175 = (bf16[1,4,8,2,512,32]{4,5,0,1,2,3:T(8,128)(2,1)S(1)}, bf16[4,8,2,512,32]{3,4,0,1,2:T(8,128)(2,1)}) fusion(bf16[1,8,2,512,32]{3,4,0,1,2:T(8,128)(2,1)S(1)} %bitcast.387, bf16[1,8,2,512,32]{3,4,0,1,2:T(8,128)(2,1)} %bitcast.389, bf16[1,8,2,512,32]{3,4,0,1,2:T(8,128)(2,1)} %bitcast.388, bf16[1,8,2,512,32]{3,4,0,1,2:T(8,128)(2,1)S(1)} %bitcast.386), kind=kLoop, calls=%fused_computation.339 | loop fusion | flops 3145728 | bytes 6291456 | tf_op jit(solution)/shard_map/stack | solution.py:135
  82.1 8.7 %collective-permute-start.10 = (bf16[4,8,2,512,32]{3,4,0,1,2:T(8,128)(2,1)}, bf16[4,8,2,512,32]{3,4,0,1,2:T(8,128)(2,1)}, u32[]{:S(2)}, u32[]{:S(2)}) collective-permute-start(bf16[4,8,2,512,32]{3,4,0,1,2:T(8,128)(2,1)} %get-tuple-element.65), channel_id=1, source_target_pairs={{0,8},{8,0},{16,24},{24,16},{32,40},{40,32},{48,56},{56,48},{64,72... | collective-permute-start | bytes 6291464 | tf_op jit(solution)/shard_map/ppermute | solution.py:130
  91.5 0.9 fusion.137
  92.3 1.2 divide_multiply_fusion.3
  93.6 2.0 fusion.9
  98.2 2.0 maximum_bitcast_fusion
  100.2 1.6 fusion.2
  101.7 1.6 fusion.1
  103.3 1.6 fusion
  104.9 1.4 convolution_convert_fusion
  106.4 0.9 copy.283
  107.2 6.8 %all-to-all-start = ((bf16[2,8,8,2432]{3,2,0,1:T(8,128)(2,1)}), bf16[2,8,8,2432]{3,2,0,1:T(8,128)(2,1)S(1)}, u32[]{:S(2)}, u32[]{:S(2)}) async-start(bf16[2,8,8,2432]{3,2,0,1:T(8,128)(2,1)} %copy.283), calls=%async_computation | async-start | bytes 1245184 | tf_op jit(solution)/shard_map/all_to_all | solution.py:247
  114.1 2.4 %collective-permute-start.21 = (bf16[2,400,2048]{2,1,0:T(8,128)(2,1)}, bf16[2,400,2048]{2,1,0:T(8,128)(2,1)}, u32[]{:S(2)}, u32[]{:S(2)}) collective-permute-start(bf16[2,400,2048]{2,1,0:T(8,128)(2,1)} %param.44), channel_id=1, source_target_pairs={{0,8},{8,0},{16,24},{24,16},{32,40},{40,32},{48,56},{56,48},{64,72... | collective-permute-start | bytes 9830408 | tf_op jit(solution)/shard_map/ppermute | solution.py:192
  118.3 1.3 broadcast_select_fusion
  119.7 0.9 scatter.19
  120.6 13.6 %all-to-all-done = bf16[2,8,8,2432]{3,2,0,1:T(8,128)(2,1)S(1)} async-done(((bf16[2,8,8,2432]{3,2,0,1:T(8,128)(2,1)}), bf16[2,8,8,2432]{3,2,0,1:T(8,128)(2,1)S(1)}, u32[]{:S(2)}, u32[]{:S(2)}) %all-to-all-start) | async-done | bytes 622624 | tf_op jit(solution)/shard_map/all_to_all | solution.py:247
  135.4 1.9 collective-permute-start.11
  137.3 3.4 %collective-permute-start.14 = (bf16[17,2048]{1,0:T(8,128)(2,1)S(1)}, bf16[17,2048]{1,0:T(8,128)(2,1)S(1)}, u32[]{:S(2)}, u32[]{:S(2)}) collective-permute-start(bf16[17,2048]{1,0:T(8,128)(2,1)S(1)} %pad_maximum_fusion.4), channel_id=1, source_target_pairs={{0,64},{8,72},{16,80},{24,88},{32,96},{40,104},{48,112},{56,120},{... | collective-permute-start | bytes 208904 | tf_op jit(solution)/shard_map/ppermute | solution.py:130
  141.2 3.4 %collective-permute-start.12 = (bf16[17,2048]{1,0:T(8,128)(2,1)S(1)}, bf16[17,2048]{1,0:T(8,128)(2,1)S(1)}, u32[]{:S(2)}, u32[]{:S(2)}) collective-permute-start(bf16[17,2048]{1,0:T(8,128)(2,1)S(1)} %collective-permute-done.11), channel_id=1, source_target_pairs={{0,448},{8,456},{16,464},{24,472},{32,480},{40,488},{48,496},{56,5... | collective-permute-start | bytes 208904 | tf_op jit(solution)/shard_map/ppermute | solution.py:133
  144.6 1.9 collective-permute-start.15
  146.6 4.6 %collective-permute-start.13 = (bf16[17,2048]{1,0:T(8,128)(2,1)S(1)}, bf16[17,2048]{1,0:T(8,128)(2,1)S(1)}, u32[]{:S(2)}, u32[]{:S(2)}) collective-permute-start(bf16[17,2048]{1,0:T(8,128)(2,1)S(1)} %collective-permute-done.12), channel_id=1, source_target_pairs={{0,448},{8,456},{16,464},{24,472},{32,480},{40,488},{48,496},{56,5... | collective-permute-start | bytes 208904 | tf_op jit(solution)/shard_map/ppermute | solution.py:133
  151.2 1.9 collective-permute-start.16
  153.1 4.6 %collective-permute-done.16 = bf16[17,2048]{1,0:T(8,128)(2,1)S(1)} collective-permute-done((bf16[17,2048]{1,0:T(8,128)(2,1)S(1)}, bf16[17,2048]{1,0:T(8,128)(2,1)S(1)}, u32[]{:S(2)}, u32[]{:S(2)}) %collective-permute-start.16) | collective-permute-done | bytes 69664 | tf_op jit(solution)/shard_map/ppermute | solution.py:130
  157.8 1.9 collective-permute-start.17
  159.7 4.6 %collective-permute-done.17 = bf16[17,2048]{1,0:T(8,128)(2,1)S(1)} collective-permute-done((bf16[17,2048]{1,0:T(8,128)(2,1)S(1)}, bf16[17,2048]{1,0:T(8,128)(2,1)S(1)}, u32[]{:S(2)}, u32[]{:S(2)}) %collective-permute-start.17) | collective-permute-done | bytes 69664 | tf_op jit(solution)/shard_map/ppermute | solution.py:130
  164.7 1.9 collective-permute-start.19
  166.7 4.6 %collective-permute-start.18 = (bf16[8,17,2048]{2,0,1:T(8,128)(2,1)S(1)}, bf16[8,17,2048]{2,0,1:T(8,128)(2,1)S(1)}, u32[]{:S(2)}, u32[]{:S(2)}) collective-permute-start(bf16[8,17,2048]{2,0,1:T(8,128)(2,1)S(1)} %copy.285), channel_id=1, source_target_pairs={{0,48},{8,56},{16,0},{24,8},{32,16},{40,24},{48,32},{56,40},{64,11... | collective-permute-start | bytes 1671176 | tf_op jit(solution)/shard_map/ppermute | solution.py:133
  171.2 6.0 %collective-permute-done.19 = bf16[8,17,2048]{2,0,1:T(8,128)(2,1)S(1)} collective-permute-done((bf16[8,17,2048]{2,0,1:T(8,128)(2,1)S(1)}, bf16[8,17,2048]{2,0,1:T(8,128)(2,1)S(1)}, u32[]{:S(2)}, u32[]{:S(2)}) %collective-permute-start.19) | collective-permute-done | bytes 557088 | tf_op jit(solution)/shard_map/ppermute | solution.py:130
  177.2 1.9 collective-permute-start.20
  179.8 8.9 %collective-permute-done.20 = bf16[8,17,2048]{2,0,1:T(8,128)(2,1)S(1)} collective-permute-done((bf16[8,17,2048]{2,0,1:T(8,128)(2,1)S(1)}, bf16[8,17,2048]{2,0,1:T(8,128)(2,1)S(1)}, u32[]{:S(2)}, u32[]{:S(2)}) %collective-permute-start.20) | collective-permute-done | bytes 557088 | tf_op jit(solution)/shard_map/ppermute | solution.py:130
  189.6 1.7 copy-done
  191.8 3.8 %fusion.184 = (f32[2,256]{1,0:T(2,128)S(1)}, f32[2,256,400]{1,2,0:T(8,128)S(1)}) fusion(bf16[2,400,2048]{2,1,0:T(8,128)(2,1)} %param.44, bf16[32,17,2048]{2,1,0:T(8,128)(2,1)} %bitcast.373), kind=kOutput, calls=%fused_computation.348 | convolution fusion | flops 839065088 | bytes 6195200 | tf_op jit(solution)/shard_map/mnd,mvd->mnv/dot_general | solution.py:115
  195.6 3.2 %fusion.185 = (f32[2,256]{1,0:T(2,128)S(1)}, f32[2,256,400]{1,2,0:T(8,128)S(1)}) fusion(bf16[2,400,2048]{2,1,0:T(8,128)(2,1)} %collective-permute-done.21, bf16[32,17,2048]{2,1,0:T(8,128)(2,1)S(1)} %bitcast.374), kind=kOutput, calls=%fused_computation.349 | convolution fusion | flops 839065088 | bytes 6195200 | tf_op jit(solution)/shard_map/mnd,mvd->mnv/dot_general | solution.py:115
  199.8 0.8 copy.292
  200.7 10.8 %all-to-all-start.1 = ((f32[3,2,64,8]{3,1,0,2:T(2,128)}), f32[3,2,64,8]{3,1,0,2:T(2,128)S(1)}, u32[]{:S(2)}, u32[]{:S(2)}) async-start(f32[3,2,64,8]{3,1,0,2:T(2,128)} %copy.292), calls=%async_computation.1 | async-start | bytes 393216 | tf_op jit(solution)/shard_map/all_to_all | solution.py:318
  211.6 12.1 %all-to-all-done.1 = f32[3,2,64,8]{3,1,0,2:T(2,128)S(1)} async-done(((f32[3,2,64,8]{3,1,0,2:T(2,128)}), f32[3,2,64,8]{3,1,0,2:T(2,128)S(1)}, u32[]{:S(2)}, u32[]{:S(2)}) %all-to-all-start.1) | async-done | bytes 12320 | tf_op jit(solution)/shard_map/all_to_all | solution.py:318
  (214 shorter events, 22.0 us)
Async XLA Ops:
  0.0 27.4 %copy-start.7 = (bf16[2,64,256]{2,1,0:T(8,128)(2,1)S(1)}, bf16[2,64,256]{2,1,0:T(8,128)(2,1)}, u32[]{:S(2)}) copy-start(bf16[2,64,256]{2,1,0:T(8,128)(2,1)} %param.33) | copy-start | bytes 196612
  0.0 26.8 %copy-start.16 = (f32[2,4,256]{2,1,0:T(4,128)S(1)}, f32[2,4,256]{2,1,0:T(4,128)}, u32[]{:S(2)}) copy-start(f32[2,4,256]{2,1,0:T(4,128)} %param.37) | copy-start | bytes 24580
  0.0 27.8 %copy-start.24 = (f32[2,8]{1,0:T(2,128)S(1)}, f32[2,8]{1,0:T(2,128)}, u32[]{:S(2)}) copy-start(f32[2,8]{1,0:T(2,128)} %param.38) | copy-start | bytes 196
  0.0 27.8 %copy-start.23 = (f32[2,8]{1,0:T(2,128)S(1)}, f32[2,8]{1,0:T(2,128)}, u32[]{:S(2)}) copy-start(f32[2,8]{1,0:T(2,128)} %param.39) | copy-start | bytes 196
  0.0 27.8 %copy-start.12 = (bf16[2,64,8]{1,2,0:T(8,128)(2,1)S(1)}, bf16[2,64,8]{1,2,0:T(8,128)(2,1)}, u32[]{:S(2)}) copy-start(bf16[2,64,8]{1,2,0:T(8,128)(2,1)} %param.34) | copy-start | bytes 6148
  0.0 31.8 %collective-permute-start = (bf16[2,512,32]{1,2,0:T(8,128)(2,1)}, bf16[2,512,32]{1,2,0:T(8,128)(2,1)S(1)}, u32[]{:S(2)}, u32[]{:S(2)}) collective-permute-start(bf16[2,512,32]{1,2,0:T(8,128)(2,1)} %param.43), channel_id=1, source_target_pairs={{0,448},{8,456},{16,464},{24,472},{32,480},{40,488},{48,496},{56,5... | collective-permute-start | bytes 196616 | tf_op jit(solution)/shard_map/ppermute | solution.py:133
  11.7 24.7 %collective-permute-start.3 = (bf16[2,512,32]{1,2,0:T(8,128)(2,1)}, bf16[2,512,32]{1,2,0:T(8,128)(2,1)S(1)}, u32[]{:S(2)}, u32[]{:S(2)}) collective-permute-start(bf16[2,512,32]{1,2,0:T(8,128)(2,1)} %param.43), channel_id=1, source_target_pairs={{0,64},{8,72},{16,80},{24,88},{32,96},{40,104},{48,112},{56,120},{... | collective-permute-start | bytes 196616 | tf_op jit(solution)/shard_map/ppermute | solution.py:130
  14.4 44.1 %copy-start.22 = (f32[2,8]{1,0:T(2,128)S(1)}, f32[2,8]{1,0:T(2,128)}, u32[]{:S(2)}) copy-start(f32[2,8]{1,0:T(2,128)} %param.40) | copy-start | bytes 196
  16.0 42.6 %copy-start.25 = (pred[3]{0:T(512)(128)(4,1)}, pred[3]{0:T(512)(128)(4,1)S(1)}, u32[]{:S(2)}) copy-start(pred[3]{0:T(512)(128)(4,1)S(1)} %get-tuple-element.62) | copy-start | bytes 13
  17.5 42.3 %copy-start.4 = (bf16[2,64,512]{2,1,0:T(8,128)(2,1)S(1)}, bf16[2,64,512]{2,1,0:T(8,128)(2,1)}, u32[]{:S(2)}) copy-start(bf16[2,64,512]{2,1,0:T(8,128)(2,1)} %param.32) | copy-start | bytes 393220
  20.4 39.7 %copy-start.9 = (s32[64]{0:T(128)}, s32[64]{0:T(128)S(1)}, u32[]{:S(2)}) copy-start(s32[64]{0:T(128)S(1)} %fusion.143) | copy-start | bytes 772
  21.1 48.2 %copy-start.40 = (f32[3]{0:T(128)}, f32[3]{0:T(128)S(1)}, u32[]{:S(2)}) copy-start(f32[3]{0:T(128)S(1)} %get-tuple-element.121) | copy-start | bytes 40
  23.3 40.3 %copy-start.27 = (pred[64]{0:T(512)(128)(4,1)}, pred[64]{0:T(512)(128)(4,1)S(1)}, u32[]{:S(2)}) copy-start(pred[64]{0:T(512)(128)(4,1)S(1)} %get-tuple-element.123) | copy-start | bytes 196
  23.3 40.3 %copy-start.28 = (pred[64]{0:T(512)(128)(4,1)}, pred[64]{0:T(512)(128)(4,1)S(1)}, u32[]{:S(2)}) copy-start(pred[64]{0:T(512)(128)(4,1)S(1)} %get-tuple-element.124) | copy-start | bytes 196
  23.3 40.3 %copy-start.29 = (pred[64]{0:T(512)(128)(4,1)}, pred[64]{0:T(512)(128)(4,1)S(1)}, u32[]{:S(2)}) copy-start(pred[64]{0:T(512)(128)(4,1)S(1)} %get-tuple-element.125) | copy-start | bytes 196
  23.3 40.3 %copy-start.30 = (pred[64]{0:T(512)(128)(4,1)}, pred[64]{0:T(512)(128)(4,1)S(1)}, u32[]{:S(2)}) copy-start(pred[64]{0:T(512)(128)(4,1)S(1)} %get-tuple-element.126) | copy-start | bytes 196
  23.3 40.3 %copy-start.31 = (pred[64]{0:T(512)(128)(4,1)}, pred[64]{0:T(512)(128)(4,1)S(1)}, u32[]{:S(2)}) copy-start(pred[64]{0:T(512)(128)(4,1)S(1)} %get-tuple-element.127) | copy-start | bytes 196
  23.3 40.3 %copy-start.32 = (pred[64]{0:T(512)(128)(4,1)}, pred[64]{0:T(512)(128)(4,1)S(1)}, u32[]{:S(2)}) copy-start(pred[64]{0:T(512)(128)(4,1)S(1)} %get-tuple-element.128) | copy-start | bytes 196
  23.3 40.3 %copy-start.33 = (pred[64]{0:T(512)(128)(4,1)}, pred[64]{0:T(512)(128)(4,1)S(1)}, u32[]{:S(2)}) copy-start(pred[64]{0:T(512)(128)(4,1)S(1)} %get-tuple-element.129) | copy-start | bytes 196
  23.3 40.3 %copy-start.34 = (pred[64]{0:T(512)(128)(4,1)}, pred[64]{0:T(512)(128)(4,1)S(1)}, u32[]{:S(2)}) copy-start(pred[64]{0:T(512)(128)(4,1)S(1)} %get-tuple-element.130) | copy-start | bytes 196
  23.3 40.3 %copy-start.35 = (pred[64]{0:T(512)(128)(4,1)}, pred[64]{0:T(512)(128)(4,1)S(1)}, u32[]{:S(2)}) copy-start(pred[64]{0:T(512)(128)(4,1)S(1)} %get-tuple-element.131) | copy-start | bytes 196
  23.4 40.3 %copy-start.36 = (pred[64]{0:T(512)(128)(4,1)}, pred[64]{0:T(512)(128)(4,1)S(1)}, u32[]{:S(2)}) copy-start(pred[64]{0:T(512)(128)(4,1)S(1)} %get-tuple-element.132) | copy-start | bytes 196
  23.4 40.3 %copy-start.37 = (pred[64]{0:T(512)(128)(4,1)}, pred[64]{0:T(512)(128)(4,1)S(1)}, u32[]{:S(2)}) copy-start(pred[64]{0:T(512)(128)(4,1)S(1)} %get-tuple-element.133) | copy-start | bytes 196
  23.4 40.3 %copy-start.38 = (pred[64]{0:T(512)(128)(4,1)}, pred[64]{0:T(512)(128)(4,1)S(1)}, u32[]{:S(2)}) copy-start(pred[64]{0:T(512)(128)(4,1)S(1)} %get-tuple-element.134) | copy-start | bytes 196
  29.9 6.5 %copy-start.17 = (s32[1024]{0:T(1024)}, s32[1024]{0:T(1024)S(1)}, u32[]{:S(2)}) copy-start(s32[1024]{0:T(1024)S(1)} %pad_clamp_fusion) | copy-start | bytes 12292
  31.8 39.7 %copy-start.19 = (f32[64,3]{0,1:T(4,128)}, f32[64,3]{0,1:T(4,128)S(1)}, u32[]{:S(2)}) copy-start(f32[64,3]{0,1:T(4,128)S(1)} %fusion.142) | copy-start | bytes 2308
  31.8 6.5 %collective-permute-start.1 = (bf16[2,512,32]{1,2,0:T(8,128)(2,1)S(1)}, bf16[2,512,32]{1,2,0:T(8,128)(2,1)S(1)}, u32[]{:S(2)}, u32[]{:S(2)}) collective-permute-start(bf16[2,512,32]{1,2,0:T(8,128)(2,1)S(1)} %collective-permute-done), channel_id=1, source_target_pairs={{0,448},{8,456},{16,464},{24,472},{32,480},{40,488},{48,496},{56,5... | collective-permute-start | bytes 196616 | tf_op jit(solution)/shard_map/ppermute | solution.py:133
  36.4 6.5 %collective-permute-start.4 = (bf16[2,512,32]{1,2,0:T(8,128)(2,1)S(1)}, bf16[2,512,32]{1,2,0:T(8,128)(2,1)S(1)}, u32[]{:S(2)}, u32[]{:S(2)}) collective-permute-start(bf16[2,512,32]{1,2,0:T(8,128)(2,1)S(1)} %collective-permute-done.3), channel_id=1, source_target_pairs={{0,64},{8,72},{16,80},{24,88},{32,96},{40,104},{48,112},{56,120},{... | collective-permute-start | bytes 196616 | tf_op jit(solution)/shard_map/ppermute | solution.py:130
  38.4 12.7 %collective-permute-start.2 = (bf16[2,512,32]{1,2,0:T(8,128)(2,1)S(1)}, bf16[2,512,32]{1,2,0:T(8,128)(2,1)S(1)}, u32[]{:S(2)}, u32[]{:S(2)}) collective-permute-start(bf16[2,512,32]{1,2,0:T(8,128)(2,1)S(1)} %collective-permute-done.1), channel_id=1, source_target_pairs={{0,448},{8,456},{16,464},{24,472},{32,480},{40,488},{48,496},{56,5... | collective-permute-start | bytes 196616 | tf_op jit(solution)/shard_map/ppermute | solution.py:133
  43.0 6.2 %collective-permute-start.5 = (bf16[2,512,32]{1,2,0:T(8,128)(2,1)S(1)}, bf16[2,512,32]{1,2,0:T(8,128)(2,1)S(1)}, u32[]{:S(2)}, u32[]{:S(2)}) collective-permute-start(bf16[2,512,32]{1,2,0:T(8,128)(2,1)S(1)} %collective-permute-done.4), channel_id=1, source_target_pairs={{0,64},{8,72},{16,80},{24,88},{32,96},{40,104},{48,112},{56,120},{... | collective-permute-start | bytes 196616 | tf_op jit(solution)/shard_map/ppermute | solution.py:130
  49.2 6.2 %collective-permute-start.6 = (bf16[2,512,32]{1,2,0:T(8,128)(2,1)S(1)}, bf16[2,512,32]{1,2,0:T(8,128)(2,1)S(1)}, u32[]{:S(2)}, u32[]{:S(2)}) collective-permute-start(bf16[2,512,32]{1,2,0:T(8,128)(2,1)S(1)} %collective-permute-done.5), channel_id=1, source_target_pairs={{0,64},{8,72},{16,80},{24,88},{32,96},{40,104},{48,112},{56,120},{... | collective-permute-start | bytes 196616 | tf_op jit(solution)/shard_map/ppermute | solution.py:130
  55.4 11.9 %collective-permute-start.8 = (bf16[8,2,512,32]{2,3,0,1:T(8,128)(2,1)S(1)}, bf16[8,2,512,32]{2,3,0,1:T(8,128)(2,1)S(1)}, u32[]{:S(2)}, u32[]{:S(2)}) collective-permute-start(bf16[8,2,512,32]{2,3,0,1:T(8,128)(2,1)S(1)} %bitcast_dynamic-update-slice_fusion.13), channel_id=1, source_target_pairs={{0,16},{8,24},{16,32},{24,40},{32,48},{40,56},{48,0},{56,8},{64,80... | collective-permute-start | bytes 1572872 | tf_op jit(solution)/shard_map/ppermute | solution.py:130
  60.1 14.1 %collective-permute-start.7 = (bf16[8,2,512,32]{2,3,0,1:T(8,128)(2,1)S(1)}, bf16[8,2,512,32]{2,3,0,1:T(8,128)(2,1)S(1)}, u32[]{:S(2)}, u32[]{:S(2)}) collective-permute-start(bf16[8,2,512,32]{2,3,0,1:T(8,128)(2,1)S(1)} %bitcast_dynamic-update-slice_fusion.13), channel_id=1, source_target_pairs={{0,48},{8,56},{16,0},{24,8},{32,16},{40,24},{48,32},{56,40},{64,11... | collective-permute-start | bytes 1572872 | tf_op jit(solution)/shard_map/ppermute | solution.py:133
  67.3 11.1 %collective-permute-start.9 = (bf16[8,2,512,32]{2,3,0,1:T(8,128)(2,1)S(1)}, bf16[8,2,512,32]{2,3,0,1:T(8,128)(2,1)S(1)}, u32[]{:S(2)}, u32[]{:S(2)}) collective-permute-start(bf16[8,2,512,32]{2,3,0,1:T(8,128)(2,1)S(1)} %collective-permute-done.8), channel_id=1, source_target_pairs={{0,16},{8,24},{16,32},{24,40},{32,48},{40,56},{48,0},{56,8},{64,80... | collective-permute-start | bytes 1572872 | tf_op jit(solution)/shard_map/ppermute | solution.py:130
  74.2 4.2 %copy-start.2 = (bf16[8,2,512,32]{2,3,0,1:T(8,128)(2,1)}, bf16[8,2,512,32]{2,3,0,1:T(8,128)(2,1)S(1)}, u32[]{:S(2)}) copy-start(bf16[8,2,512,32]{2,3,0,1:T(8,128)(2,1)S(1)} %collective-permute-done.7) | copy-start | bytes 1572868
  79.3 11.6 %copy-start.10 = (s32[64]{0:T(128)S(1)}, s32[64]{0:T(128)}, u32[]{:S(2)}) copy-start(s32[64]{0:T(128)} %copy-done.9) | copy-start | bytes 772
  79.3 11.6 %copy-start.15 = (bf16[3,1,256]{2,1,0:T(2,128)(2,1)S(1)}, bf16[3,1,256]{2,1,0:T(2,128)(2,1)}, u32[]{:S(2)}) copy-start(bf16[3,1,256]{2,1,0:T(2,128)(2,1)} %get-tuple-element.101) | copy-start | bytes 4612
  82.1 13.6 %copy-start.13 = (f32[64,8]{0,1:T(8,128)S(1)}, f32[64,8]{0,1:T(8,128)}, u32[]{:S(2)}) copy-start(f32[64,8]{0,1:T(8,128)} %get-tuple-element.107) | copy-start | bytes 6148
  82.1 14.4 %copy-start.26 = (pred[3]{0:T(512)(128)(4,1)S(1)}, pred[3]{0:T(512)(128)(4,1)}, u32[]{:S(2)}) copy-start(pred[3]{0:T(512)(128)(4,1)} %copy-done.25) | copy-start | bytes 13
  82.1 14.8 %copy-start.11 = (f32[64,8]{0,1:T(8,128)S(1)}, f32[64,8]{0,1:T(8,128)}, u32[]{:S(2)}) copy-start(f32[64,8]{0,1:T(8,128)} %get-tuple-element.106) | copy-start | bytes 6148
  82.1 14.8 %copy-start.21 = (f32[8]{0:T(128)S(1)}, f32[8]{0:T(128)}, u32[]{:S(2)}) copy-start(f32[8]{0:T(128)} %get-tuple-element.115) | copy-start | bytes 100
  82.1 15.6 %copy-start.5 = (bf16[2,64,512]{2,1,0:T(8,128)(2,1)S(1)}, bf16[2,64,512]{2,1,0:T(8,128)(2,1)}, u32[]{:S(2)}) copy-start(bf16[2,64,512]{2,1,0:T(8,128)(2,1)} %param.31) | copy-start | bytes 393220
  82.1 16.0 %collective-permute-start.10 = (bf16[4,8,2,512,32]{3,4,0,1,2:T(8,128)(2,1)}, bf16[4,8,2,512,32]{3,4,0,1,2:T(8,128)(2,1)}, u32[]{:S(2)}, u32[]{:S(2)}) collective-permute-start(bf16[4,8,2,512,32]{3,4,0,1,2:T(8,128)(2,1)} %get-tuple-element.65), channel_id=1, source_target_pairs={{0,8},{8,0},{16,24},{24,16},{32,40},{40,32},{48,56},{56,48},{64,72... | collective-permute-start | bytes 6291464 | tf_op jit(solution)/shard_map/ppermute | solution.py:130
  103.3 1.6 copy-start.18
  104.9 1.4 copy-start.8
  104.9 12.8 %copy-start.20 = (s32[64]{0:T(128)S(1)}, s32[64]{0:T(128)}, u32[]{:S(2)}) copy-start(s32[64]{0:T(128)} %param.50) | copy-start | bytes 772
  106.4 28.9 %copy-start.14 = (f32[2,2048]{1,0:T(2,128)S(1)}, f32[2,2048]{1,0:T(2,128)}, u32[]{:S(2)}) copy-start(f32[2,2048]{1,0:T(2,128)} %param.42) | copy-start | bytes 49156
  107.2 27.0 %all-to-all-start = ((bf16[2,8,8,2432]{3,2,0,1:T(8,128)(2,1)}), bf16[2,8,8,2432]{3,2,0,1:T(8,128)(2,1)S(1)}, u32[]{:S(2)}, u32[]{:S(2)}) async-start(bf16[2,8,8,2432]{3,2,0,1:T(8,128)(2,1)} %copy.283), calls=%async_computation | async-start | bytes 1245184 | tf_op jit(solution)/shard_map/all_to_all | solution.py:247
  114.1 81.6 %collective-permute-start.21 = (bf16[2,400,2048]{2,1,0:T(8,128)(2,1)}, bf16[2,400,2048]{2,1,0:T(8,128)(2,1)}, u32[]{:S(2)}, u32[]{:S(2)}) collective-permute-start(bf16[2,400,2048]{2,1,0:T(8,128)(2,1)} %param.44), channel_id=1, source_target_pairs={{0,8},{8,0},{16,24},{24,16},{32,40},{40,32},{48,56},{56,48},{64,72... | collective-permute-start | bytes 9830408 | tf_op jit(solution)/shard_map/ppermute | solution.py:192
  135.4 5.8 %collective-permute-start.11 = (bf16[17,2048]{1,0:T(8,128)(2,1)S(1)}, bf16[17,2048]{1,0:T(8,128)(2,1)S(1)}, u32[]{:S(2)}, u32[]{:S(2)}) collective-permute-start(bf16[17,2048]{1,0:T(8,128)(2,1)S(1)} %pad_maximum_fusion.4), channel_id=1, source_target_pairs={{0,448},{8,456},{16,464},{24,472},{32,480},{40,488},{48,496},{56,5... | collective-permute-start | bytes 208904 | tf_op jit(solution)/shard_map/ppermute | solution.py:133
  137.3 7.3 %collective-permute-start.14 = (bf16[17,2048]{1,0:T(8,128)(2,1)S(1)}, bf16[17,2048]{1,0:T(8,128)(2,1)S(1)}, u32[]{:S(2)}, u32[]{:S(2)}) collective-permute-start(bf16[17,2048]{1,0:T(8,128)(2,1)S(1)} %pad_maximum_fusion.4), channel_id=1, source_target_pairs={{0,64},{8,72},{16,80},{24,88},{32,96},{40,104},{48,112},{56,120},{... | collective-permute-start | bytes 208904 | tf_op jit(solution)/shard_map/ppermute | solution.py:130
  141.2 5.4 %collective-permute-start.12 = (bf16[17,2048]{1,0:T(8,128)(2,1)S(1)}, bf16[17,2048]{1,0:T(8,128)(2,1)S(1)}, u32[]{:S(2)}, u32[]{:S(2)}) collective-permute-start(bf16[17,2048]{1,0:T(8,128)(2,1)S(1)} %collective-permute-done.11), channel_id=1, source_target_pairs={{0,448},{8,456},{16,464},{24,472},{32,480},{40,488},{48,496},{56,5... | collective-permute-start | bytes 208904 | tf_op jit(solution)/shard_map/ppermute | solution.py:133
  144.6 6.6 %collective-permute-start.15 = (bf16[17,2048]{1,0:T(8,128)(2,1)S(1)}, bf16[17,2048]{1,0:T(8,128)(2,1)S(1)}, u32[]{:S(2)}, u32[]{:S(2)}) collective-permute-start(bf16[17,2048]{1,0:T(8,128)(2,1)S(1)} %collective-permute-done.14), channel_id=1, source_target_pairs={{0,64},{8,72},{16,80},{24,88},{32,96},{40,104},{48,112},{56,120},{... | collective-permute-start | bytes 208904 | tf_op jit(solution)/shard_map/ppermute | solution.py:130
  146.6 13.1 %collective-permute-start.13 = (bf16[17,2048]{1,0:T(8,128)(2,1)S(1)}, bf16[17,2048]{1,0:T(8,128)(2,1)S(1)}, u32[]{:S(2)}, u32[]{:S(2)}) collective-permute-start(bf16[17,2048]{1,0:T(8,128)(2,1)S(1)} %collective-permute-done.12), channel_id=1, source_target_pairs={{0,448},{8,456},{16,464},{24,472},{32,480},{40,488},{48,496},{56,5... | collective-permute-start | bytes 208904 | tf_op jit(solution)/shard_map/ppermute | solution.py:133
  151.2 6.6 %collective-permute-start.16 = (bf16[17,2048]{1,0:T(8,128)(2,1)S(1)}, bf16[17,2048]{1,0:T(8,128)(2,1)S(1)}, u32[]{:S(2)}, u32[]{:S(2)}) collective-permute-start(bf16[17,2048]{1,0:T(8,128)(2,1)S(1)} %collective-permute-done.15), channel_id=1, source_target_pairs={{0,64},{8,72},{16,80},{24,88},{32,96},{40,104},{48,112},{56,120},{... | collective-permute-start | bytes 208904 | tf_op jit(solution)/shard_map/ppermute | solution.py:130
  157.8 6.6 %collective-permute-start.17 = (bf16[17,2048]{1,0:T(8,128)(2,1)S(1)}, bf16[17,2048]{1,0:T(8,128)(2,1)S(1)}, u32[]{:S(2)}, u32[]{:S(2)}) collective-permute-start(bf16[17,2048]{1,0:T(8,128)(2,1)S(1)} %collective-permute-done.16), channel_id=1, source_target_pairs={{0,64},{8,72},{16,80},{24,88},{32,96},{40,104},{48,112},{56,120},{... | collective-permute-start | bytes 208904 | tf_op jit(solution)/shard_map/ppermute | solution.py:130
  164.7 12.5 %collective-permute-start.19 = (bf16[8,17,2048]{2,0,1:T(8,128)(2,1)S(1)}, bf16[8,17,2048]{2,0,1:T(8,128)(2,1)S(1)}, u32[]{:S(2)}, u32[]{:S(2)}) collective-permute-start(bf16[8,17,2048]{2,0,1:T(8,128)(2,1)S(1)} %copy.285), channel_id=1, source_target_pairs={{0,16},{8,24},{16,32},{24,40},{32,48},{40,56},{48,0},{56,8},{64,80... | collective-permute-start | bytes 1671176 | tf_op jit(solution)/shard_map/ppermute | solution.py:130
  166.7 12.8 %collective-permute-start.18 = (bf16[8,17,2048]{2,0,1:T(8,128)(2,1)S(1)}, bf16[8,17,2048]{2,0,1:T(8,128)(2,1)S(1)}, u32[]{:S(2)}, u32[]{:S(2)}) collective-permute-start(bf16[8,17,2048]{2,0,1:T(8,128)(2,1)S(1)} %copy.285), channel_id=1, source_target_pairs={{0,48},{8,56},{16,0},{24,8},{32,16},{40,24},{48,32},{56,40},{64,11... | collective-permute-start | bytes 1671176 | tf_op jit(solution)/shard_map/ppermute | solution.py:133
  177.2 11.5 %collective-permute-start.20 = (bf16[8,17,2048]{2,0,1:T(8,128)(2,1)S(1)}, bf16[8,17,2048]{2,0,1:T(8,128)(2,1)S(1)}, u32[]{:S(2)}, u32[]{:S(2)}) collective-permute-start(bf16[8,17,2048]{2,0,1:T(8,128)(2,1)S(1)} %collective-permute-done.19), channel_id=1, source_target_pairs={{0,16},{8,24},{16,32},{24,40},{32,48},{40,56},{48,0},{56,8},{64,80... | collective-permute-start | bytes 1671176 | tf_op jit(solution)/shard_map/ppermute | solution.py:130
  189.6 1.7 copy-start
  191.8 3.8 %copy-start.1 = (bf16[4,8,17,2048]{3,2,1,0:T(8,128)(2,1)S(1)}, bf16[4,8,17,2048]{3,2,1,0:T(8,128)(2,1)}, u32[]{:S(2)}) copy-start(bf16[4,8,17,2048]{3,2,1,0:T(8,128)(2,1)} %copy-done) | copy-start | bytes 6684676
  195.6 4.0 %copy-start.6 = (f32[3,2,8,4,8]{4,2,3,1,0:T(8,128)S(1)}, f32[3,2,8,4,8]{4,2,3,1,0:T(8,128)}, u32[]{:S(2)}) copy-start(f32[3,2,8,4,8]{4,2,3,1,0:T(8,128)} %constant.319.clone.1) | copy-start | bytes 18436
  198.8 12.7 %copy-start.39 = (s32[64]{0:T(128)S(1)}, s32[64]{0:T(128)}, u32[]{:S(2)}) copy-start(s32[64]{0:T(128)} %param.51) | copy-start | bytes 772
  200.7 23.0 %all-to-all-start.1 = ((f32[3,2,64,8]{3,1,0,2:T(2,128)}), f32[3,2,64,8]{3,1,0,2:T(2,128)S(1)}, u32[]{:S(2)}, u32[]{:S(2)}) async-start(f32[3,2,64,8]{3,1,0,2:T(2,128)} %copy.292), calls=%async_computation.1 | async-start | bytes 393216 | tf_op jit(solution)/shard_map/all_to_all | solution.py:318
  (1 other events, 0.8 us)

commit v8 on v7

--- a/solution.py
+++ b/solution.py
@@ -132,6 +132,13 @@
         if step < count - step:
             backward = lax.ppermute(backward, "req", perm_of(-1))
             got[step] = backward
+    return jnp.stack([got[k] for k in range(count)])
+
+
+def direct_gather(block, perm_of, count):
+    got = {0: block}
+    for shift in range(1, count):
+        got[-shift % count] = lax.ppermute(block, "req", perm_of(shift))
     return jnp.stack([got[k] for k in range(count)])
 
 
@@ -217,7 +224,7 @@
     squares = jnp.sum(gated * gated, axis=2)
     unscaled = (gated * norm_gain[:, None, :]).astype(jnp.bfloat16)
     ring_weight = ring_gather(
-        ring_gather(ring_gather(out_weight, along_z, chips_z), along_x, ROWS_X),
+        direct_gather(direct_gather(out_weight, along_z, chips_z), along_x, ROWS_X),
         along_core,
         CORES,
     )
@@ -279,7 +286,7 @@
     target_row = target_row.at[0, row_count : 2 * row_count].set(low_digit)
     packet = jnp.concatenate([final_rows.reshape(models * row_count, full_width), target_row], axis=0)
 
-    every = ring_gather(ring_gather(packet, along_z, chips_z), along_x, ROWS_X)
+    every = direct_gather(direct_gather(packet, along_z, chips_z), along_x, ROWS_X)
     peers = ROWS_X * chips_z
     every = every.reshape(peers, models * row_count + 1, full_width)
     every_rows = (

time: 226 us -> 239 us (1.058)
  waiting for transfers between devices: 66.8 us -> 79.6 us
    ppermute x8 -> x20, waiting for transfers between devices: 0.49 us -> 54.1 us  [direct_gather(): got[-shift % count] = lax.ppermute(block, 'req', perm_of(shift))]
    ppermute x13 -> x1, waiting for transfers between devices: 40.6 us -> 0.01 us  [ring_gather(): forward = lax.ppermute(forward, 'req', perm_of(1))]
    ppermute x8 -> x20, starting transfers between devices: 38.7 us -> 74.9 us  [direct_gather(): got[-shift % count] = lax.ppermute(block, 'req', perm_of(shift))]
    ppermute x13 -> x1, starting transfers between devices: 34.4 us -> 2.53 us  [ring_gather(): forward = lax.ppermute(forward, 'req', perm_of(1))]
    all_to_all x1, starting transfers between devices: 10.8 us -> 7.38 us  [local(): lax.all_to_all(send, 'req', split_axis=2, concat_axis=2, tiled=True)]
  transfers between devices with their start and end apart: 24 -> 24, of which waited for: 11 -> 11; matrix products, arithmetic and copies ran while one was open for 19% -> 18% of each run, Pallas kernels for 0% -> 0%
where the time goes in v8:
time: 239 us; the launch traced here: 237 us
  starting transfers between devices  94 us (39%)
  waiting for transfers between devices  79.6 us (33%)
  other arithmetic  22.4 us (9%)
  matrix products  21.3 us (9%)
  local copies, waits for them, and re-layouts  18.6 us (8%)
    ppermute x20, starting transfers between devices, direct_gather(): got[-shift % count] = lax.ppermute(block, 'req', perm_of(shift))  74.9 us
    ppermute x20, waiting for transfers between devices, direct_gather(): got[-shift % count] = lax.ppermute(block, 'req', perm_of(shift))  54.1 us
    all_to_all x1, waiting for transfers between devices, local(): lax.all_to_all(payload.reshape(models, groups, row_count, payload.shape[2...  13.5 us
    all_to_all x1, waiting for transfers between devices, local(): lax.all_to_all(send, 'req', split_axis=2, concat_axis=2, tiled=True)  11.9 us
    all_to_all x1, starting transfers between devices, local(): lax.all_to_all(send, 'req', split_axis=2, concat_axis=2, tiled=True)  7.38 us
    dot_general x2, matrix products, head_scores(): jnp.einsum('mnd,mvd->mnv', rows_hidden, head_weight, preferred_element_ty...  6.92 us
    all_to_all x1, starting transfers between devices, local(): lax.all_to_all(payload.reshape(models, groups, row_count, payload.shape[2...  6.82 us
    dot_general x12, matrix products, causal_conv(): jnp.dot(member_bf, history[:, slot_index, :], preferred_element_type=jnp....  5.48 us
  transfers between devices with their start and end apart: 24, of which 11 were waited for; matrix products, arithmetic and copies ran while one was open for 18% of the time, Pallas kernels for 0%

profile of v8, /device:TPU:1, one launch (start us, length us, event | category | flops | bytes accessed | tf_op | source)
XLA Modules:
  0.0 237.3 jit_solution(12499040096194304600)
XLA Ops:
  0.1 11.6 %collective-permute-start = (bf16[2,512,32]{1,2,0:T(8,128)(2,1)}, bf16[2,512,32]{1,2,0:T(8,128)(2,1)S(1)}, u32[]{:S(2)}, u32[]{:S(2)}) collective-permute-start(bf16[2,512,32]{1,2,0:T(8,128)(2,1)} %param.43), channel_id=1, source_target_pairs={{0,448},{8,456},{16,464},{24,472},{32,480},{40,488},{48,496},{56,5... | collective-permute-start | bytes 196616 | tf_op jit(solution)/shard_map/ppermute | solution.py:141
  11.7 2.2 collective-permute-start.1
  13.9 1.9 collective-permute-start.2
  15.8 7.3 %collective-permute-start.3 = (bf16[2,512,32]{1,2,0:T(8,128)(2,1)}, bf16[2,512,32]{1,2,0:T(8,128)(2,1)S(1)}, u32[]{:S(2)}, u32[]{:S(2)}) collective-permute-start(bf16[2,512,32]{1,2,0:T(8,128)(2,1)} %param.43), channel_id=1, source_target_pairs={{0,256},{8,264},{16,272},{24,280},{32,288},{40,296},{48,304},{56,3... | collective-permute-start | bytes 196616 | tf_op jit(solution)/shard_map/ppermute | solution.py:141
  23.1 1.9 collective-permute-start.4
  25.0 0.9 bitcast_dynamic-update-slice_fusion.15
  25.9 0.8 reduce-window.4
  28.0 0.9 slice_convert_fusion.1
  30.3 0.8 slice_convert_fusion.3
  33.9 0.8 fusion.176
  39.3 0.7 compare_select_fusion.1
  42.0 0.9 fusion.16
  43.8 3.1 %collective-permute-start.5 = (bf16[2,512,32]{1,2,0:T(8,128)(2,1)S(1)}, bf16[2,512,32]{1,2,0:T(8,128)(2,1)S(1)}, u32[]{:S(2)}, u32[]{:S(2)}) collective-permute-start(bf16[2,512,32]{1,2,0:T(8,128)(2,1)S(1)} %copy-done.9), channel_id=1, source_target_pairs={{0,128},{8,136},{16,144},{24,152},{32,160},{40,168},{48,176},{56,1... | collective-permute-start | bytes 196616 | tf_op jit(solution)/shard_map/ppermute | solution.py:141
  46.9 3.3 %collective-permute-start.6 = (bf16[2,512,32]{1,2,0:T(8,128)(2,1)S(1)}, bf16[2,512,32]{1,2,0:T(8,128)(2,1)S(1)}, u32[]{:S(2)}, u32[]{:S(2)}) collective-permute-start(bf16[2,512,32]{1,2,0:T(8,128)(2,1)S(1)} %copy-done.9), channel_id=1, source_target_pairs={{0,64},{8,72},{16,80},{24,88},{32,96},{40,104},{48,112},{56,120},{... | collective-permute-start | bytes 196616 | tf_op jit(solution)/shard_map/ppermute | solution.py:141
  50.3 2.2 collective-permute-done.5
  52.5 2.0 collective-permute-done.6
  54.6 4.4 %collective-permute-start.7 = (bf16[8,2,512,32]{2,3,0,1:T(8,128)(2,1)S(1)}, bf16[8,2,512,32]{2,3,0,1:T(8,128)(2,1)S(1)}, u32[]{:S(2)}, u32[]{:S(2)}) collective-permute-start(bf16[8,2,512,32]{2,3,0,1:T(8,128)(2,1)S(1)} %bitcast_dynamic-update-slice_fusion.8), channel_id=1, source_target_pairs={{0,48},{8,56},{16,0},{24,8},{32,16},{40,24},{48,32},{56,40},{64,11... | collective-permute-start | bytes 1572872 | tf_op jit(solution)/shard_map/ppermute | solution.py:141
  59.0 2.4 %collective-permute-start.8 = (bf16[8,2,512,32]{2,3,0,1:T(8,128)(2,1)S(1)}, bf16[8,2,512,32]{2,3,0,1:T(8,128)(2,1)S(1)}, u32[]{:S(2)}, u32[]{:S(2)}) collective-permute-start(bf16[8,2,512,32]{2,3,0,1:T(8,128)(2,1)S(1)} %bitcast_dynamic-update-slice_fusion.8), channel_id=1, source_target_pairs={{0,32},{8,40},{16,48},{24,56},{32,0},{40,8},{48,16},{56,24},{64,96... | collective-permute-start | bytes 1572872 | tf_op jit(solution)/shard_map/ppermute | solution.py:141
  61.5 2.5 %collective-permute-start.9 = (bf16[8,2,512,32]{2,3,0,1:T(8,128)(2,1)S(1)}, bf16[8,2,512,32]{2,3,0,1:T(8,128)(2,1)S(1)}, u32[]{:S(2)}, u32[]{:S(2)}) collective-permute-start(bf16[8,2,512,32]{2,3,0,1:T(8,128)(2,1)S(1)} %bitcast_dynamic-update-slice_fusion.8), channel_id=1, source_target_pairs={{0,16},{8,24},{16,32},{24,40},{32,48},{40,56},{48,0},{56,8},{64,80... | collective-permute-start | bytes 1572872 | tf_op jit(solution)/shard_map/ppermute | solution.py:141
  64.0 2.0 fusion.10
  66.3 1.3 divide_multiply_fusion.1
  67.6 1.3 fusion.12
  69.0 4.5 %collective-permute-done.8 = bf16[8,2,512,32]{2,3,0,1:T(8,128)(2,1)S(1)} collective-permute-done((bf16[8,2,512,32]{2,3,0,1:T(8,128)(2,1)S(1)}, bf16[8,2,512,32]{2,3,0,1:T(8,128)(2,1)S(1)}, u32[]{:S(2)}, u32[]{:S(2)}) %collective-permute-start.8) | collective-permute-done | bytes 524320 | tf_op jit(solution)/shard_map/ppermute | solution.py:141
  73.5 14.0 %collective-permute-done.9 = bf16[8,2,512,32]{2,3,0,1:T(8,128)(2,1)S(1)} collective-permute-done((bf16[8,2,512,32]{2,3,0,1:T(8,128)(2,1)S(1)}, bf16[8,2,512,32]{2,3,0,1:T(8,128)(2,1)S(1)}, u32[]{:S(2)}, u32[]{:S(2)}) %collective-permute-start.9) | collective-permute-done | bytes 524320 | tf_op jit(solution)/shard_map/ppermute | solution.py:141
  87.5 0.8 copy-done.3
  88.3 2.9 %fusion.175 = (bf16[1,4,8,2,512,32]{4,5,0,1,2,3:T(8,128)(2,1)S(1)}, bf16[4,8,2,512,32]{3,4,0,1,2:T(8,128)(2,1)}) fusion(bf16[1,8,2,512,32]{3,4,0,1,2:T(8,128)(2,1)} %bitcast.379, bf16[1,8,2,512,32]{3,4,0,1,2:T(8,128)(2,1)} %bitcast.378, bf16[1,8,2,512,32]{3,4,0,1,2:T(8,128)(2,1)S(1)} %bitcast.377, bf16[1,8,2,512,32]{3,4,0,1,2:T(8,128)(2,1)S(1)} %bitcast.376), kind=kLoop, calls=%fused_computation.339 | loop fusion | flops 3145728 | bytes 6291456 | tf_op jit(solution)/shard_map/stack | solution.py:135
  91.2 2.5 %collective-permute-start.10 = (bf16[4,8,2,512,32]{3,4,0,1,2:T(8,128)(2,1)}, bf16[4,8,2,512,32]{3,4,0,1,2:T(8,128)(2,1)}, u32[]{:S(2)}, u32[]{:S(2)}) collective-permute-start(bf16[4,8,2,512,32]{3,4,0,1,2:T(8,128)(2,1)} %get-tuple-element.65), channel_id=1, source_target_pairs={{0,8},{8,0},{16,24},{24,16},{32,40},{40,32},{48,56},{56,48},{64,72... | collective-permute-start | bytes 6291464 | tf_op jit(solution)/shard_map/ppermute | solution.py:130
  94.3 0.9 fusion.137
  95.2 1.2 divide_multiply_fusion.3
  96.4 2.0 fusion.9
  101.0 2.0 maximum_bitcast_fusion
  103.0 1.6 fusion.2
  104.6 1.6 fusion.1
  106.2 1.6 fusion
  107.8 1.4 convolution_convert_fusion
  109.2 0.9 copy.255
  110.1 6.8 %all-to-all-start = ((bf16[2,8,8,2432]{3,2,0,1:T(8,128)(2,1)}), bf16[2,8,8,2432]{3,2,0,1:T(8,128)(2,1)S(1)}, u32[]{:S(2)}, u32[]{:S(2)}) async-start(bf16[2,8,8,2432]{3,2,0,1:T(8,128)(2,1)} %copy.255), calls=%async_computation | async-start | bytes 1245184 | tf_op jit(solution)/shard_map/all_to_all | solution.py:254
  116.9 2.4 %collective-permute-start.21 = (bf16[2,400,2048]{2,1,0:T(8,128)(2,1)}, bf16[2,400,2048]{2,1,0:T(8,128)(2,1)}, u32[]{:S(2)}, u32[]{:S(2)}) collective-permute-start(bf16[2,400,2048]{2,1,0:T(8,128)(2,1)} %param.44), channel_id=1, source_target_pairs={{0,8},{8,0},{16,24},{24,16},{32,40},{40,32},{48,56},{56,48},{64,72... | collective-permute-start | bytes 9830408 | tf_op jit(solution)/shard_map/ppermute | solution.py:199
  119.9 0.7 and_reduce_fusion
  120.6 0.8 fusion.163
  121.4 1.3 broadcast_select_fusion
  122.7 0.8 scatter.19
  123.6 13.5 %all-to-all-done = bf16[2,8,8,2432]{3,2,0,1:T(8,128)(2,1)S(1)} async-done(((bf16[2,8,8,2432]{3,2,0,1:T(8,128)(2,1)}), bf16[2,8,8,2432]{3,2,0,1:T(8,128)(2,1)S(1)}, u32[]{:S(2)}, u32[]{:S(2)}) %all-to-all-start) | async-done | bytes 622624 | tf_op jit(solution)/shard_map/all_to_all | solution.py:254
  138.3 3.1 %collective-permute-start.11 = (bf16[17,2048]{1,0:T(8,128)(2,1)S(1)}, bf16[17,2048]{1,0:T(8,128)(2,1)S(1)}, u32[]{:S(2)}, u32[]{:S(2)}) collective-permute-start(bf16[17,2048]{1,0:T(8,128)(2,1)S(1)} %pad_maximum_fusion.4), channel_id=1, source_target_pairs={{0,448},{8,456},{16,464},{24,472},{32,480},{40,488},{48,496},{56,5... | collective-permute-start | bytes 208904 | tf_op jit(solution)/shard_map/ppermute | solution.py:141
  141.4 3.0 %collective-permute-start.12 = (bf16[17,2048]{1,0:T(8,128)(2,1)S(1)}, bf16[17,2048]{1,0:T(8,128)(2,1)S(1)}, u32[]{:S(2)}, u32[]{:S(2)}) collective-permute-start(bf16[17,2048]{1,0:T(8,128)(2,1)S(1)} %pad_maximum_fusion.4), channel_id=1, source_target_pairs={{0,384},{8,392},{16,400},{24,408},{32,416},{40,424},{48,432},{56,4... | collective-permute-start | bytes 208904 | tf_op jit(solution)/shard_map/ppermute | solution.py:141
  144.4 4.0 %collective-permute-start.13 = (bf16[17,2048]{1,0:T(8,128)(2,1)S(1)}, bf16[17,2048]{1,0:T(8,128)(2,1)S(1)}, u32[]{:S(2)}, u32[]{:S(2)}) collective-permute-start(bf16[17,2048]{1,0:T(8,128)(2,1)S(1)} %pad_maximum_fusion.4), channel_id=1, source_target_pairs={{0,320},{8,328},{16,336},{24,344},{32,352},{40,360},{48,368},{56,3... | collective-permute-start | bytes 208904 | tf_op jit(solution)/shard_map/ppermute | solution.py:141
  148.4 4.2 %collective-permute-start.14 = (bf16[17,2048]{1,0:T(8,128)(2,1)S(1)}, bf16[17,2048]{1,0:T(8,128)(2,1)S(1)}, u32[]{:S(2)}, u32[]{:S(2)}) collective-permute-start(bf16[17,2048]{1,0:T(8,128)(2,1)S(1)} %pad_maximum_fusion.4), channel_id=1, source_target_pairs={{0,256},{8,264},{16,272},{24,280},{32,288},{40,296},{48,304},{56,3... | collective-permute-start | bytes 208904 | tf_op jit(solution)/shard_map/ppermute | solution.py:141
  152.7 2.8 %collective-permute-start.15 = (bf16[17,2048]{1,0:T(8,128)(2,1)S(1)}, bf16[17,2048]{1,0:T(8,128)(2,1)S(1)}, u32[]{:S(2)}, u32[]{:S(2)}) collective-permute-start(bf16[17,2048]{1,0:T(8,128)(2,1)S(1)} %pad_maximum_fusion.4), channel_id=1, source_target_pairs={{0,192},{8,200},{16,208},{24,216},{32,224},{40,232},{48,240},{56,2... | collective-permute-start | bytes 208904 | tf_op jit(solution)/shard_map/ppermute | solution.py:141
  155.6 5.4 %collective-permute-start.16 = (bf16[17,2048]{1,0:T(8,128)(2,1)S(1)}, bf16[17,2048]{1,0:T(8,128)(2,1)S(1)}, u32[]{:S(2)}, u32[]{:S(2)}) collective-permute-start(bf16[17,2048]{1,0:T(8,128)(2,1)S(1)} %pad_maximum_fusion.4), channel_id=1, source_target_pairs={{0,128},{8,136},{16,144},{24,152},{32,160},{40,168},{48,176},{56,1... | collective-permute-start | bytes 208904 | tf_op jit(solution)/shard_map/ppermute | solution.py:141
  161.0 3.2 %collective-permute-start.17 = (bf16[17,2048]{1,0:T(8,128)(2,1)S(1)}, bf16[17,2048]{1,0:T(8,128)(2,1)S(1)}, u32[]{:S(2)}, u32[]{:S(2)}) collective-permute-start(bf16[17,2048]{1,0:T(8,128)(2,1)S(1)} %pad_maximum_fusion.4), channel_id=1, source_target_pairs={{0,64},{8,72},{16,80},{24,88},{32,96},{40,104},{48,112},{56,120},{... | collective-permute-start | bytes 208904 | tf_op jit(solution)/shard_map/ppermute | solution.py:141
  164.2 3.0 %collective-permute-done.15 = bf16[17,2048]{1,0:T(8,128)(2,1)S(1)} collective-permute-done((bf16[17,2048]{1,0:T(8,128)(2,1)S(1)}, bf16[17,2048]{1,0:T(8,128)(2,1)S(1)}, u32[]{:S(2)}, u32[]{:S(2)}) %collective-permute-start.15) | collective-permute-done | bytes 69664 | tf_op jit(solution)/shard_map/ppermute | solution.py:141
  167.2 2.2 collective-permute-done.16
  169.4 4.3 %collective-permute-done.17 = bf16[17,2048]{1,0:T(8,128)(2,1)S(1)} collective-permute-done((bf16[17,2048]{1,0:T(8,128)(2,1)S(1)}, bf16[17,2048]{1,0:T(8,128)(2,1)S(1)}, u32[]{:S(2)}, u32[]{:S(2)}) %collective-permute-start.17) | collective-permute-done | bytes 69664 | tf_op jit(solution)/shard_map/ppermute | solution.py:141
  174.1 1.9 collective-permute-start.20
  176.0 3.4 %collective-permute-start.19 = (bf16[8,17,2048]{2,0,1:T(8,128)(2,1)S(1)}, bf16[8,17,2048]{2,0,1:T(8,128)(2,1)S(1)}, u32[]{:S(2)}, u32[]{:S(2)}) collective-permute-start(bf16[8,17,2048]{2,0,1:T(8,128)(2,1)S(1)} %copy.257), channel_id=1, source_target_pairs={{0,32},{8,40},{16,48},{24,56},{32,0},{40,8},{48,16},{56,24},{64,96... | collective-permute-start | bytes 1671176 | tf_op jit(solution)/shard_map/ppermute | solution.py:141
  179.4 3.1 %collective-permute-start.18 = (bf16[8,17,2048]{2,0,1:T(8,128)(2,1)S(1)}, bf16[8,17,2048]{2,0,1:T(8,128)(2,1)S(1)}, u32[]{:S(2)}, u32[]{:S(2)}) collective-permute-start(bf16[8,17,2048]{2,0,1:T(8,128)(2,1)S(1)} %copy.257), channel_id=1, source_target_pairs={{0,48},{8,56},{16,0},{24,8},{32,16},{40,24},{48,32},{56,40},{64,11... | collective-permute-start | bytes 1671176 | tf_op jit(solution)/shard_map/ppermute | solution.py:141
  182.5 20.4 %collective-permute-done.20 = bf16[8,17,2048]{2,0,1:T(8,128)(2,1)S(1)} collective-permute-done((bf16[8,17,2048]{2,0,1:T(8,128)(2,1)S(1)}, bf16[8,17,2048]{2,0,1:T(8,128)(2,1)S(1)}, u32[]{:S(2)}, u32[]{:S(2)}) %collective-permute-start.20) | collective-permute-done | bytes 557088 | tf_op jit(solution)/shard_map/ppermute | solution.py:141
  203.6 1.6 collective-permute-done.18
  206.1 1.7 copy-done
  208.3 3.8 %fusion.184 = (f32[2,256]{1,0:T(2,128)S(1)}, f32[2,256,400]{1,2,0:T(8,128)S(1)}) fusion(bf16[2,400,2048]{2,1,0:T(8,128)(2,1)} %param.44, bf16[32,17,2048]{2,1,0:T(8,128)(2,1)} %bitcast.363), kind=kOutput, calls=%fused_computation.348 | convolution fusion | flops 839065088 | bytes 6195200 | tf_op jit(solution)/shard_map/mnd,mvd->mnv/dot_general | solution.py:115
  212.1 3.1 %fusion.185 = (f32[2,256]{1,0:T(2,128)S(1)}, f32[2,256,400]{1,2,0:T(8,128)S(1)}) fusion(bf16[2,400,2048]{2,1,0:T(8,128)(2,1)} %collective-permute-done.21, bf16[32,17,2048]{2,1,0:T(8,128)(2,1)S(1)} %bitcast.364), kind=kOutput, calls=%fused_computation.349 | convolution fusion | flops 839065088 | bytes 6195200 | tf_op jit(solution)/shard_map/mnd,mvd->mnv/dot_general | solution.py:115
  216.3 0.8 copy.265
  217.1 7.4 %all-to-all-start.1 = ((f32[3,2,64,8]{3,1,0,2:T(2,128)}), f32[3,2,64,8]{3,1,0,2:T(2,128)S(1)}, u32[]{:S(2)}, u32[]{:S(2)}) async-start(f32[3,2,64,8]{3,1,0,2:T(2,128)} %copy.265), calls=%async_computation.1 | async-start | bytes 393216 | tf_op jit(solution)/shard_map/all_to_all | solution.py:325
  224.6 11.9 %all-to-all-done.1 = f32[3,2,64,8]{3,1,0,2:T(2,128)S(1)} async-done(((f32[3,2,64,8]{3,1,0,2:T(2,128)}), f32[3,2,64,8]{3,1,0,2:T(2,128)S(1)}, u32[]{:S(2)}, u32[]{:S(2)}) %all-to-all-start.1) | async-done | bytes 12320 | tf_op jit(solution)/shard_map/all_to_all | solution.py:325
  (220 shorter events, 22.1 us)
Async XLA Ops:
  0.0 42.9 %copy-start.4 = (bf16[2,64,512]{2,1,0:T(8,128)(2,1)S(1)}, bf16[2,64,512]{2,1,0:T(8,128)(2,1)}, u32[]{:S(2)}) copy-start(bf16[2,64,512]{2,1,0:T(8,128)(2,1)} %param.32) | copy-start | bytes 393220
  0.0 38.4 %copy-start.7 = (bf16[2,64,256]{2,1,0:T(8,128)(2,1)S(1)}, bf16[2,64,256]{2,1,0:T(8,128)(2,1)}, u32[]{:S(2)}) copy-start(bf16[2,64,256]{2,1,0:T(8,128)(2,1)} %param.33) | copy-start | bytes 196612
  0.0 36.0 %copy-start.14 = (f32[2,4,512]{2,1,0:T(4,128)S(1)}, f32[2,4,512]{2,1,0:T(4,128)}, u32[]{:S(2)}) copy-start(f32[2,4,512]{2,1,0:T(4,128)} %param.36) | copy-start | bytes 49156
  0.0 36.7 %copy-start.12 = (bf16[2,3,3,256]{3,0,2,1:T(2,128)(2,1)S(1)}, bf16[2,3,3,256]{3,0,2,1:T(2,128)(2,1)}, u32[]{:S(2)}) copy-start(bf16[2,3,3,256]{3,0,2,1:T(2,128)(2,1)} %param.46) | copy-start | bytes 27652
  0.0 37.8 %copy-start.19 = (f32[2,4,256]{2,1,0:T(4,128)S(1)}, f32[2,4,256]{2,1,0:T(4,128)}, u32[]{:S(2)}) copy-start(f32[2,4,256]{2,1,0:T(4,128)} %param.37) | copy-start | bytes 24580
  0.0 38.9 %copy-start.27 = (f32[2,8]{1,0:T(2,128)S(1)}, f32[2,8]{1,0:T(2,128)}, u32[]{:S(2)}) copy-start(f32[2,8]{1,0:T(2,128)} %param.38) | copy-start | bytes 196
  0.0 38.9 %copy-start.26 = (f32[2,8]{1,0:T(2,128)S(1)}, f32[2,8]{1,0:T(2,128)}, u32[]{:S(2)}) copy-start(f32[2,8]{1,0:T(2,128)} %param.39) | copy-start | bytes 196
  0.0 38.9 %copy-start.15 = (bf16[2,64,8]{1,2,0:T(8,128)(2,1)S(1)}, bf16[2,64,8]{1,2,0:T(8,128)(2,1)}, u32[]{:S(2)}) copy-start(bf16[2,64,8]{1,2,0:T(8,128)(2,1)} %param.34) | copy-start | bytes 6148
  0.1 43.7 %collective-permute-start = (bf16[2,512,32]{1,2,0:T(8,128)(2,1)}, bf16[2,512,32]{1,2,0:T(8,128)(2,1)S(1)}, u32[]{:S(2)}, u32[]{:S(2)}) collective-permute-start(bf16[2,512,32]{1,2,0:T(8,128)(2,1)} %param.43), channel_id=1, source_target_pairs={{0,448},{8,456},{16,464},{24,472},{32,480},{40,488},{48,496},{56,5... | collective-permute-start | bytes 196616 | tf_op jit(solution)/shard_map/ppermute | solution.py:141
  11.7 35.2 %collective-permute-start.1 = (bf16[2,512,32]{1,2,0:T(8,128)(2,1)}, bf16[2,512,32]{1,2,0:T(8,128)(2,1)S(1)}, u32[]{:S(2)}, u32[]{:S(2)}) collective-permute-start(bf16[2,512,32]{1,2,0:T(8,128)(2,1)} %param.43), channel_id=1, source_target_pairs={{0,384},{8,392},{16,400},{24,408},{32,416},{40,424},{48,432},{56,4... | collective-permute-start | bytes 196616 | tf_op jit(solution)/shard_map/ppermute | solution.py:141
  13.9 36.4 %collective-permute-start.2 = (bf16[2,512,32]{1,2,0:T(8,128)(2,1)}, bf16[2,512,32]{1,2,0:T(8,128)(2,1)S(1)}, u32[]{:S(2)}, u32[]{:S(2)}) collective-permute-start(bf16[2,512,32]{1,2,0:T(8,128)(2,1)} %param.43), channel_id=1, source_target_pairs={{0,320},{8,328},{16,336},{24,344},{32,352},{40,360},{48,368},{56,3... | collective-permute-start | bytes 196616 | tf_op jit(solution)/shard_map/ppermute | solution.py:141
  15.8 34.5 %collective-permute-start.3 = (bf16[2,512,32]{1,2,0:T(8,128)(2,1)}, bf16[2,512,32]{1,2,0:T(8,128)(2,1)S(1)}, u32[]{:S(2)}, u32[]{:S(2)}) collective-permute-start(bf16[2,512,32]{1,2,0:T(8,128)(2,1)} %param.43), channel_id=1, source_target_pairs={{0,256},{8,264},{16,272},{24,280},{32,288},{40,296},{48,304},{56,3... | collective-permute-start | bytes 196616 | tf_op jit(solution)/shard_map/ppermute | solution.py:141
  23.1 27.2 %collective-permute-start.4 = (bf16[2,512,32]{1,2,0:T(8,128)(2,1)}, bf16[2,512,32]{1,2,0:T(8,128)(2,1)S(1)}, u32[]{:S(2)}, u32[]{:S(2)}) collective-permute-start(bf16[2,512,32]{1,2,0:T(8,128)(2,1)} %param.43), channel_id=1, source_target_pairs={{0,192},{8,200},{16,208},{24,216},{32,224},{40,232},{48,240},{56,2... | collective-permute-start | bytes 196616 | tf_op jit(solution)/shard_map/ppermute | solution.py:141
  27.4 15.8 %copy-start.28 = (pred[3]{0:T(512)(128)(4,1)}, pred[3]{0:T(512)(128)(4,1)S(1)}, u32[]{:S(2)}) copy-start(pred[3]{0:T(512)(128)(4,1)S(1)} %get-tuple-element.62) | copy-start | bytes 13
  29.6 13.6 %copy-start.25 = (f32[2,8]{1,0:T(2,128)S(1)}, f32[2,8]{1,0:T(2,128)}, u32[]{:S(2)}) copy-start(f32[2,8]{1,0:T(2,128)} %param.40) | copy-start | bytes 196
  29.6 14.2 %copy-start.9 = (bf16[2,512,32]{1,2,0:T(8,128)(2,1)S(1)}, bf16[2,512,32]{1,2,0:T(8,128)(2,1)}, u32[]{:S(2)}) copy-start(bf16[2,512,32]{1,2,0:T(8,128)(2,1)} %param.43) | copy-start | bytes 196612
  33.1 21.4 %copy-start.10 = (s32[64]{0:T(128)}, s32[64]{0:T(128)S(1)}, u32[]{:S(2)}) copy-start(s32[64]{0:T(128)S(1)} %fusion.143) | copy-start | bytes 772
  33.1 32.9 %copy-start.22 = (f32[64,3]{0,1:T(4,128)}, f32[64,3]{0,1:T(4,128)S(1)}, u32[]{:S(2)}) copy-start(f32[64,3]{0,1:T(4,128)S(1)} %fusion.142) | copy-start | bytes 2308
  33.9 32.1 %copy-start.43 = (f32[3]{0:T(128)}, f32[3]{0:T(128)S(1)}, u32[]{:S(2)}) copy-start(f32[3]{0:T(128)S(1)} %get-tuple-element.121) | copy-start | bytes 40
  36.0 18.5 %copy-start.30 = (pred[64]{0:T(512)(128)(4,1)}, pred[64]{0:T(512)(128)(4,1)S(1)}, u32[]{:S(2)}) copy-start(pred[64]{0:T(512)(128)(4,1)S(1)} %get-tuple-element.123) | copy-start | bytes 196
  36.0 18.5 %copy-start.31 = (pred[64]{0:T(512)(128)(4,1)}, pred[64]{0:T(512)(128)(4,1)S(1)}, u32[]{:S(2)}) copy-start(pred[64]{0:T(512)(128)(4,1)S(1)} %get-tuple-element.124) | copy-start | bytes 196
  36.0 18.5 %copy-start.32 = (pred[64]{0:T(512)(128)(4,1)}, pred[64]{0:T(512)(128)(4,1)S(1)}, u32[]{:S(2)}) copy-start(pred[64]{0:T(512)(128)(4,1)S(1)} %get-tuple-element.125) | copy-start | bytes 196
  36.0 18.5 %copy-start.33 = (pred[64]{0:T(512)(128)(4,1)}, pred[64]{0:T(512)(128)(4,1)S(1)}, u32[]{:S(2)}) copy-start(pred[64]{0:T(512)(128)(4,1)S(1)} %get-tuple-element.126) | copy-start | bytes 196
  36.0 18.5 %copy-start.34 = (pred[64]{0:T(512)(128)(4,1)}, pred[64]{0:T(512)(128)(4,1)S(1)}, u32[]{:S(2)}) copy-start(pred[64]{0:T(512)(128)(4,1)S(1)} %get-tuple-element.127) | copy-start | bytes 196
  36.0 18.5 %copy-start.35 = (pred[64]{0:T(512)(128)(4,1)}, pred[64]{0:T(512)(128)(4,1)S(1)}, u32[]{:S(2)}) copy-start(pred[64]{0:T(512)(128)(4,1)S(1)} %get-tuple-element.128) | copy-start | bytes 196
  36.0 18.5 %copy-start.36 = (pred[64]{0:T(512)(128)(4,1)}, pred[64]{0:T(512)(128)(4,1)S(1)}, u32[]{:S(2)}) copy-start(pred[64]{0:T(512)(128)(4,1)S(1)} %get-tuple-element.129) | copy-start | bytes 196
  36.0 18.5 %copy-start.37 = (pred[64]{0:T(512)(128)(4,1)}, pred[64]{0:T(512)(128)(4,1)S(1)}, u32[]{:S(2)}) copy-start(pred[64]{0:T(512)(128)(4,1)S(1)} %get-tuple-element.130) | copy-start | bytes 196
  36.1 18.5 %copy-start.38 = (pred[64]{0:T(512)(128)(4,1)}, pred[64]{0:T(512)(128)(4,1)S(1)}, u32[]{:S(2)}) copy-start(pred[64]{0:T(512)(128)(4,1)S(1)} %get-tuple-element.131) | copy-start | bytes 196
  36.1 18.5 %copy-start.39 = (pred[64]{0:T(512)(128)(4,1)}, pred[64]{0:T(512)(128)(4,1)S(1)}, u32[]{:S(2)}) copy-start(pred[64]{0:T(512)(128)(4,1)S(1)} %get-tuple-element.132) | copy-start | bytes 196
  36.1 18.5 %copy-start.40 = (pred[64]{0:T(512)(128)(4,1)}, pred[64]{0:T(512)(128)(4,1)S(1)}, u32[]{:S(2)}) copy-start(pred[64]{0:T(512)(128)(4,1)S(1)} %get-tuple-element.133) | copy-start | bytes 196
  36.1 18.5 %copy-start.41 = (pred[64]{0:T(512)(128)(4,1)}, pred[64]{0:T(512)(128)(4,1)S(1)}, u32[]{:S(2)}) copy-start(pred[64]{0:T(512)(128)(4,1)S(1)} %get-tuple-element.134) | copy-start | bytes 196
  41.0 18.0 %copy-start.20 = (s32[1024]{0:T(1024)}, s32[1024]{0:T(1024)S(1)}, u32[]{:S(2)}) copy-start(s32[1024]{0:T(1024)S(1)} %pad_clamp_fusion) | copy-start | bytes 12292
  43.8 8.7 %collective-permute-start.5 = (bf16[2,512,32]{1,2,0:T(8,128)(2,1)S(1)}, bf16[2,512,32]{1,2,0:T(8,128)(2,1)S(1)}, u32[]{:S(2)}, u32[]{:S(2)}) collective-permute-start(bf16[2,512,32]{1,2,0:T(8,128)(2,1)S(1)} %copy-done.9), channel_id=1, source_target_pairs={{0,128},{8,136},{16,144},{24,152},{32,160},{40,168},{48,176},{56,1... | collective-permute-start | bytes 196616 | tf_op jit(solution)/shard_map/ppermute | solution.py:141
  46.9 7.6 %collective-permute-start.6 = (bf16[2,512,32]{1,2,0:T(8,128)(2,1)S(1)}, bf16[2,512,32]{1,2,0:T(8,128)(2,1)S(1)}, u32[]{:S(2)}, u32[]{:S(2)}) collective-permute-start(bf16[2,512,32]{1,2,0:T(8,128)(2,1)S(1)} %copy-done.9), channel_id=1, source_target_pairs={{0,64},{8,72},{16,80},{24,88},{32,96},{40,104},{48,112},{56,120},{... | collective-permute-start | bytes 196616 | tf_op jit(solution)/shard_map/ppermute | solution.py:141
  54.6 14.4 %collective-permute-start.7 = (bf16[8,2,512,32]{2,3,0,1:T(8,128)(2,1)S(1)}, bf16[8,2,512,32]{2,3,0,1:T(8,128)(2,1)S(1)}, u32[]{:S(2)}, u32[]{:S(2)}) collective-permute-start(bf16[8,2,512,32]{2,3,0,1:T(8,128)(2,1)S(1)} %bitcast_dynamic-update-slice_fusion.8), channel_id=1, source_target_pairs={{0,48},{8,56},{16,0},{24,8},{32,16},{40,24},{48,32},{56,40},{64,11... | collective-permute-start | bytes 1572872 | tf_op jit(solution)/shard_map/ppermute | solution.py:141
  59.0 14.5 %collective-permute-start.8 = (bf16[8,2,512,32]{2,3,0,1:T(8,128)(2,1)S(1)}, bf16[8,2,512,32]{2,3,0,1:T(8,128)(2,1)S(1)}, u32[]{:S(2)}, u32[]{:S(2)}) collective-permute-start(bf16[8,2,512,32]{2,3,0,1:T(8,128)(2,1)S(1)} %bitcast_dynamic-update-slice_fusion.8), channel_id=1, source_target_pairs={{0,32},{8,40},{16,48},{24,56},{32,0},{40,8},{48,16},{56,24},{64,96... | collective-permute-start | bytes 1572872 | tf_op jit(solution)/shard_map/ppermute | solution.py:141
  61.5 26.0 %collective-permute-start.9 = (bf16[8,2,512,32]{2,3,0,1:T(8,128)(2,1)S(1)}, bf16[8,2,512,32]{2,3,0,1:T(8,128)(2,1)S(1)}, u32[]{:S(2)}, u32[]{:S(2)}) collective-permute-start(bf16[8,2,512,32]{2,3,0,1:T(8,128)(2,1)S(1)} %bitcast_dynamic-update-slice_fusion.8), channel_id=1, source_target_pairs={{0,16},{8,24},{16,32},{24,40},{32,48},{40,56},{48,0},{56,8},{64,80... | collective-permute-start | bytes 1572872 | tf_op jit(solution)/shard_map/ppermute | solution.py:141
  73.5 14.0 %copy-start.2 = (bf16[8,2,512,32]{2,3,0,1:T(8,128)(2,1)}, bf16[8,2,512,32]{2,3,0,1:T(8,128)(2,1)S(1)}, u32[]{:S(2)}) copy-start(bf16[8,2,512,32]{2,3,0,1:T(8,128)(2,1)S(1)} %collective-permute-done.8) | copy-start | bytes 1572868
  88.3 5.4 %copy-start.11 = (s32[64]{0:T(128)S(1)}, s32[64]{0:T(128)}, u32[]{:S(2)}) copy-start(s32[64]{0:T(128)} %copy-done.10) | copy-start | bytes 772
  88.3 5.4 %copy-start.18 = (bf16[3,1,256]{2,1,0:T(2,128)(2,1)S(1)}, bf16[3,1,256]{2,1,0:T(2,128)(2,1)}, u32[]{:S(2)}) copy-start(bf16[3,1,256]{2,1,0:T(2,128)(2,1)} %get-tuple-element.101) | copy-start | bytes 4612
  91.2 7.4 %copy-start.16 = (f32[64,8]{0,1:T(8,128)S(1)}, f32[64,8]{0,1:T(8,128)}, u32[]{:S(2)}) copy-start(f32[64,8]{0,1:T(8,128)} %get-tuple-element.107) | copy-start | bytes 6148
  91.2 8.2 %copy-start.29 = (pred[3]{0:T(512)(128)(4,1)S(1)}, pred[3]{0:T(512)(128)(4,1)}, u32[]{:S(2)}) copy-start(pred[3]{0:T(512)(128)(4,1)} %copy-done.28) | copy-start | bytes 13
  91.2 8.6 %copy-start.13 = (f32[64,8]{0,1:T(8,128)S(1)}, f32[64,8]{0,1:T(8,128)}, u32[]{:S(2)}) copy-start(f32[64,8]{0,1:T(8,128)} %get-tuple-element.106) | copy-start | bytes 6148
  91.2 8.6 %copy-start.24 = (f32[8]{0:T(128)S(1)}, f32[8]{0:T(128)}, u32[]{:S(2)}) copy-start(f32[8]{0:T(128)} %get-tuple-element.115) | copy-start | bytes 100
  91.2 9.4 %copy-start.5 = (bf16[2,64,512]{2,1,0:T(8,128)(2,1)S(1)}, bf16[2,64,512]{2,1,0:T(8,128)(2,1)}, u32[]{:S(2)}) copy-start(bf16[2,64,512]{2,1,0:T(8,128)(2,1)} %param.31) | copy-start | bytes 393220
  91.2 9.8 %collective-permute-start.10 = (bf16[4,8,2,512,32]{3,4,0,1,2:T(8,128)(2,1)}, bf16[4,8,2,512,32]{3,4,0,1,2:T(8,128)(2,1)}, u32[]{:S(2)}, u32[]{:S(2)}) collective-permute-start(bf16[4,8,2,512,32]{3,4,0,1,2:T(8,128)(2,1)} %get-tuple-element.65), channel_id=1, source_target_pairs={{0,8},{8,0},{16,24},{24,16},{32,40},{40,32},{48,56},{56,48},{64,72... | collective-permute-start | bytes 6291464 | tf_op jit(solution)/shard_map/ppermute | solution.py:130
  107.8 12.9 %copy-start.23 = (s32[64]{0:T(128)S(1)}, s32[64]{0:T(128)}, u32[]{:S(2)}) copy-start(s32[64]{0:T(128)} %param.50) | copy-start | bytes 772
  109.2 28.9 %copy-start.17 = (f32[2,2048]{1,0:T(2,128)S(1)}, f32[2,2048]{1,0:T(2,128)}, u32[]{:S(2)}) copy-start(f32[2,2048]{1,0:T(2,128)} %param.42) | copy-start | bytes 49156
  110.1 27.0 %all-to-all-start = ((bf16[2,8,8,2432]{3,2,0,1:T(8,128)(2,1)}), bf16[2,8,8,2432]{3,2,0,1:T(8,128)(2,1)S(1)}, u32[]{:S(2)}, u32[]{:S(2)}) async-start(bf16[2,8,8,2432]{3,2,0,1:T(8,128)(2,1)} %copy.255), calls=%async_computation | async-start | bytes 1245184 | tf_op jit(solution)/shard_map/all_to_all | solution.py:254
  116.9 95.1 %collective-permute-start.21 = (bf16[2,400,2048]{2,1,0:T(8,128)(2,1)}, bf16[2,400,2048]{2,1,0:T(8,128)(2,1)}, u32[]{:S(2)}, u32[]{:S(2)}) collective-permute-start(bf16[2,400,2048]{2,1,0:T(8,128)(2,1)} %param.44), channel_id=1, source_target_pairs={{0,8},{8,0},{16,24},{24,16},{32,40},{40,32},{48,56},{56,48},{64,72... | collective-permute-start | bytes 9830408 | tf_op jit(solution)/shard_map/ppermute | solution.py:199
  138.3 14.4 %collective-permute-start.11 = (bf16[17,2048]{1,0:T(8,128)(2,1)S(1)}, bf16[17,2048]{1,0:T(8,128)(2,1)S(1)}, u32[]{:S(2)}, u32[]{:S(2)}) collective-permute-start(bf16[17,2048]{1,0:T(8,128)(2,1)S(1)} %pad_maximum_fusion.4), channel_id=1, source_target_pairs={{0,448},{8,456},{16,464},{24,472},{32,480},{40,488},{48,496},{56,5... | collective-permute-start | bytes 208904 | tf_op jit(solution)/shard_map/ppermute | solution.py:141
  141.4 14.2 %collective-permute-start.12 = (bf16[17,2048]{1,0:T(8,128)(2,1)S(1)}, bf16[17,2048]{1,0:T(8,128)(2,1)S(1)}, u32[]{:S(2)}, u32[]{:S(2)}) collective-permute-start(bf16[17,2048]{1,0:T(8,128)(2,1)S(1)} %pad_maximum_fusion.4), channel_id=1, source_target_pairs={{0,384},{8,392},{16,400},{24,408},{32,416},{40,424},{48,432},{56,4... | collective-permute-start | bytes 208904 | tf_op jit(solution)/shard_map/ppermute | solution.py:141
  144.4 16.6 %collective-permute-start.13 = (bf16[17,2048]{1,0:T(8,128)(2,1)S(1)}, bf16[17,2048]{1,0:T(8,128)(2,1)S(1)}, u32[]{:S(2)}, u32[]{:S(2)}) collective-permute-start(bf16[17,2048]{1,0:T(8,128)(2,1)S(1)} %pad_maximum_fusion.4), channel_id=1, source_target_pairs={{0,320},{8,328},{16,336},{24,344},{32,352},{40,360},{48,368},{56,3... | collective-permute-start | bytes 208904 | tf_op jit(solution)/shard_map/ppermute | solution.py:141
  148.4 15.8 %collective-permute-start.14 = (bf16[17,2048]{1,0:T(8,128)(2,1)S(1)}, bf16[17,2048]{1,0:T(8,128)(2,1)S(1)}, u32[]{:S(2)}, u32[]{:S(2)}) collective-permute-start(bf16[17,2048]{1,0:T(8,128)(2,1)S(1)} %pad_maximum_fusion.4), channel_id=1, source_target_pairs={{0,256},{8,264},{16,272},{24,280},{32,288},{40,296},{48,304},{56,3... | collective-permute-start | bytes 208904 | tf_op jit(solution)/shard_map/ppermute | solution.py:141
  152.7 14.5 %collective-permute-start.15 = (bf16[17,2048]{1,0:T(8,128)(2,1)S(1)}, bf16[17,2048]{1,0:T(8,128)(2,1)S(1)}, u32[]{:S(2)}, u32[]{:S(2)}) collective-permute-start(bf16[17,2048]{1,0:T(8,128)(2,1)S(1)} %pad_maximum_fusion.4), channel_id=1, source_target_pairs={{0,192},{8,200},{16,208},{24,216},{32,224},{40,232},{48,240},{56,2... | collective-permute-start | bytes 208904 | tf_op jit(solution)/shard_map/ppermute | solution.py:141
  155.6 13.8 %collective-permute-start.16 = (bf16[17,2048]{1,0:T(8,128)(2,1)S(1)}, bf16[17,2048]{1,0:T(8,128)(2,1)S(1)}, u32[]{:S(2)}, u32[]{:S(2)}) collective-permute-start(bf16[17,2048]{1,0:T(8,128)(2,1)S(1)} %pad_maximum_fusion.4), channel_id=1, source_target_pairs={{0,128},{8,136},{16,144},{24,152},{32,160},{40,168},{48,176},{56,1... | collective-permute-start | bytes 208904 | tf_op jit(solution)/shard_map/ppermute | solution.py:141
  161.0 12.8 %collective-permute-start.17 = (bf16[17,2048]{1,0:T(8,128)(2,1)S(1)}, bf16[17,2048]{1,0:T(8,128)(2,1)S(1)}, u32[]{:S(2)}, u32[]{:S(2)}) collective-permute-start(bf16[17,2048]{1,0:T(8,128)(2,1)S(1)} %pad_maximum_fusion.4), channel_id=1, source_target_pairs={{0,64},{8,72},{16,80},{24,88},{32,96},{40,104},{48,112},{56,120},{... | collective-permute-start | bytes 208904 | tf_op jit(solution)/shard_map/ppermute | solution.py:141
  174.1 28.8 %collective-permute-start.20 = (bf16[8,17,2048]{2,0,1:T(8,128)(2,1)S(1)}, bf16[8,17,2048]{2,0,1:T(8,128)(2,1)S(1)}, u32[]{:S(2)}, u32[]{:S(2)}) collective-permute-start(bf16[8,17,2048]{2,0,1:T(8,128)(2,1)S(1)} %copy.257), channel_id=1, source_target_pairs={{0,16},{8,24},{16,32},{24,40},{32,48},{40,56},{48,0},{56,8},{64,80... | collective-permute-start | bytes 1671176 | tf_op jit(solution)/shard_map/ppermute | solution.py:141
  176.0 27.2 %collective-permute-start.19 = (bf16[8,17,2048]{2,0,1:T(8,128)(2,1)S(1)}, bf16[8,17,2048]{2,0,1:T(8,128)(2,1)S(1)}, u32[]{:S(2)}, u32[]{:S(2)}) collective-permute-start(bf16[8,17,2048]{2,0,1:T(8,128)(2,1)S(1)} %copy.257), channel_id=1, source_target_pairs={{0,32},{8,40},{16,48},{24,56},{32,0},{40,8},{48,16},{56,24},{64,96... | collective-permute-start | bytes 1671176 | tf_op jit(solution)/shard_map/ppermute | solution.py:141
  179.4 25.7 %collective-permute-start.18 = (bf16[8,17,2048]{2,0,1:T(8,128)(2,1)S(1)}, bf16[8,17,2048]{2,0,1:T(8,128)(2,1)S(1)}, u32[]{:S(2)}, u32[]{:S(2)}) collective-permute-start(bf16[8,17,2048]{2,0,1:T(8,128)(2,1)S(1)} %copy.257), channel_id=1, source_target_pairs={{0,48},{8,56},{16,0},{24,8},{32,16},{40,24},{48,32},{56,40},{64,11... | collective-permute-start | bytes 1671176 | tf_op jit(solution)/shard_map/ppermute | solution.py:141
  208.3 3.8 %copy-start.1 = (bf16[4,8,17,2048]{3,2,1,0:T(8,128)(2,1)S(1)}, bf16[4,8,17,2048]{3,2,1,0:T(8,128)(2,1)}, u32[]{:S(2)}) copy-start(bf16[4,8,17,2048]{3,2,1,0:T(8,128)(2,1)} %copy-done) | copy-start | bytes 6684676
  212.0 4.0 %copy-start.6 = (f32[3,2,8,4,8]{4,2,3,1,0:T(8,128)S(1)}, f32[3,2,8,4,8]{4,2,3,1,0:T(8,128)}, u32[]{:S(2)}) copy-start(f32[3,2,8,4,8]{4,2,3,1,0:T(8,128)} %constant.319.clone.1) | copy-start | bytes 18436
  215.2 9.3 %copy-start.42 = (s32[64]{0:T(128)S(1)}, s32[64]{0:T(128)}, u32[]{:S(2)}) copy-start(s32[64]{0:T(128)} %param.51) | copy-start | bytes 772
  217.1 19.4 %all-to-all-start.1 = ((f32[3,2,64,8]{3,1,0,2:T(2,128)}), f32[3,2,64,8]{3,1,0,2:T(2,128)S(1)}, u32[]{:S(2)}, u32[]{:S(2)}) async-start(f32[3,2,64,8]{3,1,0,2:T(2,128)} %copy.265), calls=%async_computation.1 | async-start | bytes 393216 | tf_op jit(solution)/shard_map/all_to_all | solution.py:325
  (4 other events, 5.5 us)

commit v9 on v7

--- a/solution.py
+++ b/solution.py
@@ -133,6 +133,23 @@
             backward = lax.ppermute(backward, "req", perm_of(-1))
             got[step] = backward
     return jnp.stack([got[k] for k in range(count)])
+
+
+def doubling_gather(block, coord, stride, count, shards):
+    gathered = block[None]
+    distance = 1
+    while distance < count:
+        theirs = lax.ppermute(
+            gathered, "req", [(i, i ^ (distance * stride)) for i in range(shards)]
+        )
+        upper = (coord // distance) % 2 == 1
+        gathered = jnp.where(
+            upper,
+            jnp.concatenate([theirs, gathered], axis=0),
+            jnp.concatenate([gathered, theirs], axis=0),
+        )
+        distance *= 2
+    return gathered
 
 
 DIGIT = 256
@@ -216,17 +233,20 @@
     inner_width = gated.shape[2] * groups
     squares = jnp.sum(gated * gated, axis=2)
     unscaled = (gated * norm_gain[:, None, :]).astype(jnp.bfloat16)
-    ring_weight = ring_gather(
-        ring_gather(ring_gather(out_weight, along_z, chips_z), along_x, ROWS_X),
-        along_core,
+    gathered_weight = doubling_gather(
+        doubling_gather(
+            doubling_gather(out_weight, z_index, CORES * ROWS_X, chips_z, shards),
+            x_index,
+            CORES,
+            ROWS_X,
+            shards,
+        ),
+        core_index,
+        1,
         CORES,
-    )
-    ring_weight = jnp.roll(
-        jnp.roll(jnp.roll(ring_weight.transpose(2, 1, 0, 3, 4, 5), z_index, axis=0), x_index, axis=1),
-        core_index,
-        axis=2,
-    )
-    full_weight = ring_weight.transpose(3, 4, 0, 1, 2, 5).reshape(
+        shards,
+    )
+    full_weight = gathered_weight.transpose(3, 4, 2, 1, 0, 5).reshape(
         models, out_weight.shape[1], shards * out_weight.shape[2]
     )
     partial_out = jnp.einsum(
@@ -279,7 +299,9 @@
     target_row = target_row.at[0, row_count : 2 * row_count].set(low_digit)
     packet = jnp.concatenate([final_rows.reshape(models * row_count, full_width), target_row], axis=0)
 
-    every = ring_gather(ring_gather(packet, along_z, chips_z), along_x, ROWS_X)
+    every = doubling_gather(
+        doubling_gather(packet, z_index, CORES * ROWS_X, chips_z, shards), x_index, CORES, ROWS_X, shards
+    )
     peers = ROWS_X * chips_z
     every = every.reshape(peers, models * row_count + 1, full_width)
     every_rows = (
@@ -304,7 +326,6 @@
     )
     statistics = jnp.stack([peak_logit, spread, own_picked + other_picked])
     statistics = statistics.reshape(3, models, ROWS_X, chips_z, row_count).transpose(0, 1, 3, 2, 4)
-    statistics = jnp.roll(jnp.roll(statistics, z_index, axis=2), x_index, axis=3)
     neutral = jnp.stack(
         [
             jnp.full_like(statistics[0], -1e30),

time: 226 us -> 254 us (1.12)
  waiting for transfers between devices: 66.8 us -> 140 us
  starting transfers between devices: 93.1 us -> 68.6 us
  local copies, waits for them, and re-layouts: 19.6 us -> 11.7 us
  other arithmetic: 22.3 us -> 15 us
  matrix products: 21.3 us -> 16.4 us
    ppermute x21 -> x11, waiting for transfers between devices: 41.1 us -> 113 us  [doubling_gather(): lax.ppermute(gathered, 'req', [(i, i ^ distance * stride) for i in range(...]
    ppermute x21 -> x11, starting transfers between devices: 73 us -> 50.2 us  [doubling_gather(): lax.ppermute(gathered, 'req', [(i, i ^ distance * stride) for i in range(...]
    concatenate x5 -> x1, other arithmetic: 4.75 us -> 0.1 us  [doubling_gather(): jnp.concatenate([theirs, gathered], axis=0)]
    select_n x0 -> x11, other arithmetic: none -> 4.57 us  [doubling_gather(): jnp.where(upper, jnp.concatenate([theirs, gathered], axis=0), jnp.concate...]
    another operation x7 -> x5, other arithmetic: 6.87 us -> 3.52 us
    dot_general x12, matrix products: 5.44 us -> 2.86 us  [causal_conv(): jnp.dot(member_bf, history[:, slot_index, :], preferred_element_type=jnp....]
  transfers between devices with their start and end apart: 24 -> 14, of which waited for: 11 -> 11; matrix products, arithmetic and copies ran while one was open for 19% -> 11% of each run, Pallas kernels for 0% -> 0%
where the time goes in v9:
time: 254 us; the launch traced here: 253 us
  waiting for transfers between devices  140 us (55%)
  starting transfers between devices  68.6 us (27%)
  matrix products  16.4 us (6%)
  other arithmetic  15 us (6%)
  local copies, waits for them, and re-layouts  11.7 us (5%)
    ppermute x11, waiting for transfers between devices, doubling_gather(): lax.ppermute(gathered, 'req', [(i, i ^ distance * stride) for i in range(...  113 us
    ppermute x11, starting transfers between devices, doubling_gather(): lax.ppermute(gathered, 'req', [(i, i ^ distance * stride) for i in range(...  50.2 us
    all_to_all x1, waiting for transfers between devices, local(): lax.all_to_all(payload.reshape(models, groups, row_count, payload.shape[2...  15.8 us
    all_to_all x1, waiting for transfers between devices, local(): lax.all_to_all(send, 'req', split_axis=2, concat_axis=2, tiled=True)  11.9 us
    all_to_all x1, starting transfers between devices, local(): lax.all_to_all(send, 'req', split_axis=2, concat_axis=2, tiled=True)  8.72 us
    dot_general x2, matrix products, head_scores(): jnp.einsum('mnd,mvd->mnv', rows_hidden, head_weight, preferred_element_ty...  6.89 us
    all_to_all x1, starting transfers between devices, local(): lax.all_to_all(payload.reshape(models, groups, row_count, payload.shape[2...  6.82 us
  transfers between devices with their start and end apart: 14, of which 11 were waited for; matrix products, arithmetic and copies ran while one was open for 11% of the time, Pallas kernels for 0%

profile of v9, /device:TPU:1, one launch (start us, length us, event | category | flops | bytes accessed | tf_op | source)
XLA Modules:
  0.0 253.2 jit_solution(12755552311567341524)
XLA Ops:
  0.1 5.0 %collective-permute-start = (bf16[1,2,512,32]{2,3,0,1:T(8,128)(2,1)}, bf16[1,2,512,32]{2,3,0,1:T(8,128)(2,1)S(1)}, u32[]{:S(2)}, u32[]{:S(2)}) collective-permute-start(bf16[1,2,512,32]{2,3,0,1:T(8,128)(2,1)} %bitcast.331), channel_id=1, source_target_pairs={{0,64},{8,72},{16,80},{24,88},{32,96},{40,104},{48,112},{56,120},{... | collective-permute-start | bytes 196616 | tf_op jit(solution)/shard_map/ppermute | solution.py:142
  5.0 0.8 reduce-window.4
  5.9 0.7 compare_and_fusion
  6.5 0.7 fusion.162
  7.2 0.9 slice_convert_fusion.1
  8.2 0.8 slice_convert_fusion.3
  11.5 0.6 gather_fusion.1
  12.1 0.3 divide_multiply_fusion
  12.4 0.3 fusion.13
  12.7 5.8 %collective-permute-start.1 = (bf16[2,2,512,32]{2,3,0,1:T(8,128)(2,1)S(1)}, bf16[2,2,512,32]{2,3,0,1:T(8,128)(2,1)S(1)}, u32[]{:S(2)}, u32[]{:S(2)}) collective-permute-start(bf16[2,2,512,32]{2,3,0,1:T(8,128)(2,1)S(1)} %maximum_select_fusion.10), channel_id=1, source_target_pairs={{0,128},{8,136},{16,144},{24,152},{32,160},{40,168},{48,176},{56,1... | collective-permute-start | bytes 393224 | tf_op jit(solution)/shard_map/ppermute | solution.py:142
  18.6 3.4 %collective-permute-done.1 = bf16[2,2,512,32]{2,3,0,1:T(8,128)(2,1)S(1)} collective-permute-done((bf16[2,2,512,32]{2,3,0,1:T(8,128)(2,1)S(1)}, bf16[2,2,512,32]{2,3,0,1:T(8,128)(2,1)S(1)}, u32[]{:S(2)}, u32[]{:S(2)}) %collective-permute-start.1) | collective-permute-done | bytes 131104 | tf_op jit(solution)/shard_map/ppermute | solution.py:142
  22.0 11.5 %collective-permute-start.2 = (bf16[4,2,512,32]{2,3,0,1:T(8,128)(2,1)S(1)}, bf16[4,2,512,32]{2,3,0,1:T(8,128)(2,1)S(1)}, u32[]{:S(2)}, u32[]{:S(2)}) collective-permute-start(bf16[4,2,512,32]{2,3,0,1:T(8,128)(2,1)S(1)} %maximum_select_fusion.8), channel_id=1, source_target_pairs={{0,256},{8,264},{16,272},{24,280},{32,288},{40,296},{48,304},{56,3... | collective-permute-start | bytes 786440 | tf_op jit(solution)/shard_map/ppermute | solution.py:142
  33.7 0.3 divide_multiply_fusion.2
  34.0 11.3 %collective-permute-done.2 = bf16[4,2,512,32]{2,3,0,1:T(8,128)(2,1)S(1)} collective-permute-done((bf16[4,2,512,32]{2,3,0,1:T(8,128)(2,1)S(1)}, bf16[4,2,512,32]{2,3,0,1:T(8,128)(2,1)S(1)}, u32[]{:S(2)}, u32[]{:S(2)}) %collective-permute-start.2) | collective-permute-done | bytes 262176 | tf_op jit(solution)/shard_map/ppermute | solution.py:142
  45.4 3.1 %collective-permute-start.3 = (bf16[1,8,2,512,32]{3,4,0,1,2:T(8,128)(2,1)S(1)}, bf16[1,8,2,512,32]{3,4,0,1,2:T(8,128)(2,1)S(1)}, u32[]{:S(2)}, u32[]{:S(2)}) collective-permute-start(bf16[1,8,2,512,32]{3,4,0,1,2:T(8,128)(2,1)S(1)} %maximum_select_fusion.6), channel_id=1, source_target_pairs={{0,16},{8,24},{16,0},{24,8},{32,48},{40,56},{48,32},{56,40},{64,80... | collective-permute-start | bytes 1572872 | tf_op jit(solution)/shard_map/ppermute | solution.py:142
  48.5 2.0 fusion.7
  51.1 8.6 %collective-permute-done.3 = bf16[1,8,2,512,32]{3,4,0,1,2:T(8,128)(2,1)S(1)} collective-permute-done((bf16[1,8,2,512,32]{3,4,0,1,2:T(8,128)(2,1)S(1)}, bf16[1,8,2,512,32]{3,4,0,1,2:T(8,128)(2,1)S(1)}, u32[]{:S(2)}, u32[]{:S(2)}) %collective-permute-start.3) | collective-permute-done | bytes 524320 | tf_op jit(solution)/shard_map/ppermute | solution.py:142
  59.7 4.7 %collective-permute-start.4 = (bf16[2,8,2,512,32]{3,4,0,1,2:T(8,128)(2,1)S(1)}, bf16[2,8,2,512,32]{3,4,0,1,2:T(8,128)(2,1)S(1)}, u32[]{:S(2)}, u32[]{:S(2)}) collective-permute-start(bf16[2,8,2,512,32]{3,4,0,1,2:T(8,128)(2,1)S(1)} %maximum_select_fusion.4), channel_id=1, source_target_pairs={{0,32},{8,40},{16,48},{24,56},{32,0},{40,8},{48,16},{56,24},{64,96... | collective-permute-start | bytes 3145736 | tf_op jit(solution)/shard_map/ppermute | solution.py:142
  64.6 0.3 divide_multiply_fusion.3
  64.9 0.7 fusion.9
  65.6 20.2 %collective-permute-done.4 = bf16[2,8,2,512,32]{3,4,0,1,2:T(8,128)(2,1)S(1)} collective-permute-done((bf16[2,8,2,512,32]{3,4,0,1,2:T(8,128)(2,1)S(1)}, bf16[2,8,2,512,32]{3,4,0,1,2:T(8,128)(2,1)S(1)}, u32[]{:S(2)}, u32[]{:S(2)}) %collective-permute-start.4) | collective-permute-done | bytes 1048608 | tf_op jit(solution)/shard_map/ppermute | solution.py:142
  86.0 5.0 %collective-permute-start.5 = (bf16[1,4,8,2,512,32]{4,5,0,1,2,3:T(8,128)(2,1)S(1)}, bf16[1,4,8,2,512,32]{4,5,0,1,2,3:T(8,128)(2,1)}, u32[]{:S(2)}, u32[]{:S(2)}) collective-permute-start(bf16[1,4,8,2,512,32]{4,5,0,1,2,3:T(8,128)(2,1)S(1)} %maximum_select_fusion.2), channel_id=1, source_target_pairs={{0,8},{8,0},{16,24},{24,16},{32,40},{40,32},{48,56},{56,48},{64,72... | collective-permute-start | bytes 6291464 | tf_op jit(solution)/shard_map/ppermute | solution.py:142
  91.0 1.0 fusion.6
  92.2 0.2 fusion.101
  92.7 0.3 divide_multiply_fusion.1
  93.3 0.6 gather_fusion
  93.8 0.3 fusion.15
  94.3 0.7 fusion.11
  95.5 2.7 %maximum_select_fusion = bf16[2,4,8,2,512,32]{4,5,0,1,2,3:T(8,128)(2,1)S(1)} fusion(bf16[1,4,8,2,512,32]{4,5,0,1,2,3:T(8,128)(2,1)S(1)} %maximum_select_fusion.2, bf16[1,4,8,2,512,32]{4,5,0,1,2,3:T(8,128)(2,1)} %collective-permute-done.5, pred[]{:T(512)S(6)} %eq.238), kind=kLoop, calls=%fused_computation.2 | loop fusion | flops 6291456 | bytes 8388609 | tf_op jit(solution)/shard_map/jit(_where)/select_n | solution.py:146
  98.2 1.4 convolution_convert_fusion
  99.7 0.9 copy.223
  100.5 6.8 %all-to-all-start = ((bf16[2,8,8,2432]{3,2,0,1:T(8,128)(2,1)}), bf16[2,8,8,2432]{3,2,0,1:T(8,128)(2,1)S(1)}, u32[]{:S(2)}, u32[]{:S(2)}) async-start(bf16[2,8,8,2432]{3,2,0,1:T(8,128)(2,1)} %copy.223), calls=%async_computation | async-start | bytes 1245184 | tf_op jit(solution)/shard_map/all_to_all | solution.py:267
  107.4 0.6 slice.454
  108.0 0.6 and_reduce_fusion
  108.7 0.7 fusion.158
  109.3 1.4 broadcast_select_fusion
  110.7 0.9 scatter.19
  111.7 15.8 %all-to-all-done = bf16[2,8,8,2432]{3,2,0,1:T(8,128)(2,1)S(1)} async-done(((bf16[2,8,8,2432]{3,2,0,1:T(8,128)(2,1)}), bf16[2,8,8,2432]{3,2,0,1:T(8,128)(2,1)S(1)}, u32[]{:S(2)}, u32[]{:S(2)}) %all-to-all-start) | async-done | bytes 622624 | tf_op jit(solution)/shard_map/all_to_all | solution.py:267
  127.6 0.3 slice_reduce_fusion
  128.7 1.9 collective-permute-start.6
  130.6 3.9 %collective-permute-done.6 = bf16[1,17,2048]{2,1,0:T(8,128)(2,1)S(1)} collective-permute-done((bf16[1,17,2048]{2,1,0:T(8,128)(2,1)S(1)}, bf16[1,17,2048]{2,1,0:T(8,128)(2,1)S(1)}, u32[]{:S(2)}, u32[]{:S(2)}) %collective-permute-start.6) | collective-permute-done | bytes 69664 | tf_op jit(solution)/shard_map/ppermute | solution.py:142
  134.6 1.9 collective-permute-start.7
  136.5 11.9 %collective-permute-done.7 = bf16[2,17,2048]{2,1,0:T(8,128)(2,1)S(1)} collective-permute-done((bf16[2,17,2048]{2,1,0:T(8,128)(2,1)S(1)}, bf16[2,17,2048]{2,1,0:T(8,128)(2,1)S(1)}, u32[]{:S(2)}, u32[]{:S(2)}) %collective-permute-start.7) | collective-permute-done | bytes 139296 | tf_op jit(solution)/shard_map/ppermute | solution.py:142
  148.4 3.6 %collective-permute-start.8 = (bf16[4,17,2048]{2,1,0:T(8,128)(2,1)S(1)}, bf16[4,17,2048]{2,1,0:T(8,128)(2,1)S(1)}, u32[]{:S(2)}, u32[]{:S(2)}) collective-permute-start(bf16[4,17,2048]{2,1,0:T(8,128)(2,1)S(1)} %maximum_select_fusion.7), channel_id=1, source_target_pairs={{0,256},{8,264},{16,272},{24,280},{32,288},{40,296},{48,304},{56,3... | collective-permute-start | bytes 835592 | tf_op jit(solution)/shard_map/ppermute | solution.py:142
  152.1 20.2 %collective-permute-done.8 = bf16[4,17,2048]{2,1,0:T(8,128)(2,1)S(1)} collective-permute-done((bf16[4,17,2048]{2,1,0:T(8,128)(2,1)S(1)}, bf16[4,17,2048]{2,1,0:T(8,128)(2,1)S(1)}, u32[]{:S(2)}, u32[]{:S(2)}) %collective-permute-start.8) | collective-permute-done | bytes 278560 | tf_op jit(solution)/shard_map/ppermute | solution.py:142
  172.5 0.3 copy.225
  172.8 3.1 %collective-permute-start.9 = (bf16[1,8,17,2048]{3,1,2,0:T(8,128)(2,1)S(1)}, bf16[1,8,17,2048]{3,1,2,0:T(8,128)(2,1)S(1)}, u32[]{:S(2)}, u32[]{:S(2)}) collective-permute-start(bf16[1,8,17,2048]{3,1,2,0:T(8,128)(2,1)S(1)} %copy.225), channel_id=1, source_target_pairs={{0,16},{8,24},{16,0},{24,8},{32,48},{40,56},{48,32},{56,40},{64,80... | collective-permute-start | bytes 1671176 | tf_op jit(solution)/shard_map/ppermute | solution.py:142
  176.0 2.9 %collective-permute-start.11 = (bf16[2,400,2048]{2,1,0:T(8,128)(2,1)}, bf16[2,400,2048]{2,1,0:T(8,128)(2,1)}, u32[]{:S(2)}, u32[]{:S(2)}) collective-permute-start(bf16[2,400,2048]{2,1,0:T(8,128)(2,1)} %param.44), channel_id=1, source_target_pairs={{0,8},{8,0},{16,24},{24,16},{32,40},{40,32},{48,56},{56,48},{64,72... | collective-permute-start | bytes 9830408 | tf_op jit(solution)/shard_map/ppermute | solution.py:209
  178.8 9.6 %collective-permute-done.9 = bf16[1,8,17,2048]{3,1,2,0:T(8,128)(2,1)S(1)} collective-permute-done((bf16[1,8,17,2048]{3,1,2,0:T(8,128)(2,1)S(1)}, bf16[1,8,17,2048]{3,1,2,0:T(8,128)(2,1)S(1)}, u32[]{:S(2)}, u32[]{:S(2)}) %collective-permute-start.9) | collective-permute-done | bytes 557088 | tf_op jit(solution)/shard_map/ppermute | solution.py:142
  188.4 0.3 copy.226
  188.8 0.3 maximum_select_fusion.3
  189.1 1.7 copy.228
  190.8 4.6 %collective-permute-start.10 = (bf16[2,8,17,2048]{3,1,2,0:T(8,128)(2,1)}, bf16[2,8,17,2048]{3,1,2,0:T(8,128)(2,1)S(1)}, u32[]{:S(2)}, u32[]{:S(2)}) collective-permute-start(bf16[2,8,17,2048]{3,1,2,0:T(8,128)(2,1)} %copy.228), channel_id=1, source_target_pairs={{0,32},{8,40},{16,48},{24,56},{32,0},{40,8},{48,16},{56,24},{64,96... | collective-permute-start | bytes 3342344 | tf_op jit(solution)/shard_map/ppermute | solution.py:142
  195.4 23.7 %collective-permute-done.10 = bf16[2,8,17,2048]{3,1,2,0:T(8,128)(2,1)S(1)} collective-permute-done((bf16[2,8,17,2048]{3,1,2,0:T(8,128)(2,1)}, bf16[2,8,17,2048]{3,1,2,0:T(8,128)(2,1)S(1)}, u32[]{:S(2)}, u32[]{:S(2)}) %collective-permute-start.10) | collective-permute-done | bytes 1114144 | tf_op jit(solution)/shard_map/ppermute | solution.py:142
  219.1 0.7 copy.229
  219.7 0.8 maximum_select_fusion.1
  220.6 1.7 copy-done
  222.8 3.8 %fusion.179 = (f32[2,256]{1,0:T(2,128)S(1)}, f32[2,256,400]{1,2,0:T(8,128)S(1)}) fusion(bf16[2,400,2048]{2,1,0:T(8,128)(2,1)} %param.44, bf16[32,17,2048]{2,1,0:T(8,128)(2,1)} %bitcast.315), kind=kOutput, calls=%fused_computation.322 | convolution fusion | flops 839065088 | bytes 6195200 | tf_op jit(solution)/shard_map/mnd,mvd->mnv/dot_general | solution.py:115
  226.6 3.1 %fusion.180 = (f32[2,256]{1,0:T(2,128)S(1)}, f32[2,256,400]{1,2,0:T(8,128)S(1)}) fusion(bf16[2,400,2048]{2,1,0:T(8,128)(2,1)} %collective-permute-done.11, bf16[32,17,2048]{2,1,0:T(8,128)(2,1)S(1)} %bitcast.316), kind=kOutput, calls=%fused_computation.323 | convolution fusion | flops 839065088 | bytes 6195200 | tf_op jit(solution)/shard_map/mnd,mvd->mnv/dot_general | solution.py:115
  229.8 0.4 select_reduce_fusion
  230.8 0.8 copy.233
  231.6 8.7 %all-to-all-start.1 = ((f32[3,2,64,8]{3,1,0,2:T(2,128)}), f32[3,2,64,8]{3,1,0,2:T(2,128)S(1)}, u32[]{:S(2)}, u32[]{:S(2)}) async-start(f32[3,2,64,8]{3,1,0,2:T(2,128)} %copy.233), calls=%async_computation.1 | async-start | bytes 393216 | tf_op jit(solution)/shard_map/all_to_all | solution.py:339
  240.4 11.9 %all-to-all-done.1 = f32[3,2,64,8]{3,1,0,2:T(2,128)S(1)} async-done(((f32[3,2,64,8]{3,1,0,2:T(2,128)}), f32[3,2,64,8]{3,1,0,2:T(2,128)S(1)}, u32[]{:S(2)}, u32[]{:S(2)}) %all-to-all-start.1) | async-done | bytes 12320 | tf_op jit(solution)/shard_map/all_to_all | solution.py:339
  252.6 0.6 subtract_multiply_fusion
  (147 shorter events, 7.8 us)
Async XLA Ops:
  0.0 9.2 %copy-start.20 = (s32[1,3]{1,0:T(1,128)S(1)}, s32[1,3]{1,0:T(1,128)}, u32[]{:S(2)}) copy-start(s32[1,3]{1,0:T(1,128)} %param.49) | copy-start | bytes 40
  0.0 9.2 %copy-start.5 = (bf16[2,3,3,512]{3,0,2,1:T(2,128)(2,1)S(1)}, bf16[2,3,3,512]{3,0,2,1:T(2,128)(2,1)}, u32[]{:S(2)}) copy-start(bf16[2,3,3,512]{3,0,2,1:T(2,128)(2,1)} %param.45) | copy-start | bytes 55300
  0.0 9.9 %copy-start.10 = (f32[2,4,512]{2,1,0:T(4,128)S(1)}, f32[2,4,512]{2,1,0:T(4,128)}, u32[]{:S(2)}) copy-start(f32[2,4,512]{2,1,0:T(4,128)} %param.36) | copy-start | bytes 49156
  0.0 10.0 %copy-start.9 = (bf16[2,3,3,256]{3,0,2,1:T(2,128)(2,1)S(1)}, bf16[2,3,3,256]{3,0,2,1:T(2,128)(2,1)}, u32[]{:S(2)}) copy-start(bf16[2,3,3,256]{3,0,2,1:T(2,128)(2,1)} %param.46) | copy-start | bytes 27652
  0.0 10.5 %copy-start.13 = (f32[2,4,256]{2,1,0:T(4,128)S(1)}, f32[2,4,256]{2,1,0:T(4,128)}, u32[]{:S(2)}) copy-start(f32[2,4,256]{2,1,0:T(4,128)} %param.37) | copy-start | bytes 24580
  0.0 10.5 %copy-start.18 = (f32[2,8]{1,0:T(2,128)S(1)}, f32[2,8]{1,0:T(2,128)}, u32[]{:S(2)}) copy-start(f32[2,8]{1,0:T(2,128)} %param.38) | copy-start | bytes 196
  0.0 10.5 %copy-start.17 = (f32[2,8]{1,0:T(2,128)S(1)}, f32[2,8]{1,0:T(2,128)}, u32[]{:S(2)}) copy-start(f32[2,8]{1,0:T(2,128)} %param.39) | copy-start | bytes 196
  0.0 10.6 %copy-start.11 = (bf16[2,64,8]{1,2,0:T(8,128)(2,1)S(1)}, bf16[2,64,8]{1,2,0:T(8,128)(2,1)}, u32[]{:S(2)}) copy-start(bf16[2,64,8]{1,2,0:T(8,128)(2,1)} %param.34) | copy-start | bytes 6148
  0.1 12.6 %collective-permute-start = (bf16[1,2,512,32]{2,3,0,1:T(8,128)(2,1)}, bf16[1,2,512,32]{2,3,0,1:T(8,128)(2,1)S(1)}, u32[]{:S(2)}, u32[]{:S(2)}) collective-permute-start(bf16[1,2,512,32]{2,3,0,1:T(8,128)(2,1)} %bitcast.331), channel_id=1, source_target_pairs={{0,64},{8,72},{16,80},{24,88},{32,96},{40,104},{48,112},{56,120},{... | collective-permute-start | bytes 196616 | tf_op jit(solution)/shard_map/ppermute | solution.py:142
  7.2 4.9 %copy-start.2 = (bf16[2,64,512]{2,1,0:T(8,128)(2,1)S(1)}, bf16[2,64,512]{2,1,0:T(8,128)(2,1)}, u32[]{:S(2)}) copy-start(bf16[2,64,512]{2,1,0:T(8,128)(2,1)} %param.32) | copy-start | bytes 393220
  9.0 3.7 %copy-start.8 = (bf16[2,512,32]{1,2,0:T(8,128)(2,1)S(1)}, bf16[2,512,32]{1,2,0:T(8,128)(2,1)}, u32[]{:S(2)}) copy-start(bf16[2,512,32]{1,2,0:T(8,128)(2,1)} %param.43) | copy-start | bytes 196612
  10.3 23.4 %copy-start.6 = (bf16[2,64,256]{2,1,0:T(8,128)(2,1)S(1)}, bf16[2,64,256]{2,1,0:T(8,128)(2,1)}, u32[]{:S(2)}) copy-start(bf16[2,64,256]{2,1,0:T(8,128)(2,1)} %param.33) | copy-start | bytes 196612
  12.7 9.3 %collective-permute-start.1 = (bf16[2,2,512,32]{2,3,0,1:T(8,128)(2,1)S(1)}, bf16[2,2,512,32]{2,3,0,1:T(8,128)(2,1)S(1)}, u32[]{:S(2)}, u32[]{:S(2)}) collective-permute-start(bf16[2,2,512,32]{2,3,0,1:T(8,128)(2,1)S(1)} %maximum_select_fusion.10), channel_id=1, source_target_pairs={{0,128},{8,136},{16,144},{24,152},{32,160},{40,168},{48,176},{56,1... | collective-permute-start | bytes 393224 | tf_op jit(solution)/shard_map/ppermute | solution.py:142
  22.0 23.3 %collective-permute-start.2 = (bf16[4,2,512,32]{2,3,0,1:T(8,128)(2,1)S(1)}, bf16[4,2,512,32]{2,3,0,1:T(8,128)(2,1)S(1)}, u32[]{:S(2)}, u32[]{:S(2)}) collective-permute-start(bf16[4,2,512,32]{2,3,0,1:T(8,128)(2,1)S(1)} %maximum_select_fusion.8), channel_id=1, source_target_pairs={{0,256},{8,264},{16,272},{24,280},{32,288},{40,296},{48,304},{56,3... | collective-permute-start | bytes 786440 | tf_op jit(solution)/shard_map/ppermute | solution.py:142
  45.3 19.1 %copy-start.16 = (f32[2,8]{1,0:T(2,128)S(1)}, f32[2,8]{1,0:T(2,128)}, u32[]{:S(2)}) copy-start(f32[2,8]{1,0:T(2,128)} %param.40) | copy-start | bytes 196
  45.4 14.2 %collective-permute-start.3 = (bf16[1,8,2,512,32]{3,4,0,1,2:T(8,128)(2,1)S(1)}, bf16[1,8,2,512,32]{3,4,0,1,2:T(8,128)(2,1)S(1)}, u32[]{:S(2)}, u32[]{:S(2)}) collective-permute-start(bf16[1,8,2,512,32]{3,4,0,1,2:T(8,128)(2,1)S(1)} %maximum_select_fusion.6), channel_id=1, source_target_pairs={{0,16},{8,24},{16,0},{24,8},{32,48},{40,56},{48,32},{56,40},{64,80... | collective-permute-start | bytes 1572872 | tf_op jit(solution)/shard_map/ppermute | solution.py:142
  59.7 26.1 %collective-permute-start.4 = (bf16[2,8,2,512,32]{3,4,0,1,2:T(8,128)(2,1)S(1)}, bf16[2,8,2,512,32]{3,4,0,1,2:T(8,128)(2,1)S(1)}, u32[]{:S(2)}, u32[]{:S(2)}) collective-permute-start(bf16[2,8,2,512,32]{3,4,0,1,2:T(8,128)(2,1)S(1)} %maximum_select_fusion.4), channel_id=1, source_target_pairs={{0,32},{8,40},{16,48},{24,56},{32,0},{40,8},{48,16},{56,24},{64,96... | collective-permute-start | bytes 3145736 | tf_op jit(solution)/shard_map/ppermute | solution.py:142
  85.8 5.2 %copy-start.19 = (bf16[2,3,512,128]{3,2,1,0:T(8,128)(2,1)S(1)}, bf16[2,3,512,128]{3,2,1,0:T(8,128)(2,1)}, u32[]{:S(2)}) copy-start(bf16[2,3,512,128]{3,2,1,0:T(8,128)(2,1)} %param.47) | copy-start | bytes 2359300
  86.0 9.5 %collective-permute-start.5 = (bf16[1,4,8,2,512,32]{4,5,0,1,2,3:T(8,128)(2,1)S(1)}, bf16[1,4,8,2,512,32]{4,5,0,1,2,3:T(8,128)(2,1)}, u32[]{:S(2)}, u32[]{:S(2)}) collective-permute-start(bf16[1,4,8,2,512,32]{4,5,0,1,2,3:T(8,128)(2,1)S(1)} %maximum_select_fusion.2), channel_id=1, source_target_pairs={{0,8},{8,0},{16,24},{24,16},{32,40},{40,32},{48,56},{56,48},{64,72... | collective-permute-start | bytes 6291464 | tf_op jit(solution)/shard_map/ppermute | solution.py:142
  92.5 2.6 %copy-start.3 = (bf16[2,64,512]{2,1,0:T(8,128)(2,1)S(1)}, bf16[2,64,512]{2,1,0:T(8,128)(2,1)}, u32[]{:S(2)}) copy-start(bf16[2,64,512]{2,1,0:T(8,128)(2,1)} %param.31) | copy-start | bytes 393220
  95.4 2.8 %copy-start.14 = (f32[2,512]{1,0:T(2,128)S(1)}, f32[2,512]{1,0:T(2,128)}, u32[]{:S(2)}) copy-start(f32[2,512]{1,0:T(2,128)} %param.41) | copy-start | bytes 12292
  98.2 1.4 copy-start.7
  99.6 9.1 %copy-start.15 = (s32[64]{0:T(128)S(1)}, s32[64]{0:T(128)}, u32[]{:S(2)}) copy-start(s32[64]{0:T(128)} %param.50) | copy-start | bytes 772
  100.5 27.0 %all-to-all-start = ((bf16[2,8,8,2432]{3,2,0,1:T(8,128)(2,1)}), bf16[2,8,8,2432]{3,2,0,1:T(8,128)(2,1)S(1)}, u32[]{:S(2)}, u32[]{:S(2)}) async-start(bf16[2,8,8,2432]{3,2,0,1:T(8,128)(2,1)} %copy.223), calls=%async_computation | async-start | bytes 1245184 | tf_op jit(solution)/shard_map/all_to_all | solution.py:267
  107.4 21.2 %copy-start.12 = (f32[2,2048]{1,0:T(2,128)S(1)}, f32[2,2048]{1,0:T(2,128)}, u32[]{:S(2)}) copy-start(f32[2,2048]{1,0:T(2,128)} %param.42) | copy-start | bytes 49156
  128.7 5.8 %collective-permute-start.6 = (bf16[1,17,2048]{2,1,0:T(8,128)(2,1)S(1)}, bf16[1,17,2048]{2,1,0:T(8,128)(2,1)S(1)}, u32[]{:S(2)}, u32[]{:S(2)}) collective-permute-start(bf16[1,17,2048]{2,1,0:T(8,128)(2,1)S(1)} %maximum_bitcast_fusion.1), channel_id=1, source_target_pairs={{0,64},{8,72},{16,80},{24,88},{32,96},{40,104},{48,112},{56,120},{... | collective-permute-start | bytes 208904 | tf_op jit(solution)/shard_map/ppermute | solution.py:142
  134.6 13.8 %collective-permute-start.7 = (bf16[2,17,2048]{2,1,0:T(8,128)(2,1)S(1)}, bf16[2,17,2048]{2,1,0:T(8,128)(2,1)S(1)}, u32[]{:S(2)}, u32[]{:S(2)}) collective-permute-start(bf16[2,17,2048]{2,1,0:T(8,128)(2,1)S(1)} %maximum_select_fusion.9), channel_id=1, source_target_pairs={{0,128},{8,136},{16,144},{24,152},{32,160},{40,168},{48,176},{56,1... | collective-permute-start | bytes 417800 | tf_op jit(solution)/shard_map/ppermute | solution.py:142
  148.4 23.9 %collective-permute-start.8 = (bf16[4,17,2048]{2,1,0:T(8,128)(2,1)S(1)}, bf16[4,17,2048]{2,1,0:T(8,128)(2,1)S(1)}, u32[]{:S(2)}, u32[]{:S(2)}) collective-permute-start(bf16[4,17,2048]{2,1,0:T(8,128)(2,1)S(1)} %maximum_select_fusion.7), channel_id=1, source_target_pairs={{0,256},{8,264},{16,272},{24,280},{32,288},{40,296},{48,304},{56,3... | collective-permute-start | bytes 835592 | tf_op jit(solution)/shard_map/ppermute | solution.py:142
  172.8 15.6 %collective-permute-start.9 = (bf16[1,8,17,2048]{3,1,2,0:T(8,128)(2,1)S(1)}, bf16[1,8,17,2048]{3,1,2,0:T(8,128)(2,1)S(1)}, u32[]{:S(2)}, u32[]{:S(2)}) collective-permute-start(bf16[1,8,17,2048]{3,1,2,0:T(8,128)(2,1)S(1)} %copy.225), channel_id=1, source_target_pairs={{0,16},{8,24},{16,0},{24,8},{32,48},{40,56},{48,32},{56,40},{64,80... | collective-permute-start | bytes 1671176 | tf_op jit(solution)/shard_map/ppermute | solution.py:142
  176.0 50.6 %collective-permute-start.11 = (bf16[2,400,2048]{2,1,0:T(8,128)(2,1)}, bf16[2,400,2048]{2,1,0:T(8,128)(2,1)}, u32[]{:S(2)}, u32[]{:S(2)}) collective-permute-start(bf16[2,400,2048]{2,1,0:T(8,128)(2,1)} %param.44), channel_id=1, source_target_pairs={{0,8},{8,0},{16,24},{24,16},{32,40},{40,32},{48,56},{56,48},{64,72... | collective-permute-start | bytes 9830408 | tf_op jit(solution)/shard_map/ppermute | solution.py:209
  190.8 28.3 %collective-permute-start.10 = (bf16[2,8,17,2048]{3,1,2,0:T(8,128)(2,1)}, bf16[2,8,17,2048]{3,1,2,0:T(8,128)(2,1)S(1)}, u32[]{:S(2)}, u32[]{:S(2)}) collective-permute-start(bf16[2,8,17,2048]{3,1,2,0:T(8,128)(2,1)} %copy.228), channel_id=1, source_target_pairs={{0,32},{8,40},{16,48},{24,56},{32,0},{40,8},{48,16},{56,24},{64,96... | collective-permute-start | bytes 3342344 | tf_op jit(solution)/shard_map/ppermute | solution.py:142
  220.6 1.7 copy-start
  222.8 3.8 %copy-start.1 = (bf16[4,8,17,2048]{3,2,1,0:T(8,128)(2,1)S(1)}, bf16[4,8,17,2048]{3,2,1,0:T(8,128)(2,1)}, u32[]{:S(2)}) copy-start(bf16[4,8,17,2048]{3,2,1,0:T(8,128)(2,1)} %copy-done) | copy-start | bytes 6684676
  229.7 0.9 copy-start.4
  229.7 10.6 %copy-start.21 = (s32[64]{0:T(128)S(1)}, s32[64]{0:T(128)}, u32[]{:S(2)}) copy-start(s32[64]{0:T(128)} %param.51) | copy-start | bytes 772
  231.6 20.8 %all-to-all-start.1 = ((f32[3,2,64,8]{3,1,0,2:T(2,128)}), f32[3,2,64,8]{3,1,0,2:T(2,128)S(1)}, u32[]{:S(2)}, u32[]{:S(2)}) async-start(f32[3,2,64,8]{3,1,0,2:T(2,128)} %copy.233), calls=%async_computation.1 | async-start | bytes 393216 | tf_op jit(solution)/shard_map/all_to_all | solution.py:339

commit v10 on v7

--- a/solution.py
+++ b/solution.py
@@ -217,12 +217,12 @@
     squares = jnp.sum(gated * gated, axis=2)
     unscaled = (gated * norm_gain[:, None, :]).astype(jnp.bfloat16)
     ring_weight = ring_gather(
-        ring_gather(ring_gather(out_weight, along_z, chips_z), along_x, ROWS_X),
+        ring_gather(ring_gather(out_weight, along_x, ROWS_X), along_z, chips_z),
         along_core,
         CORES,
     )
     ring_weight = jnp.roll(
-        jnp.roll(jnp.roll(ring_weight.transpose(2, 1, 0, 3, 4, 5), z_index, axis=0), x_index, axis=1),
+        jnp.roll(jnp.roll(ring_weight.transpose(1, 2, 0, 3, 4, 5), z_index, axis=0), x_index, axis=1),
         core_index,
         axis=2,
     )
@@ -279,7 +279,7 @@
     target_row = target_row.at[0, row_count : 2 * row_count].set(low_digit)
     packet = jnp.concatenate([final_rows.reshape(models * row_count, full_width), target_row], axis=0)
 
-    every = ring_gather(ring_gather(packet, along_z, chips_z), along_x, ROWS_X)
+    every = ring_gather(ring_gather(packet, along_x, ROWS_X), along_z, chips_z)
     peers = ROWS_X * chips_z
     every = every.reshape(peers, models * row_count + 1, full_width)
     every_rows = (
@@ -303,7 +303,7 @@
         jnp.exp(other_logits - peak_logit[:, :, None]), axis=2
     )
     statistics = jnp.stack([peak_logit, spread, own_picked + other_picked])
-    statistics = statistics.reshape(3, models, ROWS_X, chips_z, row_count).transpose(0, 1, 3, 2, 4)
+    statistics = statistics.reshape(3, models, chips_z, ROWS_X, row_count)
     statistics = jnp.roll(jnp.roll(statistics, z_index, axis=2), x_index, axis=3)
     neutral = jnp.stack(
         [

time: 226 us -> 212 us (0.938)
  local copies, waits for them, and re-layouts: 19.6 us -> 11.4 us
  matrix products: 21.3 us -> 16.8 us
  other arithmetic: 22.3 us -> 18.9 us
  starting transfers between devices: 93.1 us -> 95.8 us
    ppermute x13, waiting for transfers between devices: 40.6 us -> 34 us  [ring_gather(): forward = lax.ppermute(forward, 'req', perm_of(1))]
    ppermute x8, starting transfers between devices: 38.7 us -> 34.9 us  [ring_gather(): backward = lax.ppermute(backward, 'req', perm_of(-1))]
    ppermute x8, waiting for transfers between devices: 0.49 us -> 4.07 us  [ring_gather(): backward = lax.ppermute(backward, 'req', perm_of(-1))]
    ppermute x13, starting transfers between devices: 34.4 us -> 37.8 us  [ring_gather(): forward = lax.ppermute(forward, 'req', perm_of(1))]
    another operation x2 -> x3, other arithmetic: 3.4 us -> 0.11 us  [ring_gather(): return jnp.stack([got[k] for k in range(count)])]
    ppermute x1, starting transfers between devices: 2.37 us -> 4.93 us  [local(): lax.ppermute(head_weight, 'req', [(i, i ^ 1) for i in range(shards)])]
    slice x6, local copies, waits for them, and re-layouts: 2.61 us -> 0.09 us  [causal_conv(): current[:-lag_steps]]
    all_to_all x1, waiting for transfers between devices: 13.6 us -> 15.9 us  [local(): lax.all_to_all(payload.reshape(models, groups, row_count, payload.shape[2...]
  transfers between devices with their start and end apart: 24 -> 24, of which waited for: 11 -> 12; matrix products, arithmetic and copies ran while one was open for 19% -> 14% of each run, Pallas kernels for 0% -> 0%
where the time goes in v10:
time: 212 us; the launch traced here: 211 us
  starting transfers between devices  95.8 us (45%)
  waiting for transfers between devices  65.9 us (31%)
  other arithmetic  18.9 us (9%)
  matrix products  16.8 us (8%)
  local copies, waits for them, and re-layouts  11.4 us (5%)
    ppermute x13, starting transfers between devices, ring_gather(): forward = lax.ppermute(forward, 'req', perm_of(1))  37.8 us
    ppermute x8, starting transfers between devices, ring_gather(): backward = lax.ppermute(backward, 'req', perm_of(-1))  34.9 us
    ppermute x13, waiting for transfers between devices, ring_gather(): forward = lax.ppermute(forward, 'req', perm_of(1))  34 us
    all_to_all x1, waiting for transfers between devices, local(): lax.all_to_all(payload.reshape(models, groups, row_count, payload.shape[2...  15.9 us
    all_to_all x1, waiting for transfers between devices, local(): lax.all_to_all(send, 'req', split_axis=2, concat_axis=2, tiled=True)  11.9 us
    all_to_all x1, starting transfers between devices, local(): lax.all_to_all(send, 'req', split_axis=2, concat_axis=2, tiled=True)  11.4 us
    all_to_all x1, starting transfers between devices, local(): lax.all_to_all(payload.reshape(models, groups, row_count, payload.shape[2...  6.82 us
    dot_general x2, matrix products, head_scores(): jnp.einsum('mnd,mvd->mnv', rows_hidden, head_weight, preferred_element_ty...  6.79 us
  transfers between devices with their start and end apart: 24, of which 12 were waited for; matrix products, arithmetic and copies ran while one was open for 14% of the time, Pallas kernels for 0%

profile of v10, /device:TPU:1, one launch (start us, length us, event | category | flops | bytes accessed | tf_op | source)
XLA Modules:
  0.0 210.6 jit_solution(4471131862630734580)
XLA Ops:
  0.1 4.1 %collective-permute-start.1 = (bf16[2,512,32]{1,2,0:T(8,128)(2,1)}, bf16[2,512,32]{1,2,0:T(8,128)(2,1)S(1)}, u32[]{:S(2)}, u32[]{:S(2)}) collective-permute-start(bf16[2,512,32]{1,2,0:T(8,128)(2,1)} %param.43), channel_id=1, source_target_pairs={{0,16},{8,24},{16,32},{24,40},{32,48},{40,56},{48,0},{56,8},{64,80... | collective-permute-start | bytes 196616 | tf_op jit(solution)/shard_map/ppermute | solution.py:130
  4.2 3.2 %collective-permute-start = (bf16[2,512,32]{1,2,0:T(8,128)(2,1)}, bf16[2,512,32]{1,2,0:T(8,128)(2,1)S(1)}, u32[]{:S(2)}, u32[]{:S(2)}) collective-permute-start(bf16[2,512,32]{1,2,0:T(8,128)(2,1)} %param.43), channel_id=1, source_target_pairs={{0,48},{8,56},{16,0},{24,8},{32,16},{40,24},{48,32},{56,40},{64,11... | collective-permute-start | bytes 196616 | tf_op jit(solution)/shard_map/ppermute | solution.py:133
  7.3 0.8 reduce-window.4
  8.2 0.7 compare_and_fusion
  8.8 0.7 fusion.170
  9.5 0.9 slice_convert_fusion.1
  10.5 0.9 slice_convert_fusion.3
  11.7 0.7 fusion.171
  12.3 0.8 fusion.180
  16.6 0.7 compare_select_fusion.1
  19.4 2.1 collective-permute-start.2
  21.5 1.0 fusion.10
  22.8 2.8 %collective-permute-done.2 = bf16[2,512,32]{1,2,0:T(8,128)(2,1)S(1)} collective-permute-done((bf16[2,512,32]{1,2,0:T(8,128)(2,1)S(1)}, bf16[2,512,32]{1,2,0:T(8,128)(2,1)S(1)}, u32[]{:S(2)}, u32[]{:S(2)}) %collective-permute-start.2) | collective-permute-done | bytes 65568 | tf_op jit(solution)/shard_map/ppermute | solution.py:130
  25.7 4.2 %collective-permute-start.6 = (bf16[4,2,512,32]{2,3,0,1:T(8,128)(2,1)S(1)}, bf16[4,2,512,32]{2,3,0,1:T(8,128)(2,1)S(1)}, u32[]{:S(2)}, u32[]{:S(2)}) collective-permute-start(bf16[4,2,512,32]{2,3,0,1:T(8,128)(2,1)S(1)} %pad_maximum_fusion.2), channel_id=1, source_target_pairs={{0,64},{8,72},{16,80},{24,88},{32,96},{40,104},{48,112},{56,120},{... | collective-permute-start | bytes 786440 | tf_op jit(solution)/shard_map/ppermute | solution.py:130
  29.9 0.7 fusion.12
  30.6 8.6 %collective-permute-start.3 = (bf16[4,2,512,32]{2,3,0,1:T(8,128)(2,1)S(1)}, bf16[4,2,512,32]{2,3,0,1:T(8,128)(2,1)S(1)}, u32[]{:S(2)}, u32[]{:S(2)}) collective-permute-start(bf16[4,2,512,32]{2,3,0,1:T(8,128)(2,1)S(1)} %pad_maximum_fusion.2), channel_id=1, source_target_pairs={{0,448},{8,456},{16,464},{24,472},{32,480},{40,488},{48,496},{56,5... | collective-permute-start | bytes 786440 | tf_op jit(solution)/shard_map/ppermute | solution.py:133
  39.4 1.4 collective-permute-done.6
  40.8 1.9 collective-permute-start.7
  42.9 4.6 %collective-permute-start.4 = (bf16[4,2,512,32]{2,3,0,1:T(8,128)(2,1)S(1)}, bf16[4,2,512,32]{2,3,0,1:T(8,128)(2,1)S(1)}, u32[]{:S(2)}, u32[]{:S(2)}) collective-permute-start(bf16[4,2,512,32]{2,3,0,1:T(8,128)(2,1)S(1)} %collective-permute-done.3), channel_id=1, source_target_pairs={{0,448},{8,456},{16,464},{24,472},{32,480},{40,488},{48,496},{56,5... | collective-permute-start | bytes 786440 | tf_op jit(solution)/shard_map/ppermute | solution.py:133
  47.9 1.2 collective-permute-done.7
  49.1 1.9 collective-permute-start.8
  51.2 4.6 %collective-permute-start.5 = (bf16[4,2,512,32]{2,3,0,1:T(8,128)(2,1)S(1)}, bf16[4,2,512,32]{2,3,0,1:T(8,128)(2,1)S(1)}, u32[]{:S(2)}, u32[]{:S(2)}) collective-permute-start(bf16[4,2,512,32]{2,3,0,1:T(8,128)(2,1)S(1)} %collective-permute-done.4), channel_id=1, source_target_pairs={{0,448},{8,456},{16,464},{24,472},{32,480},{40,488},{48,496},{56,5... | collective-permute-start | bytes 786440 | tf_op jit(solution)/shard_map/ppermute | solution.py:133
  55.8 1.6 collective-permute-done.8
  57.4 1.9 collective-permute-start.9
  59.4 6.3 %collective-permute-done.9 = bf16[4,2,512,32]{2,3,0,1:T(8,128)(2,1)S(1)} collective-permute-done((bf16[4,2,512,32]{2,3,0,1:T(8,128)(2,1)S(1)}, bf16[4,2,512,32]{2,3,0,1:T(8,128)(2,1)S(1)}, u32[]{:S(2)}, u32[]{:S(2)}) %collective-permute-start.9) | collective-permute-done | bytes 262176 | tf_op jit(solution)/shard_map/ppermute | solution.py:130
  65.9 8.5 %collective-permute-start.10 = (bf16[8,4,2,512,32]{3,4,1,0,2:T(8,128)(2,1)S(1)}, bf16[8,4,2,512,32]{3,4,1,0,2:T(8,128)(2,1)}, u32[]{:S(2)}, u32[]{:S(2)}) collective-permute-start(bf16[8,4,2,512,32]{3,4,1,0,2:T(8,128)(2,1)S(1)} %bitcast_dynamic-update-slice_fusion.15), channel_id=1, source_target_pairs={{0,8},{8,0},{16,24},{24,16},{32,40},{40,32},{48,56},{56,48},{64,72... | collective-permute-start | bytes 6291464 | tf_op jit(solution)/shard_map/ppermute | solution.py:130
  74.4 1.0 fusion.9
  76.3 1.0 divide_multiply_fusion.1
  77.6 0.7 gather_fusion
  78.6 1.0 fusion.87
  79.6 0.7 fusion.14
  80.8 2.0 maximum_bitcast_fusion
  82.8 1.6 fusion.2
  84.3 1.6 fusion.1
  85.9 1.6 fusion
  87.5 1.4 convolution_convert_fusion
  89.0 0.9 copy.231
  89.8 6.8 %all-to-all-start = ((bf16[2,8,8,2432]{3,2,0,1:T(8,128)(2,1)}), bf16[2,8,8,2432]{3,2,0,1:T(8,128)(2,1)S(1)}, u32[]{:S(2)}, u32[]{:S(2)}) async-start(bf16[2,8,8,2432]{3,2,0,1:T(8,128)(2,1)} %copy.231), calls=%async_computation | async-start | bytes 1245184 | tf_op jit(solution)/shard_map/all_to_all | solution.py:247
  97.2 0.7 and_reduce_fusion
  98.0 0.8 fusion.167
  98.7 1.3 broadcast_select_fusion.2
  100.0 0.8 scatter.19
  100.9 15.9 %all-to-all-done = bf16[2,8,8,2432]{3,2,0,1:T(8,128)(2,1)S(1)} async-done(((bf16[2,8,8,2432]{3,2,0,1:T(8,128)(2,1)}), bf16[2,8,8,2432]{3,2,0,1:T(8,128)(2,1)S(1)}, u32[]{:S(2)}, u32[]{:S(2)}) %all-to-all-start) | async-done | bytes 622624 | tf_op jit(solution)/shard_map/all_to_all | solution.py:247
  118.0 1.9 collective-permute-start.12
  119.9 4.6 %collective-permute-start.11 = (bf16[17,2048]{1,0:T(8,128)(2,1)S(1)}, bf16[17,2048]{1,0:T(8,128)(2,1)S(1)}, u32[]{:S(2)}, u32[]{:S(2)}) collective-permute-start(bf16[17,2048]{1,0:T(8,128)(2,1)S(1)} %get-tuple-element.69), channel_id=1, source_target_pairs={{0,48},{8,56},{16,0},{24,8},{32,16},{40,24},{48,32},{56,40},{64,11... | collective-permute-start | bytes 208904 | tf_op jit(solution)/shard_map/ppermute | solution.py:133
  125.0 1.9 collective-permute-start.13
  127.0 4.6 %collective-permute-done.13 = bf16[17,2048]{1,0:T(8,128)(2,1)S(1)} collective-permute-done((bf16[17,2048]{1,0:T(8,128)(2,1)S(1)}, bf16[17,2048]{1,0:T(8,128)(2,1)S(1)}, u32[]{:S(2)}, u32[]{:S(2)}) %collective-permute-start.13) | collective-permute-done | bytes 69664 | tf_op jit(solution)/shard_map/ppermute | solution.py:130
  131.7 1.9 collective-permute-start.14
  133.6 3.4 %collective-permute-start.17 = (bf16[4,17,2048]{2,1,0:T(8,128)(2,1)S(1)}, bf16[4,17,2048]{2,1,0:T(8,128)(2,1)S(1)}, u32[]{:S(2)}, u32[]{:S(2)}) collective-permute-start(bf16[4,17,2048]{2,1,0:T(8,128)(2,1)S(1)} %pad_maximum_fusion), channel_id=1, source_target_pairs={{0,64},{8,72},{16,80},{24,88},{32,96},{40,104},{48,112},{56,120},{... | collective-permute-start | bytes 835592 | tf_op jit(solution)/shard_map/ppermute | solution.py:130
  136.9 4.9 %collective-permute-start.21 = (bf16[2,400,2048]{2,1,0:T(8,128)(2,1)}, bf16[2,400,2048]{2,1,0:T(8,128)(2,1)}, u32[]{:S(2)}, u32[]{:S(2)}) collective-permute-start(bf16[2,400,2048]{2,1,0:T(8,128)(2,1)} %param.44), channel_id=1, source_target_pairs={{0,8},{8,0},{16,24},{24,16},{32,40},{40,32},{48,56},{56,48},{64,72... | collective-permute-start | bytes 9830408 | tf_op jit(solution)/shard_map/ppermute | solution.py:192
  142.0 3.1 %collective-permute-start.15 = (bf16[4,17,2048]{2,1,0:T(8,128)(2,1)S(1)}, bf16[4,17,2048]{2,1,0:T(8,128)(2,1)S(1)}, u32[]{:S(2)}, u32[]{:S(2)}) collective-permute-start(bf16[4,17,2048]{2,1,0:T(8,128)(2,1)S(1)} %collective-permute-done.14), channel_id=1, source_target_pairs={{0,448},{8,456},{16,464},{24,472},{32,480},{40,488},{48,496},{56,5... | collective-permute-start | bytes 835592 | tf_op jit(solution)/shard_map/ppermute | solution.py:133
  145.1 2.1 %collective-permute-start.18 = (bf16[4,17,2048]{2,1,0:T(8,128)(2,1)S(1)}, bf16[4,17,2048]{2,1,0:T(8,128)(2,1)S(1)}, u32[]{:S(2)}, u32[]{:S(2)}) collective-permute-start(bf16[4,17,2048]{2,1,0:T(8,128)(2,1)S(1)} %collective-permute-done.17), channel_id=1, source_target_pairs={{0,64},{8,72},{16,80},{24,88},{32,96},{40,104},{48,112},{56,120},{... | collective-permute-start | bytes 835592 | tf_op jit(solution)/shard_map/ppermute | solution.py:130
  147.3 4.0 %collective-permute-done.15 = bf16[4,17,2048]{2,1,0:T(8,128)(2,1)S(1)} collective-permute-done((bf16[4,17,2048]{2,1,0:T(8,128)(2,1)S(1)}, bf16[4,17,2048]{2,1,0:T(8,128)(2,1)S(1)}, u32[]{:S(2)}, u32[]{:S(2)}) %collective-permute-start.15) | collective-permute-done | bytes 278560 | tf_op jit(solution)/shard_map/ppermute | solution.py:133
  151.3 4.3 %collective-permute-start.16 = (bf16[4,17,2048]{2,1,0:T(8,128)(2,1)S(1)}, bf16[4,17,2048]{2,1,0:T(8,128)(2,1)S(1)}, u32[]{:S(2)}, u32[]{:S(2)}) collective-permute-start(bf16[4,17,2048]{2,1,0:T(8,128)(2,1)S(1)} %collective-permute-done.15), channel_id=1, source_target_pairs={{0,448},{8,456},{16,464},{24,472},{32,480},{40,488},{48,496},{56,5... | collective-permute-start | bytes 835592 | tf_op jit(solution)/shard_map/ppermute | solution.py:133
  155.7 1.9 collective-permute-start.19
  157.7 7.8 %collective-permute-done.19 = bf16[4,17,2048]{2,1,0:T(8,128)(2,1)S(1)} collective-permute-done((bf16[4,17,2048]{2,1,0:T(8,128)(2,1)S(1)}, bf16[4,17,2048]{2,1,0:T(8,128)(2,1)S(1)}, u32[]{:S(2)}, u32[]{:S(2)}) %collective-permute-start.19) | collective-permute-done | bytes 278560 | tf_op jit(solution)/shard_map/ppermute | solution.py:130
  165.4 1.9 collective-permute-start.20
  167.4 7.8 %collective-permute-done.20 = bf16[4,17,2048]{2,1,0:T(8,128)(2,1)S(1)} collective-permute-done((bf16[4,17,2048]{2,1,0:T(8,128)(2,1)S(1)}, bf16[4,17,2048]{2,1,0:T(8,128)(2,1)S(1)}, u32[]{:S(2)}, u32[]{:S(2)}) %collective-permute-start.20) | collective-permute-done | bytes 278560 | tf_op jit(solution)/shard_map/ppermute | solution.py:130
  175.3 1.7 copy-done.7
  177.5 3.8 %fusion.188 = (f32[2,256]{1,0:T(2,128)S(1)}, f32[2,256,400]{1,2,0:T(8,128)S(1)}) fusion(bf16[2,400,2048]{2,1,0:T(8,128)(2,1)} %param.44, bf16[32,17,2048]{2,1,0:T(8,128)(2,1)} %bitcast.390), kind=kOutput, calls=%fused_computation.352 | convolution fusion | flops 839065088 | bytes 6195200 | tf_op jit(solution)/shard_map/mnd,mvd->mnv/dot_general | solution.py:115
  181.3 3.0 %fusion.189 = (f32[2,256]{1,0:T(2,128)S(1)}, f32[2,256,400]{1,2,0:T(8,128)S(1)}) fusion(bf16[2,400,2048]{2,1,0:T(8,128)(2,1)} %collective-permute-done.21, bf16[32,17,2048]{2,1,0:T(8,128)(2,1)S(1)} %bitcast.391), kind=kOutput, calls=%fused_computation.353 | convolution fusion | flops 839065088 | bytes 6195200 | tf_op jit(solution)/shard_map/mnd,mvd->mnv/dot_general | solution.py:115
  185.6 0.8 copy.235
  186.4 11.4 %all-to-all-start.1 = ((f32[3,2,64,8]{3,1,0,2:T(2,128)}), f32[3,2,64,8]{3,1,0,2:T(2,128)S(1)}, u32[]{:S(2)}, u32[]{:S(2)}) async-start(f32[3,2,64,8]{3,1,0,2:T(2,128)} %copy.235), calls=%async_computation.1 | async-start | bytes 393216 | tf_op jit(solution)/shard_map/all_to_all | solution.py:318
  197.9 11.9 %all-to-all-done.1 = f32[3,2,64,8]{3,1,0,2:T(2,128)S(1)} async-done(((f32[3,2,64,8]{3,1,0,2:T(2,128)}), f32[3,2,64,8]{3,1,0,2:T(2,128)S(1)}, u32[]{:S(2)}, u32[]{:S(2)}) %all-to-all-start.1) | async-done | bytes 12320 | tf_op jit(solution)/shard_map/all_to_all | solution.py:318
  (230 shorter events, 13.7 us)
Async XLA Ops:
  0.0 18.5 %copy-start.1 = (bf16[2,64,512]{2,1,0:T(8,128)(2,1)S(1)}, bf16[2,64,512]{2,1,0:T(8,128)(2,1)}, u32[]{:S(2)}) copy-start(bf16[2,64,512]{2,1,0:T(8,128)(2,1)} %param.32) | copy-start | bytes 393220
  0.0 15.7 %copy-start.4 = (bf16[2,64,256]{2,1,0:T(8,128)(2,1)S(1)}, bf16[2,64,256]{2,1,0:T(8,128)(2,1)}, u32[]{:S(2)}) copy-start(bf16[2,64,256]{2,1,0:T(8,128)(2,1)} %param.33) | copy-start | bytes 196612
  0.0 14.4 %copy-start.11 = (f32[2,4,512]{2,1,0:T(4,128)S(1)}, f32[2,4,512]{2,1,0:T(4,128)}, u32[]{:S(2)}) copy-start(f32[2,4,512]{2,1,0:T(4,128)} %param.36) | copy-start | bytes 49156
  0.0 15.2 %copy-start.9 = (bf16[2,3,3,256]{3,0,2,1:T(2,128)(2,1)S(1)}, bf16[2,3,3,256]{3,0,2,1:T(2,128)(2,1)}, u32[]{:S(2)}) copy-start(bf16[2,3,3,256]{3,0,2,1:T(2,128)(2,1)} %param.46) | copy-start | bytes 27652
  0.0 15.7 %copy-start.15 = (f32[2,4,256]{2,1,0:T(4,128)S(1)}, f32[2,4,256]{2,1,0:T(4,128)}, u32[]{:S(2)}) copy-start(f32[2,4,256]{2,1,0:T(4,128)} %param.37) | copy-start | bytes 24580
  0.0 16.2 %copy-start.22 = (f32[2,8]{1,0:T(2,128)S(1)}, f32[2,8]{1,0:T(2,128)}, u32[]{:S(2)}) copy-start(f32[2,8]{1,0:T(2,128)} %param.38) | copy-start | bytes 196
  0.0 16.2 %copy-start.21 = (f32[2,8]{1,0:T(2,128)S(1)}, f32[2,8]{1,0:T(2,128)}, u32[]{:S(2)}) copy-start(f32[2,8]{1,0:T(2,128)} %param.39) | copy-start | bytes 196
  0.0 16.2 %copy-start.12 = (bf16[2,64,8]{1,2,0:T(8,128)(2,1)S(1)}, bf16[2,64,8]{1,2,0:T(8,128)(2,1)}, u32[]{:S(2)}) copy-start(bf16[2,64,8]{1,2,0:T(8,128)(2,1)} %param.34) | copy-start | bytes 6148
  0.1 19.4 %collective-permute-start.1 = (bf16[2,512,32]{1,2,0:T(8,128)(2,1)}, bf16[2,512,32]{1,2,0:T(8,128)(2,1)S(1)}, u32[]{:S(2)}, u32[]{:S(2)}) collective-permute-start(bf16[2,512,32]{1,2,0:T(8,128)(2,1)} %param.43), channel_id=1, source_target_pairs={{0,16},{8,24},{16,32},{24,40},{32,48},{40,56},{48,0},{56,8},{64,80... | collective-permute-start | bytes 196616 | tf_op jit(solution)/shard_map/ppermute | solution.py:130
  4.2 18.7 %collective-permute-start = (bf16[2,512,32]{1,2,0:T(8,128)(2,1)}, bf16[2,512,32]{1,2,0:T(8,128)(2,1)S(1)}, u32[]{:S(2)}, u32[]{:S(2)}) collective-permute-start(bf16[2,512,32]{1,2,0:T(8,128)(2,1)} %param.43), channel_id=1, source_target_pairs={{0,48},{8,56},{16,0},{24,8},{32,16},{40,24},{48,32},{56,40},{64,11... | collective-permute-start | bytes 196616 | tf_op jit(solution)/shard_map/ppermute | solution.py:133
  11.4 14.2 %copy-start = (bf16[2,512,32]{1,2,0:T(8,128)(2,1)S(1)}, bf16[2,512,32]{1,2,0:T(8,128)(2,1)}, u32[]{:S(2)}) copy-start(bf16[2,512,32]{1,2,0:T(8,128)(2,1)} %param.43) | copy-start | bytes 196612
  14.4 33.0 %copy-start.25 = (pred[64]{0:T(512)(128)(4,1)}, pred[64]{0:T(512)(128)(4,1)S(1)}, u32[]{:S(2)}) copy-start(pred[64]{0:T(512)(128)(4,1)S(1)} %get-tuple-element.123) | copy-start | bytes 196
  14.4 33.0 %copy-start.27 = (pred[64]{0:T(512)(128)(4,1)}, pred[64]{0:T(512)(128)(4,1)S(1)}, u32[]{:S(2)}) copy-start(pred[64]{0:T(512)(128)(4,1)S(1)} %get-tuple-element.124) | copy-start | bytes 196
  14.5 33.0 %copy-start.29 = (pred[64]{0:T(512)(128)(4,1)}, pred[64]{0:T(512)(128)(4,1)S(1)}, u32[]{:S(2)}) copy-start(pred[64]{0:T(512)(128)(4,1)S(1)} %get-tuple-element.125) | copy-start | bytes 196
  14.5 33.0 %copy-start.31 = (pred[64]{0:T(512)(128)(4,1)}, pred[64]{0:T(512)(128)(4,1)S(1)}, u32[]{:S(2)}) copy-start(pred[64]{0:T(512)(128)(4,1)S(1)} %get-tuple-element.126) | copy-start | bytes 196
  14.5 33.0 %copy-start.33 = (pred[64]{0:T(512)(128)(4,1)}, pred[64]{0:T(512)(128)(4,1)S(1)}, u32[]{:S(2)}) copy-start(pred[64]{0:T(512)(128)(4,1)S(1)} %get-tuple-element.127) | copy-start | bytes 196
  14.5 33.0 %copy-start.35 = (pred[64]{0:T(512)(128)(4,1)}, pred[64]{0:T(512)(128)(4,1)S(1)}, u32[]{:S(2)}) copy-start(pred[64]{0:T(512)(128)(4,1)S(1)} %get-tuple-element.128) | copy-start | bytes 196
  14.5 33.0 %copy-start.37 = (pred[64]{0:T(512)(128)(4,1)}, pred[64]{0:T(512)(128)(4,1)S(1)}, u32[]{:S(2)}) copy-start(pred[64]{0:T(512)(128)(4,1)S(1)} %get-tuple-element.129) | copy-start | bytes 196
  14.5 33.0 %copy-start.39 = (pred[64]{0:T(512)(128)(4,1)}, pred[64]{0:T(512)(128)(4,1)S(1)}, u32[]{:S(2)}) copy-start(pred[64]{0:T(512)(128)(4,1)S(1)} %get-tuple-element.130) | copy-start | bytes 196
  14.5 33.0 %copy-start.41 = (pred[64]{0:T(512)(128)(4,1)}, pred[64]{0:T(512)(128)(4,1)S(1)}, u32[]{:S(2)}) copy-start(pred[64]{0:T(512)(128)(4,1)S(1)} %get-tuple-element.131) | copy-start | bytes 196
  14.5 33.0 %copy-start.43 = (pred[64]{0:T(512)(128)(4,1)}, pred[64]{0:T(512)(128)(4,1)S(1)}, u32[]{:S(2)}) copy-start(pred[64]{0:T(512)(128)(4,1)S(1)} %get-tuple-element.132) | copy-start | bytes 196
  14.5 33.0 %copy-start.45 = (pred[64]{0:T(512)(128)(4,1)}, pred[64]{0:T(512)(128)(4,1)S(1)}, u32[]{:S(2)}) copy-start(pred[64]{0:T(512)(128)(4,1)S(1)} %get-tuple-element.133) | copy-start | bytes 196
  14.6 33.0 %copy-start.47 = (pred[64]{0:T(512)(128)(4,1)}, pred[64]{0:T(512)(128)(4,1)S(1)}, u32[]{:S(2)}) copy-start(pred[64]{0:T(512)(128)(4,1)S(1)} %get-tuple-element.134) | copy-start | bytes 196
  17.7 30.2 %copy-start.16 = (s32[1024]{0:T(1024)}, s32[1024]{0:T(1024)S(1)}, u32[]{:S(2)}) copy-start(s32[1024]{0:T(1024)S(1)} %pad_clamp_fusion) | copy-start | bytes 12292
  19.4 6.2 %collective-permute-start.2 = (bf16[2,512,32]{1,2,0:T(8,128)(2,1)S(1)}, bf16[2,512,32]{1,2,0:T(8,128)(2,1)S(1)}, u32[]{:S(2)}, u32[]{:S(2)}) collective-permute-start(bf16[2,512,32]{1,2,0:T(8,128)(2,1)S(1)} %collective-permute-done.1), channel_id=1, source_target_pairs={{0,16},{8,24},{16,32},{24,40},{32,48},{40,56},{48,0},{56,8},{64,80... | collective-permute-start | bytes 196616 | tf_op jit(solution)/shard_map/ppermute | solution.py:130
  25.7 15.1 %collective-permute-start.6 = (bf16[4,2,512,32]{2,3,0,1:T(8,128)(2,1)S(1)}, bf16[4,2,512,32]{2,3,0,1:T(8,128)(2,1)S(1)}, u32[]{:S(2)}, u32[]{:S(2)}) collective-permute-start(bf16[4,2,512,32]{2,3,0,1:T(8,128)(2,1)S(1)} %pad_maximum_fusion.2), channel_id=1, source_target_pairs={{0,64},{8,72},{16,80},{24,88},{32,96},{40,104},{48,112},{56,120},{... | collective-permute-start | bytes 786440 | tf_op jit(solution)/shard_map/ppermute | solution.py:130
  29.9 44.5 %copy-start.50 = (bf16[2,3,512,128]{3,2,1,0:T(8,128)(2,1)S(1)}, bf16[2,3,512,128]{3,2,1,0:T(8,128)(2,1)}, u32[]{:S(2)}) copy-start(bf16[2,3,512,128]{3,2,1,0:T(8,128)(2,1)} %param.47) | copy-start | bytes 2359300
  30.6 12.3 %collective-permute-start.3 = (bf16[4,2,512,32]{2,3,0,1:T(8,128)(2,1)S(1)}, bf16[4,2,512,32]{2,3,0,1:T(8,128)(2,1)S(1)}, u32[]{:S(2)}, u32[]{:S(2)}) collective-permute-start(bf16[4,2,512,32]{2,3,0,1:T(8,128)(2,1)S(1)} %pad_maximum_fusion.2), channel_id=1, source_target_pairs={{0,448},{8,456},{16,464},{24,472},{32,480},{40,488},{48,496},{56,5... | collective-permute-start | bytes 786440 | tf_op jit(solution)/shard_map/ppermute | solution.py:133
  40.8 8.3 %collective-permute-start.7 = (bf16[4,2,512,32]{2,3,0,1:T(8,128)(2,1)S(1)}, bf16[4,2,512,32]{2,3,0,1:T(8,128)(2,1)S(1)}, u32[]{:S(2)}, u32[]{:S(2)}) collective-permute-start(bf16[4,2,512,32]{2,3,0,1:T(8,128)(2,1)S(1)} %collective-permute-done.6), channel_id=1, source_target_pairs={{0,64},{8,72},{16,80},{24,88},{32,96},{40,104},{48,112},{56,120},{... | collective-permute-start | bytes 786440 | tf_op jit(solution)/shard_map/ppermute | solution.py:130
  42.9 8.3 %collective-permute-start.4 = (bf16[4,2,512,32]{2,3,0,1:T(8,128)(2,1)S(1)}, bf16[4,2,512,32]{2,3,0,1:T(8,128)(2,1)S(1)}, u32[]{:S(2)}, u32[]{:S(2)}) collective-permute-start(bf16[4,2,512,32]{2,3,0,1:T(8,128)(2,1)S(1)} %collective-permute-done.3), channel_id=1, source_target_pairs={{0,448},{8,456},{16,464},{24,472},{32,480},{40,488},{48,496},{56,5... | collective-permute-start | bytes 786440 | tf_op jit(solution)/shard_map/ppermute | solution.py:133
  47.9 26.5 %copy-start.6 = (f32[64,256]{1,0:T(8,128)}, f32[64,256]{1,0:T(8,128)S(1)}, u32[]{:S(2)}) copy-start(f32[64,256]{1,0:T(8,128)S(1)} %divide_multiply_fusion.3) | copy-start | bytes 196612
  49.1 8.3 %collective-permute-start.8 = (bf16[4,2,512,32]{2,3,0,1:T(8,128)(2,1)S(1)}, bf16[4,2,512,32]{2,3,0,1:T(8,128)(2,1)S(1)}, u32[]{:S(2)}, u32[]{:S(2)}) collective-permute-start(bf16[4,2,512,32]{2,3,0,1:T(8,128)(2,1)S(1)} %collective-permute-done.7), channel_id=1, source_target_pairs={{0,64},{8,72},{16,80},{24,88},{32,96},{40,104},{48,112},{56,120},{... | collective-permute-start | bytes 786440 | tf_op jit(solution)/shard_map/ppermute | solution.py:130
  51.0 25.2 %copy-start.26 = (pred[64]{0:T(512)(128)(4,1)S(1)}, pred[64]{0:T(512)(128)(4,1)}, u32[]{:S(2)}) copy-start(pred[64]{0:T(512)(128)(4,1)} %copy-done.25) | copy-start | bytes 196
  51.0 25.2 %copy-start.28 = (pred[64]{0:T(512)(128)(4,1)S(1)}, pred[64]{0:T(512)(128)(4,1)}, u32[]{:S(2)}) copy-start(pred[64]{0:T(512)(128)(4,1)} %copy-done.27) | copy-start | bytes 196
  51.1 25.2 %copy-start.30 = (pred[64]{0:T(512)(128)(4,1)S(1)}, pred[64]{0:T(512)(128)(4,1)}, u32[]{:S(2)}) copy-start(pred[64]{0:T(512)(128)(4,1)} %copy-done.29) | copy-start | bytes 196
  51.1 25.2 %copy-start.32 = (pred[64]{0:T(512)(128)(4,1)S(1)}, pred[64]{0:T(512)(128)(4,1)}, u32[]{:S(2)}) copy-start(pred[64]{0:T(512)(128)(4,1)} %copy-done.31) | copy-start | bytes 196
  51.1 25.2 %copy-start.34 = (pred[64]{0:T(512)(128)(4,1)S(1)}, pred[64]{0:T(512)(128)(4,1)}, u32[]{:S(2)}) copy-start(pred[64]{0:T(512)(128)(4,1)} %copy-done.33) | copy-start | bytes 196
  51.1 25.2 %copy-start.36 = (pred[64]{0:T(512)(128)(4,1)S(1)}, pred[64]{0:T(512)(128)(4,1)}, u32[]{:S(2)}) copy-start(pred[64]{0:T(512)(128)(4,1)} %copy-done.35) | copy-start | bytes 196
  51.1 25.2 %copy-start.38 = (pred[64]{0:T(512)(128)(4,1)S(1)}, pred[64]{0:T(512)(128)(4,1)}, u32[]{:S(2)}) copy-start(pred[64]{0:T(512)(128)(4,1)} %copy-done.37) | copy-start | bytes 196
  51.1 25.2 %copy-start.40 = (pred[64]{0:T(512)(128)(4,1)S(1)}, pred[64]{0:T(512)(128)(4,1)}, u32[]{:S(2)}) copy-start(pred[64]{0:T(512)(128)(4,1)} %copy-done.39) | copy-start | bytes 196
  51.1 25.2 %copy-start.42 = (pred[64]{0:T(512)(128)(4,1)S(1)}, pred[64]{0:T(512)(128)(4,1)}, u32[]{:S(2)}) copy-start(pred[64]{0:T(512)(128)(4,1)} %copy-done.41) | copy-start | bytes 196
  51.1 25.2 %copy-start.44 = (pred[64]{0:T(512)(128)(4,1)S(1)}, pred[64]{0:T(512)(128)(4,1)}, u32[]{:S(2)}) copy-start(pred[64]{0:T(512)(128)(4,1)} %copy-done.43) | copy-start | bytes 196
  51.1 25.2 %copy-start.46 = (pred[64]{0:T(512)(128)(4,1)S(1)}, pred[64]{0:T(512)(128)(4,1)}, u32[]{:S(2)}) copy-start(pred[64]{0:T(512)(128)(4,1)} %copy-done.45) | copy-start | bytes 196
  51.1 25.2 %copy-start.48 = (pred[64]{0:T(512)(128)(4,1)S(1)}, pred[64]{0:T(512)(128)(4,1)}, u32[]{:S(2)}) copy-start(pred[64]{0:T(512)(128)(4,1)} %copy-done.47) | copy-start | bytes 196
  51.2 8.2 %collective-permute-start.5 = (bf16[4,2,512,32]{2,3,0,1:T(8,128)(2,1)S(1)}, bf16[4,2,512,32]{2,3,0,1:T(8,128)(2,1)S(1)}, u32[]{:S(2)}, u32[]{:S(2)}) collective-permute-start(bf16[4,2,512,32]{2,3,0,1:T(8,128)(2,1)S(1)} %collective-permute-done.4), channel_id=1, source_target_pairs={{0,448},{8,456},{16,464},{24,472},{32,480},{40,488},{48,496},{56,5... | collective-permute-start | bytes 786440 | tf_op jit(solution)/shard_map/ppermute | solution.py:133
  57.4 8.3 %collective-permute-start.9 = (bf16[4,2,512,32]{2,3,0,1:T(8,128)(2,1)S(1)}, bf16[4,2,512,32]{2,3,0,1:T(8,128)(2,1)S(1)}, u32[]{:S(2)}, u32[]{:S(2)}) collective-permute-start(bf16[4,2,512,32]{2,3,0,1:T(8,128)(2,1)S(1)} %collective-permute-done.8), channel_id=1, source_target_pairs={{0,64},{8,72},{16,80},{24,88},{32,96},{40,104},{48,112},{56,120},{... | collective-permute-start | bytes 786440 | tf_op jit(solution)/shard_map/ppermute | solution.py:130
  65.8 13.8 %copy-start.10 = (f32[64,8]{0,1:T(8,128)S(1)}, f32[64,8]{0,1:T(8,128)}, u32[]{:S(2)}) copy-start(f32[64,8]{0,1:T(8,128)} %get-tuple-element.104) | copy-start | bytes 6148
  65.8 13.8 %copy-start.19 = (f32[8]{0:T(128)S(1)}, f32[8]{0:T(128)}, u32[]{:S(2)}) copy-start(f32[8]{0:T(128)} %get-tuple-element.115) | copy-start | bytes 100
  65.8 14.5 %copy-start.2 = (bf16[2,64,512]{2,1,0:T(8,128)(2,1)S(1)}, bf16[2,64,512]{2,1,0:T(8,128)(2,1)}, u32[]{:S(2)}) copy-start(bf16[2,64,512]{2,1,0:T(8,128)(2,1)} %param.31) | copy-start | bytes 393220
  65.9 14.9 %collective-permute-start.10 = (bf16[8,4,2,512,32]{3,4,1,0,2:T(8,128)(2,1)S(1)}, bf16[8,4,2,512,32]{3,4,1,0,2:T(8,128)(2,1)}, u32[]{:S(2)}, u32[]{:S(2)}) collective-permute-start(bf16[8,4,2,512,32]{3,4,1,0,2:T(8,128)(2,1)S(1)} %bitcast_dynamic-update-slice_fusion.15), channel_id=1, source_target_pairs={{0,8},{8,0},{16,24},{24,16},{32,40},{40,32},{48,56},{56,48},{64,72... | collective-permute-start | bytes 6291464 | tf_op jit(solution)/shard_map/ppermute | solution.py:130
  89.0 28.9 %copy-start.14 = (f32[2,2048]{1,0:T(2,128)S(1)}, f32[2,2048]{1,0:T(2,128)}, u32[]{:S(2)}) copy-start(f32[2,2048]{1,0:T(2,128)} %param.42) | copy-start | bytes 49156
  89.8 27.0 %all-to-all-start = ((bf16[2,8,8,2432]{3,2,0,1:T(8,128)(2,1)}), bf16[2,8,8,2432]{3,2,0,1:T(8,128)(2,1)S(1)}, u32[]{:S(2)}, u32[]{:S(2)}) async-start(bf16[2,8,8,2432]{3,2,0,1:T(8,128)(2,1)} %copy.231), calls=%async_computation | async-start | bytes 1245184 | tf_op jit(solution)/shard_map/all_to_all | solution.py:247
  118.0 7.0 %collective-permute-start.12 = (bf16[17,2048]{1,0:T(8,128)(2,1)S(1)}, bf16[17,2048]{1,0:T(8,128)(2,1)S(1)}, u32[]{:S(2)}, u32[]{:S(2)}) collective-permute-start(bf16[17,2048]{1,0:T(8,128)(2,1)S(1)} %get-tuple-element.69), channel_id=1, source_target_pairs={{0,16},{8,24},{16,32},{24,40},{32,48},{40,56},{48,0},{56,8},{64,80... | collective-permute-start | bytes 208904 | tf_op jit(solution)/shard_map/ppermute | solution.py:130
  119.9 7.0 %collective-permute-start.11 = (bf16[17,2048]{1,0:T(8,128)(2,1)S(1)}, bf16[17,2048]{1,0:T(8,128)(2,1)S(1)}, u32[]{:S(2)}, u32[]{:S(2)}) collective-permute-start(bf16[17,2048]{1,0:T(8,128)(2,1)S(1)} %get-tuple-element.69), channel_id=1, source_target_pairs={{0,48},{8,56},{16,0},{24,8},{32,16},{40,24},{48,32},{56,40},{64,11... | collective-permute-start | bytes 208904 | tf_op jit(solution)/shard_map/ppermute | solution.py:133
  125.0 6.6 %collective-permute-start.13 = (bf16[17,2048]{1,0:T(8,128)(2,1)S(1)}, bf16[17,2048]{1,0:T(8,128)(2,1)S(1)}, u32[]{:S(2)}, u32[]{:S(2)}) collective-permute-start(bf16[17,2048]{1,0:T(8,128)(2,1)S(1)} %collective-permute-done.12), channel_id=1, source_target_pairs={{0,16},{8,24},{16,32},{24,40},{32,48},{40,56},{48,0},{56,8},{64,80... | collective-permute-start | bytes 208904 | tf_op jit(solution)/shard_map/ppermute | solution.py:130
  131.7 10.3 %collective-permute-start.14 = (bf16[4,17,2048]{2,1,0:T(8,128)(2,1)S(1)}, bf16[4,17,2048]{2,1,0:T(8,128)(2,1)S(1)}, u32[]{:S(2)}, u32[]{:S(2)}) collective-permute-start(bf16[4,17,2048]{2,1,0:T(8,128)(2,1)S(1)} %pad_maximum_fusion), channel_id=1, source_target_pairs={{0,448},{8,456},{16,464},{24,472},{32,480},{40,488},{48,496},{56,5... | collective-permute-start | bytes 835592 | tf_op jit(solution)/shard_map/ppermute | solution.py:133
  133.6 11.5 %collective-permute-start.17 = (bf16[4,17,2048]{2,1,0:T(8,128)(2,1)S(1)}, bf16[4,17,2048]{2,1,0:T(8,128)(2,1)S(1)}, u32[]{:S(2)}, u32[]{:S(2)}) collective-permute-start(bf16[4,17,2048]{2,1,0:T(8,128)(2,1)S(1)} %pad_maximum_fusion), channel_id=1, source_target_pairs={{0,64},{8,72},{16,80},{24,88},{32,96},{40,104},{48,112},{56,120},{... | collective-permute-start | bytes 835592 | tf_op jit(solution)/shard_map/ppermute | solution.py:130
  136.9 44.3 %collective-permute-start.21 = (bf16[2,400,2048]{2,1,0:T(8,128)(2,1)}, bf16[2,400,2048]{2,1,0:T(8,128)(2,1)}, u32[]{:S(2)}, u32[]{:S(2)}) collective-permute-start(bf16[2,400,2048]{2,1,0:T(8,128)(2,1)} %param.44), channel_id=1, source_target_pairs={{0,8},{8,0},{16,24},{24,16},{32,40},{40,32},{48,56},{56,48},{64,72... | collective-permute-start | bytes 9830408 | tf_op jit(solution)/shard_map/ppermute | solution.py:192
  142.0 9.4 %collective-permute-start.15 = (bf16[4,17,2048]{2,1,0:T(8,128)(2,1)S(1)}, bf16[4,17,2048]{2,1,0:T(8,128)(2,1)S(1)}, u32[]{:S(2)}, u32[]{:S(2)}) collective-permute-start(bf16[4,17,2048]{2,1,0:T(8,128)(2,1)S(1)} %collective-permute-done.14), channel_id=1, source_target_pairs={{0,448},{8,456},{16,464},{24,472},{32,480},{40,488},{48,496},{56,5... | collective-permute-start | bytes 835592 | tf_op jit(solution)/shard_map/ppermute | solution.py:133
  145.1 10.6 %collective-permute-start.18 = (bf16[4,17,2048]{2,1,0:T(8,128)(2,1)S(1)}, bf16[4,17,2048]{2,1,0:T(8,128)(2,1)S(1)}, u32[]{:S(2)}, u32[]{:S(2)}) collective-permute-start(bf16[4,17,2048]{2,1,0:T(8,128)(2,1)S(1)} %collective-permute-done.17), channel_id=1, source_target_pairs={{0,64},{8,72},{16,80},{24,88},{32,96},{40,104},{48,112},{56,120},{... | collective-permute-start | bytes 835592 | tf_op jit(solution)/shard_map/ppermute | solution.py:130
  151.3 16.0 %collective-permute-start.16 = (bf16[4,17,2048]{2,1,0:T(8,128)(2,1)S(1)}, bf16[4,17,2048]{2,1,0:T(8,128)(2,1)S(1)}, u32[]{:S(2)}, u32[]{:S(2)}) collective-permute-start(bf16[4,17,2048]{2,1,0:T(8,128)(2,1)S(1)} %collective-permute-done.15), channel_id=1, source_target_pairs={{0,448},{8,456},{16,464},{24,472},{32,480},{40,488},{48,496},{56,5... | collective-permute-start | bytes 835592 | tf_op jit(solution)/shard_map/ppermute | solution.py:133
  155.7 9.7 %collective-permute-start.19 = (bf16[4,17,2048]{2,1,0:T(8,128)(2,1)S(1)}, bf16[4,17,2048]{2,1,0:T(8,128)(2,1)S(1)}, u32[]{:S(2)}, u32[]{:S(2)}) collective-permute-start(bf16[4,17,2048]{2,1,0:T(8,128)(2,1)S(1)} %collective-permute-done.18), channel_id=1, source_target_pairs={{0,64},{8,72},{16,80},{24,88},{32,96},{40,104},{48,112},{56,120},{... | collective-permute-start | bytes 835592 | tf_op jit(solution)/shard_map/ppermute | solution.py:130
  165.4 9.7 %collective-permute-start.20 = (bf16[4,17,2048]{2,1,0:T(8,128)(2,1)S(1)}, bf16[4,17,2048]{2,1,0:T(8,128)(2,1)S(1)}, u32[]{:S(2)}, u32[]{:S(2)}) collective-permute-start(bf16[4,17,2048]{2,1,0:T(8,128)(2,1)S(1)} %collective-permute-done.19), channel_id=1, source_target_pairs={{0,64},{8,72},{16,80},{24,88},{32,96},{40,104},{48,112},{56,120},{... | collective-permute-start | bytes 835592 | tf_op jit(solution)/shard_map/ppermute | solution.py:130
  186.4 23.4 %all-to-all-start.1 = ((f32[3,2,64,8]{3,1,0,2:T(2,128)}), f32[3,2,64,8]{3,1,0,2:T(2,128)S(1)}, u32[]{:S(2)}, u32[]{:S(2)}) async-start(f32[3,2,64,8]{3,1,0,2:T(2,128)} %copy.235), calls=%async_computation.1 | async-start | bytes 393216 | tf_op jit(solution)/shard_map/all_to_all | solution.py:318
  (12 other events, 90.2 us)

commit v11 on v10

--- a/solution.py
+++ b/solution.py
@@ -4,7 +4,7 @@
 from jax.sharding import PartitionSpec as P
 
 EPSILON = 1e-05
-PRECISE = lax.Precision.HIGHEST
+PRECISE = lax.Precision.HIGH
 
 
 def merged_2(part, axis, combine):
@@ -279,7 +279,7 @@
     target_row = target_row.at[0, row_count : 2 * row_count].set(low_digit)
     packet = jnp.concatenate([final_rows.reshape(models * row_count, full_width), target_row], axis=0)
 
-    every = ring_gather(ring_gather(packet, along_x, ROWS_X), along_z, chips_z)
+    every = ring_gather(ring_gather(packet, along_z, chips_z), along_x, ROWS_X)
     peers = ROWS_X * chips_z
     every = every.reshape(peers, models * row_count + 1, full_width)
     every_rows = (
@@ -303,7 +303,7 @@
         jnp.exp(other_logits - peak_logit[:, :, None]), axis=2
     )
     statistics = jnp.stack([peak_logit, spread, own_picked + other_picked])
-    statistics = statistics.reshape(3, models, chips_z, ROWS_X, row_count)
+    statistics = statistics.reshape(3, models, ROWS_X, chips_z, row_count).transpose(0, 1, 3, 2, 4)
     statistics = jnp.roll(jnp.roll(statistics, z_index, axis=2), x_index, axis=3)
     neutral = jnp.stack(
         [

time: 212 us -> 205 us (0.967)
    ppermute x13, waiting for transfers between devices: 34 us -> 37.9 us  [ring_gather(): forward = lax.ppermute(forward, 'req', perm_of(1))]
    ppermute x8, waiting for transfers between devices: 4.07 us -> 0.49 us  [ring_gather(): backward = lax.ppermute(backward, 'req', perm_of(-1))]
    ppermute x1, starting transfers between devices: 4.93 us -> 2.19 us  [local(): lax.ppermute(head_weight, 'req', [(i, i ^ 1) for i in range(shards)])]
    all_to_all x1, waiting for transfers between devices: 15.9 us -> 13.8 us  [local(): lax.all_to_all(payload.reshape(models, groups, row_count, payload.shape[2...]
where the time goes in v11:
time: 205 us; the launch traced here: 204 us
  starting transfers between devices  93.8 us (46%)
  waiting for transfers between devices  64.2 us (31%)
  other arithmetic  18.3 us (9%)
  matrix products  15.1 us (7%)
  local copies, waits for them, and re-layouts  10.8 us (5%)
    ppermute x13, waiting for transfers between devices, ring_gather(): forward = lax.ppermute(forward, 'req', perm_of(1))  37.9 us
    ppermute x13, starting transfers between devices, ring_gather(): forward = lax.ppermute(forward, 'req', perm_of(1))  37.6 us
    ppermute x8, starting transfers between devices, ring_gather(): backward = lax.ppermute(backward, 'req', perm_of(-1))  35.6 us
    all_to_all x1, waiting for transfers between devices, local(): lax.all_to_all(payload.reshape(models, groups, row_count, payload.shape[2...  13.8 us
    all_to_all x1, waiting for transfers between devices, local(): lax.all_to_all(send, 'req', split_axis=2, concat_axis=2, tiled=True)  11.9 us
    all_to_all x1, starting transfers between devices, local(): lax.all_to_all(send, 'req', split_axis=2, concat_axis=2, tiled=True)  11.6 us
    dot_general x2, matrix products, head_scores(): jnp.einsum('mnd,mvd->mnv', rows_hidden, head_weight, preferred_element_ty...  6.92 us
    all_to_all x1, starting transfers between devices, local(): lax.all_to_all(payload.reshape(models, groups, row_count, payload.shape[2...  6.82 us
  transfers between devices with their start and end apart: 24, of which 12 were waited for; matrix products, arithmetic and copies ran while one was open for 14% of the time, Pallas kernels for 0%

profile of v11, /device:TPU:1, one launch (start us, length us, event | category | flops | bytes accessed | tf_op | source)
XLA Modules:
  0.0 203.5 jit_solution(4992230631525311841)
XLA Ops:
  0.1 4.1 %collective-permute-start.1 = (bf16[2,512,32]{1,2,0:T(8,128)(2,1)}, bf16[2,512,32]{1,2,0:T(8,128)(2,1)S(1)}, u32[]{:S(2)}, u32[]{:S(2)}) collective-permute-start(bf16[2,512,32]{1,2,0:T(8,128)(2,1)} %param.43), channel_id=1, source_target_pairs={{0,16},{8,24},{16,32},{24,40},{32,48},{40,56},{48,0},{56,8},{64,80... | collective-permute-start | bytes 196616 | tf_op jit(solution)/shard_map/ppermute | solution.py:130
  4.2 3.2 %collective-permute-start = (bf16[2,512,32]{1,2,0:T(8,128)(2,1)}, bf16[2,512,32]{1,2,0:T(8,128)(2,1)S(1)}, u32[]{:S(2)}, u32[]{:S(2)}) collective-permute-start(bf16[2,512,32]{1,2,0:T(8,128)(2,1)} %param.43), channel_id=1, source_target_pairs={{0,48},{8,56},{16,0},{24,8},{32,16},{40,24},{48,32},{56,40},{64,11... | collective-permute-start | bytes 196616 | tf_op jit(solution)/shard_map/ppermute | solution.py:133
  7.3 0.8 reduce-window.4
  8.2 0.7 compare_and_fusion
  8.8 0.7 fusion.166
  9.5 0.9 slice_convert_fusion.1
  10.5 0.9 slice_convert_fusion.3
  11.7 0.7 fusion.167
  12.3 0.8 fusion.175
  15.8 0.6 gather_fusion.1
  17.0 2.1 %collective-permute-start.2 = (bf16[2,512,32]{1,2,0:T(8,128)(2,1)S(1)}, bf16[2,512,32]{1,2,0:T(8,128)(2,1)S(1)}, u32[]{:S(2)}, u32[]{:S(2)}) collective-permute-start(bf16[2,512,32]{1,2,0:T(8,128)(2,1)S(1)} %collective-permute-done.1), channel_id=1, source_target_pairs={{0,16},{8,24},{16,32},{24,40},{32,48},{40,56},{48,0},{56,8},{64,80... | collective-permute-start | bytes 196616 | tf_op jit(solution)/shard_map/ppermute | solution.py:130
  19.1 0.6 fusion.10
  20.0 3.2 %collective-permute-done.2 = bf16[2,512,32]{1,2,0:T(8,128)(2,1)S(1)} collective-permute-done((bf16[2,512,32]{1,2,0:T(8,128)(2,1)S(1)}, bf16[2,512,32]{1,2,0:T(8,128)(2,1)S(1)}, u32[]{:S(2)}, u32[]{:S(2)}) %collective-permute-start.2) | collective-permute-done | bytes 65568 | tf_op jit(solution)/shard_map/ppermute | solution.py:130
  23.3 4.2 %collective-permute-start.6 = (bf16[4,2,512,32]{2,3,0,1:T(8,128)(2,1)S(1)}, bf16[4,2,512,32]{2,3,0,1:T(8,128)(2,1)S(1)}, u32[]{:S(2)}, u32[]{:S(2)}) collective-permute-start(bf16[4,2,512,32]{2,3,0,1:T(8,128)(2,1)S(1)} %pad_maximum_fusion.2), channel_id=1, source_target_pairs={{0,64},{8,72},{16,80},{24,88},{32,96},{40,104},{48,112},{56,120},{... | collective-permute-start | bytes 786440 | tf_op jit(solution)/shard_map/ppermute | solution.py:130
  27.9 8.6 %collective-permute-start.3 = (bf16[4,2,512,32]{2,3,0,1:T(8,128)(2,1)S(1)}, bf16[4,2,512,32]{2,3,0,1:T(8,128)(2,1)S(1)}, u32[]{:S(2)}, u32[]{:S(2)}) collective-permute-start(bf16[4,2,512,32]{2,3,0,1:T(8,128)(2,1)S(1)} %pad_maximum_fusion.2), channel_id=1, source_target_pairs={{0,448},{8,456},{16,464},{24,472},{32,480},{40,488},{48,496},{56,5... | collective-permute-start | bytes 786440 | tf_op jit(solution)/shard_map/ppermute | solution.py:133
  36.7 1.6 collective-permute-done.6
  38.3 1.9 collective-permute-start.7
  40.5 4.6 %collective-permute-start.4 = (bf16[4,2,512,32]{2,3,0,1:T(8,128)(2,1)S(1)}, bf16[4,2,512,32]{2,3,0,1:T(8,128)(2,1)S(1)}, u32[]{:S(2)}, u32[]{:S(2)}) collective-permute-start(bf16[4,2,512,32]{2,3,0,1:T(8,128)(2,1)S(1)} %collective-permute-done.3), channel_id=1, source_target_pairs={{0,448},{8,456},{16,464},{24,472},{32,480},{40,488},{48,496},{56,5... | collective-permute-start | bytes 786440 | tf_op jit(solution)/shard_map/ppermute | solution.py:133
  45.4 1.2 collective-permute-done.7
  46.7 1.9 collective-permute-start.8
  48.6 4.8 %collective-permute-start.5 = (bf16[4,2,512,32]{2,3,0,1:T(8,128)(2,1)S(1)}, bf16[4,2,512,32]{2,3,0,1:T(8,128)(2,1)S(1)}, u32[]{:S(2)}, u32[]{:S(2)}) collective-permute-start(bf16[4,2,512,32]{2,3,0,1:T(8,128)(2,1)S(1)} %collective-permute-done.4), channel_id=1, source_target_pairs={{0,448},{8,456},{16,464},{24,472},{32,480},{40,488},{48,496},{56,5... | collective-permute-start | bytes 786440 | tf_op jit(solution)/shard_map/ppermute | solution.py:133
  53.4 1.6 collective-permute-done.8
  55.0 1.9 collective-permute-start.9
  57.0 6.3 %collective-permute-done.9 = bf16[4,2,512,32]{2,3,0,1:T(8,128)(2,1)S(1)} collective-permute-done((bf16[4,2,512,32]{2,3,0,1:T(8,128)(2,1)S(1)}, bf16[4,2,512,32]{2,3,0,1:T(8,128)(2,1)S(1)}, u32[]{:S(2)}, u32[]{:S(2)}) %collective-permute-start.9) | collective-permute-done | bytes 262176 | tf_op jit(solution)/shard_map/ppermute | solution.py:130
  63.4 8.4 %collective-permute-start.10 = (bf16[8,4,2,512,32]{3,4,1,0,2:T(8,128)(2,1)S(1)}, bf16[8,4,2,512,32]{3,4,1,0,2:T(8,128)(2,1)}, u32[]{:S(2)}, u32[]{:S(2)}) collective-permute-start(bf16[8,4,2,512,32]{3,4,1,0,2:T(8,128)(2,1)S(1)} %bitcast_dynamic-update-slice_fusion.7), channel_id=1, source_target_pairs={{0,8},{8,0},{16,24},{24,16},{32,40},{40,32},{48,56},{56,48},{64,72... | collective-permute-start | bytes 6291464 | tf_op jit(solution)/shard_map/ppermute | solution.py:130
  72.8 1.6 fusion.9
  74.7 0.6 gather_fusion
  76.6 2.0 maximum_bitcast_fusion
  78.6 1.6 fusion.2
  80.2 1.6 fusion.1
  81.8 1.6 fusion
  83.4 1.4 convolution_convert_fusion
  84.8 0.9 copy.283
  85.7 6.8 %all-to-all-start = ((bf16[2,8,8,2432]{3,2,0,1:T(8,128)(2,1)}), bf16[2,8,8,2432]{3,2,0,1:T(8,128)(2,1)S(1)}, u32[]{:S(2)}, u32[]{:S(2)}) async-start(bf16[2,8,8,2432]{3,2,0,1:T(8,128)(2,1)} %copy.283), calls=%async_computation | async-start | bytes 1245184 | tf_op jit(solution)/shard_map/all_to_all | solution.py:247
  92.5 2.2 %collective-permute-start.21 = (bf16[2,400,2048]{2,1,0:T(8,128)(2,1)}, bf16[2,400,2048]{2,1,0:T(8,128)(2,1)}, u32[]{:S(2)}, u32[]{:S(2)}) collective-permute-start(bf16[2,400,2048]{2,1,0:T(8,128)(2,1)} %param.44), channel_id=1, source_target_pairs={{0,8},{8,0},{16,24},{24,16},{32,40},{40,32},{48,56},{56,48},{64,72... | collective-permute-start | bytes 9830408 | tf_op jit(solution)/shard_map/ppermute | solution.py:192
  94.7 0.6 slice.454
  95.4 0.6 and_reduce_fusion
  96.0 0.6 fusion.163
  96.7 1.3 broadcast_select_fusion
  98.0 0.9 scatter.19
  98.9 13.8 %all-to-all-done = bf16[2,8,8,2432]{3,2,0,1:T(8,128)(2,1)S(1)} async-done(((bf16[2,8,8,2432]{3,2,0,1:T(8,128)(2,1)}), bf16[2,8,8,2432]{3,2,0,1:T(8,128)(2,1)S(1)}, u32[]{:S(2)}, u32[]{:S(2)}) %all-to-all-start) | async-done | bytes 622624 | tf_op jit(solution)/shard_map/all_to_all | solution.py:247
  113.9 1.9 collective-permute-start.11
  115.8 3.4 %collective-permute-start.14 = (bf16[17,2048]{1,0:T(8,128)(2,1)S(1)}, bf16[17,2048]{1,0:T(8,128)(2,1)S(1)}, u32[]{:S(2)}, u32[]{:S(2)}) collective-permute-start(bf16[17,2048]{1,0:T(8,128)(2,1)S(1)} %pad_maximum_fusion.4), channel_id=1, source_target_pairs={{0,64},{8,72},{16,80},{24,88},{32,96},{40,104},{48,112},{56,120},{... | collective-permute-start | bytes 208904 | tf_op jit(solution)/shard_map/ppermute | solution.py:130
  119.2 0.5 collective-permute-done.11
  119.7 3.4 %collective-permute-start.12 = (bf16[17,2048]{1,0:T(8,128)(2,1)S(1)}, bf16[17,2048]{1,0:T(8,128)(2,1)S(1)}, u32[]{:S(2)}, u32[]{:S(2)}) collective-permute-start(bf16[17,2048]{1,0:T(8,128)(2,1)S(1)} %collective-permute-done.11), channel_id=1, source_target_pairs={{0,448},{8,456},{16,464},{24,472},{32,480},{40,488},{48,496},{56,5... | collective-permute-start | bytes 208904 | tf_op jit(solution)/shard_map/ppermute | solution.py:133
  123.1 1.9 collective-permute-start.15
  125.1 4.6 %collective-permute-start.13 = (bf16[17,2048]{1,0:T(8,128)(2,1)S(1)}, bf16[17,2048]{1,0:T(8,128)(2,1)S(1)}, u32[]{:S(2)}, u32[]{:S(2)}) collective-permute-start(bf16[17,2048]{1,0:T(8,128)(2,1)S(1)} %collective-permute-done.12), channel_id=1, source_target_pairs={{0,448},{8,456},{16,464},{24,472},{32,480},{40,488},{48,496},{56,5... | collective-permute-start | bytes 208904 | tf_op jit(solution)/shard_map/ppermute | solution.py:133
  129.7 1.9 collective-permute-start.16
  131.6 4.6 %collective-permute-done.16 = bf16[17,2048]{1,0:T(8,128)(2,1)S(1)} collective-permute-done((bf16[17,2048]{1,0:T(8,128)(2,1)S(1)}, bf16[17,2048]{1,0:T(8,128)(2,1)S(1)}, u32[]{:S(2)}, u32[]{:S(2)}) %collective-permute-start.16) | collective-permute-done | bytes 69664 | tf_op jit(solution)/shard_map/ppermute | solution.py:130
  136.2 2.1 %collective-permute-start.17 = (bf16[17,2048]{1,0:T(8,128)(2,1)S(1)}, bf16[17,2048]{1,0:T(8,128)(2,1)S(1)}, u32[]{:S(2)}, u32[]{:S(2)}) collective-permute-start(bf16[17,2048]{1,0:T(8,128)(2,1)S(1)} %collective-permute-done.16), channel_id=1, source_target_pairs={{0,64},{8,72},{16,80},{24,88},{32,96},{40,104},{48,112},{56,120},{... | collective-permute-start | bytes 208904 | tf_op jit(solution)/shard_map/ppermute | solution.py:130
  138.4 4.4 %collective-permute-done.17 = bf16[17,2048]{1,0:T(8,128)(2,1)S(1)} collective-permute-done((bf16[17,2048]{1,0:T(8,128)(2,1)S(1)}, bf16[17,2048]{1,0:T(8,128)(2,1)S(1)}, u32[]{:S(2)}, u32[]{:S(2)}) %collective-permute-start.17) | collective-permute-done | bytes 69664 | tf_op jit(solution)/shard_map/ppermute | solution.py:130
  143.2 1.9 collective-permute-start.19
  145.1 4.6 %collective-permute-start.18 = (bf16[8,17,2048]{2,0,1:T(8,128)(2,1)S(1)}, bf16[8,17,2048]{2,0,1:T(8,128)(2,1)S(1)}, u32[]{:S(2)}, u32[]{:S(2)}) collective-permute-start(bf16[8,17,2048]{2,0,1:T(8,128)(2,1)S(1)} %copy.285), channel_id=1, source_target_pairs={{0,48},{8,56},{16,0},{24,8},{32,16},{40,24},{48,32},{56,40},{64,11... | collective-permute-start | bytes 1671176 | tf_op jit(solution)/shard_map/ppermute | solution.py:133
  149.7 6.0 %collective-permute-done.19 = bf16[8,17,2048]{2,0,1:T(8,128)(2,1)S(1)} collective-permute-done((bf16[8,17,2048]{2,0,1:T(8,128)(2,1)S(1)}, bf16[8,17,2048]{2,0,1:T(8,128)(2,1)S(1)}, u32[]{:S(2)}, u32[]{:S(2)}) %collective-permute-start.19) | collective-permute-done | bytes 557088 | tf_op jit(solution)/shard_map/ppermute | solution.py:130
  155.7 1.9 collective-permute-start.20
  158.3 8.9 %collective-permute-done.20 = bf16[8,17,2048]{2,0,1:T(8,128)(2,1)S(1)} collective-permute-done((bf16[8,17,2048]{2,0,1:T(8,128)(2,1)S(1)}, bf16[8,17,2048]{2,0,1:T(8,128)(2,1)S(1)}, u32[]{:S(2)}, u32[]{:S(2)}) %collective-permute-start.20) | collective-permute-done | bytes 557088 | tf_op jit(solution)/shard_map/ppermute | solution.py:130
  167.5 0.6 pad_maximum_fusion
  168.1 1.7 copy-done
  170.3 3.8 %fusion.183 = (f32[2,256]{1,0:T(2,128)S(1)}, f32[2,256,400]{1,2,0:T(8,128)S(1)}) fusion(bf16[2,400,2048]{2,1,0:T(8,128)(2,1)} %param.44, bf16[32,17,2048]{2,1,0:T(8,128)(2,1)} %bitcast.372), kind=kOutput, calls=%fused_computation.347 | convolution fusion | flops 839065088 | bytes 6195200 | tf_op jit(solution)/shard_map/mnd,mvd->mnv/dot_general | solution.py:115
  174.1 3.1 %fusion.184 = (f32[2,256]{1,0:T(2,128)S(1)}, f32[2,256,400]{1,2,0:T(8,128)S(1)}) fusion(bf16[2,400,2048]{2,1,0:T(8,128)(2,1)} %collective-permute-done.21, bf16[32,17,2048]{2,1,0:T(8,128)(2,1)S(1)} %bitcast.373), kind=kOutput, calls=%fused_computation.348 | convolution fusion | flops 839065088 | bytes 6195200 | tf_op jit(solution)/shard_map/mnd,mvd->mnv/dot_general | solution.py:115
  178.3 0.8 copy.292
  179.1 11.6 %all-to-all-start.1 = ((f32[3,2,64,8]{3,1,0,2:T(2,128)}), f32[3,2,64,8]{3,1,0,2:T(2,128)S(1)}, u32[]{:S(2)}, u32[]{:S(2)}) async-start(f32[3,2,64,8]{3,1,0,2:T(2,128)} %copy.292), calls=%async_computation.1 | async-start | bytes 393216 | tf_op jit(solution)/shard_map/all_to_all | solution.py:318
  190.8 11.9 %all-to-all-done.1 = f32[3,2,64,8]{3,1,0,2:T(2,128)S(1)} async-done(((f32[3,2,64,8]{3,1,0,2:T(2,128)}), f32[3,2,64,8]{3,1,0,2:T(2,128)S(1)}, u32[]{:S(2)}, u32[]{:S(2)}) %all-to-all-start.1) | async-done | bytes 12320 | tf_op jit(solution)/shard_map/all_to_all | solution.py:318
  203.0 0.6 subtract_multiply_fusion
  (172 shorter events, 12.0 us)
Async XLA Ops:
  0.0 16.6 %copy-start.3 = (bf16[2,64,512]{2,1,0:T(8,128)(2,1)S(1)}, bf16[2,64,512]{2,1,0:T(8,128)(2,1)}, u32[]{:S(2)}) copy-start(bf16[2,64,512]{2,1,0:T(8,128)(2,1)} %param.32) | copy-start | bytes 393220
  0.0 14.4 %copy-start.6 = (bf16[2,64,256]{2,1,0:T(8,128)(2,1)S(1)}, bf16[2,64,256]{2,1,0:T(8,128)(2,1)}, u32[]{:S(2)}) copy-start(bf16[2,64,256]{2,1,0:T(8,128)(2,1)} %param.33) | copy-start | bytes 196612
  0.0 13.8 %copy-start.9 = (f32[2,4,512]{2,1,0:T(4,128)S(1)}, f32[2,4,512]{2,1,0:T(4,128)}, u32[]{:S(2)}) copy-start(f32[2,4,512]{2,1,0:T(4,128)} %param.36) | copy-start | bytes 49156
  0.0 13.9 %copy-start.8 = (bf16[2,3,3,256]{3,0,2,1:T(2,128)(2,1)S(1)}, bf16[2,3,3,256]{3,0,2,1:T(2,128)(2,1)}, u32[]{:S(2)}) copy-start(bf16[2,3,3,256]{3,0,2,1:T(2,128)(2,1)} %param.46) | copy-start | bytes 27652
  0.0 14.4 %copy-start.12 = (f32[2,4,256]{2,1,0:T(4,128)S(1)}, f32[2,4,256]{2,1,0:T(4,128)}, u32[]{:S(2)}) copy-start(f32[2,4,256]{2,1,0:T(4,128)} %param.37) | copy-start | bytes 24580
  0.0 14.9 %copy-start.17 = (f32[2,8]{1,0:T(2,128)S(1)}, f32[2,8]{1,0:T(2,128)}, u32[]{:S(2)}) copy-start(f32[2,8]{1,0:T(2,128)} %param.38) | copy-start | bytes 196
  0.0 14.9 %copy-start.16 = (f32[2,8]{1,0:T(2,128)S(1)}, f32[2,8]{1,0:T(2,128)}, u32[]{:S(2)}) copy-start(f32[2,8]{1,0:T(2,128)} %param.39) | copy-start | bytes 196
  0.0 14.9 %copy-start.10 = (bf16[2,64,8]{1,2,0:T(8,128)(2,1)S(1)}, bf16[2,64,8]{1,2,0:T(8,128)(2,1)}, u32[]{:S(2)}) copy-start(bf16[2,64,8]{1,2,0:T(8,128)(2,1)} %param.34) | copy-start | bytes 6148
  0.1 16.9 %collective-permute-start.1 = (bf16[2,512,32]{1,2,0:T(8,128)(2,1)}, bf16[2,512,32]{1,2,0:T(8,128)(2,1)S(1)}, u32[]{:S(2)}, u32[]{:S(2)}) collective-permute-start(bf16[2,512,32]{1,2,0:T(8,128)(2,1)} %param.43), channel_id=1, source_target_pairs={{0,16},{8,24},{16,32},{24,40},{32,48},{40,56},{48,0},{56,8},{64,80... | collective-permute-start | bytes 196616 | tf_op jit(solution)/shard_map/ppermute | solution.py:130
  4.2 15.9 %collective-permute-start = (bf16[2,512,32]{1,2,0:T(8,128)(2,1)}, bf16[2,512,32]{1,2,0:T(8,128)(2,1)S(1)}, u32[]{:S(2)}, u32[]{:S(2)}) collective-permute-start(bf16[2,512,32]{1,2,0:T(8,128)(2,1)} %param.43), channel_id=1, source_target_pairs={{0,48},{8,56},{16,0},{24,8},{32,16},{40,24},{48,32},{56,40},{64,11... | collective-permute-start | bytes 196616 | tf_op jit(solution)/shard_map/ppermute | solution.py:133
  10.4 6.5 %copy-start.15 = (f32[2,8]{1,0:T(2,128)S(1)}, f32[2,8]{1,0:T(2,128)}, u32[]{:S(2)}) copy-start(f32[2,8]{1,0:T(2,128)} %param.40) | copy-start | bytes 196
  10.5 8.7 %copy-start.18 = (bf16[2,3,512,128]{3,2,1,0:T(8,128)(2,1)S(1)}, bf16[2,3,512,128]{3,2,1,0:T(8,128)(2,1)}, u32[]{:S(2)}) copy-start(bf16[2,3,512,128]{3,2,1,0:T(8,128)(2,1)} %param.47) | copy-start | bytes 2359300
  11.4 11.8 %copy-start.2 = (bf16[2,512,32]{1,2,0:T(8,128)(2,1)S(1)}, bf16[2,512,32]{1,2,0:T(8,128)(2,1)}, u32[]{:S(2)}) copy-start(bf16[2,512,32]{1,2,0:T(8,128)(2,1)} %param.43) | copy-start | bytes 196612
  17.0 6.2 %collective-permute-start.2 = (bf16[2,512,32]{1,2,0:T(8,128)(2,1)S(1)}, bf16[2,512,32]{1,2,0:T(8,128)(2,1)S(1)}, u32[]{:S(2)}, u32[]{:S(2)}) collective-permute-start(bf16[2,512,32]{1,2,0:T(8,128)(2,1)S(1)} %collective-permute-done.1), channel_id=1, source_target_pairs={{0,16},{8,24},{16,32},{24,40},{32,48},{40,56},{48,0},{56,8},{64,80... | collective-permute-start | bytes 196616 | tf_op jit(solution)/shard_map/ppermute | solution.py:130
  23.3 15.1 %collective-permute-start.6 = (bf16[4,2,512,32]{2,3,0,1:T(8,128)(2,1)S(1)}, bf16[4,2,512,32]{2,3,0,1:T(8,128)(2,1)S(1)}, u32[]{:S(2)}, u32[]{:S(2)}) collective-permute-start(bf16[4,2,512,32]{2,3,0,1:T(8,128)(2,1)S(1)} %pad_maximum_fusion.2), channel_id=1, source_target_pairs={{0,64},{8,72},{16,80},{24,88},{32,96},{40,104},{48,112},{56,120},{... | collective-permute-start | bytes 786440 | tf_op jit(solution)/shard_map/ppermute | solution.py:130
  27.9 12.6 %collective-permute-start.3 = (bf16[4,2,512,32]{2,3,0,1:T(8,128)(2,1)S(1)}, bf16[4,2,512,32]{2,3,0,1:T(8,128)(2,1)S(1)}, u32[]{:S(2)}, u32[]{:S(2)}) collective-permute-start(bf16[4,2,512,32]{2,3,0,1:T(8,128)(2,1)S(1)} %pad_maximum_fusion.2), channel_id=1, source_target_pairs={{0,448},{8,456},{16,464},{24,472},{32,480},{40,488},{48,496},{56,5... | collective-permute-start | bytes 786440 | tf_op jit(solution)/shard_map/ppermute | solution.py:133
  38.3 8.3 %collective-permute-start.7 = (bf16[4,2,512,32]{2,3,0,1:T(8,128)(2,1)S(1)}, bf16[4,2,512,32]{2,3,0,1:T(8,128)(2,1)S(1)}, u32[]{:S(2)}, u32[]{:S(2)}) collective-permute-start(bf16[4,2,512,32]{2,3,0,1:T(8,128)(2,1)S(1)} %collective-permute-done.6), channel_id=1, source_target_pairs={{0,64},{8,72},{16,80},{24,88},{32,96},{40,104},{48,112},{56,120},{... | collective-permute-start | bytes 786440 | tf_op jit(solution)/shard_map/ppermute | solution.py:130
  40.5 8.1 %collective-permute-start.4 = (bf16[4,2,512,32]{2,3,0,1:T(8,128)(2,1)S(1)}, bf16[4,2,512,32]{2,3,0,1:T(8,128)(2,1)S(1)}, u32[]{:S(2)}, u32[]{:S(2)}) collective-permute-start(bf16[4,2,512,32]{2,3,0,1:T(8,128)(2,1)S(1)} %collective-permute-done.3), channel_id=1, source_target_pairs={{0,448},{8,456},{16,464},{24,472},{32,480},{40,488},{48,496},{56,5... | collective-permute-start | bytes 786440 | tf_op jit(solution)/shard_map/ppermute | solution.py:133
  46.7 8.3 %collective-permute-start.8 = (bf16[4,2,512,32]{2,3,0,1:T(8,128)(2,1)S(1)}, bf16[4,2,512,32]{2,3,0,1:T(8,128)(2,1)S(1)}, u32[]{:S(2)}, u32[]{:S(2)}) collective-permute-start(bf16[4,2,512,32]{2,3,0,1:T(8,128)(2,1)S(1)} %collective-permute-done.7), channel_id=1, source_target_pairs={{0,64},{8,72},{16,80},{24,88},{32,96},{40,104},{48,112},{56,120},{... | collective-permute-start | bytes 786440 | tf_op jit(solution)/shard_map/ppermute | solution.py:130
  48.6 8.3 %collective-permute-start.5 = (bf16[4,2,512,32]{2,3,0,1:T(8,128)(2,1)S(1)}, bf16[4,2,512,32]{2,3,0,1:T(8,128)(2,1)S(1)}, u32[]{:S(2)}, u32[]{:S(2)}) collective-permute-start(bf16[4,2,512,32]{2,3,0,1:T(8,128)(2,1)S(1)} %collective-permute-done.4), channel_id=1, source_target_pairs={{0,448},{8,456},{16,464},{24,472},{32,480},{40,488},{48,496},{56,5... | collective-permute-start | bytes 786440 | tf_op jit(solution)/shard_map/ppermute | solution.py:133
  55.0 8.3 %collective-permute-start.9 = (bf16[4,2,512,32]{2,3,0,1:T(8,128)(2,1)S(1)}, bf16[4,2,512,32]{2,3,0,1:T(8,128)(2,1)S(1)}, u32[]{:S(2)}, u32[]{:S(2)}) collective-permute-start(bf16[4,2,512,32]{2,3,0,1:T(8,128)(2,1)S(1)} %collective-permute-done.8), channel_id=1, source_target_pairs={{0,64},{8,72},{16,80},{24,88},{32,96},{40,104},{48,112},{56,120},{... | collective-permute-start | bytes 786440 | tf_op jit(solution)/shard_map/ppermute | solution.py:130
  63.3 12.9 %copy-start.4 = (bf16[2,64,512]{2,1,0:T(8,128)(2,1)S(1)}, bf16[2,64,512]{2,1,0:T(8,128)(2,1)}, u32[]{:S(2)}) copy-start(bf16[2,64,512]{2,1,0:T(8,128)(2,1)} %param.31) | copy-start | bytes 393220
  63.4 13.2 %collective-permute-start.10 = (bf16[8,4,2,512,32]{3,4,1,0,2:T(8,128)(2,1)S(1)}, bf16[8,4,2,512,32]{3,4,1,0,2:T(8,128)(2,1)}, u32[]{:S(2)}, u32[]{:S(2)}) collective-permute-start(bf16[8,4,2,512,32]{3,4,1,0,2:T(8,128)(2,1)S(1)} %bitcast_dynamic-update-slice_fusion.7), channel_id=1, source_target_pairs={{0,8},{8,0},{16,24},{24,16},{32,40},{40,32},{48,56},{56,48},{64,72... | collective-permute-start | bytes 6291464 | tf_op jit(solution)/shard_map/ppermute | solution.py:130
  81.8 1.6 copy-start.13
  83.4 1.4 copy-start.7
  83.4 12.6 %copy-start.14 = (s32[64]{0:T(128)S(1)}, s32[64]{0:T(128)}, u32[]{:S(2)}) copy-start(s32[64]{0:T(128)} %param.50) | copy-start | bytes 772
  84.8 28.9 %copy-start.11 = (f32[2,2048]{1,0:T(2,128)S(1)}, f32[2,2048]{1,0:T(2,128)}, u32[]{:S(2)}) copy-start(f32[2,2048]{1,0:T(2,128)} %param.42) | copy-start | bytes 49156
  85.7 27.0 %all-to-all-start = ((bf16[2,8,8,2432]{3,2,0,1:T(8,128)(2,1)}), bf16[2,8,8,2432]{3,2,0,1:T(8,128)(2,1)S(1)}, u32[]{:S(2)}, u32[]{:S(2)}) async-start(bf16[2,8,8,2432]{3,2,0,1:T(8,128)(2,1)} %copy.283), calls=%async_computation | async-start | bytes 1245184 | tf_op jit(solution)/shard_map/all_to_all | solution.py:247
  92.5 81.5 %collective-permute-start.21 = (bf16[2,400,2048]{2,1,0:T(8,128)(2,1)}, bf16[2,400,2048]{2,1,0:T(8,128)(2,1)}, u32[]{:S(2)}, u32[]{:S(2)}) collective-permute-start(bf16[2,400,2048]{2,1,0:T(8,128)(2,1)} %param.44), channel_id=1, source_target_pairs={{0,8},{8,0},{16,24},{24,16},{32,40},{40,32},{48,56},{56,48},{64,72... | collective-permute-start | bytes 9830408 | tf_op jit(solution)/shard_map/ppermute | solution.py:192
  113.9 5.8 %collective-permute-start.11 = (bf16[17,2048]{1,0:T(8,128)(2,1)S(1)}, bf16[17,2048]{1,0:T(8,128)(2,1)S(1)}, u32[]{:S(2)}, u32[]{:S(2)}) collective-permute-start(bf16[17,2048]{1,0:T(8,128)(2,1)S(1)} %pad_maximum_fusion.4), channel_id=1, source_target_pairs={{0,448},{8,456},{16,464},{24,472},{32,480},{40,488},{48,496},{56,5... | collective-permute-start | bytes 208904 | tf_op jit(solution)/shard_map/ppermute | solution.py:133
  115.8 7.3 %collective-permute-start.14 = (bf16[17,2048]{1,0:T(8,128)(2,1)S(1)}, bf16[17,2048]{1,0:T(8,128)(2,1)S(1)}, u32[]{:S(2)}, u32[]{:S(2)}) collective-permute-start(bf16[17,2048]{1,0:T(8,128)(2,1)S(1)} %pad_maximum_fusion.4), channel_id=1, source_target_pairs={{0,64},{8,72},{16,80},{24,88},{32,96},{40,104},{48,112},{56,120},{... | collective-permute-start | bytes 208904 | tf_op jit(solution)/shard_map/ppermute | solution.py:130
  119.7 5.4 %collective-permute-start.12 = (bf16[17,2048]{1,0:T(8,128)(2,1)S(1)}, bf16[17,2048]{1,0:T(8,128)(2,1)S(1)}, u32[]{:S(2)}, u32[]{:S(2)}) collective-permute-start(bf16[17,2048]{1,0:T(8,128)(2,1)S(1)} %collective-permute-done.11), channel_id=1, source_target_pairs={{0,448},{8,456},{16,464},{24,472},{32,480},{40,488},{48,496},{56,5... | collective-permute-start | bytes 208904 | tf_op jit(solution)/shard_map/ppermute | solution.py:133
  123.1 6.6 %collective-permute-start.15 = (bf16[17,2048]{1,0:T(8,128)(2,1)S(1)}, bf16[17,2048]{1,0:T(8,128)(2,1)S(1)}, u32[]{:S(2)}, u32[]{:S(2)}) collective-permute-start(bf16[17,2048]{1,0:T(8,128)(2,1)S(1)} %collective-permute-done.14), channel_id=1, source_target_pairs={{0,64},{8,72},{16,80},{24,88},{32,96},{40,104},{48,112},{56,120},{... | collective-permute-start | bytes 208904 | tf_op jit(solution)/shard_map/ppermute | solution.py:130
  125.1 13.3 %collective-permute-start.13 = (bf16[17,2048]{1,0:T(8,128)(2,1)S(1)}, bf16[17,2048]{1,0:T(8,128)(2,1)S(1)}, u32[]{:S(2)}, u32[]{:S(2)}) collective-permute-start(bf16[17,2048]{1,0:T(8,128)(2,1)S(1)} %collective-permute-done.12), channel_id=1, source_target_pairs={{0,448},{8,456},{16,464},{24,472},{32,480},{40,488},{48,496},{56,5... | collective-permute-start | bytes 208904 | tf_op jit(solution)/shard_map/ppermute | solution.py:133
  129.7 6.6 %collective-permute-start.16 = (bf16[17,2048]{1,0:T(8,128)(2,1)S(1)}, bf16[17,2048]{1,0:T(8,128)(2,1)S(1)}, u32[]{:S(2)}, u32[]{:S(2)}) collective-permute-start(bf16[17,2048]{1,0:T(8,128)(2,1)S(1)} %collective-permute-done.15), channel_id=1, source_target_pairs={{0,64},{8,72},{16,80},{24,88},{32,96},{40,104},{48,112},{56,120},{... | collective-permute-start | bytes 208904 | tf_op jit(solution)/shard_map/ppermute | solution.py:130
  136.2 6.6 %collective-permute-start.17 = (bf16[17,2048]{1,0:T(8,128)(2,1)S(1)}, bf16[17,2048]{1,0:T(8,128)(2,1)S(1)}, u32[]{:S(2)}, u32[]{:S(2)}) collective-permute-start(bf16[17,2048]{1,0:T(8,128)(2,1)S(1)} %collective-permute-done.16), channel_id=1, source_target_pairs={{0,64},{8,72},{16,80},{24,88},{32,96},{40,104},{48,112},{56,120},{... | collective-permute-start | bytes 208904 | tf_op jit(solution)/shard_map/ppermute | solution.py:130
  143.2 12.5 %collective-permute-start.19 = (bf16[8,17,2048]{2,0,1:T(8,128)(2,1)S(1)}, bf16[8,17,2048]{2,0,1:T(8,128)(2,1)S(1)}, u32[]{:S(2)}, u32[]{:S(2)}) collective-permute-start(bf16[8,17,2048]{2,0,1:T(8,128)(2,1)S(1)} %copy.285), channel_id=1, source_target_pairs={{0,16},{8,24},{16,32},{24,40},{32,48},{40,56},{48,0},{56,8},{64,80... | collective-permute-start | bytes 1671176 | tf_op jit(solution)/shard_map/ppermute | solution.py:130
  145.1 12.8 %collective-permute-start.18 = (bf16[8,17,2048]{2,0,1:T(8,128)(2,1)S(1)}, bf16[8,17,2048]{2,0,1:T(8,128)(2,1)S(1)}, u32[]{:S(2)}, u32[]{:S(2)}) collective-permute-start(bf16[8,17,2048]{2,0,1:T(8,128)(2,1)S(1)} %copy.285), channel_id=1, source_target_pairs={{0,48},{8,56},{16,0},{24,8},{32,16},{40,24},{48,32},{56,40},{64,11... | collective-permute-start | bytes 1671176 | tf_op jit(solution)/shard_map/ppermute | solution.py:133
  155.7 11.5 %collective-permute-start.20 = (bf16[8,17,2048]{2,0,1:T(8,128)(2,1)S(1)}, bf16[8,17,2048]{2,0,1:T(8,128)(2,1)S(1)}, u32[]{:S(2)}, u32[]{:S(2)}) collective-permute-start(bf16[8,17,2048]{2,0,1:T(8,128)(2,1)S(1)} %collective-permute-done.19), channel_id=1, source_target_pairs={{0,16},{8,24},{16,32},{24,40},{32,48},{40,56},{48,0},{56,8},{64,80... | collective-permute-start | bytes 1671176 | tf_op jit(solution)/shard_map/ppermute | solution.py:130
  168.1 1.7 copy-start
  170.3 3.8 %copy-start.1 = (bf16[4,8,17,2048]{3,2,1,0:T(8,128)(2,1)S(1)}, bf16[4,8,17,2048]{3,2,1,0:T(8,128)(2,1)}, u32[]{:S(2)}) copy-start(bf16[4,8,17,2048]{3,2,1,0:T(8,128)(2,1)} %copy-done) | copy-start | bytes 6684676
  174.0 4.0 %copy-start.5 = (f32[3,2,8,4,8]{4,2,3,1,0:T(8,128)S(1)}, f32[3,2,8,4,8]{4,2,3,1,0:T(8,128)}, u32[]{:S(2)}) copy-start(f32[3,2,8,4,8]{4,2,3,1,0:T(8,128)} %constant.319.clone.1) | copy-start | bytes 18436
  177.2 13.5 %copy-start.19 = (s32[64]{0:T(128)S(1)}, s32[64]{0:T(128)}, u32[]{:S(2)}) copy-start(s32[64]{0:T(128)} %param.51) | copy-start | bytes 772
  179.1 23.6 %all-to-all-start.1 = ((f32[3,2,64,8]{3,1,0,2:T(2,128)}), f32[3,2,64,8]{3,1,0,2:T(2,128)S(1)}, u32[]{:S(2)}, u32[]{:S(2)}) async-start(f32[3,2,64,8]{3,1,0,2:T(2,128)} %copy.292), calls=%async_computation.1 | async-start | bytes 393216 | tf_op jit(solution)/shard_map/all_to_all | solution.py:318

commit v12 on v7

--- a/solution.py
+++ b/solution.py
@@ -217,12 +217,12 @@
     squares = jnp.sum(gated * gated, axis=2)
     unscaled = (gated * norm_gain[:, None, :]).astype(jnp.bfloat16)
     ring_weight = ring_gather(
-        ring_gather(ring_gather(out_weight, along_z, chips_z), along_x, ROWS_X),
-        along_core,
-        CORES,
+        ring_gather(ring_gather(out_weight, along_x, ROWS_X), along_core, CORES),
+        along_z,
+        chips_z,
     )
     ring_weight = jnp.roll(
-        jnp.roll(jnp.roll(ring_weight.transpose(2, 1, 0, 3, 4, 5), z_index, axis=0), x_index, axis=1),
+        jnp.roll(jnp.roll(ring_weight.transpose(0, 2, 1, 3, 4, 5), z_index, axis=0), x_index, axis=1),
         core_index,
         axis=2,
     )

time: 226 us -> 232 us (1.027)
  waiting for transfers between devices: 66.8 us -> 79.4 us
  other arithmetic: 22.3 us -> 17.3 us
  local copies, waits for them, and re-layouts: 19.6 us -> 15 us
  starting transfers between devices: 93.1 us -> 96 us
    ppermute x13, waiting for transfers between devices: 40.6 us -> 52.9 us  [ring_gather(): forward = lax.ppermute(forward, 'req', perm_of(1))]
    ppermute x8, waiting for transfers between devices: 0.49 us -> 7.18 us  [ring_gather(): backward = lax.ppermute(backward, 'req', perm_of(-1))]
    all_to_all x1, waiting for transfers between devices: 13.6 us -> 7.15 us  [local(): lax.all_to_all(payload.reshape(models, groups, row_count, payload.shape[2...]
    ppermute x8, starting transfers between devices: 38.7 us -> 32.3 us  [ring_gather(): backward = lax.ppermute(backward, 'req', perm_of(-1))]
    all_to_all x1, starting transfers between devices: 10.8 us -> 14.4 us  [local(): lax.all_to_all(send, 'req', split_axis=2, concat_axis=2, tiled=True)]
    ppermute x1, starting transfers between devices: 2.37 us -> 5.66 us  [local(): lax.ppermute(head_weight, 'req', [(i, i ^ 1) for i in range(shards)])]
    another operation x2 -> x3, other arithmetic: 3.4 us -> 0.65 us  [ring_gather(): return jnp.stack([got[k] for k in range(count)])]
    slice x6, local copies, waits for them, and re-layouts: 2.61 us -> 0.09 us  [causal_conv(): current[:-lag_steps]]
  transfers between devices with their start and end apart: 24 -> 24, of which waited for: 11 -> 13; matrix products, arithmetic and copies ran while one was open for 19% -> 17% of each run, Pallas kernels for 0% -> 0%
where the time goes in v12:
time: 232 us; the launch traced here: 230 us
  starting transfers between devices  96 us (41%)
  waiting for transfers between devices  79.4 us (34%)
  matrix products  20.8 us (9%)
  other arithmetic  17.3 us (7%)
  local copies, waits for them, and re-layouts  15 us (6%)
    ppermute x13, waiting for transfers between devices, ring_gather(): forward = lax.ppermute(forward, 'req', perm_of(1))  52.9 us
    ppermute x13, starting transfers between devices, ring_gather(): forward = lax.ppermute(forward, 'req', perm_of(1))  36.8 us
    ppermute x8, starting transfers between devices, ring_gather(): backward = lax.ppermute(backward, 'req', perm_of(-1))  32.3 us
    all_to_all x1, starting transfers between devices, local(): lax.all_to_all(send, 'req', split_axis=2, concat_axis=2, tiled=True)  14.4 us
    all_to_all x1, waiting for transfers between devices, local(): lax.all_to_all(send, 'req', split_axis=2, concat_axis=2, tiled=True)  12.1 us
    ppermute x8, waiting for transfers between devices, ring_gather(): backward = lax.ppermute(backward, 'req', perm_of(-1))  7.18 us
    all_to_all x1, waiting for transfers between devices, local(): lax.all_to_all(payload.reshape(models, groups, row_count, payload.shape[2...  7.15 us
    dot_general x2, matrix products, head_scores(): jnp.einsum('mnd,mvd->mnv', rows_hidden, head_weight, preferred_element_ty...  6.92 us
  transfers between devices with their start and end apart: 24, of which 13 were waited for; matrix products, arithmetic and copies ran while one was open for 17% of the time, Pallas kernels for 0%

profile of v12, /device:TPU:1, one launch (start us, length us, event | category | flops | bytes accessed | tf_op | source)
XLA Modules:
  0.0 229.7 jit_solution(16755018373482134708)
XLA Ops:
  0.0 4.1 %collective-permute-start.1 = (bf16[2,512,32]{1,2,0:T(8,128)(2,1)}, bf16[2,512,32]{1,2,0:T(8,128)(2,1)S(1)}, u32[]{:S(2)}, u32[]{:S(2)}) collective-permute-start(bf16[2,512,32]{1,2,0:T(8,128)(2,1)} %param.43), channel_id=1, source_target_pairs={{0,16},{8,24},{16,32},{24,40},{32,48},{40,56},{48,0},{56,8},{64,80... | collective-permute-start | bytes 196616 | tf_op jit(solution)/shard_map/ppermute | solution.py:130
  4.1 3.2 %collective-permute-start = (bf16[2,512,32]{1,2,0:T(8,128)(2,1)}, bf16[2,512,32]{1,2,0:T(8,128)(2,1)S(1)}, u32[]{:S(2)}, u32[]{:S(2)}) collective-permute-start(bf16[2,512,32]{1,2,0:T(8,128)(2,1)} %param.43), channel_id=1, source_target_pairs={{0,48},{8,56},{16,0},{24,8},{32,16},{40,24},{48,32},{56,40},{64,11... | collective-permute-start | bytes 196616 | tf_op jit(solution)/shard_map/ppermute | solution.py:133
  7.3 0.8 reduce-window.4
  9.5 0.9 slice_convert_fusion.1
  10.5 0.8 slice_convert_fusion.3
  12.1 0.8 fusion.176
  13.6 0.9 fusion.177
  14.6 0.8 fusion.180
  15.9 0.9 fusion.181
  16.8 1.0 divide_multiply_fusion.2
  20.0 0.8 fusion.83
  22.1 2.1 collective-permute-start.2
  24.2 4.1 %collective-permute-done.2 = bf16[2,512,32]{1,2,0:T(8,128)(2,1)S(1)} collective-permute-done((bf16[2,512,32]{1,2,0:T(8,128)(2,1)S(1)}, bf16[2,512,32]{1,2,0:T(8,128)(2,1)S(1)}, u32[]{:S(2)}, u32[]{:S(2)}) %collective-permute-start.2) | collective-permute-done | bytes 65568 | tf_op jit(solution)/shard_map/ppermute | solution.py:130
  28.3 9.8 %collective-permute-start.3 = (bf16[4,2,512,32]{2,3,0,1:T(8,128)(2,1)S(1)}, bf16[4,2,512,32]{2,3,0,1:T(8,128)(2,1)S(1)}, u32[]{:S(2)}, u32[]{:S(2)}) collective-permute-start(bf16[4,2,512,32]{2,3,0,1:T(8,128)(2,1)S(1)} %get-tuple-element.65), channel_id=1, source_target_pairs={{0,8},{8,0},{16,24},{24,16},{32,40},{40,32},{48,56},{56,48},{64,72... | collective-permute-start | bytes 786440 | tf_op jit(solution)/shard_map/ppermute | solution.py:130
  38.8 1.0 divide_multiply_fusion.1
  39.8 1.9 collective-permute-start.7
  41.8 2.0 fusion.10
  45.4 5.3 %collective-permute-start.4 = (bf16[2,4,2,512,32]{3,4,0,1,2:T(8,128)(2,1)S(1)}, bf16[2,4,2,512,32]{3,4,0,1,2:T(8,128)(2,1)S(1)}, u32[]{:S(2)}, u32[]{:S(2)}) collective-permute-start(bf16[2,4,2,512,32]{3,4,0,1,2:T(8,128)(2,1)S(1)} %pad_maximum_fusion.1), channel_id=1, source_target_pairs={{0,448},{8,456},{16,464},{24,472},{32,480},{40,488},{48,496},{56,5... | collective-permute-start | bytes 1572872 | tf_op jit(solution)/shard_map/ppermute | solution.py:133
  50.7 0.9 fusion.18
  51.5 5.9 %collective-permute-done.7 = bf16[2,4,2,512,32]{3,4,0,1,2:T(8,128)(2,1)S(1)} collective-permute-done((bf16[2,4,2,512,32]{3,4,0,1,2:T(8,128)(2,1)S(1)}, bf16[2,4,2,512,32]{3,4,0,1,2:T(8,128)(2,1)S(1)}, u32[]{:S(2)}, u32[]{:S(2)}) %collective-permute-start.7) | collective-permute-done | bytes 524320 | tf_op jit(solution)/shard_map/ppermute | solution.py:130
  57.4 1.9 collective-permute-start.8
  59.3 2.1 fusion.9
  61.5 1.0 copy.295
  62.7 1.4 fusion.14
  64.2 4.6 %collective-permute-start.5 = (bf16[2,4,2,512,32]{3,4,0,1,2:T(8,128)(2,1)S(1)}, bf16[2,4,2,512,32]{3,4,0,1,2:T(8,128)(2,1)S(1)}, u32[]{:S(2)}, u32[]{:S(2)}) collective-permute-start(bf16[2,4,2,512,32]{3,4,0,1,2:T(8,128)(2,1)S(1)} %collective-permute-done.4), channel_id=1, source_target_pairs={{0,448},{8,456},{16,464},{24,472},{32,480},{40,488},{48,496},{56,5... | collective-permute-start | bytes 1572872 | tf_op jit(solution)/shard_map/ppermute | solution.py:133
  68.8 1.0 fusion.40
  70.0 3.4 %collective-permute-done.8 = bf16[2,4,2,512,32]{3,4,0,1,2:T(8,128)(2,1)S(1)} collective-permute-done((bf16[2,4,2,512,32]{3,4,0,1,2:T(8,128)(2,1)S(1)}, bf16[2,4,2,512,32]{3,4,0,1,2:T(8,128)(2,1)S(1)}, u32[]{:S(2)}, u32[]{:S(2)}) %collective-permute-start.8) | collective-permute-done | bytes 524320 | tf_op jit(solution)/shard_map/ppermute | solution.py:130
  73.4 1.9 collective-permute-start.9
  75.5 3.7 %collective-permute-done.5 = bf16[2,4,2,512,32]{3,4,0,1,2:T(8,128)(2,1)S(1)} collective-permute-done((bf16[2,4,2,512,32]{3,4,0,1,2:T(8,128)(2,1)S(1)}, bf16[2,4,2,512,32]{3,4,0,1,2:T(8,128)(2,1)S(1)}, u32[]{:S(2)}, u32[]{:S(2)}) %collective-permute-start.5) | collective-permute-done | bytes 524320 | tf_op jit(solution)/shard_map/ppermute | solution.py:133
  79.2 5.3 %collective-permute-start.6 = (bf16[2,4,2,512,32]{3,4,0,1,2:T(8,128)(2,1)S(1)}, bf16[2,4,2,512,32]{3,4,0,1,2:T(8,128)(2,1)S(1)}, u32[]{:S(2)}, u32[]{:S(2)}) collective-permute-start(bf16[2,4,2,512,32]{3,4,0,1,2:T(8,128)(2,1)S(1)} %collective-permute-done.5), channel_id=1, source_target_pairs={{0,448},{8,456},{16,464},{24,472},{32,480},{40,488},{48,496},{56,5... | collective-permute-start | bytes 1572872 | tf_op jit(solution)/shard_map/ppermute | solution.py:133
  84.5 3.9 %collective-permute-done.9 = bf16[2,4,2,512,32]{3,4,0,1,2:T(8,128)(2,1)S(1)} collective-permute-done((bf16[2,4,2,512,32]{3,4,0,1,2:T(8,128)(2,1)S(1)}, bf16[2,4,2,512,32]{3,4,0,1,2:T(8,128)(2,1)S(1)}, u32[]{:S(2)}, u32[]{:S(2)}) %collective-permute-start.9) | collective-permute-done | bytes 524320 | tf_op jit(solution)/shard_map/ppermute | solution.py:130
  88.4 1.9 collective-permute-start.10
  90.5 3.4 %collective-permute-done.6 = bf16[2,4,2,512,32]{3,4,0,1,2:T(8,128)(2,1)S(1)} collective-permute-done((bf16[2,4,2,512,32]{3,4,0,1,2:T(8,128)(2,1)S(1)}, bf16[2,4,2,512,32]{3,4,0,1,2:T(8,128)(2,1)S(1)}, u32[]{:S(2)}, u32[]{:S(2)}) %collective-permute-start.6) | collective-permute-done | bytes 524320 | tf_op jit(solution)/shard_map/ppermute | solution.py:133
  93.9 8.6 %collective-permute-done.10 = bf16[2,4,2,512,32]{3,4,0,1,2:T(8,128)(2,1)S(1)} collective-permute-done((bf16[2,4,2,512,32]{3,4,0,1,2:T(8,128)(2,1)S(1)}, bf16[2,4,2,512,32]{3,4,0,1,2:T(8,128)(2,1)S(1)}, u32[]{:S(2)}, u32[]{:S(2)}) %collective-permute-start.10) | collective-permute-done | bytes 524320 | tf_op jit(solution)/shard_map/ppermute | solution.py:130
  102.8 1.6 fusion.2
  104.3 1.6 fusion.1
  105.9 1.6 fusion
  107.5 1.4 convolution_convert_fusion
  109.0 0.9 copy.283
  109.8 6.8 %all-to-all-start = ((bf16[2,8,8,2432]{3,2,0,1:T(8,128)(2,1)}), bf16[2,8,8,2432]{3,2,0,1:T(8,128)(2,1)S(1)}, u32[]{:S(2)}, u32[]{:S(2)}) async-start(bf16[2,8,8,2432]{3,2,0,1:T(8,128)(2,1)} %copy.283), calls=%async_computation | async-start | bytes 1245184 | tf_op jit(solution)/shard_map/all_to_all | solution.py:247
  116.7 5.7 %collective-permute-start.21 = (bf16[2,400,2048]{2,1,0:T(8,128)(2,1)}, bf16[2,400,2048]{2,1,0:T(8,128)(2,1)}, u32[]{:S(2)}, u32[]{:S(2)}) collective-permute-start(bf16[2,400,2048]{2,1,0:T(8,128)(2,1)} %param.44), channel_id=1, source_target_pairs={{0,8},{8,0},{16,24},{24,16},{32,40},{40,32},{48,56},{56,48},{64,72... | collective-permute-start | bytes 9830408 | tf_op jit(solution)/shard_map/ppermute | solution.py:192
  124.3 1.4 broadcast_select_fusion
  125.7 0.9 scatter.19
  126.6 7.1 %all-to-all-done = bf16[2,8,8,2432]{3,2,0,1:T(8,128)(2,1)S(1)} async-done(((bf16[2,8,8,2432]{3,2,0,1:T(8,128)(2,1)}), bf16[2,8,8,2432]{3,2,0,1:T(8,128)(2,1)S(1)}, u32[]{:S(2)}, u32[]{:S(2)}) %all-to-all-start) | async-done | bytes 622624 | tf_op jit(solution)/shard_map/all_to_all | solution.py:247
  134.9 1.9 collective-permute-start.11
  136.9 3.4 %collective-permute-start.14 = (bf16[17,2048]{1,0:T(8,128)(2,1)S(1)}, bf16[17,2048]{1,0:T(8,128)(2,1)S(1)}, u32[]{:S(2)}, u32[]{:S(2)}) collective-permute-start(bf16[17,2048]{1,0:T(8,128)(2,1)S(1)} %pad_maximum_fusion.5), channel_id=1, source_target_pairs={{0,64},{8,72},{16,80},{24,88},{32,96},{40,104},{48,112},{56,120},{... | collective-permute-start | bytes 208904 | tf_op jit(solution)/shard_map/ppermute | solution.py:130
  140.3 3.1 %collective-permute-start.12 = (bf16[17,2048]{1,0:T(8,128)(2,1)S(1)}, bf16[17,2048]{1,0:T(8,128)(2,1)S(1)}, u32[]{:S(2)}, u32[]{:S(2)}) collective-permute-start(bf16[17,2048]{1,0:T(8,128)(2,1)S(1)} %collective-permute-done.11), channel_id=1, source_target_pairs={{0,448},{8,456},{16,464},{24,472},{32,480},{40,488},{48,496},{56,5... | collective-permute-start | bytes 208904 | tf_op jit(solution)/shard_map/ppermute | solution.py:133
  143.4 2.2 collective-permute-start.15
  145.6 4.3 %collective-permute-start.13 = (bf16[17,2048]{1,0:T(8,128)(2,1)S(1)}, bf16[17,2048]{1,0:T(8,128)(2,1)S(1)}, u32[]{:S(2)}, u32[]{:S(2)}) collective-permute-start(bf16[17,2048]{1,0:T(8,128)(2,1)S(1)} %collective-permute-done.12), channel_id=1, source_target_pairs={{0,448},{8,456},{16,464},{24,472},{32,480},{40,488},{48,496},{56,5... | collective-permute-start | bytes 208904 | tf_op jit(solution)/shard_map/ppermute | solution.py:133
  150.0 1.9 collective-permute-start.16
  151.9 4.6 %collective-permute-done.16 = bf16[17,2048]{1,0:T(8,128)(2,1)S(1)} collective-permute-done((bf16[17,2048]{1,0:T(8,128)(2,1)S(1)}, bf16[17,2048]{1,0:T(8,128)(2,1)S(1)}, u32[]{:S(2)}, u32[]{:S(2)}) %collective-permute-start.16) | collective-permute-done | bytes 69664 | tf_op jit(solution)/shard_map/ppermute | solution.py:130
  156.6 1.9 collective-permute-start.17
  158.5 5.4 %collective-permute-done.17 = bf16[17,2048]{1,0:T(8,128)(2,1)S(1)} collective-permute-done((bf16[17,2048]{1,0:T(8,128)(2,1)S(1)}, bf16[17,2048]{1,0:T(8,128)(2,1)S(1)}, u32[]{:S(2)}, u32[]{:S(2)}) %collective-permute-start.17) | collective-permute-done | bytes 69664 | tf_op jit(solution)/shard_map/ppermute | solution.py:130
  164.3 1.9 collective-permute-start.19
  166.3 4.6 %collective-permute-start.18 = (bf16[8,17,2048]{2,0,1:T(8,128)(2,1)S(1)}, bf16[8,17,2048]{2,0,1:T(8,128)(2,1)S(1)}, u32[]{:S(2)}, u32[]{:S(2)}) collective-permute-start(bf16[8,17,2048]{2,0,1:T(8,128)(2,1)S(1)} %copy.285), channel_id=1, source_target_pairs={{0,48},{8,56},{16,0},{24,8},{32,16},{40,24},{48,32},{56,40},{64,11... | collective-permute-start | bytes 1671176 | tf_op jit(solution)/shard_map/ppermute | solution.py:133
  170.8 5.0 %collective-permute-done.19 = bf16[8,17,2048]{2,0,1:T(8,128)(2,1)S(1)} collective-permute-done((bf16[8,17,2048]{2,0,1:T(8,128)(2,1)S(1)}, bf16[8,17,2048]{2,0,1:T(8,128)(2,1)S(1)}, u32[]{:S(2)}, u32[]{:S(2)}) %collective-permute-start.19) | collective-permute-done | bytes 557088 | tf_op jit(solution)/shard_map/ppermute | solution.py:130
  175.8 1.9 collective-permute-start.20
  178.4 11.9 %collective-permute-done.20 = bf16[8,17,2048]{2,0,1:T(8,128)(2,1)S(1)} collective-permute-done((bf16[8,17,2048]{2,0,1:T(8,128)(2,1)S(1)}, bf16[8,17,2048]{2,0,1:T(8,128)(2,1)S(1)}, u32[]{:S(2)}, u32[]{:S(2)}) %collective-permute-start.20) | collective-permute-done | bytes 557088 | tf_op jit(solution)/shard_map/ppermute | solution.py:130
  191.3 1.7 copy-done
  193.4 3.8 %fusion.184 = (f32[2,256]{1,0:T(2,128)S(1)}, f32[2,256,400]{1,2,0:T(8,128)S(1)}) fusion(bf16[2,400,2048]{2,1,0:T(8,128)(2,1)} %param.44, bf16[32,17,2048]{2,1,0:T(8,128)(2,1)} %bitcast.373), kind=kOutput, calls=%fused_computation.348 | convolution fusion | flops 839065088 | bytes 6195200 | tf_op jit(solution)/shard_map/mnd,mvd->mnv/dot_general | solution.py:115
  197.3 3.1 %fusion.185 = (f32[2,256]{1,0:T(2,128)S(1)}, f32[2,256,400]{1,2,0:T(8,128)S(1)}) fusion(bf16[2,400,2048]{2,1,0:T(8,128)(2,1)} %collective-permute-done.21, bf16[32,17,2048]{2,1,0:T(8,128)(2,1)S(1)} %bitcast.374), kind=kOutput, calls=%fused_computation.349 | convolution fusion | flops 839065088 | bytes 6195200 | tf_op jit(solution)/shard_map/mnd,mvd->mnv/dot_general | solution.py:115
  201.4 0.8 copy.292
  202.3 14.4 %all-to-all-start.1 = ((f32[3,2,64,8]{3,1,0,2:T(2,128)}), f32[3,2,64,8]{3,1,0,2:T(2,128)S(1)}, u32[]{:S(2)}, u32[]{:S(2)}) async-start(f32[3,2,64,8]{3,1,0,2:T(2,128)} %copy.292), calls=%async_computation.1 | async-start | bytes 393216 | tf_op jit(solution)/shard_map/all_to_all | solution.py:318
  216.7 12.1 %all-to-all-done.1 = f32[3,2,64,8]{3,1,0,2:T(2,128)S(1)} async-done(((f32[3,2,64,8]{3,1,0,2:T(2,128)}), f32[3,2,64,8]{3,1,0,2:T(2,128)S(1)}, u32[]{:S(2)}, u32[]{:S(2)}) %all-to-all-start.1) | async-done | bytes 12320 | tf_op jit(solution)/shard_map/all_to_all | solution.py:318
  (168 shorter events, 17.6 us)
Async XLA Ops:
  0.0 21.6 %copy-start.2 = (bf16[2,64,512]{2,1,0:T(8,128)(2,1)S(1)}, bf16[2,64,512]{2,1,0:T(8,128)(2,1)}, u32[]{:S(2)}) copy-start(bf16[2,64,512]{2,1,0:T(8,128)(2,1)} %param.32) | copy-start | bytes 393220
  0.0 19.7 %copy-start.4 = (bf16[2,64,256]{2,1,0:T(8,128)(2,1)S(1)}, bf16[2,64,256]{2,1,0:T(8,128)(2,1)}, u32[]{:S(2)}) copy-start(bf16[2,64,256]{2,1,0:T(8,128)(2,1)} %param.33) | copy-start | bytes 196612
  0.0 18.0 %copy-start.15 = (f32[2,8]{1,0:T(2,128)S(1)}, f32[2,8]{1,0:T(2,128)}, u32[]{:S(2)}) copy-start(f32[2,8]{1,0:T(2,128)} %param.38) | copy-start | bytes 196
  0.0 18.0 %copy-start.14 = (f32[2,8]{1,0:T(2,128)S(1)}, f32[2,8]{1,0:T(2,128)}, u32[]{:S(2)}) copy-start(f32[2,8]{1,0:T(2,128)} %param.39) | copy-start | bytes 196
  0.0 18.0 %copy-start.8 = (bf16[2,64,8]{1,2,0:T(8,128)(2,1)S(1)}, bf16[2,64,8]{1,2,0:T(8,128)(2,1)}, u32[]{:S(2)}) copy-start(bf16[2,64,8]{1,2,0:T(8,128)(2,1)} %param.34) | copy-start | bytes 6148
  0.0 22.0 %collective-permute-start.1 = (bf16[2,512,32]{1,2,0:T(8,128)(2,1)}, bf16[2,512,32]{1,2,0:T(8,128)(2,1)S(1)}, u32[]{:S(2)}, u32[]{:S(2)}) collective-permute-start(bf16[2,512,32]{1,2,0:T(8,128)(2,1)} %param.43), channel_id=1, source_target_pairs={{0,16},{8,24},{16,32},{24,40},{32,48},{40,56},{48,0},{56,8},{64,80... | collective-permute-start | bytes 196616 | tf_op jit(solution)/shard_map/ppermute | solution.py:130
  4.1 20.1 %collective-permute-start = (bf16[2,512,32]{1,2,0:T(8,128)(2,1)}, bf16[2,512,32]{1,2,0:T(8,128)(2,1)S(1)}, u32[]{:S(2)}, u32[]{:S(2)}) collective-permute-start(bf16[2,512,32]{1,2,0:T(8,128)(2,1)} %param.43), channel_id=1, source_target_pairs={{0,48},{8,56},{16,0},{24,8},{32,16},{40,24},{48,32},{56,40},{64,11... | collective-permute-start | bytes 196616 | tf_op jit(solution)/shard_map/ppermute | solution.py:133
  10.4 17.9 %copy-start.5 = (bf16[2,512,32]{1,2,0:T(8,128)(2,1)S(1)}, bf16[2,512,32]{1,2,0:T(8,128)(2,1)}, u32[]{:S(2)}) copy-start(bf16[2,512,32]{1,2,0:T(8,128)(2,1)} %param.43) | copy-start | bytes 196612
  10.5 27.7 %copy-start.13 = (f32[2,8]{1,0:T(2,128)S(1)}, f32[2,8]{1,0:T(2,128)}, u32[]{:S(2)}) copy-start(f32[2,8]{1,0:T(2,128)} %param.40) | copy-start | bytes 196
  12.1 29.6 %copy-start.17 = (f32[3]{0:T(128)}, f32[3]{0:T(128)S(1)}, u32[]{:S(2)}) copy-start(f32[3]{0:T(128)S(1)} %get-tuple-element.121) | copy-start | bytes 40
  20.0 8.3 %copy-start.7 = (f32[64,256]{1,0:T(8,128)}, f32[64,256]{1,0:T(8,128)S(1)}, u32[]{:S(2)}) copy-start(f32[64,256]{1,0:T(8,128)S(1)} %divide_multiply_fusion.3) | copy-start | bytes 196612
  22.1 6.2 %collective-permute-start.2 = (bf16[2,512,32]{1,2,0:T(8,128)(2,1)S(1)}, bf16[2,512,32]{1,2,0:T(8,128)(2,1)S(1)}, u32[]{:S(2)}, u32[]{:S(2)}) collective-permute-start(bf16[2,512,32]{1,2,0:T(8,128)(2,1)S(1)} %collective-permute-done.1), channel_id=1, source_target_pairs={{0,16},{8,24},{16,32},{24,40},{32,48},{40,56},{48,0},{56,8},{64,80... | collective-permute-start | bytes 196616 | tf_op jit(solution)/shard_map/ppermute | solution.py:130
  24.2 19.9 %copy-start.11 = (f32[64,3]{0,1:T(4,128)}, f32[64,3]{0,1:T(4,128)S(1)}, u32[]{:S(2)}) copy-start(f32[64,3]{0,1:T(4,128)S(1)} %fusion.142) | copy-start | bytes 2308
  28.3 11.4 %collective-permute-start.3 = (bf16[4,2,512,32]{2,3,0,1:T(8,128)(2,1)S(1)}, bf16[4,2,512,32]{2,3,0,1:T(8,128)(2,1)S(1)}, u32[]{:S(2)}, u32[]{:S(2)}) collective-permute-start(bf16[4,2,512,32]{2,3,0,1:T(8,128)(2,1)S(1)} %get-tuple-element.65), channel_id=1, source_target_pairs={{0,8},{8,0},{16,24},{24,16},{32,40},{40,32},{48,56},{56,48},{64,72... | collective-permute-start | bytes 786440 | tf_op jit(solution)/shard_map/ppermute | solution.py:130
  39.8 17.6 %collective-permute-start.7 = (bf16[2,4,2,512,32]{3,4,0,1,2:T(8,128)(2,1)S(1)}, bf16[2,4,2,512,32]{3,4,0,1,2:T(8,128)(2,1)S(1)}, u32[]{:S(2)}, u32[]{:S(2)}) collective-permute-start(bf16[2,4,2,512,32]{3,4,0,1,2:T(8,128)(2,1)S(1)} %pad_maximum_fusion.1), channel_id=1, source_target_pairs={{0,64},{8,72},{16,80},{24,88},{32,96},{40,104},{48,112},{56,120},{... | collective-permute-start | bytes 1572872 | tf_op jit(solution)/shard_map/ppermute | solution.py:130
  45.4 18.9 %collective-permute-start.4 = (bf16[2,4,2,512,32]{3,4,0,1,2:T(8,128)(2,1)S(1)}, bf16[2,4,2,512,32]{3,4,0,1,2:T(8,128)(2,1)S(1)}, u32[]{:S(2)}, u32[]{:S(2)}) collective-permute-start(bf16[2,4,2,512,32]{3,4,0,1,2:T(8,128)(2,1)S(1)} %pad_maximum_fusion.1), channel_id=1, source_target_pairs={{0,448},{8,456},{16,464},{24,472},{32,480},{40,488},{48,496},{56,5... | collective-permute-start | bytes 1572872 | tf_op jit(solution)/shard_map/ppermute | solution.py:133
  57.4 16.0 %collective-permute-start.8 = (bf16[2,4,2,512,32]{3,4,0,1,2:T(8,128)(2,1)S(1)}, bf16[2,4,2,512,32]{3,4,0,1,2:T(8,128)(2,1)S(1)}, u32[]{:S(2)}, u32[]{:S(2)}) collective-permute-start(bf16[2,4,2,512,32]{3,4,0,1,2:T(8,128)(2,1)S(1)} %collective-permute-done.7), channel_id=1, source_target_pairs={{0,64},{8,72},{16,80},{24,88},{32,96},{40,104},{48,112},{56,120},{... | collective-permute-start | bytes 1572872 | tf_op jit(solution)/shard_map/ppermute | solution.py:130
  64.2 14.9 %collective-permute-start.5 = (bf16[2,4,2,512,32]{3,4,0,1,2:T(8,128)(2,1)S(1)}, bf16[2,4,2,512,32]{3,4,0,1,2:T(8,128)(2,1)S(1)}, u32[]{:S(2)}, u32[]{:S(2)}) collective-permute-start(bf16[2,4,2,512,32]{3,4,0,1,2:T(8,128)(2,1)S(1)} %collective-permute-done.4), channel_id=1, source_target_pairs={{0,448},{8,456},{16,464},{24,472},{32,480},{40,488},{48,496},{56,5... | collective-permute-start | bytes 1572872 | tf_op jit(solution)/shard_map/ppermute | solution.py:133
  73.4 15.1 %collective-permute-start.9 = (bf16[2,4,2,512,32]{3,4,0,1,2:T(8,128)(2,1)S(1)}, bf16[2,4,2,512,32]{3,4,0,1,2:T(8,128)(2,1)S(1)}, u32[]{:S(2)}, u32[]{:S(2)}) collective-permute-start(bf16[2,4,2,512,32]{3,4,0,1,2:T(8,128)(2,1)S(1)} %collective-permute-done.8), channel_id=1, source_target_pairs={{0,64},{8,72},{16,80},{24,88},{32,96},{40,104},{48,112},{56,120},{... | collective-permute-start | bytes 1572872 | tf_op jit(solution)/shard_map/ppermute | solution.py:130
  79.2 14.7 %collective-permute-start.6 = (bf16[2,4,2,512,32]{3,4,0,1,2:T(8,128)(2,1)S(1)}, bf16[2,4,2,512,32]{3,4,0,1,2:T(8,128)(2,1)S(1)}, u32[]{:S(2)}, u32[]{:S(2)}) collective-permute-start(bf16[2,4,2,512,32]{3,4,0,1,2:T(8,128)(2,1)S(1)} %collective-permute-done.5), channel_id=1, source_target_pairs={{0,448},{8,456},{16,464},{24,472},{32,480},{40,488},{48,496},{56,5... | collective-permute-start | bytes 1572872 | tf_op jit(solution)/shard_map/ppermute | solution.py:133
  88.4 14.1 %collective-permute-start.10 = (bf16[2,4,2,512,32]{3,4,0,1,2:T(8,128)(2,1)S(1)}, bf16[2,4,2,512,32]{3,4,0,1,2:T(8,128)(2,1)S(1)}, u32[]{:S(2)}, u32[]{:S(2)}) collective-permute-start(bf16[2,4,2,512,32]{3,4,0,1,2:T(8,128)(2,1)S(1)} %collective-permute-done.9), channel_id=1, source_target_pairs={{0,64},{8,72},{16,80},{24,88},{32,96},{40,104},{48,112},{56,120},{... | collective-permute-start | bytes 1572872 | tf_op jit(solution)/shard_map/ppermute | solution.py:130
  105.9 1.6 copy-start.10
  107.5 1.4 copy-start.6
  107.5 16.1 %copy-start.12 = (s32[64]{0:T(128)S(1)}, s32[64]{0:T(128)}, u32[]{:S(2)}) copy-start(s32[64]{0:T(128)} %param.50) | copy-start | bytes 772
  108.9 25.9 %copy-start.9 = (f32[2,2048]{1,0:T(2,128)S(1)}, f32[2,2048]{1,0:T(2,128)}, u32[]{:S(2)}) copy-start(f32[2,2048]{1,0:T(2,128)} %param.42) | copy-start | bytes 49156
  109.8 23.9 %all-to-all-start = ((bf16[2,8,8,2432]{3,2,0,1:T(8,128)(2,1)}), bf16[2,8,8,2432]{3,2,0,1:T(8,128)(2,1)S(1)}, u32[]{:S(2)}, u32[]{:S(2)}) async-start(bf16[2,8,8,2432]{3,2,0,1:T(8,128)(2,1)} %copy.283), calls=%async_computation | async-start | bytes 1245184 | tf_op jit(solution)/shard_map/all_to_all | solution.py:247
  116.7 80.6 %collective-permute-start.21 = (bf16[2,400,2048]{2,1,0:T(8,128)(2,1)}, bf16[2,400,2048]{2,1,0:T(8,128)(2,1)}, u32[]{:S(2)}, u32[]{:S(2)}) collective-permute-start(bf16[2,400,2048]{2,1,0:T(8,128)(2,1)} %param.44), channel_id=1, source_target_pairs={{0,8},{8,0},{16,24},{24,16},{32,40},{40,32},{48,56},{56,48},{64,72... | collective-permute-start | bytes 9830408 | tf_op jit(solution)/shard_map/ppermute | solution.py:192
  134.9 5.4 %collective-permute-start.11 = (bf16[17,2048]{1,0:T(8,128)(2,1)S(1)}, bf16[17,2048]{1,0:T(8,128)(2,1)S(1)}, u32[]{:S(2)}, u32[]{:S(2)}) collective-permute-start(bf16[17,2048]{1,0:T(8,128)(2,1)S(1)} %pad_maximum_fusion.5), channel_id=1, source_target_pairs={{0,448},{8,456},{16,464},{24,472},{32,480},{40,488},{48,496},{56,5... | collective-permute-start | bytes 208904 | tf_op jit(solution)/shard_map/ppermute | solution.py:133
  136.9 6.6 %collective-permute-start.14 = (bf16[17,2048]{1,0:T(8,128)(2,1)S(1)}, bf16[17,2048]{1,0:T(8,128)(2,1)S(1)}, u32[]{:S(2)}, u32[]{:S(2)}) collective-permute-start(bf16[17,2048]{1,0:T(8,128)(2,1)S(1)} %pad_maximum_fusion.5), channel_id=1, source_target_pairs={{0,64},{8,72},{16,80},{24,88},{32,96},{40,104},{48,112},{56,120},{... | collective-permute-start | bytes 208904 | tf_op jit(solution)/shard_map/ppermute | solution.py:130
  140.3 5.3 %collective-permute-start.12 = (bf16[17,2048]{1,0:T(8,128)(2,1)S(1)}, bf16[17,2048]{1,0:T(8,128)(2,1)S(1)}, u32[]{:S(2)}, u32[]{:S(2)}) collective-permute-start(bf16[17,2048]{1,0:T(8,128)(2,1)S(1)} %collective-permute-done.11), channel_id=1, source_target_pairs={{0,448},{8,456},{16,464},{24,472},{32,480},{40,488},{48,496},{56,5... | collective-permute-start | bytes 208904 | tf_op jit(solution)/shard_map/ppermute | solution.py:133
  143.4 6.6 %collective-permute-start.15 = (bf16[17,2048]{1,0:T(8,128)(2,1)S(1)}, bf16[17,2048]{1,0:T(8,128)(2,1)S(1)}, u32[]{:S(2)}, u32[]{:S(2)}) collective-permute-start(bf16[17,2048]{1,0:T(8,128)(2,1)S(1)} %collective-permute-done.14), channel_id=1, source_target_pairs={{0,64},{8,72},{16,80},{24,88},{32,96},{40,104},{48,112},{56,120},{... | collective-permute-start | bytes 208904 | tf_op jit(solution)/shard_map/ppermute | solution.py:130
  145.6 12.8 %collective-permute-start.13 = (bf16[17,2048]{1,0:T(8,128)(2,1)S(1)}, bf16[17,2048]{1,0:T(8,128)(2,1)S(1)}, u32[]{:S(2)}, u32[]{:S(2)}) collective-permute-start(bf16[17,2048]{1,0:T(8,128)(2,1)S(1)} %collective-permute-done.12), channel_id=1, source_target_pairs={{0,448},{8,456},{16,464},{24,472},{32,480},{40,488},{48,496},{56,5... | collective-permute-start | bytes 208904 | tf_op jit(solution)/shard_map/ppermute | solution.py:133
  150.0 6.6 %collective-permute-start.16 = (bf16[17,2048]{1,0:T(8,128)(2,1)S(1)}, bf16[17,2048]{1,0:T(8,128)(2,1)S(1)}, u32[]{:S(2)}, u32[]{:S(2)}) collective-permute-start(bf16[17,2048]{1,0:T(8,128)(2,1)S(1)} %collective-permute-done.15), channel_id=1, source_target_pairs={{0,64},{8,72},{16,80},{24,88},{32,96},{40,104},{48,112},{56,120},{... | collective-permute-start | bytes 208904 | tf_op jit(solution)/shard_map/ppermute | solution.py:130
  156.6 7.4 %collective-permute-start.17 = (bf16[17,2048]{1,0:T(8,128)(2,1)S(1)}, bf16[17,2048]{1,0:T(8,128)(2,1)S(1)}, u32[]{:S(2)}, u32[]{:S(2)}) collective-permute-start(bf16[17,2048]{1,0:T(8,128)(2,1)S(1)} %collective-permute-done.16), channel_id=1, source_target_pairs={{0,64},{8,72},{16,80},{24,88},{32,96},{40,104},{48,112},{56,120},{... | collective-permute-start | bytes 208904 | tf_op jit(solution)/shard_map/ppermute | solution.py:130
  164.3 11.5 %collective-permute-start.19 = (bf16[8,17,2048]{2,0,1:T(8,128)(2,1)S(1)}, bf16[8,17,2048]{2,0,1:T(8,128)(2,1)S(1)}, u32[]{:S(2)}, u32[]{:S(2)}) collective-permute-start(bf16[8,17,2048]{2,0,1:T(8,128)(2,1)S(1)} %copy.285), channel_id=1, source_target_pairs={{0,16},{8,24},{16,32},{24,40},{32,48},{40,56},{48,0},{56,8},{64,80... | collective-permute-start | bytes 1671176 | tf_op jit(solution)/shard_map/ppermute | solution.py:130
  166.3 11.8 %collective-permute-start.18 = (bf16[8,17,2048]{2,0,1:T(8,128)(2,1)S(1)}, bf16[8,17,2048]{2,0,1:T(8,128)(2,1)S(1)}, u32[]{:S(2)}, u32[]{:S(2)}) collective-permute-start(bf16[8,17,2048]{2,0,1:T(8,128)(2,1)S(1)} %copy.285), channel_id=1, source_target_pairs={{0,48},{8,56},{16,0},{24,8},{32,16},{40,24},{48,32},{56,40},{64,11... | collective-permute-start | bytes 1671176 | tf_op jit(solution)/shard_map/ppermute | solution.py:133
  175.8 14.5 %collective-permute-start.20 = (bf16[8,17,2048]{2,0,1:T(8,128)(2,1)S(1)}, bf16[8,17,2048]{2,0,1:T(8,128)(2,1)S(1)}, u32[]{:S(2)}, u32[]{:S(2)}) collective-permute-start(bf16[8,17,2048]{2,0,1:T(8,128)(2,1)S(1)} %collective-permute-done.19), channel_id=1, source_target_pairs={{0,16},{8,24},{16,32},{24,40},{32,48},{40,56},{48,0},{56,8},{64,80... | collective-permute-start | bytes 1671176 | tf_op jit(solution)/shard_map/ppermute | solution.py:130
  191.2 1.7 copy-start
  193.4 3.8 %copy-start.1 = (bf16[4,8,17,2048]{3,2,1,0:T(8,128)(2,1)S(1)}, bf16[4,8,17,2048]{3,2,1,0:T(8,128)(2,1)}, u32[]{:S(2)}) copy-start(bf16[4,8,17,2048]{3,2,1,0:T(8,128)(2,1)} %copy-done) | copy-start | bytes 6684676
  197.2 4.0 %copy-start.3 = (f32[3,2,8,4,8]{4,2,3,1,0:T(8,128)S(1)}, f32[3,2,8,4,8]{4,2,3,1,0:T(8,128)}, u32[]{:S(2)}) copy-start(f32[3,2,8,4,8]{4,2,3,1,0:T(8,128)} %constant.319.clone.1) | copy-start | bytes 18436
  200.4 16.3 %copy-start.16 = (s32[64]{0:T(128)S(1)}, s32[64]{0:T(128)}, u32[]{:S(2)}) copy-start(s32[64]{0:T(128)} %param.51) | copy-start | bytes 772
  202.3 26.6 %all-to-all-start.1 = ((f32[3,2,64,8]{3,1,0,2:T(2,128)}), f32[3,2,64,8]{3,1,0,2:T(2,128)S(1)}, u32[]{:S(2)}, u32[]{:S(2)}) async-start(f32[3,2,64,8]{3,1,0,2:T(2,128)} %copy.292), calls=%async_computation.1 | async-start | bytes 393216 | tf_op jit(solution)/shard_map/all_to_all | solution.py:318

commit v13 on v11

--- a/solution.py
+++ b/solution.py
@@ -4,7 +4,7 @@
 from jax.sharding import PartitionSpec as P
 
 EPSILON = 1e-05
-PRECISE = lax.Precision.HIGH
+PRECISE = lax.Precision.HIGHEST
 
 
 def merged_2(part, axis, combine):
@@ -189,9 +189,6 @@
         return [(i, i ^ 1) for i in range(shards)]
 
     vocab_part = head_weight.shape[1]
-    partner_weight = lax.ppermute(
-        head_weight, "req", [(i, i ^ 1) for i in range(shards)]
-    )
     gated = jnp.stack(
         [
             mixer_block(
@@ -280,6 +277,10 @@
     packet = jnp.concatenate([final_rows.reshape(models * row_count, full_width), target_row], axis=0)
 
     every = ring_gather(ring_gather(packet, along_z, chips_z), along_x, ROWS_X)
+    late_weight, _ = lax.optimization_barrier((head_weight, packet))
+    partner_weight = lax.ppermute(
+        late_weight, "req", [(i, i ^ 1) for i in range(shards)]
+    )
     peers = ROWS_X * chips_z
     every = every.reshape(peers, models * row_count + 1, full_width)
     every_rows = (

time: 205 us -> 213 us (1.039)
  waiting for transfers between devices: 64.2 us -> 69.1 us
    ppermute x13, waiting for transfers between devices: 37.9 us -> 40.2 us  [ring_gather(): forward = lax.ppermute(forward, 'req', perm_of(1))]
    all_to_all x1, waiting for transfers between devices: 13.8 us -> 16 us  [local(): lax.all_to_all(payload.reshape(models, groups, row_count, payload.shape[2...]
  transfers between devices with their start and end apart: 24 -> 24, of which waited for: 12 -> 12; matrix products, arithmetic and copies ran while one was open for 14% -> 15% of each run, Pallas kernels for 0% -> 0%
where the time goes in v13:
time: 213 us; the launch traced here: 212 us
  starting transfers between devices  92.2 us (43%)
  waiting for transfers between devices  69.1 us (32%)
  other arithmetic  18.9 us (9%)
  matrix products  16.9 us (8%)
  local copies, waits for them, and re-layouts  12.9 us (6%)
    ppermute x13, waiting for transfers between devices, ring_gather(): forward = lax.ppermute(forward, 'req', perm_of(1))  40.2 us
    ppermute x13, starting transfers between devices, ring_gather(): forward = lax.ppermute(forward, 'req', perm_of(1))  38 us
    ppermute x8, starting transfers between devices, ring_gather(): backward = lax.ppermute(backward, 'req', perm_of(-1))  34.4 us
    all_to_all x1, waiting for transfers between devices, local(): lax.all_to_all(payload.reshape(models, groups, row_count, payload.shape[2...  16 us
    all_to_all x1, waiting for transfers between devices, local(): lax.all_to_all(send, 'req', split_axis=2, concat_axis=2, tiled=True)  11.9 us
    all_to_all x1, starting transfers between devices, local(): lax.all_to_all(send, 'req', split_axis=2, concat_axis=2, tiled=True)  9.99 us
    dot_general x2, matrix products, head_scores(): jnp.einsum('mnd,mvd->mnv', rows_hidden, head_weight, preferred_element_ty...  6.92 us
    all_to_all x1, starting transfers between devices, local(): lax.all_to_all(payload.reshape(models, groups, row_count, payload.shape[2...  6.82 us
  transfers between devices with their start and end apart: 24, of which 12 were waited for; matrix products, arithmetic and copies ran while one was open for 15% of the time, Pallas kernels for 0%

profile of v13, /device:TPU:1, one launch (start us, length us, event | category | flops | bytes accessed | tf_op | source)
XLA Modules:
  0.0 211.8 jit_solution(18318290077177783634)
XLA Ops:
  0.1 4.1 %collective-permute-start.1 = (bf16[2,512,32]{1,2,0:T(8,128)(2,1)}, bf16[2,512,32]{1,2,0:T(8,128)(2,1)S(1)}, u32[]{:S(2)}, u32[]{:S(2)}) collective-permute-start(bf16[2,512,32]{1,2,0:T(8,128)(2,1)} %param.43), channel_id=1, source_target_pairs={{0,16},{8,24},{16,32},{24,40},{32,48},{40,56},{48,0},{56,8},{64,80... | collective-permute-start | bytes 196616 | tf_op jit(solution)/shard_map/ppermute | solution.py:130
  4.2 3.2 %collective-permute-start = (bf16[2,512,32]{1,2,0:T(8,128)(2,1)}, bf16[2,512,32]{1,2,0:T(8,128)(2,1)S(1)}, u32[]{:S(2)}, u32[]{:S(2)}) collective-permute-start(bf16[2,512,32]{1,2,0:T(8,128)(2,1)} %param.43), channel_id=1, source_target_pairs={{0,48},{8,56},{16,0},{24,8},{32,16},{40,24},{48,32},{56,40},{64,11... | collective-permute-start | bytes 196616 | tf_op jit(solution)/shard_map/ppermute | solution.py:133
  7.3 0.8 reduce-window.4
  8.2 0.7 compare_and_fusion
  8.8 0.7 fusion.166
  9.5 0.9 slice_convert_fusion.1
  10.5 0.9 slice_convert_fusion.3
  11.7 0.7 fusion.167
  12.3 0.8 fusion.175
  16.6 0.7 compare_select_fusion.1
  19.5 2.1 collective-permute-start.2
  21.6 1.0 fusion.10
  22.9 2.8 %collective-permute-done.2 = bf16[2,512,32]{1,2,0:T(8,128)(2,1)S(1)} collective-permute-done((bf16[2,512,32]{1,2,0:T(8,128)(2,1)S(1)}, bf16[2,512,32]{1,2,0:T(8,128)(2,1)S(1)}, u32[]{:S(2)}, u32[]{:S(2)}) %collective-permute-start.2) | collective-permute-done | bytes 65568 | tf_op jit(solution)/shard_map/ppermute | solution.py:130
  25.7 4.2 %collective-permute-start.6 = (bf16[4,2,512,32]{2,3,0,1:T(8,128)(2,1)S(1)}, bf16[4,2,512,32]{2,3,0,1:T(8,128)(2,1)S(1)}, u32[]{:S(2)}, u32[]{:S(2)}) collective-permute-start(bf16[4,2,512,32]{2,3,0,1:T(8,128)(2,1)S(1)} %pad_maximum_fusion.2), channel_id=1, source_target_pairs={{0,64},{8,72},{16,80},{24,88},{32,96},{40,104},{48,112},{56,120},{... | collective-permute-start | bytes 786440 | tf_op jit(solution)/shard_map/ppermute | solution.py:130
  29.9 0.7 fusion.12
  30.6 8.6 %collective-permute-start.3 = (bf16[4,2,512,32]{2,3,0,1:T(8,128)(2,1)S(1)}, bf16[4,2,512,32]{2,3,0,1:T(8,128)(2,1)S(1)}, u32[]{:S(2)}, u32[]{:S(2)}) collective-permute-start(bf16[4,2,512,32]{2,3,0,1:T(8,128)(2,1)S(1)} %pad_maximum_fusion.2), channel_id=1, source_target_pairs={{0,448},{8,456},{16,464},{24,472},{32,480},{40,488},{48,496},{56,5... | collective-permute-start | bytes 786440 | tf_op jit(solution)/shard_map/ppermute | solution.py:133
  39.4 1.4 collective-permute-done.6
  40.8 1.9 collective-permute-start.7
  42.9 4.6 %collective-permute-start.4 = (bf16[4,2,512,32]{2,3,0,1:T(8,128)(2,1)S(1)}, bf16[4,2,512,32]{2,3,0,1:T(8,128)(2,1)S(1)}, u32[]{:S(2)}, u32[]{:S(2)}) collective-permute-start(bf16[4,2,512,32]{2,3,0,1:T(8,128)(2,1)S(1)} %collective-permute-done.3), channel_id=1, source_target_pairs={{0,448},{8,456},{16,464},{24,472},{32,480},{40,488},{48,496},{56,5... | collective-permute-start | bytes 786440 | tf_op jit(solution)/shard_map/ppermute | solution.py:133
  47.9 1.2 collective-permute-done.7
  49.1 1.9 collective-permute-start.8
  51.2 4.6 %collective-permute-start.5 = (bf16[4,2,512,32]{2,3,0,1:T(8,128)(2,1)S(1)}, bf16[4,2,512,32]{2,3,0,1:T(8,128)(2,1)S(1)}, u32[]{:S(2)}, u32[]{:S(2)}) collective-permute-start(bf16[4,2,512,32]{2,3,0,1:T(8,128)(2,1)S(1)} %collective-permute-done.4), channel_id=1, source_target_pairs={{0,448},{8,456},{16,464},{24,472},{32,480},{40,488},{48,496},{56,5... | collective-permute-start | bytes 786440 | tf_op jit(solution)/shard_map/ppermute | solution.py:133
  55.9 1.6 collective-permute-done.8
  57.4 1.9 collective-permute-start.9
  59.4 6.3 %collective-permute-done.9 = bf16[4,2,512,32]{2,3,0,1:T(8,128)(2,1)S(1)} collective-permute-done((bf16[4,2,512,32]{2,3,0,1:T(8,128)(2,1)S(1)}, bf16[4,2,512,32]{2,3,0,1:T(8,128)(2,1)S(1)}, u32[]{:S(2)}, u32[]{:S(2)}) %collective-permute-start.9) | collective-permute-done | bytes 262176 | tf_op jit(solution)/shard_map/ppermute | solution.py:130
  65.9 8.5 %collective-permute-start.10 = (bf16[8,4,2,512,32]{3,4,1,0,2:T(8,128)(2,1)S(1)}, bf16[8,4,2,512,32]{3,4,1,0,2:T(8,128)(2,1)}, u32[]{:S(2)}, u32[]{:S(2)}) collective-permute-start(bf16[8,4,2,512,32]{3,4,1,0,2:T(8,128)(2,1)S(1)} %bitcast_dynamic-update-slice_fusion.7), channel_id=1, source_target_pairs={{0,8},{8,0},{16,24},{24,16},{32,40},{40,32},{48,56},{56,48},{64,72... | collective-permute-start | bytes 6291464 | tf_op jit(solution)/shard_map/ppermute | solution.py:130
  74.5 1.0 fusion.9
  76.4 1.0 divide_multiply_fusion.1
  77.7 0.7 gather_fusion
  78.6 1.0 fusion.83
  79.6 0.7 fusion.14
  80.8 2.0 maximum_bitcast_fusion
  82.8 1.6 fusion.2
  84.4 1.6 fusion.1
  85.9 1.6 fusion
  87.5 1.4 convolution_convert_fusion
  89.0 0.9 copy.283
  89.9 6.8 %all-to-all-start = ((bf16[2,8,8,2432]{3,2,0,1:T(8,128)(2,1)}), bf16[2,8,8,2432]{3,2,0,1:T(8,128)(2,1)S(1)}, u32[]{:S(2)}, u32[]{:S(2)}) async-start(bf16[2,8,8,2432]{3,2,0,1:T(8,128)(2,1)} %copy.283), calls=%async_computation | async-start | bytes 1245184 | tf_op jit(solution)/shard_map/all_to_all | solution.py:244
  97.9 0.7 fusion.163
  98.6 1.4 broadcast_select_fusion
  100.0 0.9 scatter.19
  100.9 16.0 %all-to-all-done = bf16[2,8,8,2432]{3,2,0,1:T(8,128)(2,1)S(1)} async-done(((bf16[2,8,8,2432]{3,2,0,1:T(8,128)(2,1)}), bf16[2,8,8,2432]{3,2,0,1:T(8,128)(2,1)S(1)}, u32[]{:S(2)}, u32[]{:S(2)}) %all-to-all-start) | async-done | bytes 622624 | tf_op jit(solution)/shard_map/all_to_all | solution.py:244
  118.0 1.9 collective-permute-start.11
  120.0 3.4 %collective-permute-start.14 = (bf16[17,2048]{1,0:T(8,128)(2,1)S(1)}, bf16[17,2048]{1,0:T(8,128)(2,1)S(1)}, u32[]{:S(2)}, u32[]{:S(2)}) collective-permute-start(bf16[17,2048]{1,0:T(8,128)(2,1)S(1)} %pad_maximum_fusion.4), channel_id=1, source_target_pairs={{0,64},{8,72},{16,80},{24,88},{32,96},{40,104},{48,112},{56,120},{... | collective-permute-start | bytes 208904 | tf_op jit(solution)/shard_map/ppermute | solution.py:130
  123.3 2.9 %collective-permute-start.21 = (bf16[2,400,2048]{2,1,0:T(8,128)(2,1)}, bf16[2,400,2048]{2,1,0:T(8,128)(2,1)}, u32[]{:S(2)}, u32[]{:S(2)}) collective-permute-start(bf16[2,400,2048]{2,1,0:T(8,128)(2,1)} %param.44), channel_id=1, source_target_pairs={{0,8},{8,0},{16,24},{24,16},{32,40},{40,32},{48,56},{56,48},{64,72... | collective-permute-start | bytes 9830408 | tf_op jit(solution)/shard_map/ppermute | solution.py:281
  126.3 2.9 %collective-permute-start.12 = (bf16[17,2048]{1,0:T(8,128)(2,1)S(1)}, bf16[17,2048]{1,0:T(8,128)(2,1)S(1)}, u32[]{:S(2)}, u32[]{:S(2)}) collective-permute-start(bf16[17,2048]{1,0:T(8,128)(2,1)S(1)} %collective-permute-done.11), channel_id=1, source_target_pairs={{0,448},{8,456},{16,464},{24,472},{32,480},{40,488},{48,496},{56,5... | collective-permute-start | bytes 208904 | tf_op jit(solution)/shard_map/ppermute | solution.py:133
  129.2 2.4 %collective-permute-start.15 = (bf16[17,2048]{1,0:T(8,128)(2,1)S(1)}, bf16[17,2048]{1,0:T(8,128)(2,1)S(1)}, u32[]{:S(2)}, u32[]{:S(2)}) collective-permute-start(bf16[17,2048]{1,0:T(8,128)(2,1)S(1)} %collective-permute-done.14), channel_id=1, source_target_pairs={{0,64},{8,72},{16,80},{24,88},{32,96},{40,104},{48,112},{56,120},{... | collective-permute-start | bytes 208904 | tf_op jit(solution)/shard_map/ppermute | solution.py:130
  131.6 1.0 collective-permute-done.12
  132.6 4.0 %collective-permute-start.13 = (bf16[17,2048]{1,0:T(8,128)(2,1)S(1)}, bf16[17,2048]{1,0:T(8,128)(2,1)S(1)}, u32[]{:S(2)}, u32[]{:S(2)}) collective-permute-start(bf16[17,2048]{1,0:T(8,128)(2,1)S(1)} %collective-permute-done.12), channel_id=1, source_target_pairs={{0,448},{8,456},{16,464},{24,472},{32,480},{40,488},{48,496},{56,5... | collective-permute-start | bytes 208904 | tf_op jit(solution)/shard_map/ppermute | solution.py:133
  136.7 1.9 collective-permute-start.16
  138.6 4.6 %collective-permute-done.16 = bf16[17,2048]{1,0:T(8,128)(2,1)S(1)} collective-permute-done((bf16[17,2048]{1,0:T(8,128)(2,1)S(1)}, bf16[17,2048]{1,0:T(8,128)(2,1)S(1)}, u32[]{:S(2)}, u32[]{:S(2)}) %collective-permute-start.16) | collective-permute-done | bytes 69664 | tf_op jit(solution)/shard_map/ppermute | solution.py:130
  143.2 1.9 collective-permute-start.17
  145.2 4.6 %collective-permute-done.17 = bf16[17,2048]{1,0:T(8,128)(2,1)S(1)} collective-permute-done((bf16[17,2048]{1,0:T(8,128)(2,1)S(1)}, bf16[17,2048]{1,0:T(8,128)(2,1)S(1)}, u32[]{:S(2)}, u32[]{:S(2)}) %collective-permute-start.17) | collective-permute-done | bytes 69664 | tf_op jit(solution)/shard_map/ppermute | solution.py:130
  150.2 1.9 collective-permute-start.19
  152.1 4.6 %collective-permute-start.18 = (bf16[8,17,2048]{2,0,1:T(8,128)(2,1)S(1)}, bf16[8,17,2048]{2,0,1:T(8,128)(2,1)S(1)}, u32[]{:S(2)}, u32[]{:S(2)}) collective-permute-start(bf16[8,17,2048]{2,0,1:T(8,128)(2,1)S(1)} %copy.285), channel_id=1, source_target_pairs={{0,48},{8,56},{16,0},{24,8},{32,16},{40,24},{48,32},{56,40},{64,11... | collective-permute-start | bytes 1671176 | tf_op jit(solution)/shard_map/ppermute | solution.py:133
  156.7 7.3 %collective-permute-done.19 = bf16[8,17,2048]{2,0,1:T(8,128)(2,1)S(1)} collective-permute-done((bf16[8,17,2048]{2,0,1:T(8,128)(2,1)S(1)}, bf16[8,17,2048]{2,0,1:T(8,128)(2,1)S(1)}, u32[]{:S(2)}, u32[]{:S(2)}) %collective-permute-start.19) | collective-permute-done | bytes 557088 | tf_op jit(solution)/shard_map/ppermute | solution.py:130
  164.1 1.9 collective-permute-start.20
  166.7 10.3 %collective-permute-done.20 = bf16[8,17,2048]{2,0,1:T(8,128)(2,1)S(1)} collective-permute-done((bf16[8,17,2048]{2,0,1:T(8,128)(2,1)S(1)}, bf16[8,17,2048]{2,0,1:T(8,128)(2,1)S(1)}, u32[]{:S(2)}, u32[]{:S(2)}) %collective-permute-start.20) | collective-permute-done | bytes 557088 | tf_op jit(solution)/shard_map/ppermute | solution.py:130
  177.9 1.7 copy-done
  180.1 3.8 %fusion.183 = (f32[2,256]{1,0:T(2,128)S(1)}, f32[2,256,400]{1,2,0:T(8,128)S(1)}) fusion(bf16[2,400,2048]{2,1,0:T(8,128)(2,1)} %param.44, bf16[32,17,2048]{2,1,0:T(8,128)(2,1)} %bitcast.372), kind=kOutput, calls=%fused_computation.347 | convolution fusion | flops 839065088 | bytes 6195200 | tf_op jit(solution)/shard_map/mnd,mvd->mnv/dot_general | solution.py:115
  183.9 3.1 %fusion.184 = (f32[2,256]{1,0:T(2,128)S(1)}, f32[2,256,400]{1,2,0:T(8,128)S(1)}) fusion(bf16[2,400,2048]{2,1,0:T(8,128)(2,1)} %collective-permute-done.21, bf16[32,17,2048]{2,1,0:T(8,128)(2,1)S(1)} %bitcast.373), kind=kOutput, calls=%fused_computation.348 | convolution fusion | flops 839065088 | bytes 6195200 | tf_op jit(solution)/shard_map/mnd,mvd->mnv/dot_general | solution.py:115
  188.1 0.8 copy.292
  188.9 10.0 %all-to-all-start.1 = ((f32[3,2,64,8]{3,1,0,2:T(2,128)}), f32[3,2,64,8]{3,1,0,2:T(2,128)S(1)}, u32[]{:S(2)}, u32[]{:S(2)}) async-start(f32[3,2,64,8]{3,1,0,2:T(2,128)} %copy.292), calls=%async_computation.1 | async-start | bytes 393216 | tf_op jit(solution)/shard_map/all_to_all | solution.py:319
  199.0 11.9 %all-to-all-done.1 = f32[3,2,64,8]{3,1,0,2:T(2,128)S(1)} async-done(((f32[3,2,64,8]{3,1,0,2:T(2,128)}), f32[3,2,64,8]{3,1,0,2:T(2,128)S(1)}, u32[]{:S(2)}, u32[]{:S(2)}) %all-to-all-start.1) | async-done | bytes 12320 | tf_op jit(solution)/shard_map/all_to_all | solution.py:319
  (236 shorter events, 15.3 us)
Async XLA Ops:
  0.0 18.5 %copy-start.3 = (bf16[2,64,512]{2,1,0:T(8,128)(2,1)S(1)}, bf16[2,64,512]{2,1,0:T(8,128)(2,1)}, u32[]{:S(2)}) copy-start(bf16[2,64,512]{2,1,0:T(8,128)(2,1)} %param.32) | copy-start | bytes 393220
  0.0 15.7 %copy-start.6 = (bf16[2,64,256]{2,1,0:T(8,128)(2,1)S(1)}, bf16[2,64,256]{2,1,0:T(8,128)(2,1)}, u32[]{:S(2)}) copy-start(bf16[2,64,256]{2,1,0:T(8,128)(2,1)} %param.33) | copy-start | bytes 196612
  0.0 14.4 %copy-start.11 = (f32[2,4,512]{2,1,0:T(4,128)S(1)}, f32[2,4,512]{2,1,0:T(4,128)}, u32[]{:S(2)}) copy-start(f32[2,4,512]{2,1,0:T(4,128)} %param.36) | copy-start | bytes 49156
  0.0 15.2 %copy-start.9 = (bf16[2,3,3,256]{3,0,2,1:T(2,128)(2,1)S(1)}, bf16[2,3,3,256]{3,0,2,1:T(2,128)(2,1)}, u32[]{:S(2)}) copy-start(bf16[2,3,3,256]{3,0,2,1:T(2,128)(2,1)} %param.46) | copy-start | bytes 27652
  0.0 15.7 %copy-start.15 = (f32[2,4,256]{2,1,0:T(4,128)S(1)}, f32[2,4,256]{2,1,0:T(4,128)}, u32[]{:S(2)}) copy-start(f32[2,4,256]{2,1,0:T(4,128)} %param.37) | copy-start | bytes 24580
  0.0 16.2 %copy-start.22 = (f32[2,8]{1,0:T(2,128)S(1)}, f32[2,8]{1,0:T(2,128)}, u32[]{:S(2)}) copy-start(f32[2,8]{1,0:T(2,128)} %param.38) | copy-start | bytes 196
  0.0 16.2 %copy-start.21 = (f32[2,8]{1,0:T(2,128)S(1)}, f32[2,8]{1,0:T(2,128)}, u32[]{:S(2)}) copy-start(f32[2,8]{1,0:T(2,128)} %param.39) | copy-start | bytes 196
  0.0 16.2 %copy-start.12 = (bf16[2,64,8]{1,2,0:T(8,128)(2,1)S(1)}, bf16[2,64,8]{1,2,0:T(8,128)(2,1)}, u32[]{:S(2)}) copy-start(bf16[2,64,8]{1,2,0:T(8,128)(2,1)} %param.34) | copy-start | bytes 6148
  0.1 19.4 %collective-permute-start.1 = (bf16[2,512,32]{1,2,0:T(8,128)(2,1)}, bf16[2,512,32]{1,2,0:T(8,128)(2,1)S(1)}, u32[]{:S(2)}, u32[]{:S(2)}) collective-permute-start(bf16[2,512,32]{1,2,0:T(8,128)(2,1)} %param.43), channel_id=1, source_target_pairs={{0,16},{8,24},{16,32},{24,40},{32,48},{40,56},{48,0},{56,8},{64,80... | collective-permute-start | bytes 196616 | tf_op jit(solution)/shard_map/ppermute | solution.py:130
  4.2 18.7 %collective-permute-start = (bf16[2,512,32]{1,2,0:T(8,128)(2,1)}, bf16[2,512,32]{1,2,0:T(8,128)(2,1)S(1)}, u32[]{:S(2)}, u32[]{:S(2)}) collective-permute-start(bf16[2,512,32]{1,2,0:T(8,128)(2,1)} %param.43), channel_id=1, source_target_pairs={{0,48},{8,56},{16,0},{24,8},{32,16},{40,24},{48,32},{56,40},{64,11... | collective-permute-start | bytes 196616 | tf_op jit(solution)/shard_map/ppermute | solution.py:133
  11.4 14.3 %copy-start.2 = (bf16[2,512,32]{1,2,0:T(8,128)(2,1)S(1)}, bf16[2,512,32]{1,2,0:T(8,128)(2,1)}, u32[]{:S(2)}) copy-start(bf16[2,512,32]{1,2,0:T(8,128)(2,1)} %param.43) | copy-start | bytes 196612
  14.4 33.1 %copy-start.25 = (pred[64]{0:T(512)(128)(4,1)}, pred[64]{0:T(512)(128)(4,1)S(1)}, u32[]{:S(2)}) copy-start(pred[64]{0:T(512)(128)(4,1)S(1)} %get-tuple-element.123) | copy-start | bytes 196
  14.4 33.1 %copy-start.27 = (pred[64]{0:T(512)(128)(4,1)}, pred[64]{0:T(512)(128)(4,1)S(1)}, u32[]{:S(2)}) copy-start(pred[64]{0:T(512)(128)(4,1)S(1)} %get-tuple-element.124) | copy-start | bytes 196
  14.5 33.1 %copy-start.29 = (pred[64]{0:T(512)(128)(4,1)}, pred[64]{0:T(512)(128)(4,1)S(1)}, u32[]{:S(2)}) copy-start(pred[64]{0:T(512)(128)(4,1)S(1)} %get-tuple-element.125) | copy-start | bytes 196
  14.5 33.1 %copy-start.31 = (pred[64]{0:T(512)(128)(4,1)}, pred[64]{0:T(512)(128)(4,1)S(1)}, u32[]{:S(2)}) copy-start(pred[64]{0:T(512)(128)(4,1)S(1)} %get-tuple-element.126) | copy-start | bytes 196
  14.5 33.1 %copy-start.33 = (pred[64]{0:T(512)(128)(4,1)}, pred[64]{0:T(512)(128)(4,1)S(1)}, u32[]{:S(2)}) copy-start(pred[64]{0:T(512)(128)(4,1)S(1)} %get-tuple-element.127) | copy-start | bytes 196
  14.5 33.1 %copy-start.35 = (pred[64]{0:T(512)(128)(4,1)}, pred[64]{0:T(512)(128)(4,1)S(1)}, u32[]{:S(2)}) copy-start(pred[64]{0:T(512)(128)(4,1)S(1)} %get-tuple-element.128) | copy-start | bytes 196
  14.5 33.1 %copy-start.37 = (pred[64]{0:T(512)(128)(4,1)}, pred[64]{0:T(512)(128)(4,1)S(1)}, u32[]{:S(2)}) copy-start(pred[64]{0:T(512)(128)(4,1)S(1)} %get-tuple-element.129) | copy-start | bytes 196
  14.5 33.1 %copy-start.39 = (pred[64]{0:T(512)(128)(4,1)}, pred[64]{0:T(512)(128)(4,1)S(1)}, u32[]{:S(2)}) copy-start(pred[64]{0:T(512)(128)(4,1)S(1)} %get-tuple-element.130) | copy-start | bytes 196
  14.5 33.1 %copy-start.41 = (pred[64]{0:T(512)(128)(4,1)}, pred[64]{0:T(512)(128)(4,1)S(1)}, u32[]{:S(2)}) copy-start(pred[64]{0:T(512)(128)(4,1)S(1)} %get-tuple-element.131) | copy-start | bytes 196
  14.5 33.1 %copy-start.43 = (pred[64]{0:T(512)(128)(4,1)}, pred[64]{0:T(512)(128)(4,1)S(1)}, u32[]{:S(2)}) copy-start(pred[64]{0:T(512)(128)(4,1)S(1)} %get-tuple-element.132) | copy-start | bytes 196
  14.5 33.1 %copy-start.45 = (pred[64]{0:T(512)(128)(4,1)}, pred[64]{0:T(512)(128)(4,1)S(1)}, u32[]{:S(2)}) copy-start(pred[64]{0:T(512)(128)(4,1)S(1)} %get-tuple-element.133) | copy-start | bytes 196
  14.5 33.1 %copy-start.47 = (pred[64]{0:T(512)(128)(4,1)}, pred[64]{0:T(512)(128)(4,1)S(1)}, u32[]{:S(2)}) copy-start(pred[64]{0:T(512)(128)(4,1)S(1)} %get-tuple-element.134) | copy-start | bytes 196
  19.5 6.2 %collective-permute-start.2 = (bf16[2,512,32]{1,2,0:T(8,128)(2,1)S(1)}, bf16[2,512,32]{1,2,0:T(8,128)(2,1)S(1)}, u32[]{:S(2)}, u32[]{:S(2)}) collective-permute-start(bf16[2,512,32]{1,2,0:T(8,128)(2,1)S(1)} %collective-permute-done.1), channel_id=1, source_target_pairs={{0,16},{8,24},{16,32},{24,40},{32,48},{40,56},{48,0},{56,8},{64,80... | collective-permute-start | bytes 196616 | tf_op jit(solution)/shard_map/ppermute | solution.py:130
  25.7 15.1 %collective-permute-start.6 = (bf16[4,2,512,32]{2,3,0,1:T(8,128)(2,1)S(1)}, bf16[4,2,512,32]{2,3,0,1:T(8,128)(2,1)S(1)}, u32[]{:S(2)}, u32[]{:S(2)}) collective-permute-start(bf16[4,2,512,32]{2,3,0,1:T(8,128)(2,1)S(1)} %pad_maximum_fusion.2), channel_id=1, source_target_pairs={{0,64},{8,72},{16,80},{24,88},{32,96},{40,104},{48,112},{56,120},{... | collective-permute-start | bytes 786440 | tf_op jit(solution)/shard_map/ppermute | solution.py:130
  29.9 44.5 %copy-start.50 = (bf16[2,3,512,128]{3,2,1,0:T(8,128)(2,1)S(1)}, bf16[2,3,512,128]{3,2,1,0:T(8,128)(2,1)}, u32[]{:S(2)}) copy-start(bf16[2,3,512,128]{3,2,1,0:T(8,128)(2,1)} %param.47) | copy-start | bytes 2359300
  30.6 12.3 %collective-permute-start.3 = (bf16[4,2,512,32]{2,3,0,1:T(8,128)(2,1)S(1)}, bf16[4,2,512,32]{2,3,0,1:T(8,128)(2,1)S(1)}, u32[]{:S(2)}, u32[]{:S(2)}) collective-permute-start(bf16[4,2,512,32]{2,3,0,1:T(8,128)(2,1)S(1)} %pad_maximum_fusion.2), channel_id=1, source_target_pairs={{0,448},{8,456},{16,464},{24,472},{32,480},{40,488},{48,496},{56,5... | collective-permute-start | bytes 786440 | tf_op jit(solution)/shard_map/ppermute | solution.py:133
  40.8 8.3 %collective-permute-start.7 = (bf16[4,2,512,32]{2,3,0,1:T(8,128)(2,1)S(1)}, bf16[4,2,512,32]{2,3,0,1:T(8,128)(2,1)S(1)}, u32[]{:S(2)}, u32[]{:S(2)}) collective-permute-start(bf16[4,2,512,32]{2,3,0,1:T(8,128)(2,1)S(1)} %collective-permute-done.6), channel_id=1, source_target_pairs={{0,64},{8,72},{16,80},{24,88},{32,96},{40,104},{48,112},{56,120},{... | collective-permute-start | bytes 786440 | tf_op jit(solution)/shard_map/ppermute | solution.py:130
  42.9 8.3 %collective-permute-start.4 = (bf16[4,2,512,32]{2,3,0,1:T(8,128)(2,1)S(1)}, bf16[4,2,512,32]{2,3,0,1:T(8,128)(2,1)S(1)}, u32[]{:S(2)}, u32[]{:S(2)}) collective-permute-start(bf16[4,2,512,32]{2,3,0,1:T(8,128)(2,1)S(1)} %collective-permute-done.3), channel_id=1, source_target_pairs={{0,448},{8,456},{16,464},{24,472},{32,480},{40,488},{48,496},{56,5... | collective-permute-start | bytes 786440 | tf_op jit(solution)/shard_map/ppermute | solution.py:133
  47.9 26.5 %copy-start.8 = (f32[64,256]{1,0:T(8,128)}, f32[64,256]{1,0:T(8,128)S(1)}, u32[]{:S(2)}) copy-start(f32[64,256]{1,0:T(8,128)S(1)} %divide_multiply_fusion.3) | copy-start | bytes 196612
  49.1 8.3 %collective-permute-start.8 = (bf16[4,2,512,32]{2,3,0,1:T(8,128)(2,1)S(1)}, bf16[4,2,512,32]{2,3,0,1:T(8,128)(2,1)S(1)}, u32[]{:S(2)}, u32[]{:S(2)}) collective-permute-start(bf16[4,2,512,32]{2,3,0,1:T(8,128)(2,1)S(1)} %collective-permute-done.7), channel_id=1, source_target_pairs={{0,64},{8,72},{16,80},{24,88},{32,96},{40,104},{48,112},{56,120},{... | collective-permute-start | bytes 786440 | tf_op jit(solution)/shard_map/ppermute | solution.py:130
  51.1 25.2 %copy-start.26 = (pred[64]{0:T(512)(128)(4,1)S(1)}, pred[64]{0:T(512)(128)(4,1)}, u32[]{:S(2)}) copy-start(pred[64]{0:T(512)(128)(4,1)} %copy-done.25) | copy-start | bytes 196
  51.1 25.2 %copy-start.28 = (pred[64]{0:T(512)(128)(4,1)S(1)}, pred[64]{0:T(512)(128)(4,1)}, u32[]{:S(2)}) copy-start(pred[64]{0:T(512)(128)(4,1)} %copy-done.27) | copy-start | bytes 196
  51.1 25.2 %copy-start.30 = (pred[64]{0:T(512)(128)(4,1)S(1)}, pred[64]{0:T(512)(128)(4,1)}, u32[]{:S(2)}) copy-start(pred[64]{0:T(512)(128)(4,1)} %copy-done.29) | copy-start | bytes 196
  51.1 25.2 %copy-start.32 = (pred[64]{0:T(512)(128)(4,1)S(1)}, pred[64]{0:T(512)(128)(4,1)}, u32[]{:S(2)}) copy-start(pred[64]{0:T(512)(128)(4,1)} %copy-done.31) | copy-start | bytes 196
  51.1 25.2 %copy-start.34 = (pred[64]{0:T(512)(128)(4,1)S(1)}, pred[64]{0:T(512)(128)(4,1)}, u32[]{:S(2)}) copy-start(pred[64]{0:T(512)(128)(4,1)} %copy-done.33) | copy-start | bytes 196
  51.1 25.2 %copy-start.36 = (pred[64]{0:T(512)(128)(4,1)S(1)}, pred[64]{0:T(512)(128)(4,1)}, u32[]{:S(2)}) copy-start(pred[64]{0:T(512)(128)(4,1)} %copy-done.35) | copy-start | bytes 196
  51.1 25.2 %copy-start.38 = (pred[64]{0:T(512)(128)(4,1)S(1)}, pred[64]{0:T(512)(128)(4,1)}, u32[]{:S(2)}) copy-start(pred[64]{0:T(512)(128)(4,1)} %copy-done.37) | copy-start | bytes 196
  51.1 25.2 %copy-start.40 = (pred[64]{0:T(512)(128)(4,1)S(1)}, pred[64]{0:T(512)(128)(4,1)}, u32[]{:S(2)}) copy-start(pred[64]{0:T(512)(128)(4,1)} %copy-done.39) | copy-start | bytes 196
  51.2 25.2 %copy-start.42 = (pred[64]{0:T(512)(128)(4,1)S(1)}, pred[64]{0:T(512)(128)(4,1)}, u32[]{:S(2)}) copy-start(pred[64]{0:T(512)(128)(4,1)} %copy-done.41) | copy-start | bytes 196
  51.2 25.2 %copy-start.44 = (pred[64]{0:T(512)(128)(4,1)S(1)}, pred[64]{0:T(512)(128)(4,1)}, u32[]{:S(2)}) copy-start(pred[64]{0:T(512)(128)(4,1)} %copy-done.43) | copy-start | bytes 196
  51.2 25.2 %copy-start.46 = (pred[64]{0:T(512)(128)(4,1)S(1)}, pred[64]{0:T(512)(128)(4,1)}, u32[]{:S(2)}) copy-start(pred[64]{0:T(512)(128)(4,1)} %copy-done.45) | copy-start | bytes 196
  51.2 25.2 %copy-start.48 = (pred[64]{0:T(512)(128)(4,1)S(1)}, pred[64]{0:T(512)(128)(4,1)}, u32[]{:S(2)}) copy-start(pred[64]{0:T(512)(128)(4,1)} %copy-done.47) | copy-start | bytes 196
  51.2 8.2 %collective-permute-start.5 = (bf16[4,2,512,32]{2,3,0,1:T(8,128)(2,1)S(1)}, bf16[4,2,512,32]{2,3,0,1:T(8,128)(2,1)S(1)}, u32[]{:S(2)}, u32[]{:S(2)}) collective-permute-start(bf16[4,2,512,32]{2,3,0,1:T(8,128)(2,1)S(1)} %collective-permute-done.4), channel_id=1, source_target_pairs={{0,448},{8,456},{16,464},{24,472},{32,480},{40,488},{48,496},{56,5... | collective-permute-start | bytes 786440 | tf_op jit(solution)/shard_map/ppermute | solution.py:133
  57.4 8.3 %collective-permute-start.9 = (bf16[4,2,512,32]{2,3,0,1:T(8,128)(2,1)S(1)}, bf16[4,2,512,32]{2,3,0,1:T(8,128)(2,1)S(1)}, u32[]{:S(2)}, u32[]{:S(2)}) collective-permute-start(bf16[4,2,512,32]{2,3,0,1:T(8,128)(2,1)S(1)} %collective-permute-done.8), channel_id=1, source_target_pairs={{0,64},{8,72},{16,80},{24,88},{32,96},{40,104},{48,112},{56,120},{... | collective-permute-start | bytes 786440 | tf_op jit(solution)/shard_map/ppermute | solution.py:130
  65.8 12.6 %copy-start.24 = (pred[3]{0:T(512)(128)(4,1)S(1)}, pred[3]{0:T(512)(128)(4,1)}, u32[]{:S(2)}) copy-start(pred[3]{0:T(512)(128)(4,1)} %copy-done.23) | copy-start | bytes 13
  65.8 13.8 %copy-start.10 = (f32[64,8]{0,1:T(8,128)S(1)}, f32[64,8]{0,1:T(8,128)}, u32[]{:S(2)}) copy-start(f32[64,8]{0,1:T(8,128)} %get-tuple-element.106) | copy-start | bytes 6148
  65.8 13.8 %copy-start.19 = (f32[8]{0:T(128)S(1)}, f32[8]{0:T(128)}, u32[]{:S(2)}) copy-start(f32[8]{0:T(128)} %get-tuple-element.115) | copy-start | bytes 100
  65.9 14.5 %copy-start.4 = (bf16[2,64,512]{2,1,0:T(8,128)(2,1)S(1)}, bf16[2,64,512]{2,1,0:T(8,128)(2,1)}, u32[]{:S(2)}) copy-start(bf16[2,64,512]{2,1,0:T(8,128)(2,1)} %param.31) | copy-start | bytes 393220
  65.9 14.9 %collective-permute-start.10 = (bf16[8,4,2,512,32]{3,4,1,0,2:T(8,128)(2,1)S(1)}, bf16[8,4,2,512,32]{3,4,1,0,2:T(8,128)(2,1)}, u32[]{:S(2)}, u32[]{:S(2)}) collective-permute-start(bf16[8,4,2,512,32]{3,4,1,0,2:T(8,128)(2,1)S(1)} %bitcast_dynamic-update-slice_fusion.7), channel_id=1, source_target_pairs={{0,8},{8,0},{16,24},{24,16},{32,40},{40,32},{48,56},{56,48},{64,72... | collective-permute-start | bytes 6291464 | tf_op jit(solution)/shard_map/ppermute | solution.py:130
  89.0 28.9 %copy-start.14 = (f32[2,2048]{1,0:T(2,128)S(1)}, f32[2,2048]{1,0:T(2,128)}, u32[]{:S(2)}) copy-start(f32[2,2048]{1,0:T(2,128)} %param.42) | copy-start | bytes 49156
  89.9 27.0 %all-to-all-start = ((bf16[2,8,8,2432]{3,2,0,1:T(8,128)(2,1)}), bf16[2,8,8,2432]{3,2,0,1:T(8,128)(2,1)S(1)}, u32[]{:S(2)}, u32[]{:S(2)}) async-start(bf16[2,8,8,2432]{3,2,0,1:T(8,128)(2,1)} %copy.283), calls=%async_computation | async-start | bytes 1245184 | tf_op jit(solution)/shard_map/all_to_all | solution.py:244
  118.0 8.3 %collective-permute-start.11 = (bf16[17,2048]{1,0:T(8,128)(2,1)S(1)}, bf16[17,2048]{1,0:T(8,128)(2,1)S(1)}, u32[]{:S(2)}, u32[]{:S(2)}) collective-permute-start(bf16[17,2048]{1,0:T(8,128)(2,1)S(1)} %pad_maximum_fusion.4), channel_id=1, source_target_pairs={{0,448},{8,456},{16,464},{24,472},{32,480},{40,488},{48,496},{56,5... | collective-permute-start | bytes 208904 | tf_op jit(solution)/shard_map/ppermute | solution.py:133
  120.0 9.2 %collective-permute-start.14 = (bf16[17,2048]{1,0:T(8,128)(2,1)S(1)}, bf16[17,2048]{1,0:T(8,128)(2,1)S(1)}, u32[]{:S(2)}, u32[]{:S(2)}) collective-permute-start(bf16[17,2048]{1,0:T(8,128)(2,1)S(1)} %pad_maximum_fusion.4), channel_id=1, source_target_pairs={{0,64},{8,72},{16,80},{24,88},{32,96},{40,104},{48,112},{56,120},{... | collective-permute-start | bytes 208904 | tf_op jit(solution)/shard_map/ppermute | solution.py:130
  123.3 60.5 %collective-permute-start.21 = (bf16[2,400,2048]{2,1,0:T(8,128)(2,1)}, bf16[2,400,2048]{2,1,0:T(8,128)(2,1)}, u32[]{:S(2)}, u32[]{:S(2)}) collective-permute-start(bf16[2,400,2048]{2,1,0:T(8,128)(2,1)} %param.44), channel_id=1, source_target_pairs={{0,8},{8,0},{16,24},{24,16},{32,40},{40,32},{48,56},{56,48},{64,72... | collective-permute-start | bytes 9830408 | tf_op jit(solution)/shard_map/ppermute | solution.py:281
  126.3 6.3 %collective-permute-start.12 = (bf16[17,2048]{1,0:T(8,128)(2,1)S(1)}, bf16[17,2048]{1,0:T(8,128)(2,1)S(1)}, u32[]{:S(2)}, u32[]{:S(2)}) collective-permute-start(bf16[17,2048]{1,0:T(8,128)(2,1)S(1)} %collective-permute-done.11), channel_id=1, source_target_pairs={{0,448},{8,456},{16,464},{24,472},{32,480},{40,488},{48,496},{56,5... | collective-permute-start | bytes 208904 | tf_op jit(solution)/shard_map/ppermute | solution.py:133
  129.2 7.5 %collective-permute-start.15 = (bf16[17,2048]{1,0:T(8,128)(2,1)S(1)}, bf16[17,2048]{1,0:T(8,128)(2,1)S(1)}, u32[]{:S(2)}, u32[]{:S(2)}) collective-permute-start(bf16[17,2048]{1,0:T(8,128)(2,1)S(1)} %collective-permute-done.14), channel_id=1, source_target_pairs={{0,64},{8,72},{16,80},{24,88},{32,96},{40,104},{48,112},{56,120},{... | collective-permute-start | bytes 208904 | tf_op jit(solution)/shard_map/ppermute | solution.py:130
  132.6 12.6 %collective-permute-start.13 = (bf16[17,2048]{1,0:T(8,128)(2,1)S(1)}, bf16[17,2048]{1,0:T(8,128)(2,1)S(1)}, u32[]{:S(2)}, u32[]{:S(2)}) collective-permute-start(bf16[17,2048]{1,0:T(8,128)(2,1)S(1)} %collective-permute-done.12), channel_id=1, source_target_pairs={{0,448},{8,456},{16,464},{24,472},{32,480},{40,488},{48,496},{56,5... | collective-permute-start | bytes 208904 | tf_op jit(solution)/shard_map/ppermute | solution.py:133
  136.7 6.6 %collective-permute-start.16 = (bf16[17,2048]{1,0:T(8,128)(2,1)S(1)}, bf16[17,2048]{1,0:T(8,128)(2,1)S(1)}, u32[]{:S(2)}, u32[]{:S(2)}) collective-permute-start(bf16[17,2048]{1,0:T(8,128)(2,1)S(1)} %collective-permute-done.15), channel_id=1, source_target_pairs={{0,64},{8,72},{16,80},{24,88},{32,96},{40,104},{48,112},{56,120},{... | collective-permute-start | bytes 208904 | tf_op jit(solution)/shard_map/ppermute | solution.py:130
  143.2 6.6 %collective-permute-start.17 = (bf16[17,2048]{1,0:T(8,128)(2,1)S(1)}, bf16[17,2048]{1,0:T(8,128)(2,1)S(1)}, u32[]{:S(2)}, u32[]{:S(2)}) collective-permute-start(bf16[17,2048]{1,0:T(8,128)(2,1)S(1)} %collective-permute-done.16), channel_id=1, source_target_pairs={{0,64},{8,72},{16,80},{24,88},{32,96},{40,104},{48,112},{56,120},{... | collective-permute-start | bytes 208904 | tf_op jit(solution)/shard_map/ppermute | solution.py:130
  150.2 13.8 %collective-permute-start.19 = (bf16[8,17,2048]{2,0,1:T(8,128)(2,1)S(1)}, bf16[8,17,2048]{2,0,1:T(8,128)(2,1)S(1)}, u32[]{:S(2)}, u32[]{:S(2)}) collective-permute-start(bf16[8,17,2048]{2,0,1:T(8,128)(2,1)S(1)} %copy.285), channel_id=1, source_target_pairs={{0,16},{8,24},{16,32},{24,40},{32,48},{40,56},{48,0},{56,8},{64,80... | collective-permute-start | bytes 1671176 | tf_op jit(solution)/shard_map/ppermute | solution.py:130
  152.1 14.2 %collective-permute-start.18 = (bf16[8,17,2048]{2,0,1:T(8,128)(2,1)S(1)}, bf16[8,17,2048]{2,0,1:T(8,128)(2,1)S(1)}, u32[]{:S(2)}, u32[]{:S(2)}) collective-permute-start(bf16[8,17,2048]{2,0,1:T(8,128)(2,1)S(1)} %copy.285), channel_id=1, source_target_pairs={{0,48},{8,56},{16,0},{24,8},{32,16},{40,24},{48,32},{56,40},{64,11... | collective-permute-start | bytes 1671176 | tf_op jit(solution)/shard_map/ppermute | solution.py:133
  164.1 12.9 %collective-permute-start.20 = (bf16[8,17,2048]{2,0,1:T(8,128)(2,1)S(1)}, bf16[8,17,2048]{2,0,1:T(8,128)(2,1)S(1)}, u32[]{:S(2)}, u32[]{:S(2)}) collective-permute-start(bf16[8,17,2048]{2,0,1:T(8,128)(2,1)S(1)} %collective-permute-done.19), channel_id=1, source_target_pairs={{0,16},{8,24},{16,32},{24,40},{32,48},{40,56},{48,0},{56,8},{64,80... | collective-permute-start | bytes 1671176 | tf_op jit(solution)/shard_map/ppermute | solution.py:130
  188.9 22.0 %all-to-all-start.1 = ((f32[3,2,64,8]{3,1,0,2:T(2,128)}), f32[3,2,64,8]{3,1,0,2:T(2,128)S(1)}, u32[]{:S(2)}, u32[]{:S(2)}) async-start(f32[3,2,64,8]{3,1,0,2:T(2,128)} %copy.292), calls=%async_computation.1 | async-start | bytes 393216 | tf_op jit(solution)/shard_map/all_to_all | solution.py:319
  (12 other events, 81.1 us)

commit v14 on v13

--- a/solution.py
+++ b/solution.py
@@ -213,11 +213,11 @@
     inner_width = gated.shape[2] * groups
     squares = jnp.sum(gated * gated, axis=2)
     unscaled = (gated * norm_gain[:, None, :]).astype(jnp.bfloat16)
-    ring_weight = ring_gather(
-        ring_gather(ring_gather(out_weight, along_x, ROWS_X), along_z, chips_z),
-        along_core,
-        CORES,
-    )
+    near_weight = ring_gather(ring_gather(out_weight, along_x, ROWS_X), along_z, chips_z)
+    partner_weight, far_weight = lax.ppermute(
+        (head_weight, near_weight), "req", [(i, i ^ 1) for i in range(shards)]
+    )
+    ring_weight = jnp.stack([near_weight, far_weight])
     ring_weight = jnp.roll(
         jnp.roll(jnp.roll(ring_weight.transpose(1, 2, 0, 3, 4, 5), z_index, axis=0), x_index, axis=1),
         core_index,
@@ -277,10 +277,6 @@
     packet = jnp.concatenate([final_rows.reshape(models * row_count, full_width), target_row], axis=0)
 
     every = ring_gather(ring_gather(packet, along_z, chips_z), along_x, ROWS_X)
-    late_weight, _ = lax.optimization_barrier((head_weight, packet))
-    partner_weight = lax.ppermute(
-        late_weight, "req", [(i, i ^ 1) for i in range(shards)]
-    )
     peers = ROWS_X * chips_z
     every = every.reshape(peers, models * row_count + 1, full_width)
     every_rows = (

time: 213 us -> 205 us (0.962)
  waiting for transfers between devices: 69.1 us -> 63.5 us
    ppermute x13 -> x12, starting transfers between devices: 38 us -> 29 us  [ring_gather(): forward = lax.ppermute(forward, 'req', perm_of(1))]
    ppermute x1 -> x2, starting transfers between devices: 2.94 us -> 10.8 us  [local(): lax.ppermute((head_weight, near_weight), 'req', [(i, i ^ 1) for i in rang...]
    ppermute x13 -> x12, waiting for transfers between devices: 40.2 us -> 37.5 us  [ring_gather(): forward = lax.ppermute(forward, 'req', perm_of(1))]
    all_to_all x1, waiting for transfers between devices: 16 us -> 13.6 us  [local(): lax.all_to_all(payload.reshape(models, groups, row_count, payload.shape[2...]
  transfers between devices with their start and end apart: 24 -> 24, of which waited for: 12 -> 12; matrix products, arithmetic and copies ran while one was open for 15% -> 14% of each run, Pallas kernels for 0% -> 0%
where the time goes in v14:
time: 205 us; the launch traced here: 204 us
  starting transfers between devices  93.8 us (46%)
  waiting for transfers between devices  63.5 us (31%)
  other arithmetic  18.3 us (9%)
  matrix products  16.4 us (8%)
  local copies, waits for them, and re-layouts  10.8 us (5%)
    ppermute x12, waiting for transfers between devices, ring_gather(): forward = lax.ppermute(forward, 'req', perm_of(1))  37.5 us
    ppermute x8, starting transfers between devices, ring_gather(): backward = lax.ppermute(backward, 'req', perm_of(-1))  35.6 us
    ppermute x12, starting transfers between devices, ring_gather(): forward = lax.ppermute(forward, 'req', perm_of(1))  29 us
    all_to_all x1, waiting for transfers between devices, local(): lax.all_to_all(payload.reshape(models, groups, row_count, payload.shape[2...  13.6 us
    all_to_all x1, waiting for transfers between devices, local(): lax.all_to_all(send, 'req', split_axis=2, concat_axis=2, tiled=True)  11.9 us
    all_to_all x1, starting transfers between devices, local(): lax.all_to_all(send, 'req', split_axis=2, concat_axis=2, tiled=True)  11.6 us
    ppermute x2, starting transfers between devices, local(): lax.ppermute((head_weight, near_weight), 'req', [(i, i ^ 1) for i in rang...  10.8 us
    dot_general x2, matrix products, head_scores(): jnp.einsum('mnd,mvd->mnv', rows_hidden, head_weight, preferred_element_ty...  6.92 us
  transfers between devices with their start and end apart: 24, of which 12 were waited for; matrix products, arithmetic and copies ran while one was open for 14% of the time, Pallas kernels for 0%

profile of v14, /device:TPU:1, one launch (start us, length us, event | category | flops | bytes accessed | tf_op | source)
XLA Modules:
  0.0 204.2 jit_solution(4219830879167073790)
XLA Ops:
  0.1 4.1 %collective-permute-start.1 = (bf16[2,512,32]{1,2,0:T(8,128)(2,1)}, bf16[2,512,32]{1,2,0:T(8,128)(2,1)S(1)}, u32[]{:S(2)}, u32[]{:S(2)}) collective-permute-start(bf16[2,512,32]{1,2,0:T(8,128)(2,1)} %param.43), channel_id=1, source_target_pairs={{0,16},{8,24},{16,32},{24,40},{32,48},{40,56},{48,0},{56,8},{64,80... | collective-permute-start | bytes 196616 | tf_op jit(solution)/shard_map/ppermute | solution.py:130
  4.2 3.2 %collective-permute-start = (bf16[2,512,32]{1,2,0:T(8,128)(2,1)}, bf16[2,512,32]{1,2,0:T(8,128)(2,1)S(1)}, u32[]{:S(2)}, u32[]{:S(2)}) collective-permute-start(bf16[2,512,32]{1,2,0:T(8,128)(2,1)} %param.43), channel_id=1, source_target_pairs={{0,48},{8,56},{16,0},{24,8},{32,16},{40,24},{48,32},{56,40},{64,11... | collective-permute-start | bytes 196616 | tf_op jit(solution)/shard_map/ppermute | solution.py:133
  7.3 0.8 reduce-window.4
  8.2 0.7 compare_and_fusion
  8.8 0.7 fusion.166
  9.5 0.9 slice_convert_fusion.1
  10.5 0.9 slice_convert_fusion.3
  11.7 0.7 fusion.167
  12.3 0.8 fusion.175
  15.8 0.6 gather_fusion.1
  17.0 2.1 %collective-permute-start.2 = (bf16[2,512,32]{1,2,0:T(8,128)(2,1)S(1)}, bf16[2,512,32]{1,2,0:T(8,128)(2,1)S(1)}, u32[]{:S(2)}, u32[]{:S(2)}) collective-permute-start(bf16[2,512,32]{1,2,0:T(8,128)(2,1)S(1)} %collective-permute-done.1), channel_id=1, source_target_pairs={{0,16},{8,24},{16,32},{24,40},{32,48},{40,56},{48,0},{56,8},{64,80... | collective-permute-start | bytes 196616 | tf_op jit(solution)/shard_map/ppermute | solution.py:130
  19.1 1.0 fusion.10
  20.4 2.8 %collective-permute-done.2 = bf16[2,512,32]{1,2,0:T(8,128)(2,1)S(1)} collective-permute-done((bf16[2,512,32]{1,2,0:T(8,128)(2,1)S(1)}, bf16[2,512,32]{1,2,0:T(8,128)(2,1)S(1)}, u32[]{:S(2)}, u32[]{:S(2)}) %collective-permute-start.2) | collective-permute-done | bytes 65568 | tf_op jit(solution)/shard_map/ppermute | solution.py:130
  23.3 4.2 %collective-permute-start.6 = (bf16[4,2,512,32]{2,3,0,1:T(8,128)(2,1)S(1)}, bf16[4,2,512,32]{2,3,0,1:T(8,128)(2,1)S(1)}, u32[]{:S(2)}, u32[]{:S(2)}) collective-permute-start(bf16[4,2,512,32]{2,3,0,1:T(8,128)(2,1)S(1)} %pad_maximum_fusion.2), channel_id=1, source_target_pairs={{0,64},{8,72},{16,80},{24,88},{32,96},{40,104},{48,112},{56,120},{... | collective-permute-start | bytes 786440 | tf_op jit(solution)/shard_map/ppermute | solution.py:130
  27.5 0.7 fusion.12
  28.2 8.6 %collective-permute-start.3 = (bf16[4,2,512,32]{2,3,0,1:T(8,128)(2,1)S(1)}, bf16[4,2,512,32]{2,3,0,1:T(8,128)(2,1)S(1)}, u32[]{:S(2)}, u32[]{:S(2)}) collective-permute-start(bf16[4,2,512,32]{2,3,0,1:T(8,128)(2,1)S(1)} %pad_maximum_fusion.2), channel_id=1, source_target_pairs={{0,448},{8,456},{16,464},{24,472},{32,480},{40,488},{48,496},{56,5... | collective-permute-start | bytes 786440 | tf_op jit(solution)/shard_map/ppermute | solution.py:133
  37.0 1.4 collective-permute-done.6
  38.4 1.9 collective-permute-start.7
  40.5 4.6 %collective-permute-start.4 = (bf16[4,2,512,32]{2,3,0,1:T(8,128)(2,1)S(1)}, bf16[4,2,512,32]{2,3,0,1:T(8,128)(2,1)S(1)}, u32[]{:S(2)}, u32[]{:S(2)}) collective-permute-start(bf16[4,2,512,32]{2,3,0,1:T(8,128)(2,1)S(1)} %collective-permute-done.3), channel_id=1, source_target_pairs={{0,448},{8,456},{16,464},{24,472},{32,480},{40,488},{48,496},{56,5... | collective-permute-start | bytes 786440 | tf_op jit(solution)/shard_map/ppermute | solution.py:133
  45.4 1.2 collective-permute-done.7
  46.7 1.9 collective-permute-start.8
  48.6 4.8 %collective-permute-start.5 = (bf16[4,2,512,32]{2,3,0,1:T(8,128)(2,1)S(1)}, bf16[4,2,512,32]{2,3,0,1:T(8,128)(2,1)S(1)}, u32[]{:S(2)}, u32[]{:S(2)}) collective-permute-start(bf16[4,2,512,32]{2,3,0,1:T(8,128)(2,1)S(1)} %collective-permute-done.4), channel_id=1, source_target_pairs={{0,448},{8,456},{16,464},{24,472},{32,480},{40,488},{48,496},{56,5... | collective-permute-start | bytes 786440 | tf_op jit(solution)/shard_map/ppermute | solution.py:133
  53.4 1.6 collective-permute-done.8
  55.0 1.9 collective-permute-start.9
  57.0 6.3 %collective-permute-done.9 = bf16[4,2,512,32]{2,3,0,1:T(8,128)(2,1)S(1)} collective-permute-done((bf16[4,2,512,32]{2,3,0,1:T(8,128)(2,1)S(1)}, bf16[4,2,512,32]{2,3,0,1:T(8,128)(2,1)S(1)}, u32[]{:S(2)}, u32[]{:S(2)}) %collective-permute-start.9) | collective-permute-done | bytes 262176 | tf_op jit(solution)/shard_map/ppermute | solution.py:130
  63.4 8.4 %collective-permute-start.10 = (bf16[8,4,2,512,32]{3,4,1,0,2:T(8,128)(2,1)S(1)}, bf16[8,4,2,512,32]{3,4,1,0,2:T(8,128)(2,1)}, u32[]{:S(2)}, u32[]{:S(2)}) collective-permute-start(bf16[8,4,2,512,32]{3,4,1,0,2:T(8,128)(2,1)S(1)} %bitcast_dynamic-update-slice_fusion.7), channel_id=1, source_target_pairs={{0,8},{8,0},{16,24},{24,16},{32,40},{40,32},{48,56},{56,48},{64,72... | collective-permute-start | bytes 6291464 | tf_op jit(solution)/shard_map/ppermute | solution.py:217
  72.9 2.0 fusion.9
  75.1 0.6 gather_fusion
  76.1 0.7 fusion.14
  77.3 2.0 maximum_bitcast_fusion
  79.3 1.6 fusion.2
  80.9 1.6 fusion.1
  82.5 1.6 fusion
  84.1 1.4 convolution_convert_fusion
  85.5 0.9 copy.283
  86.4 6.8 %all-to-all-start = ((bf16[2,8,8,2432]{3,2,0,1:T(8,128)(2,1)}), bf16[2,8,8,2432]{3,2,0,1:T(8,128)(2,1)S(1)}, u32[]{:S(2)}, u32[]{:S(2)}) async-start(bf16[2,8,8,2432]{3,2,0,1:T(8,128)(2,1)} %copy.283), calls=%async_computation | async-start | bytes 1245184 | tf_op jit(solution)/shard_map/all_to_all | solution.py:244
  93.2 2.4 %collective-permute-start.21 = (bf16[2,400,2048]{2,1,0:T(8,128)(2,1)}, bf16[2,400,2048]{2,1,0:T(8,128)(2,1)}, u32[]{:S(2)}, u32[]{:S(2)}) collective-permute-start(bf16[2,400,2048]{2,1,0:T(8,128)(2,1)} %param.44), channel_id=1, source_target_pairs={{0,8},{8,0},{16,24},{24,16},{32,40},{40,32},{48,56},{56,48},{64,72... | collective-permute-start | bytes 9830408 | tf_op jit(solution)/shard_map/ppermute | solution.py:217
  95.6 0.6 slice.454
  96.2 0.6 and_reduce_fusion
  96.9 0.6 fusion.163
  97.5 1.3 broadcast_select_fusion
  98.9 0.9 scatter.19
  99.7 13.6 %all-to-all-done = bf16[2,8,8,2432]{3,2,0,1:T(8,128)(2,1)S(1)} async-done(((bf16[2,8,8,2432]{3,2,0,1:T(8,128)(2,1)}), bf16[2,8,8,2432]{3,2,0,1:T(8,128)(2,1)S(1)}, u32[]{:S(2)}, u32[]{:S(2)}) %all-to-all-start) | async-done | bytes 622624 | tf_op jit(solution)/shard_map/all_to_all | solution.py:244
  114.5 1.9 collective-permute-start.11
  116.5 3.4 %collective-permute-start.14 = (bf16[17,2048]{1,0:T(8,128)(2,1)S(1)}, bf16[17,2048]{1,0:T(8,128)(2,1)S(1)}, u32[]{:S(2)}, u32[]{:S(2)}) collective-permute-start(bf16[17,2048]{1,0:T(8,128)(2,1)S(1)} %pad_maximum_fusion.4), channel_id=1, source_target_pairs={{0,64},{8,72},{16,80},{24,88},{32,96},{40,104},{48,112},{56,120},{... | collective-permute-start | bytes 208904 | tf_op jit(solution)/shard_map/ppermute | solution.py:130
  120.3 3.4 %collective-permute-start.12 = (bf16[17,2048]{1,0:T(8,128)(2,1)S(1)}, bf16[17,2048]{1,0:T(8,128)(2,1)S(1)}, u32[]{:S(2)}, u32[]{:S(2)}) collective-permute-start(bf16[17,2048]{1,0:T(8,128)(2,1)S(1)} %collective-permute-done.11), channel_id=1, source_target_pairs={{0,448},{8,456},{16,464},{24,472},{32,480},{40,488},{48,496},{56,5... | collective-permute-start | bytes 208904 | tf_op jit(solution)/shard_map/ppermute | solution.py:133
  123.8 1.9 collective-permute-start.15
  125.8 4.6 %collective-permute-start.13 = (bf16[17,2048]{1,0:T(8,128)(2,1)S(1)}, bf16[17,2048]{1,0:T(8,128)(2,1)S(1)}, u32[]{:S(2)}, u32[]{:S(2)}) collective-permute-start(bf16[17,2048]{1,0:T(8,128)(2,1)S(1)} %collective-permute-done.12), channel_id=1, source_target_pairs={{0,448},{8,456},{16,464},{24,472},{32,480},{40,488},{48,496},{56,5... | collective-permute-start | bytes 208904 | tf_op jit(solution)/shard_map/ppermute | solution.py:133
  130.4 1.9 collective-permute-start.16
  132.3 4.6 %collective-permute-done.16 = bf16[17,2048]{1,0:T(8,128)(2,1)S(1)} collective-permute-done((bf16[17,2048]{1,0:T(8,128)(2,1)S(1)}, bf16[17,2048]{1,0:T(8,128)(2,1)S(1)}, u32[]{:S(2)}, u32[]{:S(2)}) %collective-permute-start.16) | collective-permute-done | bytes 69664 | tf_op jit(solution)/shard_map/ppermute | solution.py:130
  136.9 1.9 collective-permute-start.17
  138.9 4.6 %collective-permute-done.17 = bf16[17,2048]{1,0:T(8,128)(2,1)S(1)} collective-permute-done((bf16[17,2048]{1,0:T(8,128)(2,1)S(1)}, bf16[17,2048]{1,0:T(8,128)(2,1)S(1)}, u32[]{:S(2)}, u32[]{:S(2)}) %collective-permute-start.17) | collective-permute-done | bytes 69664 | tf_op jit(solution)/shard_map/ppermute | solution.py:130
  143.9 1.9 collective-permute-start.19
  145.8 4.6 %collective-permute-start.18 = (bf16[8,17,2048]{2,0,1:T(8,128)(2,1)S(1)}, bf16[8,17,2048]{2,0,1:T(8,128)(2,1)S(1)}, u32[]{:S(2)}, u32[]{:S(2)}) collective-permute-start(bf16[8,17,2048]{2,0,1:T(8,128)(2,1)S(1)} %copy.285), channel_id=1, source_target_pairs={{0,48},{8,56},{16,0},{24,8},{32,16},{40,24},{48,32},{56,40},{64,11... | collective-permute-start | bytes 1671176 | tf_op jit(solution)/shard_map/ppermute | solution.py:133
  150.4 6.0 %collective-permute-done.19 = bf16[8,17,2048]{2,0,1:T(8,128)(2,1)S(1)} collective-permute-done((bf16[8,17,2048]{2,0,1:T(8,128)(2,1)S(1)}, bf16[8,17,2048]{2,0,1:T(8,128)(2,1)S(1)}, u32[]{:S(2)}, u32[]{:S(2)}) %collective-permute-start.19) | collective-permute-done | bytes 557088 | tf_op jit(solution)/shard_map/ppermute | solution.py:130
  156.4 1.9 collective-permute-start.20
  159.0 8.9 %collective-permute-done.20 = bf16[8,17,2048]{2,0,1:T(8,128)(2,1)S(1)} collective-permute-done((bf16[8,17,2048]{2,0,1:T(8,128)(2,1)S(1)}, bf16[8,17,2048]{2,0,1:T(8,128)(2,1)S(1)}, u32[]{:S(2)}, u32[]{:S(2)}) %collective-permute-start.20) | collective-permute-done | bytes 557088 | tf_op jit(solution)/shard_map/ppermute | solution.py:130
  168.8 1.7 copy-done
  171.0 3.8 %fusion.183 = (f32[2,256]{1,0:T(2,128)S(1)}, f32[2,256,400]{1,2,0:T(8,128)S(1)}) fusion(bf16[2,400,2048]{2,1,0:T(8,128)(2,1)} %param.44, bf16[32,17,2048]{2,1,0:T(8,128)(2,1)} %bitcast.372), kind=kOutput, calls=%fused_computation.347 | convolution fusion | flops 839065088 | bytes 6195200 | tf_op jit(solution)/shard_map/mnd,mvd->mnv/dot_general | solution.py:115
  174.8 3.1 %fusion.184 = (f32[2,256]{1,0:T(2,128)S(1)}, f32[2,256,400]{1,2,0:T(8,128)S(1)}) fusion(bf16[2,400,2048]{2,1,0:T(8,128)(2,1)} %collective-permute-done.21, bf16[32,17,2048]{2,1,0:T(8,128)(2,1)S(1)} %bitcast.373), kind=kOutput, calls=%fused_computation.348 | convolution fusion | flops 839065088 | bytes 6195200 | tf_op jit(solution)/shard_map/mnd,mvd->mnv/dot_general | solution.py:115
  179.0 0.8 copy.292
  179.8 11.6 %all-to-all-start.1 = ((f32[3,2,64,8]{3,1,0,2:T(2,128)}), f32[3,2,64,8]{3,1,0,2:T(2,128)S(1)}, u32[]{:S(2)}, u32[]{:S(2)}) async-start(f32[3,2,64,8]{3,1,0,2:T(2,128)} %copy.292), calls=%async_computation.1 | async-start | bytes 393216 | tf_op jit(solution)/shard_map/all_to_all | solution.py:315
  191.5 11.9 %all-to-all-done.1 = f32[3,2,64,8]{3,1,0,2:T(2,128)S(1)} async-done(((f32[3,2,64,8]{3,1,0,2:T(2,128)}), f32[3,2,64,8]{3,1,0,2:T(2,128)S(1)}, u32[]{:S(2)}, u32[]{:S(2)}) %all-to-all-start.1) | async-done | bytes 12320 | tf_op jit(solution)/shard_map/all_to_all | solution.py:315
  203.6 0.6 subtract_multiply_fusion
  (172 shorter events, 12.2 us)
Async XLA Ops:
  0.0 16.7 %copy-start.3 = (bf16[2,64,512]{2,1,0:T(8,128)(2,1)S(1)}, bf16[2,64,512]{2,1,0:T(8,128)(2,1)}, u32[]{:S(2)}) copy-start(bf16[2,64,512]{2,1,0:T(8,128)(2,1)} %param.32) | copy-start | bytes 393220
  0.0 14.4 %copy-start.6 = (bf16[2,64,256]{2,1,0:T(8,128)(2,1)S(1)}, bf16[2,64,256]{2,1,0:T(8,128)(2,1)}, u32[]{:S(2)}) copy-start(bf16[2,64,256]{2,1,0:T(8,128)(2,1)} %param.33) | copy-start | bytes 196612
  0.0 13.8 %copy-start.9 = (f32[2,4,512]{2,1,0:T(4,128)S(1)}, f32[2,4,512]{2,1,0:T(4,128)}, u32[]{:S(2)}) copy-start(f32[2,4,512]{2,1,0:T(4,128)} %param.36) | copy-start | bytes 49156
  0.0 13.9 %copy-start.8 = (bf16[2,3,3,256]{3,0,2,1:T(2,128)(2,1)S(1)}, bf16[2,3,3,256]{3,0,2,1:T(2,128)(2,1)}, u32[]{:S(2)}) copy-start(bf16[2,3,3,256]{3,0,2,1:T(2,128)(2,1)} %param.46) | copy-start | bytes 27652
  0.0 14.4 %copy-start.12 = (f32[2,4,256]{2,1,0:T(4,128)S(1)}, f32[2,4,256]{2,1,0:T(4,128)}, u32[]{:S(2)}) copy-start(f32[2,4,256]{2,1,0:T(4,128)} %param.37) | copy-start | bytes 24580
  0.0 14.9 %copy-start.17 = (f32[2,8]{1,0:T(2,128)S(1)}, f32[2,8]{1,0:T(2,128)}, u32[]{:S(2)}) copy-start(f32[2,8]{1,0:T(2,128)} %param.38) | copy-start | bytes 196
  0.0 14.9 %copy-start.16 = (f32[2,8]{1,0:T(2,128)S(1)}, f32[2,8]{1,0:T(2,128)}, u32[]{:S(2)}) copy-start(f32[2,8]{1,0:T(2,128)} %param.39) | copy-start | bytes 196
  0.0 14.9 %copy-start.10 = (bf16[2,64,8]{1,2,0:T(8,128)(2,1)S(1)}, bf16[2,64,8]{1,2,0:T(8,128)(2,1)}, u32[]{:S(2)}) copy-start(bf16[2,64,8]{1,2,0:T(8,128)(2,1)} %param.34) | copy-start | bytes 6148
  0.1 17.0 %collective-permute-start.1 = (bf16[2,512,32]{1,2,0:T(8,128)(2,1)}, bf16[2,512,32]{1,2,0:T(8,128)(2,1)S(1)}, u32[]{:S(2)}, u32[]{:S(2)}) collective-permute-start(bf16[2,512,32]{1,2,0:T(8,128)(2,1)} %param.43), channel_id=1, source_target_pairs={{0,16},{8,24},{16,32},{24,40},{32,48},{40,56},{48,0},{56,8},{64,80... | collective-permute-start | bytes 196616 | tf_op jit(solution)/shard_map/ppermute | solution.py:130
  4.2 16.3 %collective-permute-start = (bf16[2,512,32]{1,2,0:T(8,128)(2,1)}, bf16[2,512,32]{1,2,0:T(8,128)(2,1)S(1)}, u32[]{:S(2)}, u32[]{:S(2)}) collective-permute-start(bf16[2,512,32]{1,2,0:T(8,128)(2,1)} %param.43), channel_id=1, source_target_pairs={{0,48},{8,56},{16,0},{24,8},{32,16},{40,24},{48,32},{56,40},{64,11... | collective-permute-start | bytes 196616 | tf_op jit(solution)/shard_map/ppermute | solution.py:133
  10.4 6.6 %copy-start.15 = (f32[2,8]{1,0:T(2,128)S(1)}, f32[2,8]{1,0:T(2,128)}, u32[]{:S(2)}) copy-start(f32[2,8]{1,0:T(2,128)} %param.40) | copy-start | bytes 196
  10.5 8.7 %copy-start.18 = (bf16[2,3,512,128]{3,2,1,0:T(8,128)(2,1)S(1)}, bf16[2,3,512,128]{3,2,1,0:T(8,128)(2,1)}, u32[]{:S(2)}) copy-start(bf16[2,3,512,128]{3,2,1,0:T(8,128)(2,1)} %param.47) | copy-start | bytes 2359300
  11.4 11.8 %copy-start.2 = (bf16[2,512,32]{1,2,0:T(8,128)(2,1)S(1)}, bf16[2,512,32]{1,2,0:T(8,128)(2,1)}, u32[]{:S(2)}) copy-start(bf16[2,512,32]{1,2,0:T(8,128)(2,1)} %param.43) | copy-start | bytes 196612
  17.0 6.2 %collective-permute-start.2 = (bf16[2,512,32]{1,2,0:T(8,128)(2,1)S(1)}, bf16[2,512,32]{1,2,0:T(8,128)(2,1)S(1)}, u32[]{:S(2)}, u32[]{:S(2)}) collective-permute-start(bf16[2,512,32]{1,2,0:T(8,128)(2,1)S(1)} %collective-permute-done.1), channel_id=1, source_target_pairs={{0,16},{8,24},{16,32},{24,40},{32,48},{40,56},{48,0},{56,8},{64,80... | collective-permute-start | bytes 196616 | tf_op jit(solution)/shard_map/ppermute | solution.py:130
  23.3 15.1 %collective-permute-start.6 = (bf16[4,2,512,32]{2,3,0,1:T(8,128)(2,1)S(1)}, bf16[4,2,512,32]{2,3,0,1:T(8,128)(2,1)S(1)}, u32[]{:S(2)}, u32[]{:S(2)}) collective-permute-start(bf16[4,2,512,32]{2,3,0,1:T(8,128)(2,1)S(1)} %pad_maximum_fusion.2), channel_id=1, source_target_pairs={{0,64},{8,72},{16,80},{24,88},{32,96},{40,104},{48,112},{56,120},{... | collective-permute-start | bytes 786440 | tf_op jit(solution)/shard_map/ppermute | solution.py:130
  28.2 12.4 %collective-permute-start.3 = (bf16[4,2,512,32]{2,3,0,1:T(8,128)(2,1)S(1)}, bf16[4,2,512,32]{2,3,0,1:T(8,128)(2,1)S(1)}, u32[]{:S(2)}, u32[]{:S(2)}) collective-permute-start(bf16[4,2,512,32]{2,3,0,1:T(8,128)(2,1)S(1)} %pad_maximum_fusion.2), channel_id=1, source_target_pairs={{0,448},{8,456},{16,464},{24,472},{32,480},{40,488},{48,496},{56,5... | collective-permute-start | bytes 786440 | tf_op jit(solution)/shard_map/ppermute | solution.py:133
  38.4 8.3 %collective-permute-start.7 = (bf16[4,2,512,32]{2,3,0,1:T(8,128)(2,1)S(1)}, bf16[4,2,512,32]{2,3,0,1:T(8,128)(2,1)S(1)}, u32[]{:S(2)}, u32[]{:S(2)}) collective-permute-start(bf16[4,2,512,32]{2,3,0,1:T(8,128)(2,1)S(1)} %collective-permute-done.6), channel_id=1, source_target_pairs={{0,64},{8,72},{16,80},{24,88},{32,96},{40,104},{48,112},{56,120},{... | collective-permute-start | bytes 786440 | tf_op jit(solution)/shard_map/ppermute | solution.py:130
  40.5 8.1 %collective-permute-start.4 = (bf16[4,2,512,32]{2,3,0,1:T(8,128)(2,1)S(1)}, bf16[4,2,512,32]{2,3,0,1:T(8,128)(2,1)S(1)}, u32[]{:S(2)}, u32[]{:S(2)}) collective-permute-start(bf16[4,2,512,32]{2,3,0,1:T(8,128)(2,1)S(1)} %collective-permute-done.3), channel_id=1, source_target_pairs={{0,448},{8,456},{16,464},{24,472},{32,480},{40,488},{48,496},{56,5... | collective-permute-start | bytes 786440 | tf_op jit(solution)/shard_map/ppermute | solution.py:133
  46.7 8.3 %collective-permute-start.8 = (bf16[4,2,512,32]{2,3,0,1:T(8,128)(2,1)S(1)}, bf16[4,2,512,32]{2,3,0,1:T(8,128)(2,1)S(1)}, u32[]{:S(2)}, u32[]{:S(2)}) collective-permute-start(bf16[4,2,512,32]{2,3,0,1:T(8,128)(2,1)S(1)} %collective-permute-done.7), channel_id=1, source_target_pairs={{0,64},{8,72},{16,80},{24,88},{32,96},{40,104},{48,112},{56,120},{... | collective-permute-start | bytes 786440 | tf_op jit(solution)/shard_map/ppermute | solution.py:130
  48.6 8.3 %collective-permute-start.5 = (bf16[4,2,512,32]{2,3,0,1:T(8,128)(2,1)S(1)}, bf16[4,2,512,32]{2,3,0,1:T(8,128)(2,1)S(1)}, u32[]{:S(2)}, u32[]{:S(2)}) collective-permute-start(bf16[4,2,512,32]{2,3,0,1:T(8,128)(2,1)S(1)} %collective-permute-done.4), channel_id=1, source_target_pairs={{0,448},{8,456},{16,464},{24,472},{32,480},{40,488},{48,496},{56,5... | collective-permute-start | bytes 786440 | tf_op jit(solution)/shard_map/ppermute | solution.py:133
  55.0 8.3 %collective-permute-start.9 = (bf16[4,2,512,32]{2,3,0,1:T(8,128)(2,1)S(1)}, bf16[4,2,512,32]{2,3,0,1:T(8,128)(2,1)S(1)}, u32[]{:S(2)}, u32[]{:S(2)}) collective-permute-start(bf16[4,2,512,32]{2,3,0,1:T(8,128)(2,1)S(1)} %collective-permute-done.8), channel_id=1, source_target_pairs={{0,64},{8,72},{16,80},{24,88},{32,96},{40,104},{48,112},{56,120},{... | collective-permute-start | bytes 786440 | tf_op jit(solution)/shard_map/ppermute | solution.py:130
  63.3 13.6 %copy-start.4 = (bf16[2,64,512]{2,1,0:T(8,128)(2,1)S(1)}, bf16[2,64,512]{2,1,0:T(8,128)(2,1)}, u32[]{:S(2)}) copy-start(bf16[2,64,512]{2,1,0:T(8,128)(2,1)} %param.31) | copy-start | bytes 393220
  63.4 13.9 %collective-permute-start.10 = (bf16[8,4,2,512,32]{3,4,1,0,2:T(8,128)(2,1)S(1)}, bf16[8,4,2,512,32]{3,4,1,0,2:T(8,128)(2,1)}, u32[]{:S(2)}, u32[]{:S(2)}) collective-permute-start(bf16[8,4,2,512,32]{3,4,1,0,2:T(8,128)(2,1)S(1)} %bitcast_dynamic-update-slice_fusion.7), channel_id=1, source_target_pairs={{0,8},{8,0},{16,24},{24,16},{32,40},{40,32},{48,56},{56,48},{64,72... | collective-permute-start | bytes 6291464 | tf_op jit(solution)/shard_map/ppermute | solution.py:217
  82.5 1.6 copy-start.13
  84.0 1.4 copy-start.7
  84.1 12.8 %copy-start.14 = (s32[64]{0:T(128)S(1)}, s32[64]{0:T(128)}, u32[]{:S(2)}) copy-start(s32[64]{0:T(128)} %param.50) | copy-start | bytes 772
  85.5 28.9 %copy-start.11 = (f32[2,2048]{1,0:T(2,128)S(1)}, f32[2,2048]{1,0:T(2,128)}, u32[]{:S(2)}) copy-start(f32[2,2048]{1,0:T(2,128)} %param.42) | copy-start | bytes 49156
  86.4 27.0 %all-to-all-start = ((bf16[2,8,8,2432]{3,2,0,1:T(8,128)(2,1)}), bf16[2,8,8,2432]{3,2,0,1:T(8,128)(2,1)S(1)}, u32[]{:S(2)}, u32[]{:S(2)}) async-start(bf16[2,8,8,2432]{3,2,0,1:T(8,128)(2,1)} %copy.283), calls=%async_computation | async-start | bytes 1245184 | tf_op jit(solution)/shard_map/all_to_all | solution.py:244
  93.2 81.5 %collective-permute-start.21 = (bf16[2,400,2048]{2,1,0:T(8,128)(2,1)}, bf16[2,400,2048]{2,1,0:T(8,128)(2,1)}, u32[]{:S(2)}, u32[]{:S(2)}) collective-permute-start(bf16[2,400,2048]{2,1,0:T(8,128)(2,1)} %param.44), channel_id=1, source_target_pairs={{0,8},{8,0},{16,24},{24,16},{32,40},{40,32},{48,56},{56,48},{64,72... | collective-permute-start | bytes 9830408 | tf_op jit(solution)/shard_map/ppermute | solution.py:217
  114.5 5.8 %collective-permute-start.11 = (bf16[17,2048]{1,0:T(8,128)(2,1)S(1)}, bf16[17,2048]{1,0:T(8,128)(2,1)S(1)}, u32[]{:S(2)}, u32[]{:S(2)}) collective-permute-start(bf16[17,2048]{1,0:T(8,128)(2,1)S(1)} %pad_maximum_fusion.4), channel_id=1, source_target_pairs={{0,448},{8,456},{16,464},{24,472},{32,480},{40,488},{48,496},{56,5... | collective-permute-start | bytes 208904 | tf_op jit(solution)/shard_map/ppermute | solution.py:133
  116.5 7.3 %collective-permute-start.14 = (bf16[17,2048]{1,0:T(8,128)(2,1)S(1)}, bf16[17,2048]{1,0:T(8,128)(2,1)S(1)}, u32[]{:S(2)}, u32[]{:S(2)}) collective-permute-start(bf16[17,2048]{1,0:T(8,128)(2,1)S(1)} %pad_maximum_fusion.4), channel_id=1, source_target_pairs={{0,64},{8,72},{16,80},{24,88},{32,96},{40,104},{48,112},{56,120},{... | collective-permute-start | bytes 208904 | tf_op jit(solution)/shard_map/ppermute | solution.py:130
  120.3 5.4 %collective-permute-start.12 = (bf16[17,2048]{1,0:T(8,128)(2,1)S(1)}, bf16[17,2048]{1,0:T(8,128)(2,1)S(1)}, u32[]{:S(2)}, u32[]{:S(2)}) collective-permute-start(bf16[17,2048]{1,0:T(8,128)(2,1)S(1)} %collective-permute-done.11), channel_id=1, source_target_pairs={{0,448},{8,456},{16,464},{24,472},{32,480},{40,488},{48,496},{56,5... | collective-permute-start | bytes 208904 | tf_op jit(solution)/shard_map/ppermute | solution.py:133
  123.8 6.6 %collective-permute-start.15 = (bf16[17,2048]{1,0:T(8,128)(2,1)S(1)}, bf16[17,2048]{1,0:T(8,128)(2,1)S(1)}, u32[]{:S(2)}, u32[]{:S(2)}) collective-permute-start(bf16[17,2048]{1,0:T(8,128)(2,1)S(1)} %collective-permute-done.14), channel_id=1, source_target_pairs={{0,64},{8,72},{16,80},{24,88},{32,96},{40,104},{48,112},{56,120},{... | collective-permute-start | bytes 208904 | tf_op jit(solution)/shard_map/ppermute | solution.py:130
  125.8 13.1 %collective-permute-start.13 = (bf16[17,2048]{1,0:T(8,128)(2,1)S(1)}, bf16[17,2048]{1,0:T(8,128)(2,1)S(1)}, u32[]{:S(2)}, u32[]{:S(2)}) collective-permute-start(bf16[17,2048]{1,0:T(8,128)(2,1)S(1)} %collective-permute-done.12), channel_id=1, source_target_pairs={{0,448},{8,456},{16,464},{24,472},{32,480},{40,488},{48,496},{56,5... | collective-permute-start | bytes 208904 | tf_op jit(solution)/shard_map/ppermute | solution.py:133
  130.4 6.6 %collective-permute-start.16 = (bf16[17,2048]{1,0:T(8,128)(2,1)S(1)}, bf16[17,2048]{1,0:T(8,128)(2,1)S(1)}, u32[]{:S(2)}, u32[]{:S(2)}) collective-permute-start(bf16[17,2048]{1,0:T(8,128)(2,1)S(1)} %collective-permute-done.15), channel_id=1, source_target_pairs={{0,64},{8,72},{16,80},{24,88},{32,96},{40,104},{48,112},{56,120},{... | collective-permute-start | bytes 208904 | tf_op jit(solution)/shard_map/ppermute | solution.py:130
  136.9 6.6 %collective-permute-start.17 = (bf16[17,2048]{1,0:T(8,128)(2,1)S(1)}, bf16[17,2048]{1,0:T(8,128)(2,1)S(1)}, u32[]{:S(2)}, u32[]{:S(2)}) collective-permute-start(bf16[17,2048]{1,0:T(8,128)(2,1)S(1)} %collective-permute-done.16), channel_id=1, source_target_pairs={{0,64},{8,72},{16,80},{24,88},{32,96},{40,104},{48,112},{56,120},{... | collective-permute-start | bytes 208904 | tf_op jit(solution)/shard_map/ppermute | solution.py:130
  143.9 12.5 %collective-permute-start.19 = (bf16[8,17,2048]{2,0,1:T(8,128)(2,1)S(1)}, bf16[8,17,2048]{2,0,1:T(8,128)(2,1)S(1)}, u32[]{:S(2)}, u32[]{:S(2)}) collective-permute-start(bf16[8,17,2048]{2,0,1:T(8,128)(2,1)S(1)} %copy.285), channel_id=1, source_target_pairs={{0,16},{8,24},{16,32},{24,40},{32,48},{40,56},{48,0},{56,8},{64,80... | collective-permute-start | bytes 1671176 | tf_op jit(solution)/shard_map/ppermute | solution.py:130
  145.8 12.8 %collective-permute-start.18 = (bf16[8,17,2048]{2,0,1:T(8,128)(2,1)S(1)}, bf16[8,17,2048]{2,0,1:T(8,128)(2,1)S(1)}, u32[]{:S(2)}, u32[]{:S(2)}) collective-permute-start(bf16[8,17,2048]{2,0,1:T(8,128)(2,1)S(1)} %copy.285), channel_id=1, source_target_pairs={{0,48},{8,56},{16,0},{24,8},{32,16},{40,24},{48,32},{56,40},{64,11... | collective-permute-start | bytes 1671176 | tf_op jit(solution)/shard_map/ppermute | solution.py:133
  156.4 11.5 %collective-permute-start.20 = (bf16[8,17,2048]{2,0,1:T(8,128)(2,1)S(1)}, bf16[8,17,2048]{2,0,1:T(8,128)(2,1)S(1)}, u32[]{:S(2)}, u32[]{:S(2)}) collective-permute-start(bf16[8,17,2048]{2,0,1:T(8,128)(2,1)S(1)} %collective-permute-done.19), channel_id=1, source_target_pairs={{0,16},{8,24},{16,32},{24,40},{32,48},{40,56},{48,0},{56,8},{64,80... | collective-permute-start | bytes 1671176 | tf_op jit(solution)/shard_map/ppermute | solution.py:130
  168.8 1.7 copy-start
  170.9 3.8 %copy-start.1 = (bf16[4,8,17,2048]{3,2,1,0:T(8,128)(2,1)S(1)}, bf16[4,8,17,2048]{3,2,1,0:T(8,128)(2,1)}, u32[]{:S(2)}) copy-start(bf16[4,8,17,2048]{3,2,1,0:T(8,128)(2,1)} %copy-done) | copy-start | bytes 6684676
  174.7 4.0 %copy-start.5 = (f32[3,2,8,4,8]{4,2,3,1,0:T(8,128)S(1)}, f32[3,2,8,4,8]{4,2,3,1,0:T(8,128)}, u32[]{:S(2)}) copy-start(f32[3,2,8,4,8]{4,2,3,1,0:T(8,128)} %constant.319.clone.1) | copy-start | bytes 18436
  177.9 13.5 %copy-start.19 = (s32[64]{0:T(128)S(1)}, s32[64]{0:T(128)}, u32[]{:S(2)}) copy-start(s32[64]{0:T(128)} %param.51) | copy-start | bytes 772
  179.8 23.6 %all-to-all-start.1 = ((f32[3,2,64,8]{3,1,0,2:T(2,128)}), f32[3,2,64,8]{3,1,0,2:T(2,128)S(1)}, u32[]{:S(2)}, u32[]{:S(2)}) async-start(f32[3,2,64,8]{3,1,0,2:T(2,128)} %copy.292), calls=%async_computation.1 | async-start | bytes 393216 | tf_op jit(solution)/shard_map/all_to_all | solution.py:315
